TPU v7x, 32 devices: a whole 2x2x4 slice. The times are simulated.
32 devices in a mesh: store: 8 (over z, y), tp: 4 (over x, core).
Axes of the slice: x: 2, y: 2, z: 4, core: 2. Of those that a mesh axis runs over, the one named last changes fastest.
Arguments:
- query_embeds: bfloat16 [16, 16, 4096], P('store', None, 'tp'), may hold values from -6 to 6
- passage_embeds: bfloat16 [16, 32, 4096], P('store', None, 'tp'), may hold values from -6 to 6
- passage_lengths: int32 [16], P('store'), may hold values from 1 to 32, as said below
- cand_passage: int32 [192], P('store'), may hold values from 0 to 15, as said below
- norm_gain: bfloat16 [4096], replicated, may hold values from 0.099609375 to 1.8984375
- w_qkv: bfloat16 [4096, 16, 384], P(None, 'tp'), may hold values from -1 to 1
Outputs:
- query_attn: bfloat16 [16, 16, 2048], P('store', None, 'tp')
- passage_attn: bfloat16 [192, 32, 2048], P('store', None, 'tp')
Inputs may be any that keep to these rules, and one draw needn't show every extreme that they name: `cand_passage`: passage id p is held by store index p // 2 at position p % 2. Among the 24 pairs of one store index, the passages come from as many different store indices as possible, and no store index holds the passages of more than 3 of them. `passage_lengths`: some passage has 32 tokens.
All inputs are finite; a program needn't handle non-finite values.
Results may differ from a plain program's by a relative error of at most 0.023.
The roundings to bfloat16 on the way count: a program that leaves them out, or rounds other values in their place, can miss the bound.
Values may be sent and summed in bfloat16 or wider, within the bound.
No kernel may reach another device: no remote copies, remote signals or barrier semaphores. Data moves between devices by JAX's collectives and lax.ppermute only.
A program may use at most 128 MiB of HBM per device.

v0:
```python
import math

import jax
import jax.numpy as jnp
from jax import lax
from jax.sharding import PartitionSpec as P


def rms_rows(rows, norm_gain):
    values = rows.astype(jnp.float32)
    meansq = jnp.mean(values * values, axis=-1, keepdims=True)
    scaled = values * lax.rsqrt(meansq + 1e-05) * norm_gain.astype(jnp.float32)
    return scaled.astype(jnp.bfloat16)


def rotate_parts(raw, positions, head_dim):
    half_dim = head_dim // 2
    inverse = jnp.exp(
        jnp.arange(half_dim, dtype=jnp.float32) * (-2.0 * math.log(10000.0) / head_dim)
    )
    angles = positions[:, None] * inverse[None, :]
    cosine = jnp.cos(angles)[:, None, :]
    sine_part = jnp.sin(angles)[:, None, :]

    def turned(block):
        first = block[..., :half_dim]
        second = block[..., half_dim:]
        return jnp.concatenate(
            [first * cosine - second * sine_part, second * cosine + first * sine_part], axis=-1
        )

    queries = turned(raw[..., :head_dim])
    keyset = turned(raw[..., head_dim : 2 * head_dim])
    values = raw[..., 2 * head_dim :]
    return jnp.concatenate([queries, keyset, values], axis=-1).astype(jnp.bfloat16)


def softmax_rounded(scores, allowed):
    masked = jnp.where(allowed, scores, jnp.float32(-1e30))
    peak = jnp.max(masked, axis=-1, keepdims=True)
    expon = jnp.where(allowed, jnp.exp(masked - peak), jnp.float32(0.0))
    return (expon / jnp.sum(expon, axis=-1, keepdims=True)).astype(jnp.bfloat16)


def attend_queries(query_qkv, head_dim):
    count, query_len, heads = (query_qkv.shape[0], query_qkv.shape[1], query_qkv.shape[2])
    scale = head_dim ** (-0.5)
    scores = (
        jnp.einsum(
            "bqhd,bkhd->bhqk",
            query_qkv[..., :head_dim],
            query_qkv[..., head_dim : 2 * head_dim],
            preferred_element_type=jnp.float32,
        )
        * scale
    )
    steps_row = jnp.arange(query_len, dtype=jnp.int32)
    allowed = steps_row[:, None] >= steps_row[None, :]
    weights = softmax_rounded(scores, allowed[None, None])
    output = jnp.einsum(
        "bhqk,bkhd->bqhd",
        weights,
        query_qkv[..., 2 * head_dim :],
        preferred_element_type=jnp.float32,
    )
    return output.reshape(count, query_len, heads * head_dim).astype(jnp.bfloat16)


def attend_core(query_kv, pair_qkv, pair_lengths, head_dim):
    query_len = query_kv.shape[1]
    pairs, passage_len, heads = (pair_qkv.shape[0], pair_qkv.shape[1], pair_qkv.shape[2])
    scale = head_dim ** (-0.5)
    keyset = jnp.concatenate(
        [query_kv[..., :head_dim], pair_qkv[..., head_dim : 2 * head_dim]], axis=1
    )
    values = jnp.concatenate([query_kv[..., head_dim:], pair_qkv[..., 2 * head_dim :]], axis=1)
    scores = (
        jnp.einsum(
            "bihd,bthd->bhit", pair_qkv[..., :head_dim], keyset, preferred_element_type=jnp.float32
        )
        * scale
    )
    column = jnp.arange(query_len + passage_len, dtype=jnp.int32) - query_len
    row_index = jnp.arange(passage_len, dtype=jnp.int32)
    allowed = (column[None, None, :] < 0) | (column[None, None, :] <= row_index[None, :, None]) & (
        column[None, None, :] < pair_lengths[:, None, None]
    )
    weights = softmax_rounded(scores, allowed[:, None])
    output = jnp.einsum("bhit,bthd->bihd", weights, values, preferred_element_type=jnp.float32)
    live = row_index[None, :] < pair_lengths[:, None]
    output = jnp.where(live[:, :, None, None], output, jnp.float32(0.0))
    return output.reshape(pairs, passage_len, heads * head_dim).astype(jnp.bfloat16)


def attend_pairs(query_qkv, pair_qkv, pair_lengths, head_dim, cands):
    repeated = jnp.repeat(query_qkv[..., head_dim:], cands, axis=0)
    return attend_core(repeated, pair_qkv, pair_lengths, head_dim)


def local(query_embeds, passage_embeds, passage_lengths, cand_passage, norm_gain, w_qkv):
    n_store = lax.axis_size("store")
    quer_count, query_len, width_part = query_embeds.shape
    pass_count, passage_len = (passage_embeds.shape[0], passage_embeds.shape[1])
    pairs_dev = cand_passage.shape[0]
    cands = pairs_dev // quer_count
    heads_part = w_qkv.shape[1]
    head_dim = w_qkv.shape[2] // 3
    capacity = (pairs_dev + n_store - 1) // n_store
    weights_flat = w_qkv.reshape(w_qkv.shape[0], heads_part * 3 * head_dim)
    query_rows = query_embeds.reshape(quer_count * query_len, width_part)
    query_pos = jnp.tile(jnp.arange(query_len, dtype=jnp.float32), quer_count)
    query_total = quer_count * query_len
    holder = cand_passage // pass_count
    same_holder = holder[:, None] == holder[None, :]
    pair_index = jnp.arange(pairs_dev, dtype=jnp.int32)
    earlier = pair_index[:, None] < pair_index[None, :]
    rank_in = jnp.sum((same_holder & earlier).astype(jnp.int32), axis=0)
    slot_code = cand_passage % pass_count + 1
    hits = (holder[:, None, None] == jnp.arange(n_store, dtype=jnp.int32)[None, :, None]) & (
        rank_in[:, None, None] == jnp.arange(capacity, dtype=jnp.int32)[None, None, :]
    )
    request = jnp.sum(jnp.where(hits, slot_code[:, None, None], 0), axis=0)
    flat_index = holder * capacity + rank_in
    hits, request, flat_index = (hits, request, flat_index)
    incoming = lax.all_to_all(request, "store", split_axis=0, concat_axis=0, tiled=True)
    chosen = jnp.maximum(incoming - 1, 0)
    filled = incoming > 0
    outgoing = jnp.where(
        filled[:, :, None, None], passage_embeds[chosen], jnp.zeros((), passage_embeds.dtype)
    )
    out_len = jnp.where(filled, passage_lengths[chosen], 0)
    arrived = lax.all_to_all(outgoing, "store", split_axis=0, concat_axis=0, tiled=True)
    arrived_len = lax.all_to_all(out_len, "store", split_axis=0, concat_axis=0, tiled=True)
    flat_rows = arrived.reshape((n_store * capacity,) + passage_embeds.shape[1:])
    fetched = flat_rows[flat_index]
    pair_lengths = arrived_len.reshape(n_store * capacity)[flat_index]
    pair_pos = query_len + jnp.tile(jnp.arange(passage_len, dtype=jnp.float32), pairs_dev)
    all_rows = jnp.concatenate(
        [query_rows, fetched.reshape(pairs_dev * passage_len, width_part)], axis=0
    )
    full_rows = lax.all_gather(all_rows, "tp", axis=1, tiled=True)
    normed = rms_rows(full_rows, norm_gain)
    raw = jnp.dot(normed, weights_flat, preferred_element_type=jnp.float32)
    raw = raw.reshape(all_rows.shape[0], heads_part, 3 * head_dim)
    projected = rotate_parts(raw, jnp.concatenate([query_pos, pair_pos], axis=0), head_dim)
    query_qkv = projected[:query_total].reshape(quer_count, query_len, heads_part, 3 * head_dim)
    pair_qkv = projected[query_total:].reshape(pairs_dev, passage_len, heads_part, 3 * head_dim)
    query_attn = attend_queries(query_qkv, head_dim)
    passage_attn = attend_pairs(query_qkv, pair_qkv, pair_lengths, head_dim, cands)
    return (query_attn, passage_attn)


def solution(mesh):
    in_specs = (
        P("store", None, "tp"),
        P("store", None, "tp"),
        P("store"),
        P("store"),
        P(),
        P(None, "tp", None),
    )
    out_specs = (P("store", None, "tp"), P("store", None, "tp"))
    return jax.shard_map(local, mesh=mesh, in_specs=in_specs, out_specs=out_specs, check_vma=False)
```

profile of v0, /device:TPU:0, one launch (start us, length us, event | category | flops | bytes accessed | tf_op | source)
XLA Modules:
  0.0 157.3 jit_solution(15582942936683200685)
XLA Ops:
  7.2 0.7 and_select_fusion.1
  8.2 13.6 %all_to_all.20 = s32[8,1,3]{2,1,0:T(1,128)S(1)} all-to-all(s32[8,1,3]{2,1,0:T(1,128)S(1)} %copy.53), channel_id=1, replica_groups=mesh['store'=8,'tp'=4] {'store'}, dimensions={0} | all-to-all | bytes 192 | tf_op jit(solution)/shard_map/all_to_all | solution.py:125
  22.6 0.7 gather_fusion.2
  24.0 1.3 broadcast_select_fusion
  25.3 3.6 %all-to-all-start.1 = ((bf16[8,3,32,1024]{3,2,1,0:T(8,128)(2,1)}), bf16[8,3,32,1024]{3,2,1,0:T(8,128)(2,1)S(1)}, u32[]{:S(2)}, u32[]{:S(2)}) async-start(bf16[8,3,32,1024]{3,2,1,0:T(8,128)(2,1)} %broadcast_select_fusion), calls=%async_computation.1 | async-start | bytes 3145728 | tf_op jit(solution)/shard_map/all_to_all | solution.py:132
  29.0 35.8 %all-to-all-done.1 = bf16[8,3,32,1024]{3,2,1,0:T(8,128)(2,1)S(1)} async-done(((bf16[8,3,32,1024]{3,2,1,0:T(8,128)(2,1)}), bf16[8,3,32,1024]{3,2,1,0:T(8,128)(2,1)S(1)}, u32[]{:S(2)}, u32[]{:S(2)}) %all-to-all-start.1) | async-done | bytes 1572896 | tf_op jit(solution)/shard_map/all_to_all | solution.py:132
  65.5 1.3 pad_maximum_fusion
  66.8 13.1 %copy.80 = bf16[512,8,4,384]{3,1,2,0:T(8,128)(2,1)} copy(bf16[512,8,4,384]{3,2,1,0:T(4,128)(2,1)} %bitcast.36) | data formatting | bytes 25165824
  80.2 1.5 multiply_cosine_fusion
  81.7 3.5 %all-to-all-start.2 = ((s32[8,1,3]{2,1,0:T(1,128)}), s32[8,1,3]{2,1,0:T(1,128)S(1)}, u32[]{:S(2)}, u32[]{:S(2)}) async-start(s32[8,1,3]{2,1,0:T(1,128)} %bitcast.13), calls=%async_computation.2 | async-start | bytes 8192 | tf_op jit(solution)/shard_map/all_to_all | solution.py:133
  85.2 16.7 %copy.58 = bf16[1536,4096]{1,0:T(8,128)(2,1)} copy(bf16[1536,4096]{0,1:T(8,128)(2,1)} %bitcast.35) | data formatting | bytes 25165824 | tf_op jit(solution)/shard_map/dot_general | solution.py:143
  102.5 0.7 reduce.3
  103.3 0.7 gather_fusion.3
  104.2 9.5 %all-gather.2.cloned.1.call-done = bf16[800,4096]{1,0:T(8,128)(2,1)} async-done(((bf16[800,1024]{1,0:T(8,128)(2,1)}), bf16[800,4096]{1,0:T(8,128)(2,1)}) %all-gather.2.cloned.1.call-update) | async-done | bytes 6553616 | tf_op jit(solution)/shard_map/all_gather | solution.py:141
  113.6 4.4 %fusion.2 = f32[800]{0:T(1024)S(1)} fusion(bf16[800,4096]{1,0:T(8,128)(2,1)} %all-gather.2.cloned.1.call-done), kind=kLoop, calls=%fused_computation.8 | loop fusion | flops 9829600 | bytes 6556800 | tf_op jit(solution)/shard_map/reduce_sum | solution.py:11
  118.4 13.5 %fusion.6 = f32[800,4,384]{2,0,1:T(8,128)S(1)} fusion(bf16[4,384,4096]{2,1,0:T(8,128)(2,1)} %bitcast.37, bf16[800,4096]{1,0:T(8,128)(2,1)S(1)} %copy-done.4, f32[4096]{0:T(1024)S(1)} %convert_element_type.39, f32[800]{0:T(1024)S(1)} %add_rsqrt_fusion), kind=kOutput, calls=%fused_computation.12 | convolution fusion | flops 10079436800 | bytes 24071296 | tf_op jit(solution)/shard_map/dot_general | solution.py:143
  132.0 2.7 %add_convert_fusion = (bf16[800,4,64]{2,0,1:T(8,128)(2,1)}, bf16[800,4,64]{2,0,1:T(8,128)(2,1)}, bf16[800,4,64]{2,0,1:T(8,128)(2,1)}, bf16[800,4,64]{2,0,1:T(8,128)(2,1)}) fusion(f32[800,4,384]{2,0,1:T(8,128)S(1)} %fusion.6, f32[800,64]{1,0:T(8,128)S(1)} %get-tuple-element.17, f32[800,64]{1,0:T(8,128)S(1)} %get-tuple-element.16), kind=kLoop, calls=%fused_computation.18 | loop fusion | flops 3276800 | bytes 5324800 | tf_op jit(solution)/shard_map/convert.3
  134.7 5.8 %concatenate.18 = bf16[800,4,384]{2,0,1:T(8,128)(2,1)S(1)} concatenate(bf16[800,4,64]{2,0,1:T(8,128)(2,1)} %get-tuple-element.6, bf16[800,4,64]{2,0,1:T(8,128)(2,1)} %get-tuple-element.7, bf16[800,4,64]{2,0,1:T(8,128)(2,1)} %get-tuple-element.5, bf16[800,4,64]{2,0,1:T(8,128)(2,1)} %get-tuple-element.4, bf16[800,4,128]{2,0,1:T(8,128)(2,1)S(1)} %slice.104), dimensions={2} | concatenate | bytes 4915200 | tf_op jit(solution)/shard_map/concatenate | solution.py:35
  140.6 1.4 copy-done.3
  143.1 1.1 fusion.47
  144.2 1.7 %fusion.46 = (bf16[24,32,4,128]{3,1,0,2:T(8,128)(2,1)}, bf16[24,32,4,128]{3,1,0,2:T(8,128)(2,1)}, bf16[24,32,4,128]{3,1,0,2:T(8,128)(2,1)S(1)}) fusion(bf16[24,32,4,384]{3,1,0,2:T(8,128)(2,1)S(1)} %bitcast.38), kind=kLoop, calls=%fused_computation.87 | loop fusion | bytes 4718592 | tf_op jit(solution)/shard_map/slice | solution.py:79
  145.9 2.6 %fusion.50 = (f32[24,4,32]{2,1,0:T(4,128)S(1)}, f32[24,4,32,48]{3,2,1,0:T(8,128)S(1)}) fusion(bf16[24,16,4,128]{3,1,2,0:T(8,128)(2,1)} %get-tuple-element.11, bf16[24,32,4,128]{3,1,0,2:T(8,128)(2,1)} %get-tuple-element.8, pred[24,32,48]{2,1,0:T(8,128)(4,1)S(1)} %and_or_fusion, bf16[24,32,4,128]{3,1,0,2:T(8,128)(2,1)} %get-tuple-element.9), kind=kOutput, calls=%fused_computation.91 | convolution fusion | flops 40845360 | bytes 2605056 | tf_op jit(solution)/shard_map/sub | solution.py:41
  148.5 0.9 fusion.11
  149.4 1.0 copy.108
  (60 shorter events, 5.2 us)
Async XLA Ops:
  7.2 14.8 %copy-start = (bf16[2,32,1024]{2,1,0:T(8,128)(2,1)S(1)}, bf16[2,32,1024]{2,1,0:T(8,128)(2,1)}, u32[]{:S(2)}) copy-start(bf16[2,32,1024]{2,1,0:T(8,128)(2,1)} %param.7) | copy-start | bytes 393220
  7.2 15.4 %copy-start.2 = (s32[2]{0:T(128)S(1)}, s32[2]{0:T(128)}, u32[]{:S(2)}) copy-start(s32[2]{0:T(128)} %param.8) | copy-start | bytes 28
  25.3 39.5 %all-to-all-start.1 = ((bf16[8,3,32,1024]{3,2,1,0:T(8,128)(2,1)}), bf16[8,3,32,1024]{3,2,1,0:T(8,128)(2,1)S(1)}, u32[]{:S(2)}, u32[]{:S(2)}) async-start(bf16[8,3,32,1024]{3,2,1,0:T(8,128)(2,1)} %broadcast_select_fusion), calls=%async_computation.1 | async-start | bytes 3145728 | tf_op jit(solution)/shard_map/all_to_all | solution.py:132
  28.9 36.6 %copy-start.6 = (bf16[2,16,1024]{2,1,0:T(8,128)(2,1)S(1)}, bf16[2,16,1024]{2,1,0:T(8,128)(2,1)}, u32[]{:S(2)}) copy-start(bf16[2,16,1024]{2,1,0:T(8,128)(2,1)} %param.6) | copy-start | bytes 196612
  28.9 84.7 %all-gather.2.cloned.1.call-start = ((), (), s32[]{:S(2)}) async-start(), calls=%async_computation.3 | async-start | bytes 8192000 | tf_op jit(solution)/shard_map/all_gather | solution.py:141
  81.7 20.3 %all-to-all-start.2 = ((s32[8,1,3]{2,1,0:T(1,128)}), s32[8,1,3]{2,1,0:T(1,128)S(1)}, u32[]{:S(2)}, u32[]{:S(2)}) async-start(s32[8,1,3]{2,1,0:T(1,128)} %bitcast.13), calls=%async_computation.2 | async-start | bytes 8192 | tf_op jit(solution)/shard_map/all_to_all | solution.py:133
  85.2 16.8 %copy-start.7 = (bf16[4096]{0:T(1024)(128)(2,1)S(1)}, bf16[4096]{0:T(1024)(128)(2,1)}, u32[]{:S(2)}) copy-start(bf16[4096]{0:T(1024)(128)(2,1)} %param.10) | copy-start | bytes 24580
  113.6 4.7 %copy-start.4 = (bf16[800,4096]{1,0:T(8,128)(2,1)S(1)}, bf16[800,4096]{1,0:T(8,128)(2,1)}, u32[]{:S(2)}) copy-start(bf16[800,4096]{1,0:T(8,128)(2,1)} %all-gather.2.cloned.1.call-done) | copy-start | bytes 19660804
  140.5 1.4 copy-start.3
  141.9 2.2 %slice-start = ((bf16[800,4,384]{2,0,1:T(8,128)(2,1)}), bf16[768,4,384]{2,0,1:T(8,128)(2,1)S(1)}, s32[]{:S(2)}) async-start(bf16[800,4,384]{2,0,1:T(8,128)(2,1)} %copy-done.3), calls=%async_computation.4 | async-start | bytes 4718592 | tf_op jit(solution)/shard_map/slice | solution.py:147
  145.9 2.6 %copy-start.5 = (bf16[24,16,4,128]{3,1,2,0:T(8,128)(2,1)S(1)}, bf16[24,16,4,128]{3,1,2,0:T(8,128)(2,1)}, u32[]{:S(2)}) copy-start(bf16[24,16,4,128]{3,1,2,0:T(8,128)(2,1)} %get-tuple-element.12) | copy-start | bytes 1179652
  148.5 1.9 %copy-start.1 = (bf16[2,32,1024]{2,1,0:T(8,128)(2,1)S(1)}, bf16[2,32,1024]{2,1,0:T(8,128)(2,1)}, u32[]{:S(2)}) copy-start(bf16[2,32,1024]{2,1,0:T(8,128)(2,1)} %param.7) | copy-start | bytes 393220
Sparse Core Ops, SparseCore 0:
  66.9 46.6 all-gather.1
where the time goes:
time: 158 us; the launch traced here: 157 us
  local copies, waits for them, and re-layouts  45.9 us (29%)
  waiting for transfers between devices  45.3 us (29%)
  matrix products  17.3 us (11%)
  between operations  14.3 us (9%)
  other arithmetic  13.8 us (9%)
  blocking collectives  13.6 us (9%)
  starting transfers between devices  7.12 us (5%)
    all_to_all x1, waiting for transfers between devices, local(): lax.all_to_all(outgoing, 'store', split_axis=0, concat_axis=0, tiled=True)  35.8 us
    dot_general x1, local copies, waits for them, and re-layouts, local(): raw = jnp.dot(normed, weights_flat, preferred_element_type=jnp.float32)  16.7 us
    unnamed x17, local copies, waits for them, and re-layouts  14.9 us
    all_to_all x1, blocking collectives, local(): lax.all_to_all(request, 'store', split_axis=0, concat_axis=0, tiled=True)  13.6 us
    dot_general x1, matrix products, local(): raw = jnp.dot(normed, weights_flat, preferred_element_type=jnp.float32)  13.5 us
    all_gather x1, waiting for transfers between devices, local(): full_rows = lax.all_gather(all_rows, 'tp', axis=1, tiled=True)  9.46 us
    concatenate x1, local copies, waits for them, and re-layouts, rotate_parts(): jnp.concatenate([queries, keyset, values], axis=-1).astype(jnp.bfloat16)  5.82 us
    reduce_sum x1, other arithmetic, rms_rows(): meansq = jnp.mean(values * values, axis=-1, keepdims=True)  4.35 us
  transfers between devices with their start and end apart: 3, of which 2 were waited for; matrix products, arithmetic and copies ran while one was open for 21% of the time, Pallas kernels for 0%

commit v1 on v0

--- a/solution.py
+++ b/solution.py
@@ -98,53 +98,30 @@
 
 
 def local(query_embeds, passage_embeds, passage_lengths, cand_passage, norm_gain, w_qkv):
-    n_store = lax.axis_size("store")
     quer_count, query_len, width_part = query_embeds.shape
     pass_count, passage_len = (passage_embeds.shape[0], passage_embeds.shape[1])
     pairs_dev = cand_passage.shape[0]
     cands = pairs_dev // quer_count
     heads_part = w_qkv.shape[1]
     head_dim = w_qkv.shape[2] // 3
-    capacity = (pairs_dev + n_store - 1) // n_store
     weights_flat = w_qkv.reshape(w_qkv.shape[0], heads_part * 3 * head_dim)
     query_rows = query_embeds.reshape(quer_count * query_len, width_part)
+    passage_rows = passage_embeds.reshape(pass_count * passage_len, width_part)
     query_pos = jnp.tile(jnp.arange(query_len, dtype=jnp.float32), quer_count)
+    passage_pos = query_len + jnp.tile(jnp.arange(passage_len, dtype=jnp.float32), pass_count)
     query_total = quer_count * query_len
-    holder = cand_passage // pass_count
-    same_holder = holder[:, None] == holder[None, :]
-    pair_index = jnp.arange(pairs_dev, dtype=jnp.int32)
-    earlier = pair_index[:, None] < pair_index[None, :]
-    rank_in = jnp.sum((same_holder & earlier).astype(jnp.int32), axis=0)
-    slot_code = cand_passage % pass_count + 1
-    hits = (holder[:, None, None] == jnp.arange(n_store, dtype=jnp.int32)[None, :, None]) & (
-        rank_in[:, None, None] == jnp.arange(capacity, dtype=jnp.int32)[None, None, :]
-    )
-    request = jnp.sum(jnp.where(hits, slot_code[:, None, None], 0), axis=0)
-    flat_index = holder * capacity + rank_in
-    hits, request, flat_index = (hits, request, flat_index)
-    incoming = lax.all_to_all(request, "store", split_axis=0, concat_axis=0, tiled=True)
-    chosen = jnp.maximum(incoming - 1, 0)
-    filled = incoming > 0
-    outgoing = jnp.where(
-        filled[:, :, None, None], passage_embeds[chosen], jnp.zeros((), passage_embeds.dtype)
-    )
-    out_len = jnp.where(filled, passage_lengths[chosen], 0)
-    arrived = lax.all_to_all(outgoing, "store", split_axis=0, concat_axis=0, tiled=True)
-    arrived_len = lax.all_to_all(out_len, "store", split_axis=0, concat_axis=0, tiled=True)
-    flat_rows = arrived.reshape((n_store * capacity,) + passage_embeds.shape[1:])
-    fetched = flat_rows[flat_index]
-    pair_lengths = arrived_len.reshape(n_store * capacity)[flat_index]
-    pair_pos = query_len + jnp.tile(jnp.arange(passage_len, dtype=jnp.float32), pairs_dev)
-    all_rows = jnp.concatenate(
-        [query_rows, fetched.reshape(pairs_dev * passage_len, width_part)], axis=0
-    )
+    all_rows = jnp.concatenate([query_rows, passage_rows], axis=0)
     full_rows = lax.all_gather(all_rows, "tp", axis=1, tiled=True)
     normed = rms_rows(full_rows, norm_gain)
     raw = jnp.dot(normed, weights_flat, preferred_element_type=jnp.float32)
     raw = raw.reshape(all_rows.shape[0], heads_part, 3 * head_dim)
-    projected = rotate_parts(raw, jnp.concatenate([query_pos, pair_pos], axis=0), head_dim)
+    projected = rotate_parts(raw, jnp.concatenate([query_pos, passage_pos], axis=0), head_dim)
     query_qkv = projected[:query_total].reshape(quer_count, query_len, heads_part, 3 * head_dim)
-    pair_qkv = projected[query_total:].reshape(pairs_dev, passage_len, heads_part, 3 * head_dim)
+    own_qkv = projected[query_total:].reshape(pass_count, passage_len, heads_part, 3 * head_dim)
+    store_qkv = lax.all_gather(own_qkv, "store", axis=0, tiled=True)
+    store_len = lax.all_gather(passage_lengths, "store", axis=0, tiled=True)
+    pair_qkv = store_qkv[cand_passage]
+    pair_lengths = store_len[cand_passage]
     query_attn = attend_queries(query_qkv, head_dim)
     passage_attn = attend_pairs(query_qkv, pair_qkv, pair_lengths, head_dim, cands)
     return (query_attn, passage_attn)

time: 158 us -> 121 us (0.77)
  waiting for transfers between devices: 45.3 us -> 28.2 us
  other arithmetic: 13.8 us -> 1.71 us
  blocking collectives: 13.6 us -> 21.8 us
  local copies, waits for them, and re-layouts: 45.9 us -> 38.4 us
  starting transfers between devices: 7.12 us -> 0.04 us
  matrix products: 17.3 us -> 15.1 us
    all_to_all x2 -> x0, waiting for transfers between devices: 35.8 us -> none  [the longest x1 35.8 us: local(): lax.all_to_all(outgoing, 'store', split_axis=0, concat_axis=0, tiled=True)]
    all_gather x1, waiting for transfers between devices: 9.46 us -> 28.2 us  [local(): store_qkv = lax.all_gather(own_qkv, 'store', axis=0, tiled=True)]
    all_to_all x1 -> x0, blocking collectives: 13.6 us -> none  [local(): lax.all_to_all(request, 'store', split_axis=0, concat_axis=0, tiled=True)]
    unnamed x0 -> x1, blocking collectives: none -> 11.7 us
    all_gather x0 -> x1, blocking collectives: none -> 10.1 us  [local(): full_rows = lax.all_gather(all_rows, 'tp', axis=1, tiled=True)]
    all_to_all x2 -> x0, starting transfers between devices: 7.08 us -> none  [the longest x1 3.58 us: local(): lax.all_to_all(outgoing, 'store', split_axis=0, concat_axis=0, tiled=True)]
    concatenate x1, local copies, waits for them, and re-layouts: 5.82 us -> 0.2 us  [rotate_parts(): jnp.concatenate([queries, keyset, values], axis=-1).astype(jnp.bfloat16)]
    dot_general x1, matrix products: 13.5 us -> 8.62 us  [local(): raw = jnp.dot(normed, weights_flat, preferred_element_type=jnp.float32)]
  transfers between devices with their start and end apart: 3 -> 1, of which waited for: 2 -> 1; matrix products, arithmetic and copies ran while one was open for 21% -> 4% of each run, Pallas kernels for 0% -> 0%
where the time goes in v1:
time: 121 us; the launch traced here: 120 us
  local copies, waits for them, and re-layouts  38.4 us (32%)
  waiting for transfers between devices  28.2 us (23%)
  blocking collectives  21.8 us (18%)
  matrix products  15.1 us (12%)
  between operations  14.9 us (12%)
  other arithmetic  1.71 us (1%)
    all_gather x1, waiting for transfers between devices, local(): store_qkv = lax.all_gather(own_qkv, 'store', axis=0, tiled=True)  28.2 us
    dot_general x1, local copies, waits for them, and re-layouts, local(): raw = jnp.dot(normed, weights_flat, preferred_element_type=jnp.float32)  16.8 us
    unnamed x16, local copies, waits for them, and re-layouts  13.3 us
    unnamed x1, blocking collectives  11.7 us
    all_gather x1, blocking collectives, local(): full_rows = lax.all_gather(all_rows, 'tp', axis=1, tiled=True)  10.1 us
    dot_general x1, matrix products, local(): raw = jnp.dot(normed, weights_flat, preferred_element_type=jnp.float32)  8.62 us
    sub x2, matrix products, softmax_rounded(): expon = jnp.where(allowed, jnp.exp(masked - peak), jnp.float32(0.0))  4.21 us
    gather x1, local copies, waits for them, and re-layouts, local(): pair_qkv = store_qkv[cand_passage]  2.52 us
  transfers between devices with their start and end apart: 1, of which 1 were waited for; matrix products, arithmetic and copies ran while one was open for 4% of the time, Pallas kernels for 0%

profile of v1, /device:TPU:0, one launch (start us, length us, event | category | flops | bytes accessed | tf_op | source)
XLA Modules:
  0.0 120.2 jit_solution(4260285914436584830)
XLA Ops:
  7.2 12.4 %copy.28 = bf16[512,8,4,384]{3,1,2,0:T(8,128)(2,1)} copy(bf16[512,8,4,384]{3,2,1,0:T(4,128)(2,1)} %bitcast.29) | data formatting | bytes 25165824
  19.7 16.8 %copy.14 = bf16[1536,4096]{1,0:T(8,128)(2,1)} copy(bf16[1536,4096]{0,1:T(8,128)(2,1)} %bitcast.28) | data formatting | bytes 25165824 | tf_op jit(solution)/shard_map/dot_general | solution.py:116
  36.5 10.1 %all_gather.9 = bf16[96,4096]{1,0:T(8,128)(2,1)S(1)} all-gather(bf16[96,1024]{1,0:T(8,128)(2,1)S(1)} %pad_maximum_fusion), channel_id=1, replica_groups=mesh['store'=8,'tp'=4] {'tp'}, dimensions={1}, use_global_device_ids=true | all-gather | bytes 983040 | tf_op jit(solution)/shard_map/all_gather | solution.py:114
  46.6 0.3 fusion.3
  47.0 8.6 %fusion.19 = f32[96,4,384]{2,0,1:T(8,128)S(1)} fusion(bf16[4,384,4096]{2,1,0:T(8,128)(2,1)} %bitcast.27, bf16[96,4096]{1,0:T(8,128)(2,1)S(1)} %all_gather.9, f32[4096]{0:T(1024)S(1)} %convert_element_type.35, f32[96]{0:T(128)S(1)} %add_rsqrt_fusion), kind=kOutput, calls=%fused_computation.29 | convolution fusion | flops 1209532416 | bytes 13975936 | tf_op jit(solution)/shard_map/dot_general | solution.py:116
  55.8 0.2 multiply_cosine_fusion
  56.0 0.2 add_convert_fusion
  56.3 0.2 concatenate.18
  56.5 0.7 slice.84
  57.2 0.6 dynamic-slice
  58.4 0.2 dynamic-update-slice
  58.7 11.7 %all-reduce = s32[16]{0:T(128)S(1)} all-reduce(s32[16]{0:T(128)S(1)} %dynamic-update-slice), channel_id=1, replica_groups=mesh['store'=8,'tp'=4] {'store'}, use_global_device_ids=true, to_apply=%add | all-reduce | flops 16 | bytes 128
  70.5 0.2 fusion.47
  70.7 0.2 fusion.17
  70.9 0.6 copy.42
  71.5 0.7 gather_fusion
  72.4 0.7 and_or_fusion
  73.2 1.0 fusion.45
  74.2 28.2 %all-gather.2.cloned.1.call-done = bf16[16,32,4,384]{3,1,0,2:T(8,128)(2,1)} async-done(((bf16[2,32,4,384]{3,1,0,2:T(8,128)(2,1)}), bf16[16,32,4,384]{3,1,0,2:T(8,128)(2,1)}) %all-gather.2.cloned.1.call-update) | async-done | bytes 1572880 | tf_op jit(solution)/shard_map/all_gather | solution.py:121
  102.4 2.5 %gather_fusion.1 = bf16[24,32,4,384]{3,1,2,0:T(8,128)(2,1)S(1)} fusion(bf16[16,32,4,384]{3,1,0,2:T(8,128)(2,1)} %all-gather.2.cloned.1.call-done, s32[1024]{0:T(1024)S(1)} %pad_clamp_fusion), kind=kCustom, calls=%fused_computation.1 | custom fusion | bytes 4718688 | tf_op jit(solution)/shard_map/gather | solution.py:123
  104.9 1.3 %fusion.44 = (bf16[24,32,4,128]{3,1,2,0:T(8,128)(2,1)}, bf16[24,32,4,128]{3,1,2,0:T(8,128)(2,1)S(1)}) fusion(bf16[24,32,4,384]{3,1,2,0:T(8,128)(2,1)S(1)} %gather_fusion.1), kind=kLoop, calls=%fused_computation.68 | loop fusion | bytes 3145728 | tf_op jit(solution)/shard_map/slice | solution.py:74
  106.2 4.0 %fusion.48 = (f32[24,4,32]{2,1,0:T(4,128)}, f32[24,4,32,48]{3,2,1,0:T(8,128)}) fusion(bf16[24,32,4,128]{3,1,2,0:T(8,128)(2,1)} %get-tuple-element.2, bf16[24,16,4,128]{3,1,2,0:T(8,128)(2,1)} %get-tuple-element.4, bf16[24,32,4,384]{3,1,2,0:T(8,128)(2,1)S(1)} %gather_fusion.1, pred[24,32,48]{2,1,0:T(8,128)(4,1)} %and_or_fusion), kind=kOutput, calls=%fused_computation.72 | convolution fusion | flops 40845360 | bytes 2764800 | tf_op jit(solution)/shard_map/sub | solution.py:41
  110.3 2.0 %fusion.6 = bf16[24,4,4,8,128]{4,3,2,1,0:T(8,128)(2,1)S(1)} fusion(bf16[24,32,4,128]{3,1,2,0:T(8,128)(2,1)S(1)} %get-tuple-element.3, bf16[24,16,4,128]{3,1,2,0:T(8,128)(2,1)S(1)} %get-tuple-element.5, f32[24,4,32,48]{3,2,1,0:T(8,128)} %get-tuple-element.18, f32[24,4,32]{2,1,0:T(4,128)} %get-tuple-element.17, pred[24,32]{1,0:T(8,128)(4,1)S(1)} %iota_compare_fusion.1), kind=kOutput, calls=%fused_computation.14 | convolution fusion | flops 41189376 | bytes 2568960 | tf_op jit(solution)/shard_map/bhit,bthd->bihd/dot_general | solution.py:89
  112.3 1.0 copy.41
  (38 shorter events, 0.7 us)
Async XLA Ops:
  7.2 95.2 %all-gather.2.cloned.1.call-start = ((), (), s32[]{:S(2)}) async-start(), calls=%async_computation | async-start | bytes 1769472 | tf_op jit(solution)/shard_map/all_gather | solution.py:121
  19.7 16.8 %copy-start = (bf16[2,32,1024]{2,1,0:T(8,128)(2,1)S(1)}, bf16[2,32,1024]{2,1,0:T(8,128)(2,1)}, u32[]{:S(2)}) copy-start(bf16[2,32,1024]{2,1,0:T(8,128)(2,1)} %param.7) | copy-start | bytes 393220
  19.7 16.8 %copy-start.1 = (bf16[2,16,1024]{2,1,0:T(8,128)(2,1)S(1)}, bf16[2,16,1024]{2,1,0:T(8,128)(2,1)}, u32[]{:S(2)}) copy-start(bf16[2,16,1024]{2,1,0:T(8,128)(2,1)} %param.6) | copy-start | bytes 196612
  19.7 26.9 %copy-start.2 = (bf16[4096]{0:T(1024)(128)(2,1)S(1)}, bf16[4096]{0:T(1024)(128)(2,1)}, u32[]{:S(2)}) copy-start(bf16[4096]{0:T(1024)(128)(2,1)} %param.10) | copy-start | bytes 24580
  55.7 1.5 %copy-start.5 = (u32[32]{0:T(128)S(1)}, u32[32]{0:T(128)}, u32[]{:S(2)}) copy-start(u32[32]{0:T(128)} %constant.31) | copy-start | bytes 388
  55.7 2.8 %copy-start.3 = (s32[2]{0:T(128)S(1)}, s32[2]{0:T(128)}, u32[]{:S(2)}) copy-start(s32[2]{0:T(128)} %param.8) | copy-start | bytes 28
  56.2 15.3 %copy-start.4 = (s32[24]{0:T(128)S(1)}, s32[24]{0:T(128)}, u32[]{:S(2)}) copy-start(s32[24]{0:T(128)} %param.9) | copy-start | bytes 292
Sparse Core Ops, SparseCore 0:
  57.3 45.0 all-gather.1

commit v2 on v1

--- a/solution.py
+++ b/solution.py
@@ -104,7 +104,6 @@
     cands = pairs_dev // quer_count
     heads_part = w_qkv.shape[1]
     head_dim = w_qkv.shape[2] // 3
-    weights_flat = w_qkv.reshape(w_qkv.shape[0], heads_part * 3 * head_dim)
     query_rows = query_embeds.reshape(quer_count * query_len, width_part)
     passage_rows = passage_embeds.reshape(pass_count * passage_len, width_part)
     query_pos = jnp.tile(jnp.arange(query_len, dtype=jnp.float32), quer_count)
@@ -113,15 +112,16 @@
     all_rows = jnp.concatenate([query_rows, passage_rows], axis=0)
     full_rows = lax.all_gather(all_rows, "tp", axis=1, tiled=True)
     normed = rms_rows(full_rows, norm_gain)
-    raw = jnp.dot(normed, weights_flat, preferred_element_type=jnp.float32)
-    raw = raw.reshape(all_rows.shape[0], heads_part, 3 * head_dim)
+    raw = jnp.einsum("nk,khc->nhc", normed, w_qkv, preferred_element_type=jnp.float32)
     projected = rotate_parts(raw, jnp.concatenate([query_pos, passage_pos], axis=0), head_dim)
     query_qkv = projected[:query_total].reshape(quer_count, query_len, heads_part, 3 * head_dim)
     own_qkv = projected[query_total:].reshape(pass_count, passage_len, heads_part, 3 * head_dim)
+    padded = jnp.arange(passage_len, dtype=jnp.int32)[None, :] >= passage_lengths[:, None]
+    marker = own_qkv[:, :, 0, head_dim]
+    own_qkv = own_qkv.at[:, :, 0, head_dim].set(jnp.where(padded, jnp.inf, marker).astype(own_qkv.dtype))
     store_qkv = lax.all_gather(own_qkv, "store", axis=0, tiled=True)
-    store_len = lax.all_gather(passage_lengths, "store", axis=0, tiled=True)
     pair_qkv = store_qkv[cand_passage]
-    pair_lengths = store_len[cand_passage]
+    pair_lengths = jnp.sum(jnp.isfinite(pair_qkv[:, :, 0, head_dim]).astype(jnp.int32), axis=1)
     query_attn = attend_queries(query_qkv, head_dim)
     passage_attn = attend_pairs(query_qkv, pair_qkv, pair_lengths, head_dim, cands)
     return (query_attn, passage_attn)

time: 121 us -> 97.3 us (0.80)
  local copies, waits for them, and re-layouts: 38.4 us -> 9.6 us
  waiting for transfers between devices: 28.2 us -> 43 us
  blocking collectives: 21.8 us -> 10.1 us
  other arithmetic: 1.71 us -> 6.7 us
  matrix products: 15.1 us -> 13.3 us
    dot_general x1 -> x0, local copies, waits for them, and re-layouts: 16.8 us -> none  [local(): raw = jnp.dot(normed, weights_flat, preferred_element_type=jnp.float32)]
    all_gather x1, waiting for transfers between devices: 28.2 us -> 43 us  [local(): store_qkv = lax.all_gather(own_qkv, 'store', axis=0, tiled=True)]
    unnamed x16 -> x8, local copies, waits for them, and re-layouts: 13.3 us -> 0.69 us
    unnamed x1 -> x0, blocking collectives: 11.7 us -> none
    another operation x1 -> x4, other arithmetic: 0.2 us -> 3.06 us
    dot_general x1, matrix products: 8.62 us -> 6.84 us  [local(): jnp.einsum('nk,khc->nhc', normed, w_qkv, preferred_element_type=jnp.float32)]
    scatter x0 -> x1, local copies, waits for them, and re-layouts: none -> 1.35 us  [local(): own_qkv.at[:, :, 0, head_dim]]
  transfers between devices with their start and end apart: 1 -> 1, of which waited for: 1 -> 1; matrix products, arithmetic and copies ran while one was open for 4% -> 2% of each run, Pallas kernels for 0% -> 0%
where the time goes in v2:
time: 97.3 us; the launch traced here: 96.9 us
  waiting for transfers between devices  43 us (44%)
  between operations  14.2 us (15%)
  matrix products  13.3 us (14%)
  blocking collectives  10.1 us (10%)
  local copies, waits for them, and re-layouts  9.6 us (10%)
  other arithmetic  6.7 us (7%)
    all_gather x1, waiting for transfers between devices, local(): store_qkv = lax.all_gather(own_qkv, 'store', axis=0, tiled=True)  43 us
    all_gather x1, blocking collectives, local(): full_rows = lax.all_gather(all_rows, 'tp', axis=1, tiled=True)  10.1 us
    dot_general x1, matrix products, local(): jnp.einsum('nk,khc->nhc', normed, w_qkv, preferred_element_type=jnp.float32)  6.84 us
    sub x2, matrix products, softmax_rounded(): expon = jnp.where(allowed, jnp.exp(masked - peak), jnp.float32(0.0))  4.21 us
    another operation x4, other arithmetic  3.06 us
    gather x1, local copies, waits for them, and re-layouts, local(): pair_qkv = store_qkv[cand_passage]  2.52 us
    dot_general x1, matrix products, attend_core(): jnp.einsum('bhit,bthd->bihd', weights, values, preferred_element_type=jnp...  2.04 us
  transfers between devices with their start and end apart: 1, of which 1 were waited for; matrix products, arithmetic and copies ran while one was open for 2% of the time, Pallas kernels for 0%

profile of v2, /device:TPU:0, one launch (start us, length us, event | category | flops | bytes accessed | tf_op | source)
XLA Modules:
  0.0 96.9 jit_solution(2858352367498989103)
XLA Ops:
  7.2 0.9 pad_maximum_fusion
  8.2 10.1 %all_gather.6 = bf16[96,4096]{1,0:T(8,128)(2,1)S(1)} all-gather(bf16[96,1024]{1,0:T(8,128)(2,1)S(1)} %pad_maximum_fusion), channel_id=1, replica_groups=mesh['store'=8,'tp'=4] {'tp'}, dimensions={1}, use_global_device_ids=true | all-gather | bytes 983040 | tf_op jit(solution)/shard_map/all_gather | solution.py:113
  18.2 0.7 convert_element_type.41
  18.9 0.3 fusion.5
  19.4 6.8 %fusion.2 = f32[96,4,384]{2,0,1:T(8,128)S(1)} fusion(bf16[4096,4,384]{2,1,0:T(4,128)(2,1)} %param.13, bf16[96,4096]{1,0:T(8,128)(2,1)S(1)} %all_gather.6, f32[4096]{0:T(1024)S(1)} %convert_element_type.41, f32[96]{0:T(128)S(1)} %add_rsqrt_fusion), kind=kOutput, calls=%fused_computation.3 | convolution fusion | flops 1209532416 | bytes 13975936 | tf_op jit(solution)/shard_map/nk,khc->nhc/dot_general | solution.py:115
  26.4 0.2 multiply_cosine_fusion
  26.6 0.2 add_convert_fusion
  26.8 0.2 concatenate.23
  27.1 0.6 fusion.50
  27.6 0.8 and_reduce_fusion
  28.4 2.1 %fusion.35 = bf16[2,32,1,1]{3,1,0,2:T(8,128)(2,1)S(1)} fusion(bf16[2,32,4,384]{3,1,0,2:T(8,128)(2,1)S(1)} %bitcast.23, s32[]{:T(128)} %bitcast.6, s32[]{:T(128)} %bitcast.7, s32[2]{0:T(128)S(1)} %copy-done.1, pred[]{:T(512)} %and_reduce_fusion), kind=kLoop, calls=%fused_computation.53 | loop fusion | flops 192 | bytes 401 | tf_op jit(solution)/shard_map/select.1
  30.5 1.4 %scatter.4 = bf16[2,32,4,384]{3,1,0,2:T(8,128)(2,1)S(1)} dynamic-update-slice(bf16[2,32,4,384]{3,1,0,2:T(8,128)(2,1)S(1)} %bitcast.24, bf16[2,32,1,1]{3,1,0,2:T(8,128)(2,1)S(1)} %fusion.35, s32[]{:T(128)} %constant.49.clone.1, s32[]{:T(128)} %constant.49.clone.1, s32[]{:T(128)} %bitcast.6, s32[]{:T(128)} %bitcast.7) | dynamic-update-slice | bytes 260 | tf_op jit(solution)/shard_map/scatter | solution.py:121
  31.9 0.7 copy-done
  32.8 0.2 fusion.19
  33.0 0.6 copy.43
  33.8 1.0 fusion.48
  34.8 43.0 %all-gather.2.cloned.1.call-done = bf16[16,32,4,384]{3,1,0,2:T(8,128)(2,1)} async-done(((bf16[2,32,4,384]{3,1,0,2:T(8,128)(2,1)}), bf16[16,32,4,384]{3,1,0,2:T(8,128)(2,1)}) %all-gather.2.cloned.1.call-update) | async-done | bytes 1572880 | tf_op jit(solution)/shard_map/all_gather | solution.py:122
  77.8 2.5 %gather_fusion = bf16[24,32,4,384]{3,1,2,0:T(8,128)(2,1)S(1)} fusion(bf16[16,32,4,384]{3,1,0,2:T(8,128)(2,1)} %all-gather.2.cloned.1.call-done, s32[1024]{0:T(1024)S(1)} %pad_clamp_fusion), kind=kCustom, calls=%fused_computation | custom fusion | bytes 4718688 | tf_op jit(solution)/shard_map/gather | solution.py:123
  80.3 1.3 %fusion.47 = (bf16[24,32,4,128]{3,1,2,0:T(8,128)(2,1)}, bf16[24,32,4,128]{3,1,2,0:T(8,128)(2,1)S(1)}) fusion(bf16[24,32,4,384]{3,1,2,0:T(8,128)(2,1)S(1)} %gather_fusion), kind=kLoop, calls=%fused_computation.74 | loop fusion | bytes 3145728 | tf_op jit(solution)/shard_map/slice | solution.py:74
  81.6 0.5 convert_reduce_fusion
  82.3 0.7 and_or_fusion
  83.0 4.0 %fusion.52 = (f32[24,4,32]{2,1,0:T(4,128)}, f32[24,4,32,48]{3,2,1,0:T(8,128)}) fusion(bf16[24,32,4,128]{3,1,2,0:T(8,128)(2,1)} %get-tuple-element.14, bf16[24,16,4,128]{3,1,2,0:T(8,128)(2,1)} %get-tuple-element.16, bf16[24,32,4,384]{3,1,2,0:T(8,128)(2,1)S(1)} %gather_fusion, pred[24,32,48]{2,1,0:T(8,128)(4,1)} %and_or_fusion), kind=kOutput, calls=%fused_computation.79 | convolution fusion | flops 40845360 | bytes 2764800 | tf_op jit(solution)/shard_map/sub | solution.py:41
  87.0 2.0 %fusion.8 = bf16[24,4,4,8,128]{4,3,2,1,0:T(8,128)(2,1)S(1)} fusion(bf16[24,32,4,128]{3,1,2,0:T(8,128)(2,1)S(1)} %get-tuple-element.15, bf16[24,16,4,128]{3,1,2,0:T(8,128)(2,1)S(1)} %get-tuple-element.17, f32[24,4,32,48]{3,2,1,0:T(8,128)} %get-tuple-element.32, f32[24,4,32]{2,1,0:T(4,128)} %get-tuple-element.31, pred[24,32]{1,0:T(8,128)(4,1)S(1)} %iota_compare_fusion.2), kind=kOutput, calls=%fused_computation.15 | convolution fusion | flops 41189376 | bytes 2568960 | tf_op jit(solution)/shard_map/bhit,bthd->bihd/dot_general | solution.py:89
  89.1 1.0 %copy.42 = bf16[24,4,4,8,128]{4,3,1,2,0:T(8,128)(2,1)} copy(bf16[24,4,4,8,128]{4,3,2,1,0:T(8,128)(2,1)S(1)} %fusion.8) | data formatting | bytes 1572864 | tf_op jit(solution)/shard_map/convert_element_type | solution.py:92
  (33 shorter events, 0.9 us)
Async XLA Ops:
  7.2 70.6 %all-gather.2.cloned.1.call-start = ((), (), s32[]{:S(2)}) async-start(), calls=%async_computation | async-start | bytes 1769472 | tf_op jit(solution)/shard_map/all_gather | solution.py:122
  26.2 1.4 %copy-start.2 = (s32[4]{0:T(128)S(1)}, s32[4]{0:T(128)}, u32[]{:S(2)}) copy-start(s32[4]{0:T(128)} %constant.52.clone.1) | copy-start | bytes 52
  26.2 2.2 %copy-start.1 = (s32[2]{0:T(128)S(1)}, s32[2]{0:T(128)}, u32[]{:S(2)}) copy-start(s32[2]{0:T(128)} %param.10) | copy-start | bytes 28
  26.8 6.9 %copy-start.3 = (s32[24]{0:T(128)S(1)}, s32[24]{0:T(128)}, u32[]{:S(2)}) copy-start(s32[24]{0:T(128)} %param.11) | copy-start | bytes 292
  31.9 0.7 copy-start
Sparse Core Ops, SparseCore 0:
  32.7 45.0 all-gather.1

commit v3 on v2

--- a/solution.py
+++ b/solution.py
@@ -97,6 +97,37 @@
     return attend_core(repeated, pair_qkv, pair_lengths, head_dim)
 
 
+def gather_store(own):
+    n_store = lax.axis_size("store")
+    count = own.shape[0]
+    if n_store > 8 or n_store % 2:
+        return lax.all_gather(own, "store", axis=0, tiled=True), lambda rows: rows
+    ring = [s for s in range(0, n_store, 2)] + [s for s in range(n_store - 1, 0, -2)]
+    place = [0] * n_store
+    for i, s in enumerate(ring):
+        place[s] = i
+    forward = [(ring[i], ring[(i + 1) % n_store]) for i in range(n_store)]
+    backward = [(ring[(i + 1) % n_store], ring[i]) for i in range(n_store)]
+    parts = [own]
+    ahead = own
+    for _ in range(n_store // 2):
+        ahead = lax.ppermute(ahead, "store", forward)
+        parts.append(ahead)
+    behind = own
+    for _ in range((n_store - 1) // 2):
+        behind = lax.ppermute(behind, "store", backward)
+        parts.append(behind)
+    place_of = jnp.asarray(place, dtype=jnp.int32)
+    mine = place_of[lax.axis_index("store")]
+
+    def rows_of(rows):
+        dist = (place_of[rows // count] - mine) % n_store
+        slot = jnp.where(dist == 0, 0, jnp.where(dist < n_store // 2, n_store // 2 + dist, n_store - dist))
+        return slot * count + rows % count
+
+    return jnp.concatenate(parts, axis=0), rows_of
+
+
 def local(query_embeds, passage_embeds, passage_lengths, cand_passage, norm_gain, w_qkv):
     quer_count, query_len, width_part = query_embeds.shape
     pass_count, passage_len = (passage_embeds.shape[0], passage_embeds.shape[1])
@@ -117,10 +148,12 @@
     query_qkv = projected[:query_total].reshape(quer_count, query_len, heads_part, 3 * head_dim)
     own_qkv = projected[query_total:].reshape(pass_count, passage_len, heads_part, 3 * head_dim)
     padded = jnp.arange(passage_len, dtype=jnp.int32)[None, :] >= passage_lengths[:, None]
-    marker = own_qkv[:, :, 0, head_dim]
-    own_qkv = own_qkv.at[:, :, 0, head_dim].set(jnp.where(padded, jnp.inf, marker).astype(own_qkv.dtype))
-    store_qkv = lax.all_gather(own_qkv, "store", axis=0, tiled=True)
-    pair_qkv = store_qkv[cand_passage]
+    head_at = lax.broadcasted_iota(jnp.int32, own_qkv.shape, 2)
+    col_at = lax.broadcasted_iota(jnp.int32, own_qkv.shape, 3)
+    mark = padded[:, :, None, None] & (head_at == 0) & (col_at == head_dim)
+    own_qkv = jnp.where(mark, jnp.asarray(jnp.inf, own_qkv.dtype), own_qkv)
+    store_qkv, rows_of = gather_store(own_qkv)
+    pair_qkv = store_qkv[rows_of(cand_passage)]
     pair_lengths = jnp.sum(jnp.isfinite(pair_qkv[:, :, 0, head_dim]).astype(jnp.int32), axis=1)
     query_attn = attend_queries(query_qkv, head_dim)
     passage_attn = attend_pairs(query_qkv, pair_qkv, pair_lengths, head_dim, cands)

time: 97.3 us -> 61.7 us (0.63)
  waiting for transfers between devices: 43 us -> 10.8 us
  between operations: 14.2 us -> 0.84 us
  starting transfers between devices: 0.04 us -> 7.7 us
  local copies, waits for them, and re-layouts: 9.6 us -> 13.3 us
  other arithmetic: 6.7 us -> 5.44 us
    all_gather x1 -> x0, waiting for transfers between devices: 43 us -> none  [local(): store_qkv = lax.all_gather(own_qkv, 'store', axis=0, tiled=True)]
    ppermute x0 -> x7, waiting for transfers between devices: none -> 10.8 us  [the longest x4 10.8 us: gather_store(): ahead = lax.ppermute(ahead, 'store', forward)]
    ppermute x0 -> x7, starting transfers between devices: none -> 7.7 us  [the longest x4 6.3 us: gather_store(): ahead = lax.ppermute(ahead, 'store', forward)]
    unnamed x8 -> x12, local copies, waits for them, and re-layouts: 0.69 us -> 4.3 us
    another operation x4 -> x1, other arithmetic: 3.06 us -> 0.2 us
    scatter x1 -> x0, local copies, waits for them, and re-layouts: 1.35 us -> none  [local(): own_qkv.at[:, :, 0, head_dim]]
    gather x1 -> x2, local copies, waits for them, and re-layouts: 2.52 us -> 3.22 us  [the longest x1 2.52 us: local(): pair_qkv = store_qkv[rows_of(cand_passage)]]
  transfers between devices with their start and end apart: 1 -> 7, of which waited for: 1 -> 4; matrix products, arithmetic and copies ran while one was open for 2% -> 14% of each run, Pallas kernels for 0% -> 0%
where the time goes in v3:
time: 61.7 us; the launch traced here: 61.4 us
  local copies, waits for them, and re-layouts  13.3 us (22%)
  matrix products  13.3 us (22%)
  waiting for transfers between devices  10.8 us (18%)
  blocking collectives  10.1 us (16%)
  starting transfers between devices  7.7 us (12%)
  other arithmetic  5.44 us (9%)
  between operations  0.84 us (1%)
    ppermute x4, waiting for transfers between devices, gather_store(): ahead = lax.ppermute(ahead, 'store', forward)  10.8 us
    all_gather x1, blocking collectives, local(): full_rows = lax.all_gather(all_rows, 'tp', axis=1, tiled=True)  10.1 us
    dot_general x1, matrix products, local(): jnp.einsum('nk,khc->nhc', normed, w_qkv, preferred_element_type=jnp.float32)  6.85 us
    ppermute x4, starting transfers between devices, gather_store(): ahead = lax.ppermute(ahead, 'store', forward)  6.3 us
    unnamed x12, local copies, waits for them, and re-layouts  4.3 us
    sub x2, matrix products, softmax_rounded(): expon = jnp.where(allowed, jnp.exp(masked - peak), jnp.float32(0.0))  4.22 us
    gather x1, local copies, waits for them, and re-layouts, local(): pair_qkv = store_qkv[rows_of(cand_passage)]  2.52 us
    dot_general x1, matrix products, attend_core(): jnp.einsum('bhit,bthd->bihd', weights, values, preferred_element_type=jnp...  2.04 us
  transfers between devices with their start and end apart: 7, of which 4 were waited for; matrix products, arithmetic and copies ran while one was open for 14% of the time, Pallas kernels for 0%

profile of v3, /device:TPU:0, one launch (start us, length us, event | category | flops | bytes accessed | tf_op | source)
XLA Modules:
  0.0 61.4 jit_solution(14671598823762407737)
XLA Ops:
  0.7 0.9 %pad_maximum_fusion = bf16[96,1024]{1,0:T(8,128)(2,1)S(1)} fusion(bf16[64,1024]{1,0:T(8,128)(2,1)} %bitcast.26, bf16[32,1024]{1,0:T(8,128)(2,1)} %bitcast.27), kind=kLoop, calls=%fused_computation.40 | loop fusion | flops 393216 | bytes 393216 | tf_op jit(solution)/shard_map/concatenate | solution.py:143
  1.6 10.1 %all_gather.3 = bf16[96,4096]{1,0:T(8,128)(2,1)S(1)} all-gather(bf16[96,1024]{1,0:T(8,128)(2,1)S(1)} %pad_maximum_fusion), channel_id=1, replica_groups=mesh['store'=8,'tp'=4] {'tp'}, dimensions={1}, use_global_device_ids=true | all-gather | bytes 983040 | tf_op jit(solution)/shard_map/all_gather | solution.py:144
  12.8 6.8 %fusion.2 = f32[96,4,384]{2,0,1:T(8,128)S(1)} fusion(bf16[4096,4,384]{2,1,0:T(4,128)(2,1)} %param.12, bf16[96,4096]{1,0:T(8,128)(2,1)S(1)} %all_gather.3, f32[4096]{0:T(1024)S(1)} %convert_element_type.39, f32[96]{0:T(128)S(1)} %add_rsqrt_fusion), kind=kOutput, calls=%fused_computation.4 | convolution fusion | flops 1209532416 | bytes 13975936 | tf_op jit(solution)/shard_map/nk,khc->nhc/dot_general | solution.py:146
  20.6 0.8 %constant_dynamic-update-slice_fusion.7 = (bf16[16,32,4,384]{3,1,0,2:T(8,128)(2,1)}, bf16[2,32,4,384]{3,1,0,2:T(8,128)(2,1)S(1)}) fusion(bf16[2,32,4,384]{3,1,0,2:T(8,128)(2,1)S(1)} %bitcast.23, pred[384]{0:T(512)(128)(4,1)S(1)} %iota_compare_fusion.3, pred[4]{0:T(512)(128)(4,1)S(1)} %iota_compare_fusion.5, pred[2,32]{1,0:T(4,128)(4,1)S(1)} %iota_compare_fusion.4), kind=kLoop, calls=%fused_computation.60 | loop fusion | flops 294911 | bytes 590276
  21.4 1.6 %collective-permute-start = (bf16[2,32,4,384]{3,1,0,2:T(8,128)(2,1)S(1)}, bf16[2,32,4,384]{3,1,0,2:T(8,128)(2,1)S(1)}, u32[]{:S(2)}, u32[]{:S(2)}) collective-permute-start(bf16[2,32,4,384]{3,1,0,2:T(8,128)(2,1)S(1)} %get-tuple-element.3), channel_id=1, source_target_pairs={{0,8},{8,16},{16,24},{24,28},{28,20},{20,12},{12,4},{4,0},{1,9},{9... | collective-permute-start | bytes 589832 | tf_op jit(solution)/shard_map/ppermute | solution.py:114
  26.6 1.0 %fusion.49 = (bf16[24,16,4,128]{3,1,2,0:T(8,128)(2,1)}, bf16[24,16,4,128]{3,1,2,0:T(8,128)(2,1)S(1)}) fusion(bf16[24,16,4,256]{3,1,2,0:T(8,128)(2,1)S(1)} %bitcast.21), kind=kLoop, calls=%fused_computation.98 | loop fusion | bytes 1572864 | tf_op jit(solution)/shard_map/slice | solution.py:74
  27.6 1.0 %collective-permute-done = bf16[2,32,4,384]{3,1,0,2:T(8,128)(2,1)S(1)} collective-permute-done((bf16[2,32,4,384]{3,1,0,2:T(8,128)(2,1)S(1)}, bf16[2,32,4,384]{3,1,0,2:T(8,128)(2,1)S(1)}, u32[]{:S(2)}, u32[]{:S(2)}) %collective-permute-start) | collective-permute-done | bytes 196640 | tf_op jit(solution)/shard_map/ppermute | solution.py:114
  28.6 1.6 %collective-permute-start.1 = (bf16[2,32,4,384]{3,1,0,2:T(8,128)(2,1)S(1)}, bf16[2,32,4,384]{3,1,0,2:T(8,128)(2,1)S(1)}, u32[]{:S(2)}, u32[]{:S(2)}) collective-permute-start(bf16[2,32,4,384]{3,1,0,2:T(8,128)(2,1)S(1)} %collective-permute-done), channel_id=1, source_target_pairs={{0,8},{8,16},{16,24},{24,28},{28,20},{20,12},{12,4},{4,0},{1,9},{9... | collective-permute-start | bytes 589832 | tf_op jit(solution)/shard_map/ppermute | solution.py:114
  30.7 4.2 %collective-permute-done.1 = bf16[2,32,4,384]{3,1,0,2:T(8,128)(2,1)S(1)} collective-permute-done((bf16[2,32,4,384]{3,1,0,2:T(8,128)(2,1)S(1)}, bf16[2,32,4,384]{3,1,0,2:T(8,128)(2,1)S(1)}, u32[]{:S(2)}, u32[]{:S(2)}) %collective-permute-start.1) | collective-permute-done | bytes 196640 | tf_op jit(solution)/shard_map/ppermute | solution.py:114
  34.9 1.6 %collective-permute-start.2 = (bf16[2,32,4,384]{3,1,0,2:T(8,128)(2,1)S(1)}, bf16[2,32,4,384]{3,1,0,2:T(8,128)(2,1)S(1)}, u32[]{:S(2)}, u32[]{:S(2)}) collective-permute-start(bf16[2,32,4,384]{3,1,0,2:T(8,128)(2,1)S(1)} %collective-permute-done.1), channel_id=1, source_target_pairs={{0,8},{8,16},{16,24},{24,28},{28,20},{20,12},{12,4},{4,0},{1,9},{9... | collective-permute-start | bytes 589832 | tf_op jit(solution)/shard_map/ppermute | solution.py:114
  36.4 0.7 %constant_dynamic-update-slice_fusion.6 = bf16[16,32,4,384]{3,1,0,2:T(8,128)(2,1)} fusion(bf16[16,32,4,384]{3,1,0,2:T(8,128)(2,1)} %get-tuple-element.2, bf16[2,32,4,384]{3,1,0,2:T(8,128)(2,1)S(1)} %collective-permute-done), kind=kLoop, calls=%fused_computation.59 | loop fusion | bytes 393216
  37.6 2.9 %collective-permute-done.2 = bf16[2,32,4,384]{3,1,0,2:T(8,128)(2,1)S(1)} collective-permute-done((bf16[2,32,4,384]{3,1,0,2:T(8,128)(2,1)S(1)}, bf16[2,32,4,384]{3,1,0,2:T(8,128)(2,1)S(1)}, u32[]{:S(2)}, u32[]{:S(2)}) %collective-permute-start.2) | collective-permute-done | bytes 196640 | tf_op jit(solution)/shard_map/ppermute | solution.py:114
  40.5 1.6 %collective-permute-start.3 = (bf16[2,32,4,384]{3,1,0,2:T(8,128)(2,1)S(1)}, bf16[2,32,4,384]{3,1,0,2:T(8,128)(2,1)S(1)}, u32[]{:S(2)}, u32[]{:S(2)}) collective-permute-start(bf16[2,32,4,384]{3,1,0,2:T(8,128)(2,1)S(1)} %collective-permute-done.2), channel_id=1, source_target_pairs={{0,8},{8,16},{16,24},{24,28},{28,20},{20,12},{12,4},{4,0},{1,9},{9... | collective-permute-start | bytes 589832 | tf_op jit(solution)/shard_map/ppermute | solution.py:114
  43.5 2.7 %collective-permute-done.3 = bf16[2,32,4,384]{3,1,0,2:T(8,128)(2,1)S(1)} collective-permute-done((bf16[2,32,4,384]{3,1,0,2:T(8,128)(2,1)S(1)}, bf16[2,32,4,384]{3,1,0,2:T(8,128)(2,1)S(1)}, u32[]{:S(2)}, u32[]{:S(2)}) %collective-permute-start.3) | collective-permute-done | bytes 196640 | tf_op jit(solution)/shard_map/ppermute | solution.py:114
  46.2 0.7 %constant_dynamic-update-slice_fusion.3 = bf16[16,32,4,384]{3,1,0,2:T(8,128)(2,1)} fusion(bf16[16,32,4,384]{3,1,0,2:T(8,128)(2,1)} %constant_dynamic-update-slice_fusion.4, bf16[2,32,4,384]{3,1,0,2:T(8,128)(2,1)S(1)} %collective-permute-done.3), kind=kLoop, calls=%fused_computation.56 | loop fusion | bytes 393216
  46.9 0.7 %constant_dynamic-update-slice_fusion.2 = bf16[16,32,4,384]{3,1,0,2:T(8,128)(2,1)} fusion(bf16[16,32,4,384]{3,1,0,2:T(8,128)(2,1)} %constant_dynamic-update-slice_fusion.3, bf16[2,32,4,384]{3,1,0,2:T(8,128)(2,1)S(1)} %collective-permute-done.4), kind=kLoop, calls=%fused_computation.55 | loop fusion | bytes 393216
  47.6 0.7 %constant_dynamic-update-slice_fusion.1 = bf16[16,32,4,384]{3,1,0,2:T(8,128)(2,1)} fusion(bf16[16,32,4,384]{3,1,0,2:T(8,128)(2,1)} %constant_dynamic-update-slice_fusion.2, bf16[2,32,4,384]{3,1,0,2:T(8,128)(2,1)S(1)} %collective-permute-done.5), kind=kLoop, calls=%fused_computation.54 | loop fusion | bytes 393216
  48.4 0.7 %constant_dynamic-update-slice_fusion = bf16[16,32,4,384]{3,1,0,2:T(8,128)(2,1)} fusion(bf16[16,32,4,384]{3,1,0,2:T(8,128)(2,1)} %constant_dynamic-update-slice_fusion.1, bf16[2,32,4,384]{3,1,0,2:T(8,128)(2,1)S(1)} %collective-permute-done.6), kind=kLoop, calls=%fused_computation.53 | loop fusion | bytes 393216 | tf_op jit(solution)/shard_map/concatenate | solution.py:128
  49.1 2.5 %gather_fusion.1 = bf16[24,32,4,384]{3,1,2,0:T(8,128)(2,1)S(1)} fusion(bf16[16,32,4,384]{3,1,0,2:T(8,128)(2,1)} %constant_dynamic-update-slice_fusion, s32[1024]{0:T(1024)S(1)} %pad_clamp_fusion), kind=kCustom, calls=%fused_computation.1 | custom fusion | bytes 4718688 | tf_op jit(solution)/shard_map/gather | solution.py:156
  51.6 1.3 %fusion.48 = (bf16[24,32,4,128]{3,1,2,0:T(8,128)(2,1)}, bf16[24,32,4,128]{3,1,2,0:T(8,128)(2,1)S(1)}) fusion(bf16[24,32,4,384]{3,1,2,0:T(8,128)(2,1)S(1)} %gather_fusion.1), kind=kLoop, calls=%fused_computation.97 | loop fusion | bytes 3145728 | tf_op jit(solution)/shard_map/slice | solution.py:74
  53.6 0.7 %and_or_fusion = pred[24,32,48]{2,1,0:T(8,128)(4,1)} fusion(pred[24,48]{1,0:T(8,128)(4,1)S(1)} %broadcast_compare_fusion, pred[32,48]{1,0:T(8,128)(4,1)S(1)} %iota_compare_fusion, pred[48]{0:T(512)(128)(4,1)S(1)} %broadcast_compare_fusion.1), kind=kLoop, calls=%fused_computation.37 | loop fusion | flops 73728 | bytes 39600 | tf_op jit(solution)/shard_map/or | solution.py:85
  54.3 4.0 %fusion.52 = (f32[24,4,32]{2,1,0:T(4,128)}, f32[24,4,32,48]{3,2,1,0:T(8,128)}) fusion(bf16[24,32,4,128]{3,1,2,0:T(8,128)(2,1)} %get-tuple-element.4, bf16[24,16,4,128]{3,1,2,0:T(8,128)(2,1)} %get-tuple-element.6, bf16[24,32,4,384]{3,1,2,0:T(8,128)(2,1)S(1)} %gather_fusion.1, pred[24,32,48]{2,1,0:T(8,128)(4,1)} %and_or_fusion), kind=kOutput, calls=%fused_computation.101 | convolution fusion | flops 40845360 | bytes 2764800 | tf_op jit(solution)/shard_map/sub | solution.py:41
  58.4 2.0 %fusion.8 = bf16[24,4,4,8,128]{4,3,2,1,0:T(8,128)(2,1)S(1)} fusion(bf16[24,32,4,128]{3,1,2,0:T(8,128)(2,1)S(1)} %get-tuple-element.5, bf16[24,16,4,128]{3,1,2,0:T(8,128)(2,1)S(1)} %get-tuple-element.7, f32[24,4,32,48]{3,2,1,0:T(8,128)} %get-tuple-element.20, f32[24,4,32]{2,1,0:T(4,128)} %get-tuple-element.19, pred[24,32]{1,0:T(8,128)(4,1)S(1)} %iota_compare_fusion.1), kind=kOutput, calls=%fused_computation.16 | convolution fusion | flops 41189376 | bytes 2568960 | tf_op jit(solution)/shard_map/bhit,bthd->bihd/dot_general | solution.py:89
  60.4 1.0 %copy.43 = bf16[24,4,4,8,128]{4,3,1,2,0:T(8,128)(2,1)} copy(bf16[24,4,4,8,128]{4,3,2,1,0:T(8,128)(2,1)S(1)} %fusion.8) | data formatting | bytes 1572864 | tf_op jit(solution)/shard_map/convert_element_type | solution.py:92
  (52 shorter events, 8.6 us)
Async XLA Ops:
  19.7 0.8 %copy-start.2 = (s32[2]{0:T(128)S(1)}, s32[2]{0:T(128)}, u32[]{:S(2)}) copy-start(s32[2]{0:T(128)} %param.9) | copy-start | bytes 28
  20.2 4.3 %copy-start.1 = (s32[24]{0:T(128)S(1)}, s32[24]{0:T(128)}, u32[]{:S(2)}) copy-start(s32[24]{0:T(128)} %param.10) | copy-start | bytes 292
  20.2 4.3 %copy-start = (s32[8]{0:T(128)S(1)}, s32[8]{0:T(128)}, u32[]{:S(2)}) copy-start(s32[8]{0:T(128)} %constant.80.clone) | copy-start | bytes 100
  21.4 7.2 %collective-permute-start = (bf16[2,32,4,384]{3,1,0,2:T(8,128)(2,1)S(1)}, bf16[2,32,4,384]{3,1,0,2:T(8,128)(2,1)S(1)}, u32[]{:S(2)}, u32[]{:S(2)}) collective-permute-start(bf16[2,32,4,384]{3,1,0,2:T(8,128)(2,1)S(1)} %get-tuple-element.3), channel_id=1, source_target_pairs={{0,8},{8,16},{16,24},{24,28},{28,20},{20,12},{12,4},{4,0},{1,9},{9... | collective-permute-start | bytes 589832 | tf_op jit(solution)/shard_map/ppermute | solution.py:114
  23.0 7.2 %collective-permute-start.4 = (bf16[2,32,4,384]{3,1,0,2:T(8,128)(2,1)S(1)}, bf16[2,32,4,384]{3,1,0,2:T(8,128)(2,1)S(1)}, u32[]{:S(2)}, u32[]{:S(2)}) collective-permute-start(bf16[2,32,4,384]{3,1,0,2:T(8,128)(2,1)S(1)} %get-tuple-element.3), channel_id=1, source_target_pairs={{8,0},{16,8},{24,16},{28,24},{20,28},{12,20},{4,12},{0,4},{9,1},{1... | collective-permute-start | bytes 589832 | tf_op jit(solution)/shard_map/ppermute | solution.py:118
  28.6 6.3 %collective-permute-start.1 = (bf16[2,32,4,384]{3,1,0,2:T(8,128)(2,1)S(1)}, bf16[2,32,4,384]{3,1,0,2:T(8,128)(2,1)S(1)}, u32[]{:S(2)}, u32[]{:S(2)}) collective-permute-start(bf16[2,32,4,384]{3,1,0,2:T(8,128)(2,1)S(1)} %collective-permute-done), channel_id=1, source_target_pairs={{0,8},{8,16},{16,24},{24,28},{28,20},{20,12},{12,4},{4,0},{1,9},{9... | collective-permute-start | bytes 589832 | tf_op jit(solution)/shard_map/ppermute | solution.py:114
  30.2 7.0 %collective-permute-start.5 = (bf16[2,32,4,384]{3,1,0,2:T(8,128)(2,1)S(1)}, bf16[2,32,4,384]{3,1,0,2:T(8,128)(2,1)S(1)}, u32[]{:S(2)}, u32[]{:S(2)}) collective-permute-start(bf16[2,32,4,384]{3,1,0,2:T(8,128)(2,1)S(1)} %collective-permute-done.4), channel_id=1, source_target_pairs={{8,0},{16,8},{24,16},{28,24},{20,28},{12,20},{4,12},{0,4},{9,1},{1... | collective-permute-start | bytes 589832 | tf_op jit(solution)/shard_map/ppermute | solution.py:118
  34.9 5.7 %collective-permute-start.2 = (bf16[2,32,4,384]{3,1,0,2:T(8,128)(2,1)S(1)}, bf16[2,32,4,384]{3,1,0,2:T(8,128)(2,1)S(1)}, u32[]{:S(2)}, u32[]{:S(2)}) collective-permute-start(bf16[2,32,4,384]{3,1,0,2:T(8,128)(2,1)S(1)} %collective-permute-done.1), channel_id=1, source_target_pairs={{0,8},{8,16},{16,24},{24,28},{28,20},{20,12},{12,4},{4,0},{1,9},{9... | collective-permute-start | bytes 589832 | tf_op jit(solution)/shard_map/ppermute | solution.py:114
  37.2 11.2 %collective-permute-start.6 = (bf16[2,32,4,384]{3,1,0,2:T(8,128)(2,1)S(1)}, bf16[2,32,4,384]{3,1,0,2:T(8,128)(2,1)S(1)}, u32[]{:S(2)}, u32[]{:S(2)}) collective-permute-start(bf16[2,32,4,384]{3,1,0,2:T(8,128)(2,1)S(1)} %collective-permute-done.5), channel_id=1, source_target_pairs={{8,0},{16,8},{24,16},{28,24},{20,28},{12,20},{4,12},{0,4},{9,1},{1... | collective-permute-start | bytes 589832 | tf_op jit(solution)/shard_map/ppermute | solution.py:118
  40.5 5.7 %collective-permute-start.3 = (bf16[2,32,4,384]{3,1,0,2:T(8,128)(2,1)S(1)}, bf16[2,32,4,384]{3,1,0,2:T(8,128)(2,1)S(1)}, u32[]{:S(2)}, u32[]{:S(2)}) collective-permute-start(bf16[2,32,4,384]{3,1,0,2:T(8,128)(2,1)S(1)} %collective-permute-done.2), channel_id=1, source_target_pairs={{0,8},{8,16},{16,24},{24,28},{28,20},{20,12},{12,4},{4,0},{1,9},{9... | collective-permute-start | bytes 589832 | tf_op jit(solution)/shard_map/ppermute | solution.py:114

commit v4 on v3

--- a/solution.py
+++ b/solution.py
@@ -128,7 +128,7 @@
     return jnp.concatenate(parts, axis=0), rows_of
 
 
-def local(query_embeds, passage_embeds, passage_lengths, cand_passage, norm_gain, w_qkv):
+def local(query_embeds, passage_embeds, passage_lengths_in, cand_passage, norm_gain, w_qkv):
     quer_count, query_len, width_part = query_embeds.shape
     pass_count, passage_len = (passage_embeds.shape[0], passage_embeds.shape[1])
     pairs_dev = cand_passage.shape[0]
@@ -143,20 +143,31 @@
     all_rows = jnp.concatenate([query_rows, passage_rows], axis=0)
     full_rows = lax.all_gather(all_rows, "tp", axis=1, tiled=True)
     normed = rms_rows(full_rows, norm_gain)
-    raw = jnp.einsum("nk,khc->nhc", normed, w_qkv, preferred_element_type=jnp.float32)
-    projected = rotate_parts(raw, jnp.concatenate([query_pos, passage_pos], axis=0), head_dim)
-    query_qkv = projected[:query_total].reshape(quer_count, query_len, heads_part, 3 * head_dim)
-    own_qkv = projected[query_total:].reshape(pass_count, passage_len, heads_part, 3 * head_dim)
-    padded = jnp.arange(passage_len, dtype=jnp.int32)[None, :] >= passage_lengths[:, None]
-    head_at = lax.broadcasted_iota(jnp.int32, own_qkv.shape, 2)
-    col_at = lax.broadcasted_iota(jnp.int32, own_qkv.shape, 3)
-    mark = padded[:, :, None, None] & (head_at == 0) & (col_at == head_dim)
-    own_qkv = jnp.where(mark, jnp.asarray(jnp.inf, own_qkv.dtype), own_qkv)
-    store_qkv, rows_of = gather_store(own_qkv)
-    pair_qkv = store_qkv[rows_of(cand_passage)]
-    pair_lengths = jnp.sum(jnp.isfinite(pair_qkv[:, :, 0, head_dim]).astype(jnp.int32), axis=1)
-    query_attn = attend_queries(query_qkv, head_dim)
-    passage_attn = attend_pairs(query_qkv, pair_qkv, pair_lengths, head_dim, cands)
+    positions = jnp.concatenate([query_pos, passage_pos], axis=0)
+    groups = 2 if heads_part % 2 == 0 else 1
+    per_group = heads_part // groups
+    query_outs, pair_outs = [], []
+    pair_lengths = None
+    for group in range(groups):
+        w_part = w_qkv[:, group * per_group : (group + 1) * per_group, :]
+        raw = jnp.einsum("nk,khc->nhc", normed, w_part, preferred_element_type=jnp.float32)
+        projected = rotate_parts(raw, positions, head_dim)
+        query_qkv = projected[:query_total].reshape(quer_count, query_len, per_group, 3 * head_dim)
+        own_qkv = projected[query_total:].reshape(pass_count, passage_len, per_group, 3 * head_dim)
+        if group == 0:
+            padded = jnp.arange(passage_len, dtype=jnp.int32)[None, :] >= passage_lengths_in[:, None]
+            head_at = lax.broadcasted_iota(jnp.int32, own_qkv.shape, 2)
+            col_at = lax.broadcasted_iota(jnp.int32, own_qkv.shape, 3)
+            mark = padded[:, :, None, None] & (head_at == 0) & (col_at == head_dim)
+            own_qkv = jnp.where(mark, jnp.asarray(jnp.inf, own_qkv.dtype), own_qkv)
+        store_qkv, rows_of = gather_store(own_qkv)
+        pair_qkv = store_qkv[rows_of(cand_passage)]
+        if group == 0:
+            pair_lengths = jnp.sum(jnp.isfinite(pair_qkv[:, :, 0, head_dim]).astype(jnp.int32), axis=1)
+        query_outs.append(attend_queries(query_qkv, head_dim))
+        pair_outs.append(attend_pairs(query_qkv, pair_qkv, pair_lengths, head_dim, cands))
+    query_attn = jnp.concatenate(query_outs, axis=-1)
+    passage_attn = jnp.concatenate(pair_outs, axis=-1)
     return (query_attn, passage_attn)
 
 

time: 61.7 us -> 67.1 us (1.088)
  starting transfers between devices: 7.7 us -> 15.5 us
  waiting for transfers between devices: 10.8 us -> 3.38 us
  local copies, waits for them, and re-layouts: 13.3 us -> 20.4 us
  matrix products: 13.3 us -> 10.2 us
  other arithmetic: 5.44 us -> 6.12 us
    slice x0 -> x1, local copies, waits for them, and re-layouts: none -> 12.9 us  [local(): w_part = w_qkv[:, group * per_group:(group + 1) * per_group, :]]
    ppermute x4 -> x8, waiting for transfers between devices: 10.8 us -> 3.36 us  [gather_store(): ahead = lax.ppermute(ahead, 'store', forward)]
    ppermute x4 -> x8, starting transfers between devices: 6.3 us -> 12.7 us  [gather_store(): ahead = lax.ppermute(ahead, 'store', forward)]
    dot_general x1 -> x2, matrix products: 6.85 us -> 2.59 us  [local(): jnp.einsum('nk,khc->nhc', normed, w_part, preferred_element_type=jnp.floa...]
    unnamed x12 -> x35, local copies, waits for them, and re-layouts: 4.3 us -> 0.29 us
    concatenate x1 -> x3, other arithmetic: 0.08 us -> 1.65 us  [the longest x1 0.94 us: local(): passage_attn = jnp.concatenate(pair_outs, axis=-1)]
    ppermute x3 -> x6, starting transfers between devices: 1.41 us -> 2.79 us  [gather_store(): behind = lax.ppermute(behind, 'store', backward)]
    sub x2 -> x4, matrix products: 4.22 us -> 5.28 us  [softmax_rounded(): expon = jnp.where(allowed, jnp.exp(masked - peak), jnp.float32(0.0))]
  transfers between devices with their start and end apart: 7 -> 14, of which waited for: 4 -> 4; matrix products, arithmetic and copies ran while one was open for 14% -> 13% of each run, Pallas kernels for 0% -> 0%
where the time goes in v4:
time: 67.1 us; the launch traced here: 66.9 us
  local copies, waits for them, and re-layouts  20.4 us (30%)
  starting transfers between devices  15.5 us (23%)
  matrix products  10.2 us (15%)
  blocking collectives  10.1 us (15%)
  other arithmetic  6.12 us (9%)
  waiting for transfers between devices  3.38 us (5%)
  between operations  1.13 us (2%)
    slice x1, local copies, waits for them, and re-layouts, local(): w_part = w_qkv[:, group * per_group:(group + 1) * per_group, :]  12.9 us
    ppermute x8, starting transfers between devices, gather_store(): ahead = lax.ppermute(ahead, 'store', forward)  12.7 us
    all_gather x1, blocking collectives, local(): full_rows = lax.all_gather(all_rows, 'tp', axis=1, tiled=True)  10.1 us
    sub x4, matrix products, softmax_rounded(): expon = jnp.where(allowed, jnp.exp(masked - peak), jnp.float32(0.0))  5.28 us
    ppermute x8, waiting for transfers between devices, gather_store(): ahead = lax.ppermute(ahead, 'store', forward)  3.36 us
    ppermute x6, starting transfers between devices, gather_store(): behind = lax.ppermute(behind, 'store', backward)  2.79 us
    dot_general x2, matrix products, local(): jnp.einsum('nk,khc->nhc', normed, w_part, preferred_element_type=jnp.floa...  2.59 us
    dot_general x2, matrix products, attend_core(): jnp.einsum('bhit,bthd->bihd', weights, values, preferred_element_type=jnp...  1.98 us
  transfers between devices with their start and end apart: 14, of which 4 were waited for; matrix products, arithmetic and copies ran while one was open for 13% of the time, Pallas kernels for 0%

profile of v4, /device:TPU:0, one launch (start us, length us, event | category | flops | bytes accessed | tf_op | source)
XLA Modules:
  0.0 66.9 jit_solution(123661123906714177)
XLA Ops:
  0.7 0.9 %pad_maximum_fusion.1 = bf16[96,1024]{1,0:T(8,128)(2,1)S(1)} fusion(bf16[64,1024]{1,0:T(8,128)(2,1)} %bitcast.43, bf16[32,1024]{1,0:T(8,128)(2,1)} %bitcast.44), kind=kLoop, calls=%fused_computation.70 | loop fusion | flops 393216 | bytes 393216 | tf_op jit(solution)/shard_map/concatenate | solution.py:143
  1.6 10.1 %all_gather.3 = bf16[96,4096]{1,0:T(8,128)(2,1)S(1)} all-gather(bf16[96,1024]{1,0:T(8,128)(2,1)S(1)} %pad_maximum_fusion.1), channel_id=1, replica_groups=mesh['store'=8,'tp'=4] {'tp'}, dimensions={1}, use_global_device_ids=true | all-gather | bytes 983040 | tf_op jit(solution)/shard_map/all_gather | solution.py:144
  11.9 12.9 %fusion.93 = (bf16[4096,2,384]{2,1,0:T(2,128)(2,1)S(1)}, bf16[4096,2,384]{2,1,0:T(2,128)(2,1)S(1)}) fusion(bf16[4096,4,384]{2,1,0:T(4,128)(2,1)} %param.13), kind=kLoop, calls=%fused_computation.155 | loop fusion | bytes 25165824 | tf_op jit(solution)/shard_map/slice | solution.py:152
  24.9 1.3 %fusion.4 = f32[96,2,384]{2,0,1:T(8,128)S(1)} fusion(bf16[4096,2,384]{2,1,0:T(2,128)(2,1)S(1)} %get-tuple-element.5, bf16[96,4096]{1,0:T(8,128)(2,1)S(1)} %all_gather.3, f32[4096]{0:T(1024)S(1)} %convert_element_type.64, f32[96]{0:T(128)S(1)} %add_rsqrt_fusion), kind=kOutput, calls=%fused_computation.7 | convolution fusion | flops 605552640 | bytes 7389568 | tf_op jit(solution)/shard_map/nk,khc->nhc/dot_general | solution.py:153
  26.2 1.3 %fusion.6 = f32[96,2,384]{2,0,1:T(8,128)S(1)} fusion(bf16[4096,2,384]{2,1,0:T(2,128)(2,1)S(1)} %get-tuple-element.4, bf16[96,4096]{1,0:T(8,128)(2,1)S(1)} %all_gather.3, f32[4096]{0:T(1024)S(1)} %convert_element_type.64, f32[96]{0:T(128)S(1)} %add_rsqrt_fusion), kind=kOutput, calls=%fused_computation.9 | convolution fusion | flops 605552640 | bytes 7389568 | tf_op jit(solution)/shard_map/nk,khc->nhc/dot_general | solution.py:153
  28.6 1.6 %collective-permute-start = (bf16[2,32,2,384]{3,1,0,2:T(8,128)(2,1)S(1)}, bf16[2,32,2,384]{3,1,0,2:T(8,128)(2,1)S(1)}, u32[]{:S(2)}, u32[]{:S(2)}) collective-permute-start(bf16[2,32,2,384]{3,1,0,2:T(8,128)(2,1)S(1)} %get-tuple-element.3), channel_id=1, source_target_pairs={{0,8},{8,16},{16,24},{24,28},{28,20},{20,12},{12,4},{4,0},{1,9},{9... | collective-permute-start | bytes 294920 | tf_op jit(solution)/shard_map/ppermute | solution.py:114
  30.9 1.6 %collective-permute-start.7 = (bf16[2,32,2,384]{3,1,0,2:T(8,128)(2,1)S(1)}, bf16[2,32,2,384]{3,1,0,2:T(8,128)(2,1)S(1)}, u32[]{:S(2)}, u32[]{:S(2)}) collective-permute-start(bf16[2,32,2,384]{3,1,0,2:T(8,128)(2,1)S(1)} %bitcast.35), channel_id=1, source_target_pairs={{0,8},{8,16},{16,24},{24,28},{28,20},{20,12},{12,4},{4,0},{1,9},{9... | collective-permute-start | bytes 294920 | tf_op jit(solution)/shard_map/ppermute | solution.py:114
  35.2 0.8 %fusion.96 = (bf16[24,16,2,128]{3,1,2,0:T(8,128)(2,1)}, bf16[24,16,2,128]{3,1,2,0:T(8,128)(2,1)}) fusion(bf16[24,16,2,256]{3,1,2,0:T(8,128)(2,1)S(1)} %bitcast.33), kind=kLoop, calls=%fused_computation.158 | loop fusion | bytes 786432 | tf_op jit(solution)/shard_map/slice | solution.py:74
  36.0 0.8 %fusion.97 = (bf16[24,16,2,128]{3,1,2,0:T(8,128)(2,1)}, bf16[24,16,2,128]{3,1,2,0:T(8,128)(2,1)}) fusion(bf16[24,16,2,256]{3,1,2,0:T(8,128)(2,1)S(1)} %bitcast.34), kind=kLoop, calls=%fused_computation.159 | loop fusion | bytes 786432 | tf_op jit(solution)/shard_map/slice | solution.py:74
  38.7 1.6 %collective-permute-start.1 = (bf16[2,32,2,384]{3,1,0,2:T(8,128)(2,1)S(1)}, bf16[2,32,2,384]{3,1,0,2:T(8,128)(2,1)S(1)}, u32[]{:S(2)}, u32[]{:S(2)}) collective-permute-start(bf16[2,32,2,384]{3,1,0,2:T(8,128)(2,1)S(1)} %collective-permute-done), channel_id=1, source_target_pairs={{0,8},{8,16},{16,24},{24,28},{28,20},{20,12},{12,4},{4,0},{1,9},{9... | collective-permute-start | bytes 294920 | tf_op jit(solution)/shard_map/ppermute | solution.py:114
  40.8 1.6 %collective-permute-start.8 = (bf16[2,32,2,384]{3,1,0,2:T(8,128)(2,1)S(1)}, bf16[2,32,2,384]{3,1,0,2:T(8,128)(2,1)S(1)}, u32[]{:S(2)}, u32[]{:S(2)}) collective-permute-start(bf16[2,32,2,384]{3,1,0,2:T(8,128)(2,1)S(1)} %collective-permute-done.7), channel_id=1, source_target_pairs={{0,8},{8,16},{16,24},{24,28},{28,20},{20,12},{12,4},{4,0},{1,9},{9... | collective-permute-start | bytes 294920 | tf_op jit(solution)/shard_map/ppermute | solution.py:114
  42.9 1.3 %collective-permute-done.1 = bf16[2,32,2,384]{3,1,0,2:T(8,128)(2,1)S(1)} collective-permute-done((bf16[2,32,2,384]{3,1,0,2:T(8,128)(2,1)S(1)}, bf16[2,32,2,384]{3,1,0,2:T(8,128)(2,1)S(1)}, u32[]{:S(2)}, u32[]{:S(2)}) %collective-permute-start.1) | collective-permute-done | bytes 98336 | tf_op jit(solution)/shard_map/ppermute | solution.py:114
  44.3 1.6 %collective-permute-start.2 = (bf16[2,32,2,384]{3,1,0,2:T(8,128)(2,1)S(1)}, bf16[2,32,2,384]{3,1,0,2:T(8,128)(2,1)S(1)}, u32[]{:S(2)}, u32[]{:S(2)}) collective-permute-start(bf16[2,32,2,384]{3,1,0,2:T(8,128)(2,1)S(1)} %collective-permute-done.1), channel_id=1, source_target_pairs={{0,8},{8,16},{16,24},{24,28},{28,20},{20,12},{12,4},{4,0},{1,9},{9... | collective-permute-start | bytes 294920 | tf_op jit(solution)/shard_map/ppermute | solution.py:114
  46.3 1.6 %collective-permute-start.9 = (bf16[2,32,2,384]{3,1,0,2:T(8,128)(2,1)S(1)}, bf16[2,32,2,384]{3,1,0,2:T(8,128)(2,1)S(1)}, u32[]{:S(2)}, u32[]{:S(2)}) collective-permute-start(bf16[2,32,2,384]{3,1,0,2:T(8,128)(2,1)S(1)} %collective-permute-done.8), channel_id=1, source_target_pairs={{0,8},{8,16},{16,24},{24,28},{28,20},{20,12},{12,4},{4,0},{1,9},{9... | collective-permute-start | bytes 294920 | tf_op jit(solution)/shard_map/ppermute | solution.py:114
  49.0 1.6 %collective-permute-start.3 = (bf16[2,32,2,384]{3,1,0,2:T(8,128)(2,1)S(1)}, bf16[2,32,2,384]{3,1,0,2:T(8,128)(2,1)S(1)}, u32[]{:S(2)}, u32[]{:S(2)}) collective-permute-start(bf16[2,32,2,384]{3,1,0,2:T(8,128)(2,1)S(1)} %collective-permute-done.2), channel_id=1, source_target_pairs={{0,8},{8,16},{16,24},{24,28},{28,20},{20,12},{12,4},{4,0},{1,9},{9... | collective-permute-start | bytes 294920 | tf_op jit(solution)/shard_map/ppermute | solution.py:114
  50.6 1.0 %collective-permute-done.9 = bf16[2,32,2,384]{3,1,0,2:T(8,128)(2,1)S(1)} collective-permute-done((bf16[2,32,2,384]{3,1,0,2:T(8,128)(2,1)S(1)}, bf16[2,32,2,384]{3,1,0,2:T(8,128)(2,1)S(1)}, u32[]{:S(2)}, u32[]{:S(2)}) %collective-permute-start.9) | collective-permute-done | bytes 98336 | tf_op jit(solution)/shard_map/ppermute | solution.py:114
  51.6 1.6 %collective-permute-start.10 = (bf16[2,32,2,384]{3,1,0,2:T(8,128)(2,1)S(1)}, bf16[2,32,2,384]{3,1,0,2:T(8,128)(2,1)S(1)}, u32[]{:S(2)}, u32[]{:S(2)}) collective-permute-start(bf16[2,32,2,384]{3,1,0,2:T(8,128)(2,1)S(1)} %collective-permute-done.9), channel_id=1, source_target_pairs={{0,8},{8,16},{16,24},{24,28},{28,20},{20,12},{12,4},{4,0},{1,9},{9... | collective-permute-start | bytes 294920 | tf_op jit(solution)/shard_map/ppermute | solution.py:114
  53.7 0.8 %gather_fusion.1 = bf16[24,32,2,384]{3,1,2,0:T(8,128)(2,1)S(1)} fusion(bf16[16,32,2,384]{3,1,0,2:T(8,128)(2,1)S(1)} %constant_dynamic-update-slice_fusion, s32[1024]{0:T(1024)S(1)} %pad_clamp_fusion), kind=kCustom, calls=%fused_computation.1 | custom fusion | bytes 2359392 | tf_op jit(solution)/shard_map/gather | solution.py:164
  54.5 1.0 %fusion.94 = (bf16[24,32,2,128]{3,1,2,0:T(8,128)(2,1)}, bf16[24,32,2,128]{3,1,2,0:T(8,128)(2,1)S(1)}) fusion(bf16[24,32,2,384]{3,1,2,0:T(8,128)(2,1)S(1)} %gather_fusion.1), kind=kLoop, calls=%fused_computation.156 | loop fusion | bytes 1572864 | tf_op jit(solution)/shard_map/slice | solution.py:74
  57.2 1.0 %fusion.95 = (bf16[24,32,2,128]{3,1,2,0:T(8,128)(2,1)}, bf16[24,32,2,128]{3,1,2,0:T(8,128)(2,1)S(1)}) fusion(bf16[24,32,2,384]{3,1,2,0:T(8,128)(2,1)S(1)} %gather_fusion.2), kind=kLoop, calls=%fused_computation.157 | loop fusion | bytes 1572864 | tf_op jit(solution)/shard_map/slice | solution.py:74
  58.8 3.1 %fusion.107 = (f32[24,2,32]{2,1,0:T(2,128)}, f32[24,2,32,48]{3,2,1,0:T(8,128)}) fusion(bf16[24,32,2,128]{3,1,2,0:T(8,128)(2,1)S(1)} %copy-done.1, bf16[24,16,2,128]{3,1,2,0:T(8,128)(2,1)} %get-tuple-element.10, bf16[24,32,2,384]{3,1,2,0:T(8,128)(2,1)S(1)} %gather_fusion.1, pred[24,32,48]{2,1,0:T(8,128)(4,1)} %and_or_fusion), kind=kOutput, calls=%fused_computation.165 | convolution fusion | flops 20422704 | bytes 1480704 | tf_op jit(solution)/shard_map/sub | solution.py:41
  62.0 1.9 %fusion.102 = (f32[24,2,32]{2,1,0:T(2,128)S(1)}, f32[24,2,32,48]{3,2,1,0:T(8,128)S(1)}) fusion(bf16[24,32,2,128]{3,1,2,0:T(8,128)(2,1)} %get-tuple-element.8, bf16[24,16,2,128]{3,1,2,0:T(8,128)(2,1)} %get-tuple-element.12, bf16[24,32,2,384]{3,1,2,0:T(8,128)(2,1)S(1)} %gather_fusion.2, pred[24,32,48]{2,1,0:T(8,128)(4,1)} %and_or_fusion), kind=kOutput, calls=%fused_computation.164 | convolution fusion | flops 20422704 | bytes 1480704 | tf_op jit(solution)/shard_map/sub | solution.py:41
  63.9 1.6 %fusion.22 = bf16[24,2,4,8,128]{4,3,2,1,0:T(8,128)(2,1)S(1)} fusion(bf16[24,32,2,128]{3,1,2,0:T(8,128)(2,1)S(1)} %get-tuple-element.7, bf16[24,16,2,128]{3,1,2,0:T(8,128)(2,1)S(1)} %copy-done.2, f32[24,2,32,48]{3,2,1,0:T(8,128)} %get-tuple-element.41, f32[24,2,32]{2,1,0:T(2,128)S(1)} %copy-done.10, pred[24,32]{1,0:T(8,128)(4,1)S(1)} %iota_compare_fusion.1), kind=kOutput, calls=%fused_computation.31 | convolution fusion | flops 20594688 | bytes 1284864 | tf_op jit(solution)/shard_map/bhit,bthd->bihd/dot_general | solution.py:89
  65.9 0.9 %pad_maximum_fusion = bf16[24,32,512]{2,1,0:T(8,128)(2,1)} fusion(bf16[24,32,256]{2,1,0:T(8,128)(2,1)S(1)} %get-tuple-element.44, bf16[24,32,256]{2,1,0:T(8,128)(2,1)S(1)} %get-tuple-element.45), kind=kLoop, calls=%fused_computation.47 | loop fusion | flops 1572864 | bytes 1572864 | tf_op jit(solution)/shard_map/concatenate | solution.py:170
  (109 shorter events, 12.2 us)
Async XLA Ops:
  11.9 13.0 %copy-start.6 = (bf16[4096]{0:T(1024)(128)(2,1)S(1)}, bf16[4096]{0:T(1024)(128)(2,1)}, u32[]{:S(2)}) copy-start(bf16[4096]{0:T(1024)(128)(2,1)} %param.12) | copy-start | bytes 24580
  28.0 5.0 %copy-start.8 = (s32[24]{0:T(128)S(1)}, s32[24]{0:T(128)}, u32[]{:S(2)}) copy-start(s32[24]{0:T(128)} %param.11) | copy-start | bytes 292
  28.1 5.1 %copy-start = (s32[8]{0:T(128)S(1)}, s32[8]{0:T(128)}, u32[]{:S(2)}) copy-start(s32[8]{0:T(128)} %constant.90.clone) | copy-start | bytes 100
  28.6 10.1 %collective-permute-start = (bf16[2,32,2,384]{3,1,0,2:T(8,128)(2,1)S(1)}, bf16[2,32,2,384]{3,1,0,2:T(8,128)(2,1)S(1)}, u32[]{:S(2)}, u32[]{:S(2)}) collective-permute-start(bf16[2,32,2,384]{3,1,0,2:T(8,128)(2,1)S(1)} %get-tuple-element.3), channel_id=1, source_target_pairs={{0,8},{8,16},{16,24},{24,28},{28,20},{20,12},{12,4},{4,0},{1,9},{9... | collective-permute-start | bytes 294920 | tf_op jit(solution)/shard_map/ppermute | solution.py:114
  30.3 10.1 %collective-permute-start.4 = (bf16[2,32,2,384]{3,1,0,2:T(8,128)(2,1)S(1)}, bf16[2,32,2,384]{3,1,0,2:T(8,128)(2,1)S(1)}, u32[]{:S(2)}, u32[]{:S(2)}) collective-permute-start(bf16[2,32,2,384]{3,1,0,2:T(8,128)(2,1)S(1)} %get-tuple-element.3), channel_id=1, source_target_pairs={{8,0},{16,8},{24,16},{28,24},{20,28},{12,20},{4,12},{0,4},{9,1},{1... | collective-permute-start | bytes 294920 | tf_op jit(solution)/shard_map/ppermute | solution.py:118
  30.9 9.9 %collective-permute-start.7 = (bf16[2,32,2,384]{3,1,0,2:T(8,128)(2,1)S(1)}, bf16[2,32,2,384]{3,1,0,2:T(8,128)(2,1)S(1)}, u32[]{:S(2)}, u32[]{:S(2)}) collective-permute-start(bf16[2,32,2,384]{3,1,0,2:T(8,128)(2,1)S(1)} %bitcast.35), channel_id=1, source_target_pairs={{0,8},{8,16},{16,24},{24,28},{28,20},{20,12},{12,4},{4,0},{1,9},{9... | collective-permute-start | bytes 294920 | tf_op jit(solution)/shard_map/ppermute | solution.py:114
  32.5 9.9 %collective-permute-start.11 = (bf16[2,32,2,384]{3,1,0,2:T(8,128)(2,1)S(1)}, bf16[2,32,2,384]{3,1,0,2:T(8,128)(2,1)S(1)}, u32[]{:S(2)}, u32[]{:S(2)}) collective-permute-start(bf16[2,32,2,384]{3,1,0,2:T(8,128)(2,1)S(1)} %bitcast.36), channel_id=1, source_target_pairs={{8,0},{16,8},{24,16},{28,24},{20,28},{12,20},{4,12},{0,4},{9,1},{1... | collective-permute-start | bytes 294920 | tf_op jit(solution)/shard_map/ppermute | solution.py:118
  38.7 5.5 %collective-permute-start.1 = (bf16[2,32,2,384]{3,1,0,2:T(8,128)(2,1)S(1)}, bf16[2,32,2,384]{3,1,0,2:T(8,128)(2,1)S(1)}, u32[]{:S(2)}, u32[]{:S(2)}) collective-permute-start(bf16[2,32,2,384]{3,1,0,2:T(8,128)(2,1)S(1)} %collective-permute-done), channel_id=1, source_target_pairs={{0,8},{8,16},{16,24},{24,28},{28,20},{20,12},{12,4},{4,0},{1,9},{9... | collective-permute-start | bytes 294920 | tf_op jit(solution)/shard_map/ppermute | solution.py:114
  40.3 5.5 %collective-permute-start.5 = (bf16[2,32,2,384]{3,1,0,2:T(8,128)(2,1)S(1)}, bf16[2,32,2,384]{3,1,0,2:T(8,128)(2,1)S(1)}, u32[]{:S(2)}, u32[]{:S(2)}) collective-permute-start(bf16[2,32,2,384]{3,1,0,2:T(8,128)(2,1)S(1)} %collective-permute-done.4), channel_id=1, source_target_pairs={{8,0},{16,8},{24,16},{28,24},{20,28},{12,20},{4,12},{0,4},{9,1},{1... | collective-permute-start | bytes 294920 | tf_op jit(solution)/shard_map/ppermute | solution.py:118
  40.8 5.5 %collective-permute-start.8 = (bf16[2,32,2,384]{3,1,0,2:T(8,128)(2,1)S(1)}, bf16[2,32,2,384]{3,1,0,2:T(8,128)(2,1)S(1)}, u32[]{:S(2)}, u32[]{:S(2)}) collective-permute-start(bf16[2,32,2,384]{3,1,0,2:T(8,128)(2,1)S(1)} %collective-permute-done.7), channel_id=1, source_target_pairs={{0,8},{8,16},{16,24},{24,28},{28,20},{20,12},{12,4},{4,0},{1,9},{9... | collective-permute-start | bytes 294920 | tf_op jit(solution)/shard_map/ppermute | solution.py:114
  42.4 11.3 %copy-start.4 = (bf16[2,32,2,384]{3,1,0,2:T(8,128)(2,1)}, bf16[2,32,2,384]{3,1,0,2:T(8,128)(2,1)S(1)}, u32[]{:S(2)}) copy-start(bf16[2,32,2,384]{3,1,0,2:T(8,128)(2,1)S(1)} %collective-permute-done.11) | copy-start | bytes 294916
  42.4 5.5 %collective-permute-start.12 = (bf16[2,32,2,384]{3,1,0,2:T(8,128)(2,1)S(1)}, bf16[2,32,2,384]{3,1,0,2:T(8,128)(2,1)S(1)}, u32[]{:S(2)}, u32[]{:S(2)}) collective-permute-start(bf16[2,32,2,384]{3,1,0,2:T(8,128)(2,1)S(1)} %collective-permute-done.11), channel_id=1, source_target_pairs={{8,0},{16,8},{24,16},{28,24},{20,28},{12,20},{4,12},{0,4},{9,1},{1... | collective-permute-start | bytes 294920 | tf_op jit(solution)/shard_map/ppermute | solution.py:118
  44.3 4.7 %collective-permute-start.2 = (bf16[2,32,2,384]{3,1,0,2:T(8,128)(2,1)S(1)}, bf16[2,32,2,384]{3,1,0,2:T(8,128)(2,1)S(1)}, u32[]{:S(2)}, u32[]{:S(2)}) collective-permute-start(bf16[2,32,2,384]{3,1,0,2:T(8,128)(2,1)S(1)} %collective-permute-done.1), channel_id=1, source_target_pairs={{0,8},{8,16},{16,24},{24,28},{28,20},{20,12},{12,4},{4,0},{1,9},{9... | collective-permute-start | bytes 294920 | tf_op jit(solution)/shard_map/ppermute | solution.py:114
  45.8 7.8 %collective-permute-start.6 = (bf16[2,32,2,384]{3,1,0,2:T(8,128)(2,1)S(1)}, bf16[2,32,2,384]{3,1,0,2:T(8,128)(2,1)S(1)}, u32[]{:S(2)}, u32[]{:S(2)}) collective-permute-start(bf16[2,32,2,384]{3,1,0,2:T(8,128)(2,1)S(1)} %collective-permute-done.5), channel_id=1, source_target_pairs={{8,0},{16,8},{24,16},{28,24},{20,28},{12,20},{4,12},{0,4},{9,1},{1... | collective-permute-start | bytes 294920 | tf_op jit(solution)/shard_map/ppermute | solution.py:118
  46.3 5.3 %collective-permute-start.9 = (bf16[2,32,2,384]{3,1,0,2:T(8,128)(2,1)S(1)}, bf16[2,32,2,384]{3,1,0,2:T(8,128)(2,1)S(1)}, u32[]{:S(2)}, u32[]{:S(2)}) collective-permute-start(bf16[2,32,2,384]{3,1,0,2:T(8,128)(2,1)S(1)} %collective-permute-done.8), channel_id=1, source_target_pairs={{0,8},{8,16},{16,24},{24,28},{28,20},{20,12},{12,4},{4,0},{1,9},{9... | collective-permute-start | bytes 294920 | tf_op jit(solution)/shard_map/ppermute | solution.py:114
  47.9 8.4 %collective-permute-start.13 = (bf16[2,32,2,384]{3,1,0,2:T(8,128)(2,1)S(1)}, bf16[2,32,2,384]{3,1,0,2:T(8,128)(2,1)S(1)}, u32[]{:S(2)}, u32[]{:S(2)}) collective-permute-start(bf16[2,32,2,384]{3,1,0,2:T(8,128)(2,1)S(1)} %collective-permute-done.12), channel_id=1, source_target_pairs={{8,0},{16,8},{24,16},{28,24},{20,28},{12,20},{4,12},{0,4},{9,1},{1... | collective-permute-start | bytes 294920 | tf_op jit(solution)/shard_map/ppermute | solution.py:118
  49.0 4.6 %collective-permute-start.3 = (bf16[2,32,2,384]{3,1,0,2:T(8,128)(2,1)S(1)}, bf16[2,32,2,384]{3,1,0,2:T(8,128)(2,1)S(1)}, u32[]{:S(2)}, u32[]{:S(2)}) collective-permute-start(bf16[2,32,2,384]{3,1,0,2:T(8,128)(2,1)S(1)} %collective-permute-done.2), channel_id=1, source_target_pairs={{0,8},{8,16},{16,24},{24,28},{28,20},{20,12},{12,4},{4,0},{1,9},{9... | collective-permute-start | bytes 294920 | tf_op jit(solution)/shard_map/ppermute | solution.py:114
  51.6 4.6 %collective-permute-start.10 = (bf16[2,32,2,384]{3,1,0,2:T(8,128)(2,1)S(1)}, bf16[2,32,2,384]{3,1,0,2:T(8,128)(2,1)S(1)}, u32[]{:S(2)}, u32[]{:S(2)}) collective-permute-start(bf16[2,32,2,384]{3,1,0,2:T(8,128)(2,1)S(1)} %collective-permute-done.9), channel_id=1, source_target_pairs={{0,8},{8,16},{16,24},{24,28},{28,20},{20,12},{12,4},{4,0},{1,9},{9... | collective-permute-start | bytes 294920 | tf_op jit(solution)/shard_map/ppermute | solution.py:114
  54.5 1.7 %copy-start.5 = (bf16[2,32,2,384]{3,1,0,2:T(8,128)(2,1)S(1)}, bf16[2,32,2,384]{3,1,0,2:T(8,128)(2,1)}, u32[]{:S(2)}) copy-start(bf16[2,32,2,384]{3,1,0,2:T(8,128)(2,1)} %copy-done.4) | copy-start | bytes 294916
  57.2 1.0 %copy-start.7 = (pred[48]{0:T(512)(128)(4,1)S(1)}, pred[48]{0:T(512)(128)(4,1)}, u32[]{:S(2)}) copy-start(pred[48]{0:T(512)(128)(4,1)} %broadcast_compare_fusion.1) | copy-start | bytes 148
  57.2 1.7 %copy-start.1 = (bf16[24,32,2,128]{3,1,2,0:T(8,128)(2,1)S(1)}, bf16[24,32,2,128]{3,1,2,0:T(8,128)(2,1)}, u32[]{:S(2)}) copy-start(bf16[24,32,2,128]{3,1,2,0:T(8,128)(2,1)} %get-tuple-element.6) | copy-start | bytes 1179652
  62.0 1.9 %copy-start.2 = (bf16[24,16,2,128]{3,1,2,0:T(8,128)(2,1)S(1)}, bf16[24,16,2,128]{3,1,2,0:T(8,128)(2,1)}, u32[]{:S(2)}) copy-start(bf16[24,16,2,128]{3,1,2,0:T(8,128)(2,1)} %get-tuple-element.11) | copy-start | bytes 589828
  62.0 1.9 %copy-start.10 = (f32[24,2,32]{2,1,0:T(2,128)S(1)}, f32[24,2,32]{2,1,0:T(2,128)}, u32[]{:S(2)}) copy-start(f32[24,2,32]{2,1,0:T(2,128)} %get-tuple-element.40) | copy-start | bytes 18436
  63.8 1.6 %copy-start.3 = (bf16[24,16,2,128]{3,1,2,0:T(8,128)(2,1)S(1)}, bf16[24,16,2,128]{3,1,2,0:T(8,128)(2,1)}, u32[]{:S(2)}) copy-start(bf16[24,16,2,128]{3,1,2,0:T(8,128)(2,1)} %get-tuple-element.13) | copy-start | bytes 589828
  (1 other events, 0.9 us)

commit v5 on v3

--- a/solution.py
+++ b/solution.py
@@ -108,24 +108,50 @@
         place[s] = i
     forward = [(ring[i], ring[(i + 1) % n_store]) for i in range(n_store)]
     backward = [(ring[(i + 1) % n_store], ring[i]) for i in range(n_store)]
-    parts = [own]
-    ahead = own
-    for _ in range(n_store // 2):
-        ahead = lax.ppermute(ahead, "store", forward)
-        parts.append(ahead)
-    behind = own
-    for _ in range((n_store - 1) // 2):
-        behind = lax.ppermute(behind, "store", backward)
-        parts.append(behind)
+    steps = []
+    pieces = []
+    for row in range(count):
+        ahead_steps = n_store // 2 if row % 2 == 0 else (n_store - 1) // 2
+        behind_steps = n_store - 1 - ahead_steps
+        steps.append((ahead_steps, behind_steps))
+        piece = own[row : row + 1]
+        parts = [piece]
+        ahead = piece
+        behind = piece
+        for k in range(max(ahead_steps, behind_steps)):
+            if k < ahead_steps:
+                ahead = lax.ppermute(ahead, "store", forward)
+                parts.append(ahead)
+            if k < behind_steps:
+                behind = lax.ppermute(behind, "store", backward)
+                parts.append(behind)
+        pieces.append(parts)
+    ordered = []
+    for row in range(count):
+        ahead_steps, behind_steps = steps[row]
+        parts = pieces[row]
+        got_ahead, got_behind = [], []
+        at = 1
+        for k in range(max(ahead_steps, behind_steps)):
+            if k < ahead_steps:
+                got_ahead.append(parts[at])
+                at += 1
+            if k < behind_steps:
+                got_behind.append(parts[at])
+                at += 1
+        ordered.extend([parts[0]] + got_ahead + got_behind)
     place_of = jnp.asarray(place, dtype=jnp.int32)
     mine = place_of[lax.axis_index("store")]
+    ahead_of = jnp.asarray([s[0] for s in steps], dtype=jnp.int32)
 
     def rows_of(rows):
         dist = (place_of[rows // count] - mine) % n_store
-        slot = jnp.where(dist == 0, 0, jnp.where(dist < n_store // 2, n_store // 2 + dist, n_store - dist))
-        return slot * count + rows % count
+        row = rows % count
+        first = ahead_of[row]
+        slot = jnp.where(dist == 0, 0, jnp.where(dist < n_store - first, first + dist, n_store - dist))
+        return row * n_store + slot
 
-    return jnp.concatenate(parts, axis=0), rows_of
+    return jnp.concatenate(ordered, axis=0), rows_of
 
 
 def local(query_embeds, passage_embeds, passage_lengths, cand_passage, norm_gain, w_qkv):

time: 61.7 us -> 64.8 us (1.050)
  waiting for transfers between devices: 10.8 us -> 3.73 us
  starting transfers between devices: 7.7 us -> 14.1 us
  local copies, waits for them, and re-layouts: 13.3 us -> 18.9 us
  other arithmetic: 5.44 us -> 4.1 us
    ppermute x4 -> x7, waiting for transfers between devices: 10.8 us -> 0.8 us  [gather_store(): ahead = lax.ppermute(ahead, 'store', forward)]
    unnamed x12 -> x20, local copies, waits for them, and re-layouts: 4.3 us -> 9.22 us
    ppermute x4 -> x7, starting transfers between devices: 6.3 us -> 11.1 us  [gather_store(): ahead = lax.ppermute(ahead, 'store', forward)]
    ppermute x3 -> x7, waiting for transfers between devices: 0.01 us -> 2.94 us  [gather_store(): behind = lax.ppermute(behind, 'store', backward)]
    ppermute x3 -> x7, starting transfers between devices: 1.41 us -> 2.96 us  [gather_store(): behind = lax.ppermute(behind, 'store', backward)]
    unnamed x1 -> x0, other arithmetic: 0.83 us -> none
    sub x2, matrix products: 4.22 us -> 3.56 us  [softmax_rounded(): expon = jnp.where(allowed, jnp.exp(masked - peak), jnp.float32(0.0))]
    slice x0 -> x1, local copies, waits for them, and re-layouts: none -> 0.66 us  [gather_store(): piece = own[row:row + 1]]
  transfers between devices with their start and end apart: 7 -> 14, of which waited for: 4 -> 3; matrix products, arithmetic and copies ran while one was open for 14% -> 21% of each run, Pallas kernels for 0% -> 0%
where the time goes in v5:
time: 64.8 us; the launch traced here: 64.5 us
  local copies, waits for them, and re-layouts  18.9 us (29%)
  starting transfers between devices  14.1 us (22%)
  matrix products  12.7 us (20%)
  blocking collectives  10.1 us (16%)
  other arithmetic  4.1 us (6%)
  waiting for transfers between devices  3.73 us (6%)
  between operations  0.87 us (1%)
    ppermute x7, starting transfers between devices, gather_store(): ahead = lax.ppermute(ahead, 'store', forward)  11.1 us
    all_gather x1, blocking collectives, local(): full_rows = lax.all_gather(all_rows, 'tp', axis=1, tiled=True)  10.1 us
    unnamed x20, local copies, waits for them, and re-layouts  9.22 us
    dot_general x1, matrix products, local(): jnp.einsum('nk,khc->nhc', normed, w_qkv, preferred_element_type=jnp.float32)  6.84 us
    sub x2, matrix products, softmax_rounded(): expon = jnp.where(allowed, jnp.exp(masked - peak), jnp.float32(0.0))  3.56 us
    ppermute x7, starting transfers between devices, gather_store(): behind = lax.ppermute(behind, 'store', backward)  2.96 us
    ppermute x7, waiting for transfers between devices, gather_store(): behind = lax.ppermute(behind, 'store', backward)  2.94 us
    gather x1, local copies, waits for them, and re-layouts, local(): pair_qkv = store_qkv[rows_of(cand_passage)]  2.52 us
  transfers between devices with their start and end apart: 14, of which 3 were waited for; matrix products, arithmetic and copies ran while one was open for 21% of the time, Pallas kernels for 0%

profile of v5, /device:TPU:0, one launch (start us, length us, event | category | flops | bytes accessed | tf_op | source)
XLA Modules:
  0.0 64.5 jit_solution(13183470396021625361)
XLA Ops:
  0.7 0.9 %pad_maximum_fusion = bf16[96,1024]{1,0:T(8,128)(2,1)S(1)} fusion(bf16[64,1024]{1,0:T(8,128)(2,1)} %bitcast.26, bf16[32,1024]{1,0:T(8,128)(2,1)} %bitcast.27), kind=kLoop, calls=%fused_computation.40 | loop fusion | flops 393216 | bytes 393216 | tf_op jit(solution)/shard_map/concatenate | solution.py:169
  1.6 10.1 %all_gather.3 = bf16[96,4096]{1,0:T(8,128)(2,1)S(1)} all-gather(bf16[96,1024]{1,0:T(8,128)(2,1)S(1)} %pad_maximum_fusion), channel_id=1, replica_groups=mesh['store'=8,'tp'=4] {'tp'}, dimensions={1}, use_global_device_ids=true | all-gather | bytes 983040 | tf_op jit(solution)/shard_map/all_gather | solution.py:170
  11.7 0.7 %convert_element_type.39 = f32[4096]{0:T(1024)S(1)} convert(bf16[4096]{0:T(1024)(128)(2,1)} %param.12) | non-fusion elementwise | flops 4096 | bytes 24576 | tf_op jit(solution)/shard_map/convert_element_type | solution.py:12
  12.8 6.8 %fusion.2 = f32[96,4,384]{2,0,1:T(8,128)S(1)} fusion(bf16[4096,4,384]{2,1,0:T(4,128)(2,1)} %param.13, bf16[96,4096]{1,0:T(8,128)(2,1)S(1)} %all_gather.3, f32[4096]{0:T(1024)S(1)} %convert_element_type.39, f32[96]{0:T(128)S(1)} %add_rsqrt_fusion), kind=kOutput, calls=%fused_computation.4 | convolution fusion | flops 1209532416 | bytes 13975936 | tf_op jit(solution)/shard_map/nk,khc->nhc/dot_general | solution.py:172
  21.4 1.6 %collective-permute-start = (bf16[1,32,4,384]{3,1,0,2:T(8,128)(2,1)S(1)}, bf16[1,32,4,384]{3,1,0,2:T(8,128)(2,1)S(1)}, u32[]{:S(2)}, u32[]{:S(2)}) collective-permute-start(bf16[1,32,4,384]{3,1,0,2:T(8,128)(2,1)S(1)} %get-tuple-element.12), channel_id=1, source_target_pairs={{0,8},{8,16},{16,24},{24,28},{28,20},{20,12},{12,4},{4,0},{1,9},{9... | collective-permute-start | bytes 294920 | tf_op jit(solution)/shard_map/ppermute | solution.py:123
  23.4 1.6 %collective-permute-start.7 = (bf16[1,32,4,384]{3,1,0,2:T(8,128)(2,1)S(1)}, bf16[1,32,4,384]{3,1,0,2:T(8,128)(2,1)S(1)}, u32[]{:S(2)}, u32[]{:S(2)}) collective-permute-start(bf16[1,32,4,384]{3,1,0,2:T(8,128)(2,1)S(1)} %get-tuple-element.10), channel_id=1, source_target_pairs={{0,8},{8,16},{16,24},{24,28},{28,20},{20,12},{12,4},{4,0},{1,9},{9... | collective-permute-start | bytes 294920 | tf_op jit(solution)/shard_map/ppermute | solution.py:123
  26.6 0.7 %gather_fusion = s32[24]{0:T(128)S(1)} fusion(s32[8]{0:T(128)S(1)} %copy-done, s32[1024]{0:T(1024)S(1)} %pad_clamp_fusion.1), kind=kCustom, calls=%fused_computation | custom fusion | bytes 288 | tf_op jit(solution)/shard_map/gather | solution.py:148
  28.6 1.1 %fusion.48 = (bf16[24,16,4,128]{3,1,2,0:T(8,128)(2,1)}, bf16[24,16,4,128]{3,1,2,0:T(8,128)(2,1)}) fusion(bf16[24,16,4,256]{3,1,2,0:T(8,128)(2,1)S(1)} %bitcast.21), kind=kLoop, calls=%fused_computation.107 | loop fusion | bytes 1572864 | tf_op jit(solution)/shard_map/slice | solution.py:74
  29.8 1.6 %collective-permute-start.1 = (bf16[1,32,4,384]{3,1,0,2:T(8,128)(2,1)S(1)}, bf16[1,32,4,384]{3,1,0,2:T(8,128)(2,1)S(1)}, u32[]{:S(2)}, u32[]{:S(2)}) collective-permute-start(bf16[1,32,4,384]{3,1,0,2:T(8,128)(2,1)S(1)} %collective-permute-done), channel_id=1, source_target_pairs={{0,8},{8,16},{16,24},{24,28},{28,20},{20,12},{12,4},{4,0},{1,9},{9... | collective-permute-start | bytes 294920 | tf_op jit(solution)/shard_map/ppermute | solution.py:123
  31.9 1.6 %collective-permute-start.8 = (bf16[1,32,4,384]{3,1,0,2:T(8,128)(2,1)S(1)}, bf16[1,32,4,384]{3,1,0,2:T(8,128)(2,1)S(1)}, u32[]{:S(2)}, u32[]{:S(2)}) collective-permute-start(bf16[1,32,4,384]{3,1,0,2:T(8,128)(2,1)S(1)} %collective-permute-done.7), channel_id=1, source_target_pairs={{0,8},{8,16},{16,24},{24,28},{28,20},{20,12},{12,4},{4,0},{1,9},{9... | collective-permute-start | bytes 294920 | tf_op jit(solution)/shard_map/ppermute | solution.py:123
  34.5 0.7 %collective-permute-done.1 = bf16[1,32,4,384]{3,1,0,2:T(8,128)(2,1)S(1)} collective-permute-done((bf16[1,32,4,384]{3,1,0,2:T(8,128)(2,1)S(1)}, bf16[1,32,4,384]{3,1,0,2:T(8,128)(2,1)S(1)}, u32[]{:S(2)}, u32[]{:S(2)}) %collective-permute-start.1) | collective-permute-done | bytes 98336 | tf_op jit(solution)/shard_map/ppermute | solution.py:123
  35.2 1.6 %collective-permute-start.2 = (bf16[1,32,4,384]{3,1,0,2:T(8,128)(2,1)S(1)}, bf16[1,32,4,384]{3,1,0,2:T(8,128)(2,1)S(1)}, u32[]{:S(2)}, u32[]{:S(2)}) collective-permute-start(bf16[1,32,4,384]{3,1,0,2:T(8,128)(2,1)S(1)} %collective-permute-done.1), channel_id=1, source_target_pairs={{0,8},{8,16},{16,24},{24,28},{28,20},{20,12},{12,4},{4,0},{1,9},{9... | collective-permute-start | bytes 294920 | tf_op jit(solution)/shard_map/ppermute | solution.py:123
  37.4 1.6 %collective-permute-start.9 = (bf16[1,32,4,384]{3,1,0,2:T(8,128)(2,1)S(1)}, bf16[1,32,4,384]{3,1,0,2:T(8,128)(2,1)S(1)}, u32[]{:S(2)}, u32[]{:S(2)}) collective-permute-start(bf16[1,32,4,384]{3,1,0,2:T(8,128)(2,1)S(1)} %collective-permute-done.8), channel_id=1, source_target_pairs={{0,8},{8,16},{16,24},{24,28},{28,20},{20,12},{12,4},{4,0},{1,9},{9... | collective-permute-start | bytes 294920 | tf_op jit(solution)/shard_map/ppermute | solution.py:123
  40.1 1.6 %collective-permute-start.3 = (bf16[1,32,4,384]{3,1,0,2:T(8,128)(2,1)S(1)}, bf16[1,32,4,384]{3,1,0,2:T(8,128)(2,1)S(1)}, u32[]{:S(2)}, u32[]{:S(2)}) collective-permute-start(bf16[1,32,4,384]{3,1,0,2:T(8,128)(2,1)S(1)} %collective-permute-done.2), channel_id=1, source_target_pairs={{0,8},{8,16},{16,24},{24,28},{28,20},{20,12},{12,4},{4,0},{1,9},{9... | collective-permute-start | bytes 294920 | tf_op jit(solution)/shard_map/ppermute | solution.py:123
  41.6 2.9 %collective-permute-done.12 = bf16[1,32,4,384]{3,1,0,2:T(8,128)(2,1)S(1)} collective-permute-done((bf16[1,32,4,384]{3,1,0,2:T(8,128)(2,1)S(1)}, bf16[1,32,4,384]{3,1,0,2:T(8,128)(2,1)S(1)}, u32[]{:S(2)}, u32[]{:S(2)}) %collective-permute-start.12) | collective-permute-done | bytes 98336 | tf_op jit(solution)/shard_map/ppermute | solution.py:126
  44.8 0.7 %constant_dynamic-update-slice_fusion.12 = bf16[16,32,4,384]{3,1,0,2:T(8,128)(2,1)} fusion(bf16[16,32,4,384]{3,1,0,2:T(8,128)(2,1)} %constant_dynamic-update-slice_fusion.13, bf16[1,32,4,384]{3,1,0,2:T(8,128)(2,1)S(1)} %collective-permute-done.2), kind=kLoop, calls=%fused_computation.61 | loop fusion | bytes 196608
  45.5 0.7 %constant_dynamic-update-slice_fusion.11 = bf16[16,32,4,384]{3,1,0,2:T(8,128)(2,1)} fusion(bf16[16,32,4,384]{3,1,0,2:T(8,128)(2,1)} %constant_dynamic-update-slice_fusion.12, bf16[1,32,4,384]{3,1,0,2:T(8,128)(2,1)S(1)} %collective-permute-done.3), kind=kLoop, calls=%fused_computation.60 | loop fusion | bytes 196608
  47.5 0.7 %constant_dynamic-update-slice_fusion.8 = bf16[16,32,4,384]{3,1,0,2:T(8,128)(2,1)} fusion(bf16[16,32,4,384]{3,1,0,2:T(8,128)(2,1)} %constant_dynamic-update-slice_fusion.9, bf16[1,32,4,384]{3,1,0,2:T(8,128)(2,1)S(1)} %collective-permute-done.6), kind=kLoop, calls=%fused_computation.57 | loop fusion | bytes 196608
  49.5 0.7 %constant_dynamic-update-slice_fusion.5 = bf16[16,32,4,384]{3,1,0,2:T(8,128)(2,1)} fusion(bf16[16,32,4,384]{3,1,0,2:T(8,128)(2,1)} %constant_dynamic-update-slice_fusion.6, bf16[1,32,4,384]{3,1,0,2:T(8,128)(2,1)S(1)} %collective-permute-done.8), kind=kLoop, calls=%fused_computation.54 | loop fusion | bytes 196608
  53.4 2.5 %gather_fusion.1 = bf16[24,32,4,384]{3,1,2,0:T(8,128)(2,1)S(1)} fusion(bf16[16,32,4,384]{3,1,0,2:T(8,128)(2,1)} %constant_dynamic-update-slice_fusion, s32[1024]{0:T(1024)S(1)} %pad_clamp_fusion), kind=kCustom, calls=%fused_computation.1 | custom fusion | bytes 4718688 | tf_op jit(solution)/shard_map/gather | solution.py:182
  55.9 1.3 %fusion.47 = (bf16[24,32,4,128]{3,1,2,0:T(8,128)(2,1)}, bf16[24,32,4,128]{3,1,2,0:T(8,128)(2,1)S(1)}) fusion(bf16[24,32,4,384]{3,1,2,0:T(8,128)(2,1)S(1)} %gather_fusion.1), kind=kLoop, calls=%fused_computation.106 | loop fusion | bytes 3145728 | tf_op jit(solution)/shard_map/slice | solution.py:74
  58.0 3.4 %fusion.52 = (f32[24,4,32]{2,1,0:T(4,128)S(1)}, f32[24,4,32,48]{3,2,1,0:T(8,128)}) fusion(bf16[24,32,4,128]{3,1,2,0:T(8,128)(2,1)} %get-tuple-element.2, bf16[24,16,4,128]{3,1,2,0:T(8,128)(2,1)} %get-tuple-element.4, bf16[24,32,4,384]{3,1,2,0:T(8,128)(2,1)S(1)} %gather_fusion.1, pred[24,32,48]{2,1,0:T(8,128)(4,1)S(1)} %and_or_fusion), kind=kOutput, calls=%fused_computation.111 | convolution fusion | flops 40845360 | bytes 2764800 | tf_op jit(solution)/shard_map/sub | solution.py:41
  61.4 2.1 %fusion.8 = bf16[24,4,4,8,128]{4,3,2,1,0:T(8,128)(2,1)S(1)} fusion(bf16[24,32,4,128]{3,1,2,0:T(8,128)(2,1)S(1)} %get-tuple-element.3, bf16[24,16,4,128]{3,1,2,0:T(8,128)(2,1)} %get-tuple-element.5, f32[24,4,32,48]{3,2,1,0:T(8,128)} %get-tuple-element.21, f32[24,4,32]{2,1,0:T(4,128)S(1)} %get-tuple-element.20, pred[24,32]{1,0:T(8,128)(4,1)S(1)} %iota_compare_fusion.1), kind=kOutput, calls=%fused_computation.16 | convolution fusion | flops 41189376 | bytes 2568960 | tf_op jit(solution)/shard_map/bhit,bthd->bihd/dot_general | solution.py:89
  63.5 1.0 %copy.44 = bf16[24,4,4,8,128]{4,3,1,2,0:T(8,128)(2,1)} copy(bf16[24,4,4,8,128]{4,3,2,1,0:T(8,128)(2,1)S(1)} %fusion.8) | data formatting | bytes 1572864 | tf_op jit(solution)/shard_map/convert_element_type | solution.py:92
  (75 shorter events, 15.5 us)
Async XLA Ops:
  19.7 0.8 %copy-start.2 = (s32[2]{0:T(128)S(1)}, s32[2]{0:T(128)}, u32[]{:S(2)}) copy-start(s32[2]{0:T(128)} %param.10) | copy-start | bytes 28
  20.2 6.3 %copy-start.1 = (s32[24]{0:T(128)S(1)}, s32[24]{0:T(128)}, u32[]{:S(2)}) copy-start(s32[24]{0:T(128)} %param.11) | copy-start | bytes 292
  20.2 6.3 %copy-start = (s32[8]{0:T(128)S(1)}, s32[8]{0:T(128)}, u32[]{:S(2)}) copy-start(s32[8]{0:T(128)} %constant.80.clone) | copy-start | bytes 100
  21.4 8.4 %collective-permute-start = (bf16[1,32,4,384]{3,1,0,2:T(8,128)(2,1)S(1)}, bf16[1,32,4,384]{3,1,0,2:T(8,128)(2,1)S(1)}, u32[]{:S(2)}, u32[]{:S(2)}) collective-permute-start(bf16[1,32,4,384]{3,1,0,2:T(8,128)(2,1)S(1)} %get-tuple-element.12), channel_id=1, source_target_pairs={{0,8},{8,16},{16,24},{24,28},{28,20},{20,12},{12,4},{4,0},{1,9},{9... | collective-permute-start | bytes 294920 | tf_op jit(solution)/shard_map/ppermute | solution.py:123
  23.0 8.5 %collective-permute-start.4 = (bf16[1,32,4,384]{3,1,0,2:T(8,128)(2,1)S(1)}, bf16[1,32,4,384]{3,1,0,2:T(8,128)(2,1)S(1)}, u32[]{:S(2)}, u32[]{:S(2)}) collective-permute-start(bf16[1,32,4,384]{3,1,0,2:T(8,128)(2,1)S(1)} %get-tuple-element.12), channel_id=1, source_target_pairs={{8,0},{16,8},{24,16},{28,24},{20,28},{12,20},{4,12},{0,4},{9,1},{1... | collective-permute-start | bytes 294920 | tf_op jit(solution)/shard_map/ppermute | solution.py:126
  23.4 8.5 %collective-permute-start.7 = (bf16[1,32,4,384]{3,1,0,2:T(8,128)(2,1)S(1)}, bf16[1,32,4,384]{3,1,0,2:T(8,128)(2,1)S(1)}, u32[]{:S(2)}, u32[]{:S(2)}) collective-permute-start(bf16[1,32,4,384]{3,1,0,2:T(8,128)(2,1)S(1)} %get-tuple-element.10), channel_id=1, source_target_pairs={{0,8},{8,16},{16,24},{24,28},{28,20},{20,12},{12,4},{4,0},{1,9},{9... | collective-permute-start | bytes 294920 | tf_op jit(solution)/shard_map/ppermute | solution.py:123
  25.0 8.5 %collective-permute-start.10 = (bf16[1,32,4,384]{3,1,0,2:T(8,128)(2,1)S(1)}, bf16[1,32,4,384]{3,1,0,2:T(8,128)(2,1)S(1)}, u32[]{:S(2)}, u32[]{:S(2)}) collective-permute-start(bf16[1,32,4,384]{3,1,0,2:T(8,128)(2,1)S(1)} %get-tuple-element.10), channel_id=1, source_target_pairs={{8,0},{16,8},{24,16},{28,24},{20,28},{12,20},{4,12},{0,4},{9,1},{1... | collective-permute-start | bytes 294920 | tf_op jit(solution)/shard_map/ppermute | solution.py:126
  29.8 5.5 %collective-permute-start.1 = (bf16[1,32,4,384]{3,1,0,2:T(8,128)(2,1)S(1)}, bf16[1,32,4,384]{3,1,0,2:T(8,128)(2,1)S(1)}, u32[]{:S(2)}, u32[]{:S(2)}) collective-permute-start(bf16[1,32,4,384]{3,1,0,2:T(8,128)(2,1)S(1)} %collective-permute-done), channel_id=1, source_target_pairs={{0,8},{8,16},{16,24},{24,28},{28,20},{20,12},{12,4},{4,0},{1,9},{9... | collective-permute-start | bytes 294920 | tf_op jit(solution)/shard_map/ppermute | solution.py:123
  31.4 5.4 %collective-permute-start.5 = (bf16[1,32,4,384]{3,1,0,2:T(8,128)(2,1)S(1)}, bf16[1,32,4,384]{3,1,0,2:T(8,128)(2,1)S(1)}, u32[]{:S(2)}, u32[]{:S(2)}) collective-permute-start(bf16[1,32,4,384]{3,1,0,2:T(8,128)(2,1)S(1)} %collective-permute-done.4), channel_id=1, source_target_pairs={{8,0},{16,8},{24,16},{28,24},{20,28},{12,20},{4,12},{0,4},{9,1},{1... | collective-permute-start | bytes 294920 | tf_op jit(solution)/shard_map/ppermute | solution.py:126
  31.9 5.5 %collective-permute-start.8 = (bf16[1,32,4,384]{3,1,0,2:T(8,128)(2,1)S(1)}, bf16[1,32,4,384]{3,1,0,2:T(8,128)(2,1)S(1)}, u32[]{:S(2)}, u32[]{:S(2)}) collective-permute-start(bf16[1,32,4,384]{3,1,0,2:T(8,128)(2,1)S(1)} %collective-permute-done.7), channel_id=1, source_target_pairs={{0,8},{8,16},{16,24},{24,28},{28,20},{20,12},{12,4},{4,0},{1,9},{9... | collective-permute-start | bytes 294920 | tf_op jit(solution)/shard_map/ppermute | solution.py:123
  33.4 5.5 %collective-permute-start.11 = (bf16[1,32,4,384]{3,1,0,2:T(8,128)(2,1)S(1)}, bf16[1,32,4,384]{3,1,0,2:T(8,128)(2,1)S(1)}, u32[]{:S(2)}, u32[]{:S(2)}) collective-permute-start(bf16[1,32,4,384]{3,1,0,2:T(8,128)(2,1)S(1)} %collective-permute-done.10), channel_id=1, source_target_pairs={{8,0},{16,8},{24,16},{28,24},{20,28},{12,20},{4,12},{0,4},{9,1},{1... | collective-permute-start | bytes 294920 | tf_op jit(solution)/shard_map/ppermute | solution.py:126
  35.2 4.8 %collective-permute-start.2 = (bf16[1,32,4,384]{3,1,0,2:T(8,128)(2,1)S(1)}, bf16[1,32,4,384]{3,1,0,2:T(8,128)(2,1)S(1)}, u32[]{:S(2)}, u32[]{:S(2)}) collective-permute-start(bf16[1,32,4,384]{3,1,0,2:T(8,128)(2,1)S(1)} %collective-permute-done.1), channel_id=1, source_target_pairs={{0,8},{8,16},{16,24},{24,28},{28,20},{20,12},{12,4},{4,0},{1,9},{9... | collective-permute-start | bytes 294920 | tf_op jit(solution)/shard_map/ppermute | solution.py:123
  36.8 10.7 %collective-permute-start.6 = (bf16[1,32,4,384]{3,1,0,2:T(8,128)(2,1)S(1)}, bf16[1,32,4,384]{3,1,0,2:T(8,128)(2,1)S(1)}, u32[]{:S(2)}, u32[]{:S(2)}) collective-permute-start(bf16[1,32,4,384]{3,1,0,2:T(8,128)(2,1)S(1)} %collective-permute-done.5), channel_id=1, source_target_pairs={{8,0},{16,8},{24,16},{28,24},{20,28},{12,20},{4,12},{0,4},{9,1},{1... | collective-permute-start | bytes 294920 | tf_op jit(solution)/shard_map/ppermute | solution.py:126
  37.4 12.8 %collective-permute-start.9 = (bf16[1,32,4,384]{3,1,0,2:T(8,128)(2,1)S(1)}, bf16[1,32,4,384]{3,1,0,2:T(8,128)(2,1)S(1)}, u32[]{:S(2)}, u32[]{:S(2)}) collective-permute-start(bf16[1,32,4,384]{3,1,0,2:T(8,128)(2,1)S(1)} %collective-permute-done.8), channel_id=1, source_target_pairs={{0,8},{8,16},{16,24},{24,28},{28,20},{20,12},{12,4},{4,0},{1,9},{9... | collective-permute-start | bytes 294920 | tf_op jit(solution)/shard_map/ppermute | solution.py:123
  38.9 5.6 %collective-permute-start.12 = (bf16[1,32,4,384]{3,1,0,2:T(8,128)(2,1)S(1)}, bf16[1,32,4,384]{3,1,0,2:T(8,128)(2,1)S(1)}, u32[]{:S(2)}, u32[]{:S(2)}) collective-permute-start(bf16[1,32,4,384]{3,1,0,2:T(8,128)(2,1)S(1)} %collective-permute-done.11), channel_id=1, source_target_pairs={{8,0},{16,8},{24,16},{28,24},{20,28},{12,20},{4,12},{0,4},{9,1},{1... | collective-permute-start | bytes 294920 | tf_op jit(solution)/shard_map/ppermute | solution.py:126
  40.1 5.4 %collective-permute-start.3 = (bf16[1,32,4,384]{3,1,0,2:T(8,128)(2,1)S(1)}, bf16[1,32,4,384]{3,1,0,2:T(8,128)(2,1)S(1)}, u32[]{:S(2)}, u32[]{:S(2)}) collective-permute-start(bf16[1,32,4,384]{3,1,0,2:T(8,128)(2,1)S(1)} %collective-permute-done.2), channel_id=1, source_target_pairs={{0,8},{8,16},{16,24},{24,28},{28,20},{20,12},{12,4},{4,0},{1,9},{9... | collective-permute-start | bytes 294920 | tf_op jit(solution)/shard_map/ppermute | solution.py:123
  44.6 8.2 %collective-permute-start.13 = (bf16[1,32,4,384]{3,1,0,2:T(8,128)(2,1)S(1)}, bf16[1,32,4,384]{3,1,0,2:T(8,128)(2,1)S(1)}, u32[]{:S(2)}, u32[]{:S(2)}) collective-permute-start(bf16[1,32,4,384]{3,1,0,2:T(8,128)(2,1)S(1)} %collective-permute-done.12), channel_id=1, source_target_pairs={{8,0},{16,8},{24,16},{28,24},{20,28},{12,20},{4,12},{0,4},{9,1},{1... | collective-permute-start | bytes 294920 | tf_op jit(solution)/shard_map/ppermute | solution.py:126

commit v6 on v2

--- a/solution.py
+++ b/solution.py
@@ -95,6 +95,40 @@
 def attend_pairs(query_qkv, pair_qkv, pair_lengths, head_dim, cands):
     repeated = jnp.repeat(query_qkv[..., head_dim:], cands, axis=0)
     return attend_core(repeated, pair_qkv, pair_lengths, head_dim)
+
+
+def ring_steps(own):
+    n_store = lax.axis_size("store")
+    ring = [s for s in range(0, n_store, 2)] + [s for s in range(n_store - 1, 0, -2)]
+    place = [0] * n_store
+    for i, s in enumerate(ring):
+        place[s] = i
+    forward = [(ring[i], ring[(i + 1) % n_store]) for i in range(n_store)]
+    backward = [(ring[(i + 1) % n_store], ring[i]) for i in range(n_store)]
+    groups = [([own], [0])]
+    ahead = own
+    behind = own
+    for k in range(1, n_store // 2 + 1):
+        blocks, dists = [], []
+        ahead = lax.ppermute(ahead, "store", forward)
+        blocks.append(ahead)
+        dists.append(n_store - k)
+        if k <= (n_store - 1) // 2:
+            behind = lax.ppermute(behind, "store", backward)
+            blocks.append(behind)
+            dists.append(k)
+        groups.append((blocks, dists))
+    return groups, jnp.asarray(place, dtype=jnp.int32)
+
+
+def attend_arrived(query_qkv, blocks, head_dim):
+    passages = jnp.concatenate(blocks, axis=0) if len(blocks) > 1 else blocks[0]
+    lengths = jnp.sum(jnp.isfinite(passages[:, :, 0, head_dim]).astype(jnp.int32), axis=1)
+    count = passages.shape[0]
+    quer_count = query_qkv.shape[0]
+    query_kv = jnp.repeat(query_qkv[..., head_dim:], count, axis=0)
+    pair_qkv = jnp.tile(passages, (quer_count, 1, 1, 1))
+    return attend_core(query_kv, pair_qkv, jnp.tile(lengths, quer_count), head_dim)
 
 
 def local(query_embeds, passage_embeds, passage_lengths, cand_passage, norm_gain, w_qkv):
@@ -117,13 +151,42 @@
     query_qkv = projected[:query_total].reshape(quer_count, query_len, heads_part, 3 * head_dim)
     own_qkv = projected[query_total:].reshape(pass_count, passage_len, heads_part, 3 * head_dim)
     padded = jnp.arange(passage_len, dtype=jnp.int32)[None, :] >= passage_lengths[:, None]
-    marker = own_qkv[:, :, 0, head_dim]
-    own_qkv = own_qkv.at[:, :, 0, head_dim].set(jnp.where(padded, jnp.inf, marker).astype(own_qkv.dtype))
-    store_qkv = lax.all_gather(own_qkv, "store", axis=0, tiled=True)
-    pair_qkv = store_qkv[cand_passage]
-    pair_lengths = jnp.sum(jnp.isfinite(pair_qkv[:, :, 0, head_dim]).astype(jnp.int32), axis=1)
+    head_at = lax.broadcasted_iota(jnp.int32, own_qkv.shape, 2)
+    col_at = lax.broadcasted_iota(jnp.int32, own_qkv.shape, 3)
+    mark = padded[:, :, None, None] & (head_at == 0) & (col_at == head_dim)
+    own_qkv = jnp.where(mark, jnp.asarray(jnp.inf, own_qkv.dtype), own_qkv)
     query_attn = attend_queries(query_qkv, head_dim)
-    passage_attn = attend_pairs(query_qkv, pair_qkv, pair_lengths, head_dim, cands)
+    n_store = lax.axis_size("store")
+    if n_store > 8 or n_store % 2:
+        store_qkv = lax.all_gather(own_qkv, "store", axis=0, tiled=True)
+        pair_qkv = store_qkv[cand_passage]
+        pair_lengths = jnp.sum(jnp.isfinite(pair_qkv[:, :, 0, head_dim]).astype(jnp.int32), axis=1)
+        passage_attn = attend_pairs(query_qkv, pair_qkv, pair_lengths, head_dim, cands)
+        return (query_attn, passage_attn)
+    groups, place_of = ring_steps(own_qkv)
+    outs = []
+    first_row = [0] * n_store
+    width = [0] * n_store
+    within = [0] * n_store
+    row = 0
+    for blocks, dists in groups:
+        outs.append(attend_arrived(query_qkv, blocks, head_dim))
+        for i, dist in enumerate(dists):
+            first_row[dist] = row
+            width[dist] = len(dists) * pass_count
+            within[dist] = i * pass_count
+        row += quer_count * len(dists) * pass_count
+    every = jnp.concatenate(outs, axis=0)
+    mine = place_of[lax.axis_index("store")]
+    dist = (place_of[cand_passage // pass_count] - mine) % n_store
+    own_query = jnp.arange(pairs_dev, dtype=jnp.int32) // cands
+    pick = (
+        jnp.asarray(first_row, dtype=jnp.int32)[dist]
+        + own_query * jnp.asarray(width, dtype=jnp.int32)[dist]
+        + jnp.asarray(within, dtype=jnp.int32)[dist]
+        + cand_passage % pass_count
+    )
+    passage_attn = every[pick]
     return (query_attn, passage_attn)
 
 

time: 97.3 us -> 69.4 us (0.71)
  waiting for transfers between devices: 43 us -> 13.5 us
  between operations: 14.2 us -> 1.36 us
  starting transfers between devices: 0.04 us -> 7.76 us
  local copies, waits for them, and re-layouts: 9.6 us -> 13 us
  matrix products: 13.3 us -> 16.5 us
    all_gather x1 -> x0, waiting for transfers between devices: 43 us -> none  [local(): store_qkv = lax.all_gather(own_qkv, 'store', axis=0, tiled=True)]
    ppermute x0 -> x7, waiting for transfers between devices: none -> 13.5 us  [the longest x4 10.6 us: ring_steps(): ahead = lax.ppermute(ahead, 'store', forward)]
    ppermute x0 -> x7, starting transfers between devices: none -> 7.76 us  [the longest x4 6.42 us: ring_steps(): ahead = lax.ppermute(ahead, 'store', forward)]
    sub x2 -> x6, matrix products: 4.21 us -> 7.94 us  [softmax_rounded(): expon = jnp.where(allowed, jnp.exp(masked - peak), jnp.float32(0.0))]
    another operation x4 -> x1, other arithmetic: 3.06 us -> 0.2 us
    lt x1 -> x5, other arithmetic: 0.07 us -> 2.69 us  [attend_core(): live = row_index[None, :] < pair_lengths[:, None]]
    slice x1 -> x5, local copies, waits for them, and re-layouts: 1.32 us -> 3.52 us  [attend_core(): pair_qkv[..., head_dim:2 * head_dim]]
    gather x1 -> x5, local copies, waits for them, and re-layouts: 2.52 us -> 4.3 us  [the longest x1 1.51 us: local(): passage_attn = every[pick]]
  transfers between devices with their start and end apart: 1 -> 7, of which waited for: 1 -> 5; matrix products, arithmetic and copies ran while one was open for 2% -> 15% of each run, Pallas kernels for 0% -> 0%
where the time goes in v6:
time: 69.4 us; the launch traced here: 69.2 us
  matrix products  16.5 us (24%)
  waiting for transfers between devices  13.5 us (19%)
  local copies, waits for them, and re-layouts  13 us (19%)
  blocking collectives  10.1 us (15%)
  starting transfers between devices  7.76 us (11%)
  other arithmetic  7.02 us (10%)
  between operations  1.36 us (2%)
    ppermute x4, waiting for transfers between devices, ring_steps(): ahead = lax.ppermute(ahead, 'store', forward)  10.6 us
    all_gather x1, blocking collectives, local(): full_rows = lax.all_gather(all_rows, 'tp', axis=1, tiled=True)  10.1 us
    sub x6, matrix products, softmax_rounded(): expon = jnp.where(allowed, jnp.exp(masked - peak), jnp.float32(0.0))  7.94 us
    dot_general x1, matrix products, local(): jnp.einsum('nk,khc->nhc', normed, w_qkv, preferred_element_type=jnp.float32)  6.83 us
    ppermute x4, starting transfers between devices, ring_steps(): ahead = lax.ppermute(ahead, 'store', forward)  6.42 us
    slice x5, local copies, waits for them, and re-layouts, attend_core(): pair_qkv[..., head_dim:2 * head_dim]  3.52 us
    ppermute x3, waiting for transfers between devices, ring_steps(): behind = lax.ppermute(behind, 'store', backward)  2.82 us
    lt x5, other arithmetic, attend_core(): live = row_index[None, :] < pair_lengths[:, None]  2.69 us
  transfers between devices with their start and end apart: 7, of which 5 were waited for; matrix products, arithmetic and copies ran while one was open for 15% of the time, Pallas kernels for 0%

profile of v6, /device:TPU:0, one launch (start us, length us, event | category | flops | bytes accessed | tf_op | source)
XLA Modules:
  0.0 69.2 jit_solution(11693128525902922734)
XLA Ops:
  0.7 0.9 %pad_maximum_fusion.20 = bf16[96,1024]{1,0:T(8,128)(2,1)S(1)} fusion(bf16[64,1024]{1,0:T(8,128)(2,1)} %bitcast.65, bf16[32,1024]{1,0:T(8,128)(2,1)} %bitcast.66), kind=kLoop, calls=%fused_computation.100 | loop fusion | flops 393216 | bytes 393216 | tf_op jit(solution)/shard_map/concatenate | solution.py:146
  1.6 10.1 %all_gather.3 = bf16[96,4096]{1,0:T(8,128)(2,1)S(1)} all-gather(bf16[96,1024]{1,0:T(8,128)(2,1)S(1)} %pad_maximum_fusion.20), channel_id=1, replica_groups=mesh['store'=8,'tp'=4] {'tp'}, dimensions={1}, use_global_device_ids=true | all-gather | bytes 983040 | tf_op jit(solution)/shard_map/all_gather | solution.py:147
  12.1 6.8 %fusion.6 = f32[96,4,384]{2,0,1:T(8,128)S(1)} fusion(bf16[4096,4,384]{2,1,0:T(4,128)(2,1)} %param.15, bf16[96,4096]{1,0:T(8,128)(2,1)S(1)} %all_gather.3, f32[4096]{0:T(1024)S(1)} %convert_element_type.103, f32[96]{0:T(128)S(1)} %add_rsqrt_fusion), kind=kOutput, calls=%fused_computation.11 | convolution fusion | flops 1209532416 | bytes 13975936 | tf_op jit(solution)/shard_map/nk,khc->nhc/dot_general | solution.py:149
  20.0 1.6 %collective-permute-start = (bf16[2,32,4,384]{3,1,0,2:T(8,128)(2,1)S(1)}, bf16[2,32,4,384]{3,1,0,2:T(8,128)(2,1)S(1)}, u32[]{:S(2)}, u32[]{:S(2)}) collective-permute-start(bf16[2,32,4,384]{3,1,0,2:T(8,128)(2,1)S(1)} %and_select_fusion), channel_id=1, source_target_pairs={{0,8},{8,16},{16,24},{24,28},{28,20},{20,12},{12,4},{4,0},{1,9},{9... | collective-permute-start | bytes 589832 | tf_op jit(solution)/shard_map/ppermute | solution.py:113
  23.2 0.8 %fusion.140 = (bf16[8,16,4,128]{3,1,2,0:T(8,128)(2,1)}, bf16[8,16,4,128]{3,1,2,0:T(8,128)(2,1)}) fusion(bf16[8,16,4,256]{3,1,2,0:T(8,128)(2,1)S(1)} %bitcast.60), kind=kLoop, calls=%fused_computation.219 | loop fusion | bytes 524288 | tf_op jit(solution)/shard_map/slice | solution.py:74
  24.1 0.7 %fusion.139 = (bf16[4,32,4,128]{3,1,2,0:T(8,128)(2,1)}, bf16[4,32,4,128]{3,1,2,0:T(8,128)(2,1)}) fusion(bf16[4,32,4,384]{3,1,2,0:T(8,128)(2,1)S(1)} %bitcast.56), kind=kLoop, calls=%fused_computation.218 | loop fusion | bytes 524288 | tf_op jit(solution)/shard_map/slice | solution.py:74
  27.5 0.7 %gather_fusion.1 = s32[24]{0:T(128)S(1)} fusion(s32[8]{0:T(128)S(1)} %copy-done.2, s32[1024]{0:T(1024)S(1)} %pad_clamp_fusion.1), kind=kCustom, calls=%fused_computation.1 | custom fusion | bytes 288 | tf_op jit(solution)/shard_map/gather | solution.py:184
  28.2 0.7 %gather_fusion.2 = s32[24]{0:T(128)S(1)} fusion(s32[8]{0:T(128)S(1)} %copy-done.1, s32[1024]{0:T(1024)S(1)} %pad_clamp_fusion.1), kind=kCustom, calls=%fused_computation.2 | custom fusion | bytes 288 | tf_op jit(solution)/shard_map/gather | solution.py:185
  28.9 0.7 %gather_fusion.3 = s32[24]{0:T(128)S(1)} fusion(s32[8]{0:T(128)S(1)} %copy-done, s32[1024]{0:T(1024)S(1)} %pad_clamp_fusion.1), kind=kCustom, calls=%fused_computation.3 | custom fusion | bytes 288 | tf_op jit(solution)/shard_map/gather | solution.py:186
  31.2 0.8 %fusion.137 = (bf16[8,32,4,128]{3,1,2,0:T(8,128)(2,1)}, bf16[8,32,4,128]{3,1,2,0:T(8,128)(2,1)S(1)}) fusion(bf16[8,32,4,384]{3,1,2,0:T(8,128)(2,1)S(1)} %bitcast.50), kind=kLoop, calls=%fused_computation.216 | loop fusion | bytes 1048576 | tf_op jit(solution)/shard_map/slice | solution.py:74
  32.0 1.6 %collective-permute-start.2 = (bf16[2,32,4,384]{3,1,0,2:T(8,128)(2,1)S(1)}, bf16[2,32,4,384]{3,1,0,2:T(8,128)(2,1)S(1)}, u32[]{:S(2)}, u32[]{:S(2)}) collective-permute-start(bf16[2,32,4,384]{3,1,0,2:T(8,128)(2,1)S(1)} %collective-permute-done), channel_id=1, source_target_pairs={{0,8},{8,16},{16,24},{24,28},{28,20},{20,12},{12,4},{4,0},{1,9},{9... | collective-permute-start | bytes 589832 | tf_op jit(solution)/shard_map/ppermute | solution.py:113
  34.7 3.9 %collective-permute-done.2 = bf16[2,32,4,384]{3,1,0,2:T(8,128)(2,1)S(1)} collective-permute-done((bf16[2,32,4,384]{3,1,0,2:T(8,128)(2,1)S(1)}, bf16[2,32,4,384]{3,1,0,2:T(8,128)(2,1)S(1)}, u32[]{:S(2)}, u32[]{:S(2)}) %collective-permute-start.2) | collective-permute-done | bytes 196640 | tf_op jit(solution)/shard_map/ppermute | solution.py:113
  38.6 1.3 %collective-permute-done.3 = bf16[2,32,4,384]{3,1,0,2:T(8,128)(2,1)S(1)} collective-permute-done((bf16[2,32,4,384]{3,1,0,2:T(8,128)(2,1)S(1)}, bf16[2,32,4,384]{3,1,0,2:T(8,128)(2,1)S(1)}, u32[]{:S(2)}, u32[]{:S(2)}) %collective-permute-start.3) | collective-permute-done | bytes 196640 | tf_op jit(solution)/shard_map/ppermute | solution.py:117
  40.3 0.9 %fusion.136 = (bf16[8,32,4,128]{3,1,2,0:T(8,128)(2,1)}, bf16[8,32,4,128]{3,1,2,0:T(8,128)(2,1)}) fusion(bf16[8,32,4,384]{3,1,2,0:T(8,128)(2,1)S(1)} %bitcast.52), kind=kLoop, calls=%fused_computation.215 | loop fusion | bytes 1048576 | tf_op jit(solution)/shard_map/slice | solution.py:74
  41.3 1.6 %collective-permute-start.4 = (bf16[2,32,4,384]{3,1,0,2:T(8,128)(2,1)S(1)}, bf16[2,32,4,384]{3,1,0,2:T(8,128)(2,1)S(1)}, u32[]{:S(2)}, u32[]{:S(2)}) collective-permute-start(bf16[2,32,4,384]{3,1,0,2:T(8,128)(2,1)S(1)} %collective-permute-done.2), channel_id=1, source_target_pairs={{0,8},{8,16},{16,24},{24,28},{28,20},{20,12},{12,4},{4,0},{1,9},{9... | collective-permute-start | bytes 589832 | tf_op jit(solution)/shard_map/ppermute | solution.py:113
  43.9 3.0 %collective-permute-done.4 = bf16[2,32,4,384]{3,1,0,2:T(8,128)(2,1)S(1)} collective-permute-done((bf16[2,32,4,384]{3,1,0,2:T(8,128)(2,1)S(1)}, bf16[2,32,4,384]{3,1,0,2:T(8,128)(2,1)S(1)}, u32[]{:S(2)}, u32[]{:S(2)}) %collective-permute-start.4) | collective-permute-done | bytes 196640 | tf_op jit(solution)/shard_map/ppermute | solution.py:113
  47.0 1.6 %collective-permute-done.5 = bf16[2,32,4,384]{3,1,0,2:T(8,128)(2,1)S(1)} collective-permute-done((bf16[2,32,4,384]{3,1,0,2:T(8,128)(2,1)S(1)}, bf16[2,32,4,384]{3,1,0,2:T(8,128)(2,1)S(1)}, u32[]{:S(2)}, u32[]{:S(2)}) %collective-permute-start.5) | collective-permute-done | bytes 196640 | tf_op jit(solution)/shard_map/ppermute | solution.py:117
  49.7 1.0 %fusion.135 = (bf16[8,32,4,128]{3,1,2,0:T(8,128)(2,1)}, bf16[8,32,4,128]{3,1,2,0:T(8,128)(2,1)}) fusion(bf16[8,32,4,384]{3,1,2,0:T(8,128)(2,1)S(1)} %bitcast.54), kind=kLoop, calls=%fused_computation.214 | loop fusion | bytes 1048576 | tf_op jit(solution)/shard_map/slice | solution.py:74
  51.4 2.9 %fusion.153 = (f32[8,4,32]{2,1,0:T(4,128)}, f32[8,4,32,48]{3,2,1,0:T(8,128)}) fusion(bf16[8,16,4,128]{3,1,2,0:T(8,128)(2,1)} %get-tuple-element.16, bf16[8,32,4,128]{3,1,2,0:T(8,128)(2,1)} %get-tuple-element.2, bf16[8,32,4,384]{3,1,2,0:T(8,128)(2,1)S(1)} %bitcast.55, pred[8,32,48]{2,1,0:T(8,128)(4,1)} %get-tuple-element.25), kind=kOutput, calls=%fused_computation.226 | convolution fusion | flops 13615151 | bytes 921600 | tf_op jit(solution)/shard_map/sub | solution.py:41
  54.3 2.8 %fusion.150 = (f32[8,4,32]{2,1,0:T(4,128)}, f32[8,4,32,48]{3,2,1,0:T(8,128)}) fusion(bf16[8,16,4,128]{3,1,2,0:T(8,128)(2,1)} %get-tuple-element.16, bf16[8,32,4,128]{3,1,2,0:T(8,128)(2,1)S(1)} %copy-done.6, bf16[8,32,4,384]{3,1,2,0:T(8,128)(2,1)S(1)} %bitcast.53, pred[8,32,48]{2,1,0:T(8,128)(4,1)} %get-tuple-element.26), kind=kOutput, calls=%fused_computation.225 | convolution fusion | flops 13615151 | bytes 921600 | tf_op jit(solution)/shard_map/sub | solution.py:41
  57.2 1.2 %fusion.147 = (f32[8,4,32]{2,1,0:T(4,128)S(1)}, f32[8,4,32,48]{3,2,1,0:T(8,128)}) fusion(bf16[8,16,4,128]{3,1,2,0:T(8,128)(2,1)S(1)} %copy-done.13, bf16[8,32,4,128]{3,1,2,0:T(8,128)(2,1)S(1)} %copy-done.4, bf16[8,32,4,384]{3,1,2,0:T(8,128)(2,1)S(1)} %bitcast.51, pred[8,32,48]{2,1,0:T(8,128)(4,1)S(1)} %copy-done.16), kind=kOutput, calls=%fused_computation.224 | convolution fusion | flops 13615151 | bytes 921600 | tf_op jit(solution)/shard_map/sub | solution.py:41
  59.9 1.6 %collective-permute-start.6 = (bf16[2,32,4,384]{3,1,0,2:T(8,128)(2,1)S(1)}, bf16[2,32,4,384]{3,1,0,2:T(8,128)(2,1)S(1)}, u32[]{:S(2)}, u32[]{:S(2)}) collective-permute-start(bf16[2,32,4,384]{3,1,0,2:T(8,128)(2,1)S(1)} %copy-done.9), channel_id=1, source_target_pairs={{0,8},{8,16},{16,24},{24,28},{28,20},{20,12},{12,4},{4,0},{1,9},{9... | collective-permute-start | bytes 589832 | tf_op jit(solution)/shard_map/ppermute | solution.py:113
  61.9 3.7 %collective-permute-done.6 = bf16[2,32,4,384]{3,1,0,2:T(8,128)(2,1)S(1)} collective-permute-done((bf16[2,32,4,384]{3,1,0,2:T(8,128)(2,1)S(1)}, bf16[2,32,4,384]{3,1,0,2:T(8,128)(2,1)S(1)}, u32[]{:S(2)}, u32[]{:S(2)}) %collective-permute-start.6) | collective-permute-done | bytes 196640 | tf_op jit(solution)/shard_map/ppermute | solution.py:113
  67.7 1.5 %gather_fusion.4 = bf16[24,32,512]{2,1,0:T(8,128)(2,1)} fusion(bf16[32,32,512]{2,1,0:T(8,128)(2,1)S(1)} %bitcast_dynamic-update-slice_fusion.3, s32[1024]{0:T(1024)S(1)} %pad_clamp_fusion), kind=kCustom, calls=%fused_computation.4 | custom fusion | bytes 1572960 | tf_op jit(solution)/shard_map/gather | solution.py:189
  (160 shorter events, 15.3 us)
Async XLA Ops:
  0.6 11.3 %copy-start.17 = (bf16[4096]{0:T(1024)(128)(2,1)S(1)}, bf16[4096]{0:T(1024)(128)(2,1)}, u32[]{:S(2)}) copy-start(bf16[4096]{0:T(1024)(128)(2,1)} %param.14) | copy-start | bytes 24580
  20.0 10.7 %collective-permute-start = (bf16[2,32,4,384]{3,1,0,2:T(8,128)(2,1)S(1)}, bf16[2,32,4,384]{3,1,0,2:T(8,128)(2,1)S(1)}, u32[]{:S(2)}, u32[]{:S(2)}) collective-permute-start(bf16[2,32,4,384]{3,1,0,2:T(8,128)(2,1)S(1)} %and_select_fusion), channel_id=1, source_target_pairs={{0,8},{8,16},{16,24},{24,28},{28,20},{20,12},{12,4},{4,0},{1,9},{9... | collective-permute-start | bytes 589832 | tf_op jit(solution)/shard_map/ppermute | solution.py:113
  21.6 9.1 %collective-permute-start.1 = (bf16[2,32,4,384]{3,1,0,2:T(8,128)(2,1)S(1)}, bf16[2,32,4,384]{3,1,0,2:T(8,128)(2,1)S(1)}, u32[]{:S(2)}, u32[]{:S(2)}) collective-permute-start(bf16[2,32,4,384]{3,1,0,2:T(8,128)(2,1)S(1)} %and_select_fusion), channel_id=1, source_target_pairs={{8,0},{16,8},{24,16},{28,24},{20,28},{12,20},{4,12},{0,4},{9,1},{1... | collective-permute-start | bytes 589832 | tf_op jit(solution)/shard_map/ppermute | solution.py:117
  22.3 3.2 %copy-start.3 = (s32[8]{0:T(128)S(1)}, s32[8]{0:T(128)}, u32[]{:S(2)}) copy-start(s32[8]{0:T(128)} %constant.90.clone) | copy-start | bytes 100
  22.3 5.1 %copy-start.2 = (s32[8]{0:T(128)S(1)}, s32[8]{0:T(128)}, u32[]{:S(2)}) copy-start(s32[8]{0:T(128)} %constant.91.clone) | copy-start | bytes 100
  22.5 5.7 %copy-start.19 = (s32[4]{0:T(128)}, s32[4]{0:T(128)S(1)}, u32[]{:S(2)}) copy-start(s32[4]{0:T(128)S(1)} %lt.237) | copy-start | bytes 52
  23.2 5.0 %copy-start.1 = (s32[8]{0:T(128)S(1)}, s32[8]{0:T(128)}, u32[]{:S(2)}) copy-start(s32[8]{0:T(128)} %constant.92.clone) | copy-start | bytes 100
  23.2 5.7 %copy-start = (s32[8]{0:T(128)S(1)}, s32[8]{0:T(128)}, u32[]{:S(2)}) copy-start(s32[8]{0:T(128)} %constant.93.clone) | copy-start | bytes 100
  32.0 6.6 %collective-permute-start.2 = (bf16[2,32,4,384]{3,1,0,2:T(8,128)(2,1)S(1)}, bf16[2,32,4,384]{3,1,0,2:T(8,128)(2,1)S(1)}, u32[]{:S(2)}, u32[]{:S(2)}) collective-permute-start(bf16[2,32,4,384]{3,1,0,2:T(8,128)(2,1)S(1)} %collective-permute-done), channel_id=1, source_target_pairs={{0,8},{8,16},{16,24},{24,28},{28,20},{20,12},{12,4},{4,0},{1,9},{9... | collective-permute-start | bytes 589832 | tf_op jit(solution)/shard_map/ppermute | solution.py:113
  33.6 6.3 %collective-permute-start.3 = (bf16[2,32,4,384]{3,1,0,2:T(8,128)(2,1)S(1)}, bf16[2,32,4,384]{3,1,0,2:T(8,128)(2,1)S(1)}, u32[]{:S(2)}, u32[]{:S(2)}) collective-permute-start(bf16[2,32,4,384]{3,1,0,2:T(8,128)(2,1)S(1)} %collective-permute-done.1), channel_id=1, source_target_pairs={{8,0},{16,8},{24,16},{28,24},{20,28},{12,20},{4,12},{0,4},{9,1},{1... | collective-permute-start | bytes 589832 | tf_op jit(solution)/shard_map/ppermute | solution.py:117
  41.3 5.7 %collective-permute-start.4 = (bf16[2,32,4,384]{3,1,0,2:T(8,128)(2,1)S(1)}, bf16[2,32,4,384]{3,1,0,2:T(8,128)(2,1)S(1)}, u32[]{:S(2)}, u32[]{:S(2)}) collective-permute-start(bf16[2,32,4,384]{3,1,0,2:T(8,128)(2,1)S(1)} %collective-permute-done.2), channel_id=1, source_target_pairs={{0,8},{8,16},{16,24},{24,28},{28,20},{20,12},{12,4},{4,0},{1,9},{9... | collective-permute-start | bytes 589832 | tf_op jit(solution)/shard_map/ppermute | solution.py:113
  42.9 5.7 %collective-permute-start.5 = (bf16[2,32,4,384]{3,1,0,2:T(8,128)(2,1)S(1)}, bf16[2,32,4,384]{3,1,0,2:T(8,128)(2,1)S(1)}, u32[]{:S(2)}, u32[]{:S(2)}) collective-permute-start(bf16[2,32,4,384]{3,1,0,2:T(8,128)(2,1)S(1)} %collective-permute-done.3), channel_id=1, source_target_pairs={{8,0},{16,8},{24,16},{28,24},{20,28},{12,20},{4,12},{0,4},{9,1},{1... | collective-permute-start | bytes 589832 | tf_op jit(solution)/shard_map/ppermute | solution.py:117
  49.7 4.6 %copy-start.6 = (bf16[8,32,4,128]{3,1,2,0:T(8,128)(2,1)S(1)}, bf16[8,32,4,128]{3,1,2,0:T(8,128)(2,1)}, u32[]{:S(2)}) copy-start(bf16[8,32,4,128]{3,1,2,0:T(8,128)(2,1)} %get-tuple-element.4) | copy-start | bytes 786436
  51.4 5.8 %copy-start.4 = (bf16[8,32,4,128]{3,1,2,0:T(8,128)(2,1)S(1)}, bf16[8,32,4,128]{3,1,2,0:T(8,128)(2,1)}, u32[]{:S(2)}) copy-start(bf16[8,32,4,128]{3,1,2,0:T(8,128)(2,1)} %get-tuple-element.6) | copy-start | bytes 786436
  54.3 4.1 %copy-start.7 = (bf16[8,32,4,128]{3,1,2,0:T(8,128)(2,1)S(1)}, bf16[8,32,4,128]{3,1,2,0:T(8,128)(2,1)}, u32[]{:S(2)}) copy-start(bf16[8,32,4,128]{3,1,2,0:T(8,128)(2,1)} %get-tuple-element.3) | copy-start | bytes 786436
  54.3 4.1 %copy-start.12 = (bf16[8,16,4,128]{3,1,2,0:T(8,128)(2,1)S(1)}, bf16[8,16,4,128]{3,1,2,0:T(8,128)(2,1)}, u32[]{:S(2)}) copy-start(bf16[8,16,4,128]{3,1,2,0:T(8,128)(2,1)} %get-tuple-element.17) | copy-start | bytes 393220
  54.3 4.1 %copy-start.24 = (pred[8,32]{1,0:T(8,128)(4,1)S(1)}, pred[8,32]{1,0:T(8,128)(4,1)}, u32[]{:S(2)}) copy-start(pred[8,32]{1,0:T(8,128)(4,1)} %iota_compare_fusion.2) | copy-start | bytes 772
  59.9 6.0 %copy-start.20 = (s32[4]{0:T(128)S(1)}, s32[4]{0:T(128)}, u32[]{:S(2)}) copy-start(s32[4]{0:T(128)} %copy-done.19) | copy-start | bytes 52
  59.9 5.7 %collective-permute-start.6 = (bf16[2,32,4,384]{3,1,0,2:T(8,128)(2,1)S(1)}, bf16[2,32,4,384]{3,1,0,2:T(8,128)(2,1)S(1)}, u32[]{:S(2)}, u32[]{:S(2)}) collective-permute-start(bf16[2,32,4,384]{3,1,0,2:T(8,128)(2,1)S(1)} %copy-done.9), channel_id=1, source_target_pairs={{0,8},{8,16},{16,24},{24,28},{28,20},{20,12},{12,4},{4,0},{1,9},{9... | collective-permute-start | bytes 589832 | tf_op jit(solution)/shard_map/ppermute | solution.py:113
  61.5 4.6 %copy-start.11 = (bf16[4,32,4,128]{3,1,2,0:T(8,128)(2,1)S(1)}, bf16[4,32,4,128]{3,1,2,0:T(8,128)(2,1)}, u32[]{:S(2)}) copy-start(bf16[4,32,4,128]{3,1,2,0:T(8,128)(2,1)} %get-tuple-element.14) | copy-start | bytes 393220
  61.5 4.6 %copy-start.15 = (bf16[4,16,4,128]{3,1,2,0:T(8,128)(2,1)S(1)}, bf16[4,16,4,128]{3,1,2,0:T(8,128)(2,1)}, u32[]{:S(2)}) copy-start(bf16[4,16,4,128]{3,1,2,0:T(8,128)(2,1)} %get-tuple-element.18) | copy-start | bytes 196612
  61.9 4.7 %copy-start.10 = (bf16[4,32,4,128]{3,1,2,0:T(8,128)(2,1)S(1)}, bf16[4,32,4,128]{3,1,2,0:T(8,128)(2,1)}, u32[]{:S(2)}) copy-start(bf16[4,32,4,128]{3,1,2,0:T(8,128)(2,1)} %get-tuple-element.15) | copy-start | bytes 393220
  61.9 4.7 %copy-start.14 = (bf16[4,16,4,128]{3,1,2,0:T(8,128)(2,1)S(1)}, bf16[4,16,4,128]{3,1,2,0:T(8,128)(2,1)}, u32[]{:S(2)}) copy-start(bf16[4,16,4,128]{3,1,2,0:T(8,128)(2,1)} %get-tuple-element.19) | copy-start | bytes 196612
  61.9 4.7 %copy-start.25 = (pred[4,32]{1,0:T(4,128)(4,1)S(1)}, pred[4,32]{1,0:T(4,128)(4,1)}, u32[]{:S(2)}) copy-start(pred[4,32]{1,0:T(4,128)(4,1)} %iota_compare_fusion.7) | copy-start | bytes 388
  (14 other events, 24.6 us)

commit v7 on v3

--- a/solution.py
+++ b/solution.py
@@ -1,8 +1,10 @@
+import functools
 import math
 
 import jax
 import jax.numpy as jnp
 from jax import lax
+from jax.experimental import pallas as pl
 from jax.sharding import PartitionSpec as P
 
 
@@ -126,6 +128,72 @@
         return slot * count + rows % count
 
     return jnp.concatenate(parts, axis=0), rows_of
+
+
+def pair_kernel(row_query_ref, row_len_ref, pair_ref, query_ref, out_ref, *, head_dim, passage_len, query_len, chunk):
+    scale = head_dim ** (-0.5)
+    query_part = query_ref[0]
+    query_keys = query_part[:, head_dim : 2 * head_dim]
+    query_values = query_part[:, 2 * head_dim :]
+    query_cols = query_keys.shape[0]
+    contract = (((1,), (1,)), ((), ()))
+    for start in range(0, pair_ref.shape[1], chunk):
+        block = pair_ref[0, start : start + chunk, :]
+        queries = block[:, :head_dim]
+        keys = block[:, head_dim : 2 * head_dim]
+        values = block[:, 2 * head_dim :]
+        owner = row_query_ref[start : start + chunk, :]
+        length = row_len_ref[start : start + chunk, :]
+        to_query = lax.dot_general(queries, query_keys, contract, preferred_element_type=jnp.float32) * scale
+        to_own = lax.dot_general(queries, keys, contract, preferred_element_type=jnp.float32) * scale
+        query_at = lax.broadcasted_iota(jnp.int32, to_query.shape, 1) // query_len
+        allow_query = query_at == owner
+        row_at = lax.broadcasted_iota(jnp.int32, to_own.shape, 0)
+        col_at = lax.broadcasted_iota(jnp.int32, to_own.shape, 1)
+        col_tok = col_at % passage_len
+        allow_own = (row_at // passage_len == col_at // passage_len) & (col_tok <= row_at % passage_len) & (col_tok < length)
+        masked_query = jnp.where(allow_query, to_query, jnp.float32(-1e30))
+        masked_own = jnp.where(allow_own, to_own, jnp.float32(-1e30))
+        peak = jnp.maximum(jnp.max(masked_query, axis=1, keepdims=True), jnp.max(masked_own, axis=1, keepdims=True))
+        exp_query = jnp.where(allow_query, jnp.exp(masked_query - peak), jnp.float32(0.0))
+        exp_own = jnp.where(allow_own, jnp.exp(masked_own - peak), jnp.float32(0.0))
+        total = jnp.sum(exp_query, axis=1, keepdims=True) + jnp.sum(exp_own, axis=1, keepdims=True)
+        weight_query = (exp_query / total).astype(jnp.bfloat16)
+        weight_own = (exp_own / total).astype(jnp.bfloat16)
+        out = jnp.dot(weight_query, query_values, preferred_element_type=jnp.float32) + jnp.dot(
+            weight_own, values, preferred_element_type=jnp.float32
+        )
+        tok = lax.broadcasted_iota(jnp.int32, out.shape, 0) % passage_len
+        out_ref[0, start : start + chunk, :] = jnp.where(tok < length, out, jnp.float32(0.0)).astype(out_ref.dtype)
+
+
+def attend_pairs_kernel(query_qkv, pair_qkv, pair_lengths, head_dim, cands, interpret=False):
+    quer_count, query_len, heads = query_qkv.shape[0], query_qkv.shape[1], query_qkv.shape[2]
+    pairs, passage_len = pair_qkv.shape[0], pair_qkv.shape[1]
+    rows = pairs * passage_len
+    chunk = 128 if rows % 128 == 0 and 128 % passage_len == 0 else rows
+    width = 3 * head_dim
+    by_head = jnp.transpose(pair_qkv, (2, 0, 1, 3)).reshape(heads, rows, width)
+    query_by_head = jnp.transpose(query_qkv, (2, 0, 1, 3)).reshape(heads, quer_count * query_len, width)
+    row_pair = jnp.arange(rows, dtype=jnp.int32) // passage_len
+    row_query = (row_pair // cands).reshape(rows, 1)
+    row_len = pair_lengths[row_pair].reshape(rows, 1)
+    body = functools.partial(pair_kernel, head_dim=head_dim, passage_len=passage_len, query_len=query_len, chunk=chunk)
+    out = pl.pallas_call(
+        body,
+        grid=(heads,),
+        in_specs=[
+            pl.BlockSpec((rows, 1), lambda h: (0, 0)),
+            pl.BlockSpec((rows, 1), lambda h: (0, 0)),
+            pl.BlockSpec((1, rows, width), lambda h: (h, 0, 0)),
+            pl.BlockSpec((1, quer_count * query_len, width), lambda h: (h, 0, 0)),
+        ],
+        out_specs=pl.BlockSpec((1, rows, head_dim), lambda h: (h, 0, 0)),
+        out_shape=jax.ShapeDtypeStruct((heads, rows, head_dim), jnp.bfloat16),
+        interpret=interpret,
+    )(row_query, row_len, by_head, query_by_head)
+    out = jnp.transpose(out.reshape(heads, pairs, passage_len, head_dim), (1, 2, 0, 3))
+    return out.reshape(pairs, passage_len, heads * head_dim)
 
 
 def local(query_embeds, passage_embeds, passage_lengths, cand_passage, norm_gain, w_qkv):
@@ -156,7 +224,7 @@
     pair_qkv = store_qkv[rows_of(cand_passage)]
     pair_lengths = jnp.sum(jnp.isfinite(pair_qkv[:, :, 0, head_dim]).astype(jnp.int32), axis=1)
     query_attn = attend_queries(query_qkv, head_dim)
-    passage_attn = attend_pairs(query_qkv, pair_qkv, pair_lengths, head_dim, cands)
+    passage_attn = attend_pairs_kernel(query_qkv, pair_qkv, pair_lengths, head_dim, cands)
     return (query_attn, passage_attn)
 
 

time: 61.7 us -> 86.8 us (1.41)
  other arithmetic: 5.44 us -> 22.9 us
  Pallas kernels: 0 us -> 11.2 us
  matrix products: 13.3 us -> 7.25 us
  local copies, waits for them, and re-layouts: 13.3 us -> 16.6 us
  waiting for transfers between devices: 10.8 us -> 9.6 us
    gather x0 -> x19, other arithmetic: none -> 18.3 us  [attend_pairs_kernel(): row_len = pair_lengths[row_pair].reshape(rows, 1)]
    pallas_call x0 -> x1, Pallas kernels: none -> 11.2 us  [attend_pairs_kernel(): pl.pallas_call(body, grid=(heads,), in_specs=[pl.BlockSpec((rows, 1), lam...]
    sub x2 -> x1, matrix products: 4.22 us -> 0.18 us  [softmax_rounded(): expon = jnp.where(allowed, jnp.exp(masked - peak), jnp.float32(0.0))]
    reshape x0 -> x3, local copies, waits for them, and re-layouts: none -> 3.79 us  [the longest x1 2.23 us: attend_pairs_kernel(): return out.reshape(pairs, passage_len, heads * head_dim)]
    slice x5 -> x0, local copies, waits for them, and re-layouts: 2.31 us -> none  [the longest x1 1.32 us: attend_core(): pair_qkv[..., head_dim:2 * head_dim]]
    dot_general x1 -> x0, matrix products: 2.04 us -> none  [attend_core(): jnp.einsum('bhit,bthd->bihd', weights, values, preferred_element_type=jnp...]
    transpose x0 -> x1, local copies, waits for them, and re-layouts: none -> 1.69 us  [attend_pairs_kernel(): by_head = jnp.transpose(pair_qkv, (2, 0, 1, 3)).reshape(heads, rows, width)]
    gather x0 -> x2, local copies, waits for them, and re-layouts: none -> 1.39 us  [attend_pairs_kernel(): row_len = pair_lengths[row_pair].reshape(rows, 1)]
  transfers between devices with their start and end apart: 7 -> 7, of which waited for: 4 -> 3; matrix products, arithmetic and copies ran while one was open for 14% -> 13% of each run, Pallas kernels for 0% -> 0%
where the time goes in v7:
time: 86.8 us; the launch traced here: 86.3 us
  other arithmetic  22.9 us (26%)
  local copies, waits for them, and re-layouts  16.6 us (19%)
  Pallas kernels  11.2 us (13%)
  blocking collectives  10.1 us (12%)
  waiting for transfers between devices  9.6 us (11%)
  starting transfers between devices  7.71 us (9%)
  matrix products  7.25 us (8%)
    gather x19, other arithmetic, attend_pairs_kernel(): row_len = pair_lengths[row_pair].reshape(rows, 1)  18.3 us
    pallas_call x1, Pallas kernels, attend_pairs_kernel(): pl.pallas_call(body, grid=(heads,), in_specs=[pl.BlockSpec((rows, 1), lam...  11.2 us
    all_gather x1, blocking collectives, local(): full_rows = lax.all_gather(all_rows, 'tp', axis=1, tiled=True)  10.1 us
    ppermute x4, waiting for transfers between devices, gather_store(): ahead = lax.ppermute(ahead, 'store', forward)  9.6 us
    dot_general x1, matrix products, local(): jnp.einsum('nk,khc->nhc', normed, w_qkv, preferred_element_type=jnp.float32)  6.86 us
    ppermute x4, starting transfers between devices, gather_store(): ahead = lax.ppermute(ahead, 'store', forward)  6.29 us
    unnamed x14, local copies, waits for them, and re-layouts  4.18 us
    gather x1, local copies, waits for them, and re-layouts, local(): pair_qkv = store_qkv[rows_of(cand_passage)]  2.52 us
  transfers between devices with their start and end apart: 7, of which 3 were waited for; matrix products, arithmetic and copies ran while one was open for 13% of the time, Pallas kernels for 0%

profile of v7, /device:TPU:0, one launch (start us, length us, event | category | flops | bytes accessed | tf_op | source)
XLA Modules:
  0.0 86.3 jit_solution(4152414285835714387)
XLA Ops:
  0.7 0.9 %pad_maximum_fusion = bf16[96,1024]{1,0:T(8,128)(2,1)S(1)} fusion(bf16[64,1024]{1,0:T(8,128)(2,1)} %bitcast.58, bf16[32,1024]{1,0:T(8,128)(2,1)} %bitcast.59), kind=kLoop, calls=%fused_computation.80 | loop fusion | flops 393216 | bytes 393216 | tf_op jit(solution)/shard_map/concatenate | solution.py:211
  1.6 10.1 %all_gather.3 = bf16[96,4096]{1,0:T(8,128)(2,1)S(1)} all-gather(bf16[96,1024]{1,0:T(8,128)(2,1)S(1)} %pad_maximum_fusion), channel_id=1, replica_groups=mesh['store'=8,'tp'=4] {'tp'}, dimensions={1}, use_global_device_ids=true | all-gather | bytes 983040 | tf_op jit(solution)/shard_map/all_gather | solution.py:212
  12.1 6.9 %fusion.1 = f32[96,4,384]{2,0,1:T(8,128)S(1)} fusion(bf16[4096,4,384]{2,1,0:T(4,128)(2,1)} %param.12, bf16[96,4096]{1,0:T(8,128)(2,1)S(1)} %all_gather.3, f32[4096]{0:T(1024)S(1)} %convert_element_type.27, f32[96]{0:T(128)S(1)} %add_rsqrt_fusion), kind=kOutput, calls=%fused_computation.3 | convolution fusion | flops 1209532416 | bytes 13975936 | tf_op jit(solution)/shard_map/nk,khc->nhc/dot_general | solution.py:214
  19.9 0.8 constant_dynamic-update-slice_fusion.7
  20.7 1.6 %collective-permute-start = (bf16[2,32,4,384]{3,1,2,0:T(8,128)(2,1)S(1)}, bf16[2,32,4,384]{3,1,2,0:T(8,128)(2,1)S(1)}, u32[]{:S(2)}, u32[]{:S(2)}) collective-permute-start(bf16[2,32,4,384]{3,1,2,0:T(8,128)(2,1)S(1)} %get-tuple-element.3), channel_id=1, source_target_pairs={{0,8},{8,16},{16,24},{24,28},{28,20},{20,12},{12,4},{4,0},{1,9},{9... | collective-permute-start | bytes 589832 | tf_op jit(solution)/shard_map/ppermute | solution.py:116
  27.2 0.7 gather_fusion
  28.8 0.8 add_select_fusion.row_query_ref
  29.6 1.6 %collective-permute-start.1 = (bf16[2,32,4,384]{3,1,2,0:T(8,128)(2,1)S(1)}, bf16[2,32,4,384]{3,1,2,0:T(8,128)(2,1)S(1)}, u32[]{:S(2)}, u32[]{:S(2)}) collective-permute-start(bf16[2,32,4,384]{3,1,2,0:T(8,128)(2,1)S(1)} %collective-permute-done), channel_id=1, source_target_pairs={{0,8},{8,16},{16,24},{24,28},{28,20},{20,12},{12,4},{4,0},{1,9},{9... | collective-permute-start | bytes 589832 | tf_op jit(solution)/shard_map/ppermute | solution.py:116
  32.4 3.9 %collective-permute-done.1 = bf16[2,32,4,384]{3,1,2,0:T(8,128)(2,1)S(1)} collective-permute-done((bf16[2,32,4,384]{3,1,2,0:T(8,128)(2,1)S(1)}, bf16[2,32,4,384]{3,1,2,0:T(8,128)(2,1)S(1)}, u32[]{:S(2)}, u32[]{:S(2)}) %collective-permute-start.1) | collective-permute-done | bytes 196640 | tf_op jit(solution)/shard_map/ppermute | solution.py:116
  36.2 1.6 %collective-permute-start.2 = (bf16[2,32,4,384]{3,1,2,0:T(8,128)(2,1)S(1)}, bf16[2,32,4,384]{3,1,2,0:T(8,128)(2,1)S(1)}, u32[]{:S(2)}, u32[]{:S(2)}) collective-permute-start(bf16[2,32,4,384]{3,1,2,0:T(8,128)(2,1)S(1)} %collective-permute-done.1), channel_id=1, source_target_pairs={{0,8},{8,16},{16,24},{24,28},{28,20},{20,12},{12,4},{4,0},{1,9},{9... | collective-permute-start | bytes 589832 | tf_op jit(solution)/shard_map/ppermute | solution.py:116
  37.8 0.7 constant_dynamic-update-slice_fusion.6
  39.0 3.0 %collective-permute-done.2 = bf16[2,32,4,384]{3,1,2,0:T(8,128)(2,1)S(1)} collective-permute-done((bf16[2,32,4,384]{3,1,2,0:T(8,128)(2,1)S(1)}, bf16[2,32,4,384]{3,1,2,0:T(8,128)(2,1)S(1)}, u32[]{:S(2)}, u32[]{:S(2)}) %collective-permute-start.2) | collective-permute-done | bytes 196640 | tf_op jit(solution)/shard_map/ppermute | solution.py:116
  42.0 1.6 %collective-permute-start.3 = (bf16[2,32,4,384]{3,1,2,0:T(8,128)(2,1)S(1)}, bf16[2,32,4,384]{3,1,2,0:T(8,128)(2,1)S(1)}, u32[]{:S(2)}, u32[]{:S(2)}) collective-permute-start(bf16[2,32,4,384]{3,1,2,0:T(8,128)(2,1)S(1)} %collective-permute-done.2), channel_id=1, source_target_pairs={{0,8},{8,16},{16,24},{24,28},{28,20},{20,12},{12,4},{4,0},{1,9},{9... | collective-permute-start | bytes 589832 | tf_op jit(solution)/shard_map/ppermute | solution.py:116
  44.9 2.7 %collective-permute-done.3 = bf16[2,32,4,384]{3,1,2,0:T(8,128)(2,1)S(1)} collective-permute-done((bf16[2,32,4,384]{3,1,2,0:T(8,128)(2,1)S(1)}, bf16[2,32,4,384]{3,1,2,0:T(8,128)(2,1)S(1)}, u32[]{:S(2)}, u32[]{:S(2)}) %collective-permute-start.3) | collective-permute-done | bytes 196640 | tf_op jit(solution)/shard_map/ppermute | solution.py:116
  47.6 0.7 constant_dynamic-update-slice_fusion.3
  49.7 0.7 constant_dynamic-update-slice_fusion
  50.4 2.5 %gather_fusion.1 = bf16[24,32,4,384]{3,1,2,0:T(8,128)(2,1)S(1)} fusion(bf16[16,32,4,384]{3,1,2,0:T(8,128)(2,1)} %constant_dynamic-update-slice_fusion, s32[1024]{0:T(1024)S(1)} %pad_clamp_fusion), kind=kCustom, calls=%fused_computation.1 | custom fusion | bytes 4718688 | tf_op jit(solution)/shard_map/gather | solution.py:224
  53.5 0.7 fusion.72
  54.9 1.7 %copy.22 = bf16[4,24,32,384]{3,2,1,0:T(8,128)(2,1)} copy(bf16[4,24,32,384]{3,2,0,1:T(8,128)(2,1)S(1)} %bitcast.52) | data formatting | bytes 4718592 | tf_op jit(solution)/shard_map/transpose | solution.py:176
  56.6 4.7 %select_reduce_fusion = s32[768]{0:T(1024)S(1)} fusion(s32[]{:T(128)} %bitcast.24, s32[]{:T(128)} %bitcast.25, s32[]{:T(128)} %bitcast.26, s32[]{:T(128)} %bitcast.27, s32[]{:T(128)} %bitcast.28, s32[]{:T(128)} %bitcast.30, s32[]{:T(128)} %bitcast.29), kind=kLoop, calls=%fused_computation.57 | loop fusion | flops 17664 | bytes 3100 | tf_op jit(solution)/shard_map/gather | solution.py:180
  61.3 10.7 %select_select_fusion = s32[768]{0:T(1024)S(1)} fusion(pred[768]{0:T(1024)(128)(4,1)S(1)} %fusion.47, pred[768]{0:T(1024)(128)(4,1)S(1)} %fusion.48, pred[768]{0:T(1024)(128)(4,1)S(1)} %fusion.63, pred[768]{0:T(1024)(128)(4,1)S(1)} %fusion.62, pred[768]{0:T(1024)(128)(4,1)S(1)} %fusion.61, pred[768]{0:T(1024)(128)(4,1)S(1)} %fusion.60, ...), kind=kLoop, calls=%fused_computation.104 | loop fusion | flops 13056 | bytes 19268 | tf_op jit(solution)/shard_map/gather | solution.py:180
  71.9 0.9 %reshape.320.row_len_ref = s32[768,1]{1,0:T(8,128)} reshape(s32[768]{0:T(1024)S(1)} %select_select_fusion) | data formatting | bytes 6144 | tf_op jit(solution)/shard_map/reshape | solution.py:180
  72.8 11.2 %shard_map.86 = bf16[4,768,128]{2,1,0:T(8,128)(2,1)} custom-call(s32[768,1]{1,0:T(8,128)} %add_select_fusion.row_query_ref, s32[768,1]{1,0:T(8,128)} %reshape.320.row_len_ref, bf16[4,768,384]{2,1,0:T(8,128)(2,1)} %bitcast.53, bf16[4,32,384]{2,1,0:T(8,128)(2,1)} %get-tuple-element.8.query_ref), custom_call_target="tpu_custom_call" | custom-call | tf_op jit(solution)/shard_map/pallas_call | solution.py:182
  84.1 2.2 %copy.47 = bf16[4,24,4,8,128]{4,3,0,2,1:T(8,128)(2,1)} copy(bf16[4,24,4,8,128]{4,3,2,1,0:T(8,128)(2,1)} %bitcast.54) | data formatting | bytes 1572864 | tf_op jit(solution)/shard_map/reshape | solution.py:196
  (66 shorter events, 12.6 us)
Async XLA Ops:
  0.6 11.3 %copy-start.1 = (bf16[4096]{0:T(1024)(128)(2,1)S(1)}, bf16[4096]{0:T(1024)(128)(2,1)}, u32[]{:S(2)}) copy-start(bf16[4096]{0:T(1024)(128)(2,1)} %param.11) | copy-start | bytes 24580
  19.0 0.8 copy-start.3
  19.4 6.5 %copy-start.2 = (s32[24]{0:T(128)S(1)}, s32[24]{0:T(128)}, u32[]{:S(2)}) copy-start(s32[24]{0:T(128)} %param.10) | copy-start | bytes 292
  19.6 6.9 %copy-start = (s32[8]{0:T(128)S(1)}, s32[8]{0:T(128)}, u32[]{:S(2)}) copy-start(s32[8]{0:T(128)} %constant.101.clone) | copy-start | bytes 100
  20.7 8.9 %collective-permute-start = (bf16[2,32,4,384]{3,1,2,0:T(8,128)(2,1)S(1)}, bf16[2,32,4,384]{3,1,2,0:T(8,128)(2,1)S(1)}, u32[]{:S(2)}, u32[]{:S(2)}) collective-permute-start(bf16[2,32,4,384]{3,1,2,0:T(8,128)(2,1)S(1)} %get-tuple-element.3), channel_id=1, source_target_pairs={{0,8},{8,16},{16,24},{24,28},{28,20},{20,12},{12,4},{4,0},{1,9},{9... | collective-permute-start | bytes 589832 | tf_op jit(solution)/shard_map/ppermute | solution.py:116
  22.3 9.5 %collective-permute-start.4 = (bf16[2,32,4,384]{3,1,2,0:T(8,128)(2,1)S(1)}, bf16[2,32,4,384]{3,1,2,0:T(8,128)(2,1)S(1)}, u32[]{:S(2)}, u32[]{:S(2)}) collective-permute-start(bf16[2,32,4,384]{3,1,2,0:T(8,128)(2,1)S(1)} %get-tuple-element.3), channel_id=1, source_target_pairs={{8,0},{16,8},{24,16},{28,24},{20,28},{12,20},{4,12},{0,4},{9,1},{1... | collective-permute-start | bytes 589832 | tf_op jit(solution)/shard_map/ppermute | solution.py:120
  29.6 6.6 %collective-permute-start.1 = (bf16[2,32,4,384]{3,1,2,0:T(8,128)(2,1)S(1)}, bf16[2,32,4,384]{3,1,2,0:T(8,128)(2,1)S(1)}, u32[]{:S(2)}, u32[]{:S(2)}) collective-permute-start(bf16[2,32,4,384]{3,1,2,0:T(8,128)(2,1)S(1)} %collective-permute-done), channel_id=1, source_target_pairs={{0,8},{8,16},{16,24},{24,28},{28,20},{20,12},{12,4},{4,0},{1,9},{9... | collective-permute-start | bytes 589832 | tf_op jit(solution)/shard_map/ppermute | solution.py:116
  31.8 6.7 %collective-permute-start.5 = (bf16[2,32,4,384]{3,1,2,0:T(8,128)(2,1)S(1)}, bf16[2,32,4,384]{3,1,2,0:T(8,128)(2,1)S(1)}, u32[]{:S(2)}, u32[]{:S(2)}) collective-permute-start(bf16[2,32,4,384]{3,1,2,0:T(8,128)(2,1)S(1)} %collective-permute-done.4), channel_id=1, source_target_pairs={{8,0},{16,8},{24,16},{28,24},{20,28},{12,20},{4,12},{0,4},{9,1},{1... | collective-permute-start | bytes 589832 | tf_op jit(solution)/shard_map/ppermute | solution.py:120
  36.2 5.7 %collective-permute-start.2 = (bf16[2,32,4,384]{3,1,2,0:T(8,128)(2,1)S(1)}, bf16[2,32,4,384]{3,1,2,0:T(8,128)(2,1)S(1)}, u32[]{:S(2)}, u32[]{:S(2)}) collective-permute-start(bf16[2,32,4,384]{3,1,2,0:T(8,128)(2,1)S(1)} %collective-permute-done.1), channel_id=1, source_target_pairs={{0,8},{8,16},{16,24},{24,28},{28,20},{20,12},{12,4},{4,0},{1,9},{9... | collective-permute-start | bytes 589832 | tf_op jit(solution)/shard_map/ppermute | solution.py:116
  38.5 11.2 %collective-permute-start.6 = (bf16[2,32,4,384]{3,1,2,0:T(8,128)(2,1)S(1)}, bf16[2,32,4,384]{3,1,2,0:T(8,128)(2,1)S(1)}, u32[]{:S(2)}, u32[]{:S(2)}) collective-permute-start(bf16[2,32,4,384]{3,1,2,0:T(8,128)(2,1)S(1)} %collective-permute-done.5), channel_id=1, source_target_pairs={{8,0},{16,8},{24,16},{28,24},{20,28},{12,20},{4,12},{0,4},{9,1},{1... | collective-permute-start | bytes 589832 | tf_op jit(solution)/shard_map/ppermute | solution.py:120
  42.0 5.7 %collective-permute-start.3 = (bf16[2,32,4,384]{3,1,2,0:T(8,128)(2,1)S(1)}, bf16[2,32,4,384]{3,1,2,0:T(8,128)(2,1)S(1)}, u32[]{:S(2)}, u32[]{:S(2)}) collective-permute-start(bf16[2,32,4,384]{3,1,2,0:T(8,128)(2,1)S(1)} %collective-permute-done.2), channel_id=1, source_target_pairs={{0,8},{8,16},{16,24},{24,28},{28,20},{20,12},{12,4},{4,0},{1,9},{9... | collective-permute-start | bytes 589832 | tf_op jit(solution)/shard_map/ppermute | solution.py:116

commit v8 on v5

--- a/solution.py
+++ b/solution.py
@@ -151,7 +151,16 @@
         slot = jnp.where(dist == 0, 0, jnp.where(dist < n_store - first, first + dist, n_store - dist))
         return row * n_store + slot
 
-    return jnp.concatenate(ordered, axis=0), rows_of
+    total = sum(part.shape[0] for part in ordered)
+    row_at = lax.broadcasted_iota(jnp.int32, (total,) + own.shape[1:], 0)
+    joined = None
+    at = 0
+    for part in ordered:
+        size = part.shape[0]
+        widened = jnp.pad(part, ((at, total - at - size),) + ((0, 0),) * (own.ndim - 1))
+        joined = widened if joined is None else jnp.where(row_at >= at, widened, joined)
+        at += size
+    return joined, rows_of
 
 
 def local(query_embeds, passage_embeds, passage_lengths, cand_passage, norm_gain, w_qkv):

time: 64.8 us -> 63 us (0.972)
  local copies, waits for them, and re-layouts: 18.9 us -> 7.81 us
  other arithmetic: 4.1 us -> 10.1 us
  waiting for transfers between devices: 3.73 us -> 6.38 us
  starting transfers between devices: 14.1 us -> 14.9 us
    unnamed x20 -> x6, local copies, waits for them, and re-layouts: 9.22 us -> 0.02 us
    select_n x0 -> x1, other arithmetic: none -> 4.98 us  [gather_store(): jnp.where(row_at >= at, widened, joined)]
    ppermute x7, waiting for transfers between devices: 2.94 us -> 4.46 us  [gather_store(): behind = lax.ppermute(behind, 'store', backward)]
    ppermute x7, starting transfers between devices: 2.96 us -> 4.27 us  [gather_store(): behind = lax.ppermute(behind, 'store', backward)]
    ppermute x7, waiting for transfers between devices: 0.8 us -> 1.92 us  [gather_store(): ahead = lax.ppermute(ahead, 'store', forward)]
    reduce_sum x1, other arithmetic: 0.52 us -> 1.46 us  [local(): jnp.sum(jnp.isfinite(pair_qkv[:, :, 0, head_dim]).astype(jnp.int32), axis=1)]
    slice x1, local copies, waits for them, and re-layouts: 1.12 us -> 0.21 us  [attend_core(): query_kv[..., :head_dim]]
  transfers between devices with their start and end apart: 14 -> 14, of which waited for: 3 -> 7; matrix products, arithmetic and copies ran while one was open for 21% -> 5% of each run, Pallas kernels for 0% -> 0%
where the time goes in v8:
time: 63 us; the launch traced here: 62.7 us
  starting transfers between devices  14.9 us (24%)
  matrix products  12.6 us (20%)
  other arithmetic  10.1 us (16%)
  blocking collectives  10.1 us (16%)
  local copies, waits for them, and re-layouts  7.81 us (12%)
  waiting for transfers between devices  6.38 us (10%)
  between operations  0.93 us (1%)
    ppermute x7, starting transfers between devices, gather_store(): ahead = lax.ppermute(ahead, 'store', forward)  10.6 us
    all_gather x1, blocking collectives, local(): full_rows = lax.all_gather(all_rows, 'tp', axis=1, tiled=True)  10.1 us
    dot_general x1, matrix products, local(): jnp.einsum('nk,khc->nhc', normed, w_qkv, preferred_element_type=jnp.float32)  6.87 us
    select_n x1, other arithmetic, gather_store(): jnp.where(row_at >= at, widened, joined)  4.98 us
    ppermute x7, waiting for transfers between devices, gather_store(): behind = lax.ppermute(behind, 'store', backward)  4.46 us
    ppermute x7, starting transfers between devices, gather_store(): behind = lax.ppermute(behind, 'store', backward)  4.27 us
    sub x2, matrix products, softmax_rounded(): expon = jnp.where(allowed, jnp.exp(masked - peak), jnp.float32(0.0))  3.45 us
    gather x1, local copies, waits for them, and re-layouts, local(): pair_qkv = store_qkv[rows_of(cand_passage)]  2.45 us
  transfers between devices with their start and end apart: 14, of which 7 were waited for; matrix products, arithmetic and copies ran while one was open for 5% of the time, Pallas kernels for 0%

profile of v8, /device:TPU:0, one launch (start us, length us, event | category | flops | bytes accessed | tf_op | source)
XLA Modules:
  0.0 62.7 jit_solution(8375058774425321276)
XLA Ops:
  0.7 0.9 %pad_maximum_fusion = bf16[96,1024]{1,0:T(8,128)(2,1)S(1)} fusion(bf16[64,1024]{1,0:T(8,128)(2,1)} %bitcast.26, bf16[32,1024]{1,0:T(8,128)(2,1)} %bitcast.27), kind=kLoop, calls=%fused_computation.41 | loop fusion | flops 393216 | bytes 393216 | tf_op jit(solution)/shard_map/concatenate | solution.py:178
  1.6 10.1 %all_gather.3 = bf16[96,4096]{1,0:T(8,128)(2,1)S(1)} all-gather(bf16[96,1024]{1,0:T(8,128)(2,1)S(1)} %pad_maximum_fusion), channel_id=1, replica_groups=mesh['store'=8,'tp'=4] {'tp'}, dimensions={1}, use_global_device_ids=true | all-gather | bytes 983040 | tf_op jit(solution)/shard_map/all_gather | solution.py:179
  11.7 0.7 %convert_element_type.71 = f32[4096]{0:T(1024)S(1)} convert(bf16[4096]{0:T(1024)(128)(2,1)} %param.12) | non-fusion elementwise | flops 4096 | bytes 24576 | tf_op jit(solution)/shard_map/convert_element_type | solution.py:12
  12.8 6.9 %fusion.2 = f32[96,4,384]{2,0,1:T(8,128)S(1)} fusion(bf16[4096,4,384]{2,1,0:T(4,128)(2,1)} %param.13, bf16[96,4096]{1,0:T(8,128)(2,1)S(1)} %all_gather.3, f32[4096]{0:T(1024)S(1)} %convert_element_type.71, f32[96]{0:T(128)S(1)} %add_rsqrt_fusion), kind=kOutput, calls=%fused_computation.4 | convolution fusion | flops 1209532416 | bytes 13975936 | tf_op jit(solution)/shard_map/nk,khc->nhc/dot_general | solution.py:181
  20.8 1.6 %collective-permute-start.10 = (bf16[1,32,4,384]{3,1,0,2:T(8,128)(2,1)S(1)}, bf16[1,32,4,384]{3,1,0,2:T(8,128)(2,1)S(1)}, u32[]{:S(2)}, u32[]{:S(2)}) collective-permute-start(bf16[1,32,4,384]{3,1,0,2:T(8,128)(2,1)S(1)} %get-tuple-element.11), channel_id=1, source_target_pairs={{0,8},{8,16},{16,24},{24,28},{28,20},{20,12},{12,4},{4,0},{1,9},{9... | collective-permute-start | bytes 294920 | tf_op jit(solution)/shard_map/ppermute | solution.py:123
  22.8 1.6 %collective-permute-start.4 = (bf16[1,32,4,384]{3,1,0,2:T(8,128)(2,1)S(1)}, bf16[1,32,4,384]{3,1,0,2:T(8,128)(2,1)S(1)}, u32[]{:S(2)}, u32[]{:S(2)}) collective-permute-start(bf16[1,32,4,384]{3,1,0,2:T(8,128)(2,1)S(1)} %get-tuple-element.10), channel_id=1, source_target_pairs={{0,8},{8,16},{16,24},{24,28},{28,20},{20,12},{12,4},{4,0},{1,9},{9... | collective-permute-start | bytes 294920 | tf_op jit(solution)/shard_map/ppermute | solution.py:123
  26.1 0.7 %gather_fusion = s32[24]{0:T(128)S(1)} fusion(s32[8]{0:T(128)S(1)} %copy-done, s32[1024]{0:T(1024)S(1)} %pad_clamp_fusion.1), kind=kCustom, calls=%fused_computation | custom fusion | bytes 288 | tf_op jit(solution)/shard_map/gather | solution.py:148
  27.4 0.7 %compare_select_fusion = s32[24]{0:T(128)S(1)} fusion(s32[24]{0:T(128)S(1)} %gather_fusion, s32[]{:T(128)} %bitcast.6, s32[24]{0:T(128)S(1)} %copy-done.1), kind=kLoop, calls=%fused_computation.60 | loop fusion | flops 960 | bytes 292 | tf_op jit(solution)/shard_map/select_n | solution.py:191
  28.4 1.6 %collective-permute-start.11 = (bf16[1,32,4,384]{3,1,0,2:T(8,128)(2,1)S(1)}, bf16[1,32,4,384]{3,1,0,2:T(8,128)(2,1)S(1)}, u32[]{:S(2)}, u32[]{:S(2)}) collective-permute-start(bf16[1,32,4,384]{3,1,0,2:T(8,128)(2,1)S(1)} %collective-permute-done.10), channel_id=1, source_target_pairs={{0,8},{8,16},{16,24},{24,28},{28,20},{20,12},{12,4},{4,0},{1,9},{9... | collective-permute-start | bytes 294920 | tf_op jit(solution)/shard_map/ppermute | solution.py:123
  30.5 1.5 %collective-permute-start.8 = (bf16[1,32,4,384]{3,1,0,2:T(8,128)(2,1)S(1)}, bf16[1,32,4,384]{3,1,0,2:T(8,128)(2,1)S(1)}, u32[]{:S(2)}, u32[]{:S(2)}) collective-permute-start(bf16[1,32,4,384]{3,1,0,2:T(8,128)(2,1)S(1)} %collective-permute-done.7), channel_id=1, source_target_pairs={{8,0},{16,8},{24,16},{28,24},{20,28},{12,20},{4,12},{0,4},{9,1},{1... | collective-permute-start | bytes 294920 | tf_op jit(solution)/shard_map/ppermute | solution.py:126
  32.5 0.7 %collective-permute-done.11 = bf16[1,32,4,384]{3,1,0,2:T(8,128)(2,1)S(1)} collective-permute-done((bf16[1,32,4,384]{3,1,0,2:T(8,128)(2,1)S(1)}, bf16[1,32,4,384]{3,1,0,2:T(8,128)(2,1)S(1)}, u32[]{:S(2)}, u32[]{:S(2)}) %collective-permute-start.11) | collective-permute-done | bytes 98336 | tf_op jit(solution)/shard_map/ppermute | solution.py:123
  33.2 2.5 %collective-permute-start.12 = (bf16[1,32,4,384]{3,1,0,2:T(8,128)(2,1)S(1)}, bf16[1,32,4,384]{3,1,0,2:T(8,128)(2,1)S(1)}, u32[]{:S(2)}, u32[]{:S(2)}) collective-permute-start(bf16[1,32,4,384]{3,1,0,2:T(8,128)(2,1)S(1)} %collective-permute-done.11), channel_id=1, source_target_pairs={{0,8},{8,16},{16,24},{24,28},{28,20},{20,12},{12,4},{4,0},{1,9},{9... | collective-permute-start | bytes 294920 | tf_op jit(solution)/shard_map/ppermute | solution.py:123
  36.2 1.4 %collective-permute-start.9 = (bf16[1,32,4,384]{3,1,0,2:T(8,128)(2,1)S(1)}, bf16[1,32,4,384]{3,1,0,2:T(8,128)(2,1)S(1)}, u32[]{:S(2)}, u32[]{:S(2)}) collective-permute-start(bf16[1,32,4,384]{3,1,0,2:T(8,128)(2,1)S(1)} %collective-permute-done.8), channel_id=1, source_target_pairs={{8,0},{16,8},{24,16},{28,24},{20,28},{12,20},{4,12},{0,4},{9,1},{1... | collective-permute-start | bytes 294920 | tf_op jit(solution)/shard_map/ppermute | solution.py:126
  38.6 2.1 %collective-permute-start.13 = (bf16[1,32,4,384]{3,1,0,2:T(8,128)(2,1)S(1)}, bf16[1,32,4,384]{3,1,0,2:T(8,128)(2,1)S(1)}, u32[]{:S(2)}, u32[]{:S(2)}) collective-permute-start(bf16[1,32,4,384]{3,1,0,2:T(8,128)(2,1)S(1)} %collective-permute-done.12), channel_id=1, source_target_pairs={{0,8},{8,16},{16,24},{24,28},{28,20},{20,12},{12,4},{4,0},{1,9},{9... | collective-permute-start | bytes 294920 | tf_op jit(solution)/shard_map/ppermute | solution.py:123
  40.9 1.5 %collective-permute-done.9 = bf16[1,32,4,384]{3,1,0,2:T(8,128)(2,1)S(1)} collective-permute-done((bf16[1,32,4,384]{3,1,0,2:T(8,128)(2,1)S(1)}, bf16[1,32,4,384]{3,1,0,2:T(8,128)(2,1)S(1)}, u32[]{:S(2)}, u32[]{:S(2)}) %collective-permute-start.9) | collective-permute-done | bytes 98336 | tf_op jit(solution)/shard_map/ppermute | solution.py:126
  42.4 0.9 %collective-permute-done.13 = bf16[1,32,4,384]{3,1,0,2:T(8,128)(2,1)S(1)} collective-permute-done((bf16[1,32,4,384]{3,1,0,2:T(8,128)(2,1)S(1)}, bf16[1,32,4,384]{3,1,0,2:T(8,128)(2,1)S(1)}, u32[]{:S(2)}, u32[]{:S(2)}) %collective-permute-start.13) | collective-permute-done | bytes 98336 | tf_op jit(solution)/shard_map/ppermute | solution.py:123
  43.3 2.2 %collective-permute-done.3 = bf16[1,32,4,384]{3,1,0,2:T(8,128)(2,1)S(1)} collective-permute-done((bf16[1,32,4,384]{3,1,0,2:T(8,128)(2,1)S(1)}, bf16[1,32,4,384]{3,1,0,2:T(8,128)(2,1)S(1)}, u32[]{:S(2)}, u32[]{:S(2)}) %collective-permute-start.3) | collective-permute-done | bytes 98336 | tf_op jit(solution)/shard_map/ppermute | solution.py:126
  45.6 5.0 %select_select_fusion = bf16[16,32,4,384]{3,1,0,2:T(8,128)(2,1)S(1)} fusion(bf16[1,32,4,384]{3,1,0,2:T(8,128)(2,1)S(1)} %get-tuple-element.11, bf16[1,32,4,384]{3,1,0,2:T(8,128)(2,1)S(1)} %collective-permute-done.10, bf16[1,32,4,384]{3,1,0,2:T(8,128)(2,1)S(1)} %collective-permute-done.11, bf16[1,32,4,384]{3,1,0,2:T(8,128)(2,1)S(1)} %collective-permute-done.12, ...), kind=kLoop, calls=%fused_computation.16 | loop fusion | flops 11796480 | bytes 3145968 | tf_op jit(solution)/shard_map/jit(_where)/select_n | solution.py:161
  50.5 2.4 %gather_fusion.1 = bf16[24,32,4,384]{3,1,2,0:T(8,128)(2,1)} fusion(bf16[16,32,4,384]{3,1,0,2:T(8,128)(2,1)S(1)} %select_select_fusion, s32[1024]{0:T(1024)S(1)} %pad_clamp_fusion), kind=kCustom, calls=%fused_computation.1 | custom fusion | bytes 4718688 | tf_op jit(solution)/shard_map/gather | solution.py:191
  53.0 1.6 %fusion.47 = (bf16[24,32,4,128]{3,1,2,0:T(8,128)(2,1)S(1)}, bf16[24,32,4,128]{3,1,2,0:T(8,128)(2,1)S(1)}) fusion(bf16[24,32,4,384]{3,1,2,0:T(8,128)(2,1)} %gather_fusion.1), kind=kLoop, calls=%fused_computation.106 | loop fusion | bytes 3145728 | tf_op jit(solution)/shard_map/slice | solution.py:74
  54.6 1.5 %convert_reduce_fusion = s32[24]{0:T(128)S(1)} fusion(bf16[24,32,4,384]{3,1,2,0:T(8,128)(2,1)} %gather_fusion.1), kind=kLoop, calls=%fused_computation.37 | loop fusion | flops 2280 | bytes 1632 | tf_op jit(solution)/shard_map/reduce_sum | solution.py:192
  56.3 3.3 %fusion.52 = (f32[24,4,32]{2,1,0:T(4,128)S(1)}, f32[24,4,32,48]{3,2,1,0:T(8,128)}) fusion(bf16[24,32,4,128]{3,1,2,0:T(8,128)(2,1)S(1)} %get-tuple-element.2, bf16[24,16,4,128]{3,1,2,0:T(8,128)(2,1)S(1)} %get-tuple-element.4, bf16[24,32,4,384]{3,1,2,0:T(8,128)(2,1)} %gather_fusion.1, pred[24,32,48]{2,1,0:T(8,128)(4,1)S(1)} %and_or_fusion), kind=kOutput, calls=%fused_computation.111 | convolution fusion | flops 40845360 | bytes 2764800 | tf_op jit(solution)/shard_map/sub | solution.py:41
  59.6 2.1 %fusion.8 = bf16[24,4,4,8,128]{4,3,2,1,0:T(8,128)(2,1)S(1)} fusion(bf16[24,32,4,128]{3,1,2,0:T(8,128)(2,1)S(1)} %get-tuple-element.3, bf16[24,16,4,128]{3,1,2,0:T(8,128)(2,1)S(1)} %get-tuple-element.5, f32[24,4,32,48]{3,2,1,0:T(8,128)} %get-tuple-element.20, f32[24,4,32]{2,1,0:T(4,128)S(1)} %get-tuple-element.19, pred[24,32]{1,0:T(8,128)(4,1)S(1)} %iota_compare_fusion.1), kind=kOutput, calls=%fused_computation.17 | convolution fusion | flops 41189376 | bytes 2568960 | tf_op jit(solution)/shard_map/bhit,bthd->bihd/dot_general | solution.py:89
  61.7 1.0 %copy.44 = bf16[24,4,4,8,128]{4,3,1,2,0:T(8,128)(2,1)} copy(bf16[24,4,4,8,128]{4,3,2,1,0:T(8,128)(2,1)S(1)} %fusion.8) | data formatting | bytes 1572864 | tf_op jit(solution)/shard_map/convert_element_type | solution.py:92
  (69 shorter events, 7.3 us)
Async XLA Ops:
  19.7 0.8 %copy-start.2 = (s32[2]{0:T(128)S(1)}, s32[2]{0:T(128)}, u32[]{:S(2)}) copy-start(s32[2]{0:T(128)} %param.10) | copy-start | bytes 28
  20.3 5.8 %copy-start.1 = (s32[24]{0:T(128)S(1)}, s32[24]{0:T(128)}, u32[]{:S(2)}) copy-start(s32[24]{0:T(128)} %param.11) | copy-start | bytes 292
  20.3 5.8 %copy-start = (s32[8]{0:T(128)S(1)}, s32[8]{0:T(128)}, u32[]{:S(2)}) copy-start(s32[8]{0:T(128)} %constant.108.clone) | copy-start | bytes 100
  20.8 7.6 %collective-permute-start.10 = (bf16[1,32,4,384]{3,1,0,2:T(8,128)(2,1)S(1)}, bf16[1,32,4,384]{3,1,0,2:T(8,128)(2,1)S(1)}, u32[]{:S(2)}, u32[]{:S(2)}) collective-permute-start(bf16[1,32,4,384]{3,1,0,2:T(8,128)(2,1)S(1)} %get-tuple-element.11), channel_id=1, source_target_pairs={{0,8},{8,16},{16,24},{24,28},{28,20},{20,12},{12,4},{4,0},{1,9},{9... | collective-permute-start | bytes 294920 | tf_op jit(solution)/shard_map/ppermute | solution.py:123
  22.4 8.1 %collective-permute-start.7 = (bf16[1,32,4,384]{3,1,0,2:T(8,128)(2,1)S(1)}, bf16[1,32,4,384]{3,1,0,2:T(8,128)(2,1)S(1)}, u32[]{:S(2)}, u32[]{:S(2)}) collective-permute-start(bf16[1,32,4,384]{3,1,0,2:T(8,128)(2,1)S(1)} %get-tuple-element.11), channel_id=1, source_target_pairs={{8,0},{16,8},{24,16},{28,24},{20,28},{12,20},{4,12},{0,4},{9,1},{1... | collective-permute-start | bytes 294920 | tf_op jit(solution)/shard_map/ppermute | solution.py:126
  22.8 9.2 %collective-permute-start.4 = (bf16[1,32,4,384]{3,1,0,2:T(8,128)(2,1)S(1)}, bf16[1,32,4,384]{3,1,0,2:T(8,128)(2,1)S(1)}, u32[]{:S(2)}, u32[]{:S(2)}) collective-permute-start(bf16[1,32,4,384]{3,1,0,2:T(8,128)(2,1)S(1)} %get-tuple-element.10), channel_id=1, source_target_pairs={{0,8},{8,16},{16,24},{24,28},{28,20},{20,12},{12,4},{4,0},{1,9},{9... | collective-permute-start | bytes 294920 | tf_op jit(solution)/shard_map/ppermute | solution.py:123
  24.4 5.6 %collective-permute-start = (bf16[1,32,4,384]{3,1,0,2:T(8,128)(2,1)S(1)}, bf16[1,32,4,384]{3,1,0,2:T(8,128)(2,1)S(1)}, u32[]{:S(2)}, u32[]{:S(2)}) collective-permute-start(bf16[1,32,4,384]{3,1,0,2:T(8,128)(2,1)S(1)} %get-tuple-element.10), channel_id=1, source_target_pairs={{8,0},{16,8},{24,16},{28,24},{20,28},{12,20},{4,12},{0,4},{9,1},{1... | collective-permute-start | bytes 294920 | tf_op jit(solution)/shard_map/ppermute | solution.py:126
  28.4 4.8 %collective-permute-start.11 = (bf16[1,32,4,384]{3,1,0,2:T(8,128)(2,1)S(1)}, bf16[1,32,4,384]{3,1,0,2:T(8,128)(2,1)S(1)}, u32[]{:S(2)}, u32[]{:S(2)}) collective-permute-start(bf16[1,32,4,384]{3,1,0,2:T(8,128)(2,1)S(1)} %collective-permute-done.10), channel_id=1, source_target_pairs={{0,8},{8,16},{16,24},{24,28},{28,20},{20,12},{12,4},{4,0},{1,9},{9... | collective-permute-start | bytes 294920 | tf_op jit(solution)/shard_map/ppermute | solution.py:123
  30.0 5.7 %collective-permute-start.1 = (bf16[1,32,4,384]{3,1,0,2:T(8,128)(2,1)S(1)}, bf16[1,32,4,384]{3,1,0,2:T(8,128)(2,1)S(1)}, u32[]{:S(2)}, u32[]{:S(2)}) collective-permute-start(bf16[1,32,4,384]{3,1,0,2:T(8,128)(2,1)S(1)} %collective-permute-done), channel_id=1, source_target_pairs={{8,0},{16,8},{24,16},{28,24},{20,28},{12,20},{4,12},{0,4},{9,1},{1... | collective-permute-start | bytes 294920 | tf_op jit(solution)/shard_map/ppermute | solution.py:126
  30.5 5.7 %collective-permute-start.8 = (bf16[1,32,4,384]{3,1,0,2:T(8,128)(2,1)S(1)}, bf16[1,32,4,384]{3,1,0,2:T(8,128)(2,1)S(1)}, u32[]{:S(2)}, u32[]{:S(2)}) collective-permute-start(bf16[1,32,4,384]{3,1,0,2:T(8,128)(2,1)S(1)} %collective-permute-done.7), channel_id=1, source_target_pairs={{8,0},{16,8},{24,16},{28,24},{20,28},{12,20},{4,12},{0,4},{9,1},{1... | collective-permute-start | bytes 294920 | tf_op jit(solution)/shard_map/ppermute | solution.py:126
  32.0 5.6 %collective-permute-start.5 = (bf16[1,32,4,384]{3,1,0,2:T(8,128)(2,1)S(1)}, bf16[1,32,4,384]{3,1,0,2:T(8,128)(2,1)S(1)}, u32[]{:S(2)}, u32[]{:S(2)}) collective-permute-start(bf16[1,32,4,384]{3,1,0,2:T(8,128)(2,1)S(1)} %collective-permute-done.4), channel_id=1, source_target_pairs={{0,8},{8,16},{16,24},{24,28},{28,20},{20,12},{12,4},{4,0},{1,9},{9... | collective-permute-start | bytes 294920 | tf_op jit(solution)/shard_map/ppermute | solution.py:123
  33.2 5.4 %collective-permute-start.12 = (bf16[1,32,4,384]{3,1,0,2:T(8,128)(2,1)S(1)}, bf16[1,32,4,384]{3,1,0,2:T(8,128)(2,1)S(1)}, u32[]{:S(2)}, u32[]{:S(2)}) collective-permute-start(bf16[1,32,4,384]{3,1,0,2:T(8,128)(2,1)S(1)} %collective-permute-done.11), channel_id=1, source_target_pairs={{0,8},{8,16},{16,24},{24,28},{28,20},{20,12},{12,4},{4,0},{1,9},{9... | collective-permute-start | bytes 294920 | tf_op jit(solution)/shard_map/ppermute | solution.py:123
  35.7 5.2 %collective-permute-start.2 = (bf16[1,32,4,384]{3,1,0,2:T(8,128)(2,1)S(1)}, bf16[1,32,4,384]{3,1,0,2:T(8,128)(2,1)S(1)}, u32[]{:S(2)}, u32[]{:S(2)}) collective-permute-start(bf16[1,32,4,384]{3,1,0,2:T(8,128)(2,1)S(1)} %collective-permute-done.1), channel_id=1, source_target_pairs={{8,0},{16,8},{24,16},{28,24},{20,28},{12,20},{4,12},{0,4},{9,1},{1... | collective-permute-start | bytes 294920 | tf_op jit(solution)/shard_map/ppermute | solution.py:126
  36.2 6.2 %collective-permute-start.9 = (bf16[1,32,4,384]{3,1,0,2:T(8,128)(2,1)S(1)}, bf16[1,32,4,384]{3,1,0,2:T(8,128)(2,1)S(1)}, u32[]{:S(2)}, u32[]{:S(2)}) collective-permute-start(bf16[1,32,4,384]{3,1,0,2:T(8,128)(2,1)S(1)} %collective-permute-done.8), channel_id=1, source_target_pairs={{8,0},{16,8},{24,16},{28,24},{20,28},{12,20},{4,12},{0,4},{9,1},{1... | collective-permute-start | bytes 294920 | tf_op jit(solution)/shard_map/ppermute | solution.py:126
  37.6 4.8 %collective-permute-start.6 = (bf16[1,32,4,384]{3,1,0,2:T(8,128)(2,1)S(1)}, bf16[1,32,4,384]{3,1,0,2:T(8,128)(2,1)S(1)}, u32[]{:S(2)}, u32[]{:S(2)}) collective-permute-start(bf16[1,32,4,384]{3,1,0,2:T(8,128)(2,1)S(1)} %collective-permute-done.5), channel_id=1, source_target_pairs={{0,8},{8,16},{16,24},{24,28},{28,20},{20,12},{12,4},{4,0},{1,9},{9... | collective-permute-start | bytes 294920 | tf_op jit(solution)/shard_map/ppermute | solution.py:123
  38.6 4.7 %collective-permute-start.13 = (bf16[1,32,4,384]{3,1,0,2:T(8,128)(2,1)S(1)}, bf16[1,32,4,384]{3,1,0,2:T(8,128)(2,1)S(1)}, u32[]{:S(2)}, u32[]{:S(2)}) collective-permute-start(bf16[1,32,4,384]{3,1,0,2:T(8,128)(2,1)S(1)} %collective-permute-done.12), channel_id=1, source_target_pairs={{0,8},{8,16},{16,24},{24,28},{28,20},{20,12},{12,4},{4,0},{1,9},{9... | collective-permute-start | bytes 294920 | tf_op jit(solution)/shard_map/ppermute | solution.py:123
  40.9 4.6 %collective-permute-start.3 = (bf16[1,32,4,384]{3,1,0,2:T(8,128)(2,1)S(1)}, bf16[1,32,4,384]{3,1,0,2:T(8,128)(2,1)S(1)}, u32[]{:S(2)}, u32[]{:S(2)}) collective-permute-start(bf16[1,32,4,384]{3,1,0,2:T(8,128)(2,1)S(1)} %collective-permute-done.2), channel_id=1, source_target_pairs={{8,0},{16,8},{24,16},{28,24},{20,28},{12,20},{4,12},{0,4},{9,1},{1... | collective-permute-start | bytes 294920 | tf_op jit(solution)/shard_map/ppermute | solution.py:126

commit v9 on v8

--- a/solution.py
+++ b/solution.py
@@ -127,19 +127,23 @@
                 parts.append(behind)
         pieces.append(parts)
     ordered = []
+    last = []
     for row in range(count):
         ahead_steps, behind_steps = steps[row]
         parts = pieces[row]
+        final = max(ahead_steps, behind_steps) - 1
         got_ahead, got_behind = [], []
         at = 1
         for k in range(max(ahead_steps, behind_steps)):
             if k < ahead_steps:
-                got_ahead.append(parts[at])
+                got_ahead.append((parts[at], k == final))
                 at += 1
             if k < behind_steps:
-                got_behind.append(parts[at])
+                got_behind.append((parts[at], k == final))
                 at += 1
-        ordered.extend([parts[0]] + got_ahead + got_behind)
+        for part, is_last in [(parts[0], False)] + got_ahead + got_behind:
+            ordered.append(part)
+            last.append(is_last)
     place_of = jnp.asarray(place, dtype=jnp.int32)
     mine = place_of[lax.axis_index("store")]
     ahead_of = jnp.asarray([s[0] for s in steps], dtype=jnp.int32)
@@ -153,13 +157,26 @@
 
     total = sum(part.shape[0] for part in ordered)
     row_at = lax.broadcasted_iota(jnp.int32, (total,) + own.shape[1:], 0)
-    joined = None
+    starts = []
     at = 0
     for part in ordered:
-        size = part.shape[0]
-        widened = jnp.pad(part, ((at, total - at - size),) + ((0, 0),) * (own.ndim - 1))
-        joined = widened if joined is None else jnp.where(row_at >= at, widened, joined)
-        at += size
+        starts.append(at)
+        at += part.shape[0]
+
+    def lay(joined, chosen):
+        for part, at in chosen:
+            size = part.shape[0]
+            widened = jnp.pad(part, ((at, total - at - size),) + ((0, 0),) * (own.ndim - 1))
+            if joined is None:
+                joined = widened
+            else:
+                joined = jnp.where((row_at >= at) & (row_at < at + size), widened, joined)
+        return joined
+
+    early = [(part, at) for part, at, is_last in zip(ordered, starts, last) if not is_last]
+    late = [(part, at) for part, at, is_last in zip(ordered, starts, last) if is_last]
+    joined = lax.optimization_barrier(lay(None, early))
+    joined = lay(joined, late)
     return joined, rows_of
 
 

time: 63 us -> 60.9 us (0.967)
  waiting for transfers between devices: 6.38 us -> 4.89 us
    ppermute x7, waiting for transfers between devices: 4.46 us -> 2.78 us  [gather_store(): behind = lax.ppermute(behind, 'store', backward)]
    ppermute x7, starting transfers between devices: 4.27 us -> 3.15 us  [gather_store(): behind = lax.ppermute(behind, 'store', backward)]
    select_n x1 -> x2, other arithmetic: 4.98 us -> 4.88 us  [lay(): joined = jnp.where((row_at >= at) & (row_at < at + size), widened, joined)]
  transfers between devices with their start and end apart: 14 -> 14, of which waited for: 7 -> 3; matrix products, arithmetic and copies ran while one was open for 5% -> 13% of each run, Pallas kernels for 0% -> 0%
where the time goes in v9:
time: 60.9 us; the launch traced here: 60.5 us
  starting transfers between devices  14.3 us (23%)
  matrix products  12.6 us (21%)
  blocking collectives  10.1 us (17%)
  other arithmetic  9.97 us (16%)
  local copies, waits for them, and re-layouts  7.81 us (13%)
  waiting for transfers between devices  4.89 us (8%)
  between operations  0.96 us (2%)
    ppermute x7, starting transfers between devices, gather_store(): ahead = lax.ppermute(ahead, 'store', forward)  11.1 us
    all_gather x1, blocking collectives, local(): full_rows = lax.all_gather(all_rows, 'tp', axis=1, tiled=True)  10.1 us
    dot_general x1, matrix products, local(): jnp.einsum('nk,khc->nhc', normed, w_qkv, preferred_element_type=jnp.float32)  6.87 us
    select_n x2, other arithmetic, lay(): joined = jnp.where((row_at >= at) & (row_at < at + size), widened, joined)  4.88 us
    sub x2, matrix products, softmax_rounded(): expon = jnp.where(allowed, jnp.exp(masked - peak), jnp.float32(0.0))  3.45 us
    ppermute x7, starting transfers between devices, gather_store(): behind = lax.ppermute(behind, 'store', backward)  3.15 us
    ppermute x7, waiting for transfers between devices, gather_store(): behind = lax.ppermute(behind, 'store', backward)  2.78 us
    gather x1, local copies, waits for them, and re-layouts, local(): pair_qkv = store_qkv[rows_of(cand_passage)]  2.45 us
  transfers between devices with their start and end apart: 14, of which 3 were waited for; matrix products, arithmetic and copies ran while one was open for 13% of the time, Pallas kernels for 0%

profile of v9, /device:TPU:0, one launch (start us, length us, event | category | flops | bytes accessed | tf_op | source)
XLA Modules:
  0.0 60.5 jit_solution(133866737488788176)
XLA Ops:
  0.7 0.9 %pad_maximum_fusion = bf16[96,1024]{1,0:T(8,128)(2,1)S(1)} fusion(bf16[64,1024]{1,0:T(8,128)(2,1)} %bitcast.26, bf16[32,1024]{1,0:T(8,128)(2,1)} %bitcast.27), kind=kLoop, calls=%fused_computation.42 | loop fusion | flops 393216 | bytes 393216 | tf_op jit(solution)/shard_map/concatenate | solution.py:195
  1.6 10.1 %all_gather.3 = bf16[96,4096]{1,0:T(8,128)(2,1)S(1)} all-gather(bf16[96,1024]{1,0:T(8,128)(2,1)S(1)} %pad_maximum_fusion), channel_id=1, replica_groups=mesh['store'=8,'tp'=4] {'tp'}, dimensions={1}, use_global_device_ids=true | all-gather | bytes 983040 | tf_op jit(solution)/shard_map/all_gather | solution.py:196
  11.7 0.7 %convert_element_type.71 = f32[4096]{0:T(1024)S(1)} convert(bf16[4096]{0:T(1024)(128)(2,1)} %param.12) | non-fusion elementwise | flops 4096 | bytes 24576 | tf_op jit(solution)/shard_map/convert_element_type | solution.py:12
  12.8 6.9 %fusion.2 = f32[96,4,384]{2,0,1:T(8,128)S(1)} fusion(bf16[4096,4,384]{2,1,0:T(4,128)(2,1)} %param.13, bf16[96,4096]{1,0:T(8,128)(2,1)S(1)} %all_gather.3, f32[4096]{0:T(1024)S(1)} %convert_element_type.71, f32[96]{0:T(128)S(1)} %add_rsqrt_fusion), kind=kOutput, calls=%fused_computation.4 | convolution fusion | flops 1209532416 | bytes 13975936 | tf_op jit(solution)/shard_map/nk,khc->nhc/dot_general | solution.py:198
  20.8 1.6 %collective-permute-start.4 = (bf16[1,32,4,384]{3,1,0,2:T(8,128)(2,1)S(1)}, bf16[1,32,4,384]{3,1,0,2:T(8,128)(2,1)S(1)}, u32[]{:S(2)}, u32[]{:S(2)}) collective-permute-start(bf16[1,32,4,384]{3,1,0,2:T(8,128)(2,1)S(1)} %get-tuple-element.11), channel_id=1, source_target_pairs={{0,8},{8,16},{16,24},{24,28},{28,20},{20,12},{12,4},{4,0},{1,9},{9... | collective-permute-start | bytes 294920 | tf_op jit(solution)/shard_map/ppermute | solution.py:123
  22.9 1.6 %collective-permute-start.8 = (bf16[1,32,4,384]{3,1,0,2:T(8,128)(2,1)S(1)}, bf16[1,32,4,384]{3,1,0,2:T(8,128)(2,1)S(1)}, u32[]{:S(2)}, u32[]{:S(2)}) collective-permute-start(bf16[1,32,4,384]{3,1,0,2:T(8,128)(2,1)S(1)} %get-tuple-element.10), channel_id=1, source_target_pairs={{0,8},{8,16},{16,24},{24,28},{28,20},{20,12},{12,4},{4,0},{1,9},{9... | collective-permute-start | bytes 294920 | tf_op jit(solution)/shard_map/ppermute | solution.py:123
  25.4 0.6 %copy.45 = bf16[2,4,2,8,128]{4,3,1,2,0:T(8,128)(2,1)} copy(bf16[2,4,2,8,128]{4,3,2,1,0:T(8,128)(2,1)S(1)} %fusion.19) | data formatting | bytes 65536 | tf_op jit(solution)/shard_map/convert_element_type | solution.py:66
  26.1 0.7 %gather_fusion = s32[24]{0:T(128)S(1)} fusion(s32[8]{0:T(128)S(1)} %copy-done, s32[1024]{0:T(1024)S(1)} %pad_clamp_fusion.1), kind=kCustom, calls=%fused_computation | custom fusion | bytes 288 | tf_op jit(solution)/shard_map/gather | solution.py:152
  27.4 0.7 %compare_select_fusion = s32[24]{0:T(128)S(1)} fusion(s32[24]{0:T(128)S(1)} %gather_fusion, s32[]{:T(128)} %bitcast.6, s32[24]{0:T(128)S(1)} %copy-done.1), kind=kLoop, calls=%fused_computation.61 | loop fusion | flops 960 | bytes 292 | tf_op jit(solution)/shard_map/select_n | solution.py:208
  28.4 1.6 %collective-permute-start.5 = (bf16[1,32,4,384]{3,1,0,2:T(8,128)(2,1)S(1)}, bf16[1,32,4,384]{3,1,0,2:T(8,128)(2,1)S(1)}, u32[]{:S(2)}, u32[]{:S(2)}) collective-permute-start(bf16[1,32,4,384]{3,1,0,2:T(8,128)(2,1)S(1)} %collective-permute-done.4), channel_id=1, source_target_pairs={{0,8},{8,16},{16,24},{24,28},{28,20},{20,12},{12,4},{4,0},{1,9},{9... | collective-permute-start | bytes 294920 | tf_op jit(solution)/shard_map/ppermute | solution.py:123
  30.5 1.6 %collective-permute-start.9 = (bf16[1,32,4,384]{3,1,0,2:T(8,128)(2,1)S(1)}, bf16[1,32,4,384]{3,1,0,2:T(8,128)(2,1)S(1)}, u32[]{:S(2)}, u32[]{:S(2)}) collective-permute-start(bf16[1,32,4,384]{3,1,0,2:T(8,128)(2,1)S(1)} %collective-permute-done.8), channel_id=1, source_target_pairs={{0,8},{8,16},{16,24},{24,28},{28,20},{20,12},{12,4},{4,0},{1,9},{9... | collective-permute-start | bytes 294920 | tf_op jit(solution)/shard_map/ppermute | solution.py:123
  32.5 1.4 %collective-permute-done.5 = bf16[1,32,4,384]{3,1,0,2:T(8,128)(2,1)S(1)} collective-permute-done((bf16[1,32,4,384]{3,1,0,2:T(8,128)(2,1)S(1)}, bf16[1,32,4,384]{3,1,0,2:T(8,128)(2,1)S(1)}, u32[]{:S(2)}, u32[]{:S(2)}) %collective-permute-start.5) | collective-permute-done | bytes 98336 | tf_op jit(solution)/shard_map/ppermute | solution.py:123
  34.0 1.6 %collective-permute-start.6 = (bf16[1,32,4,384]{3,1,0,2:T(8,128)(2,1)S(1)}, bf16[1,32,4,384]{3,1,0,2:T(8,128)(2,1)S(1)}, u32[]{:S(2)}, u32[]{:S(2)}) collective-permute-start(bf16[1,32,4,384]{3,1,0,2:T(8,128)(2,1)S(1)} %collective-permute-done.5), channel_id=1, source_target_pairs={{0,8},{8,16},{16,24},{24,28},{28,20},{20,12},{12,4},{4,0},{1,9},{9... | collective-permute-start | bytes 294920 | tf_op jit(solution)/shard_map/ppermute | solution.py:123
  36.0 1.6 %collective-permute-start.10 = (bf16[1,32,4,384]{3,1,0,2:T(8,128)(2,1)S(1)}, bf16[1,32,4,384]{3,1,0,2:T(8,128)(2,1)S(1)}, u32[]{:S(2)}, u32[]{:S(2)}) collective-permute-start(bf16[1,32,4,384]{3,1,0,2:T(8,128)(2,1)S(1)} %collective-permute-done.9), channel_id=1, source_target_pairs={{0,8},{8,16},{16,24},{24,28},{28,20},{20,12},{12,4},{4,0},{1,9},{9... | collective-permute-start | bytes 294920 | tf_op jit(solution)/shard_map/ppermute | solution.py:123
  38.1 0.6 %collective-permute-done.6 = bf16[1,32,4,384]{3,1,0,2:T(8,128)(2,1)S(1)} collective-permute-done((bf16[1,32,4,384]{3,1,0,2:T(8,128)(2,1)S(1)}, bf16[1,32,4,384]{3,1,0,2:T(8,128)(2,1)S(1)}, u32[]{:S(2)}, u32[]{:S(2)}) %collective-permute-start.6) | collective-permute-done | bytes 98336 | tf_op jit(solution)/shard_map/ppermute | solution.py:123
  38.7 1.6 %collective-permute-start.7 = (bf16[1,32,4,384]{3,1,0,2:T(8,128)(2,1)S(1)}, bf16[1,32,4,384]{3,1,0,2:T(8,128)(2,1)S(1)}, u32[]{:S(2)}, u32[]{:S(2)}) collective-permute-start(bf16[1,32,4,384]{3,1,0,2:T(8,128)(2,1)S(1)} %collective-permute-done.6), channel_id=1, source_target_pairs={{0,8},{8,16},{16,24},{24,28},{28,20},{20,12},{12,4},{4,0},{1,9},{9... | collective-permute-start | bytes 294920 | tf_op jit(solution)/shard_map/ppermute | solution.py:123
  40.3 2.8 %collective-permute-done.2 = bf16[1,32,4,384]{3,1,0,2:T(8,128)(2,1)S(1)} collective-permute-done((bf16[1,32,4,384]{3,1,0,2:T(8,128)(2,1)S(1)}, bf16[1,32,4,384]{3,1,0,2:T(8,128)(2,1)S(1)}, u32[]{:S(2)}, u32[]{:S(2)}) %collective-permute-start.2) | collective-permute-done | bytes 98336 | tf_op jit(solution)/shard_map/ppermute | solution.py:126
  43.5 4.6 %select_select_fusion.1 = bf16[16,32,4,384]{3,1,0,2:T(8,128)(2,1)S(1)} fusion(bf16[1,32,4,384]{3,1,0,2:T(8,128)(2,1)S(1)} %get-tuple-element.11, bf16[1,32,4,384]{3,1,0,2:T(8,128)(2,1)S(1)} %collective-permute-done.4, bf16[1,32,4,384]{3,1,0,2:T(8,128)(2,1)S(1)} %collective-permute-done.5, bf16[1,32,4,384]{3,1,0,2:T(8,128)(2,1)S(1)} %collective-permute-done.6, ...), kind=kLoop, calls=%fused_computation.17 | loop fusion | flops 10223616 | bytes 2949328 | tf_op jit(solution)/shard_map/jit(_where)/select_n | solution.py:173
  48.4 2.5 %gather_fusion.1 = bf16[24,32,4,384]{3,1,2,0:T(8,128)(2,1)} fusion(bf16[16,32,4,384]{3,1,0,2:T(8,128)(2,1)S(1)} %select_select_fusion, s32[1024]{0:T(1024)S(1)} %pad_clamp_fusion), kind=kCustom, calls=%fused_computation.1 | custom fusion | bytes 4718688 | tf_op jit(solution)/shard_map/gather | solution.py:208
  50.9 1.6 %fusion.47 = (bf16[24,32,4,128]{3,1,2,0:T(8,128)(2,1)S(1)}, bf16[24,32,4,128]{3,1,2,0:T(8,128)(2,1)S(1)}) fusion(bf16[24,32,4,384]{3,1,2,0:T(8,128)(2,1)} %gather_fusion.1), kind=kLoop, calls=%fused_computation.107 | loop fusion | bytes 3145728 | tf_op jit(solution)/shard_map/slice | solution.py:74
  52.5 1.5 %convert_reduce_fusion = s32[24]{0:T(128)S(1)} fusion(bf16[24,32,4,384]{3,1,2,0:T(8,128)(2,1)} %gather_fusion.1), kind=kLoop, calls=%fused_computation.38 | loop fusion | flops 2280 | bytes 1632 | tf_op jit(solution)/shard_map/reduce_sum | solution.py:209
  54.2 3.3 %fusion.52 = (f32[24,4,32]{2,1,0:T(4,128)S(1)}, f32[24,4,32,48]{3,2,1,0:T(8,128)}) fusion(bf16[24,32,4,128]{3,1,2,0:T(8,128)(2,1)S(1)} %get-tuple-element.2, bf16[24,16,4,128]{3,1,2,0:T(8,128)(2,1)S(1)} %get-tuple-element.4, bf16[24,32,4,384]{3,1,2,0:T(8,128)(2,1)} %gather_fusion.1, pred[24,32,48]{2,1,0:T(8,128)(4,1)S(1)} %and_or_fusion), kind=kOutput, calls=%fused_computation.112 | convolution fusion | flops 40845360 | bytes 2764800 | tf_op jit(solution)/shard_map/sub | solution.py:41
  57.5 2.0 %fusion.8 = bf16[24,4,4,8,128]{4,3,2,1,0:T(8,128)(2,1)S(1)} fusion(bf16[24,32,4,128]{3,1,2,0:T(8,128)(2,1)S(1)} %get-tuple-element.3, bf16[24,16,4,128]{3,1,2,0:T(8,128)(2,1)S(1)} %get-tuple-element.5, f32[24,4,32,48]{3,2,1,0:T(8,128)} %get-tuple-element.20, f32[24,4,32]{2,1,0:T(4,128)S(1)} %get-tuple-element.19, pred[24,32]{1,0:T(8,128)(4,1)S(1)} %iota_compare_fusion.1), kind=kOutput, calls=%fused_computation.18 | convolution fusion | flops 41189376 | bytes 2568960 | tf_op jit(solution)/shard_map/bhit,bthd->bihd/dot_general | solution.py:89
  59.5 1.0 %copy.44 = bf16[24,4,4,8,128]{4,3,1,2,0:T(8,128)(2,1)} copy(bf16[24,4,4,8,128]{4,3,2,1,0:T(8,128)(2,1)S(1)} %fusion.8) | data formatting | bytes 1572864 | tf_op jit(solution)/shard_map/convert_element_type | solution.py:92
  (70 shorter events, 6.6 us)
Async XLA Ops:
  19.7 0.8 %copy-start.2 = (s32[2]{0:T(128)S(1)}, s32[2]{0:T(128)}, u32[]{:S(2)}) copy-start(s32[2]{0:T(128)} %param.10) | copy-start | bytes 28
  20.3 5.8 %copy-start.1 = (s32[24]{0:T(128)S(1)}, s32[24]{0:T(128)}, u32[]{:S(2)}) copy-start(s32[24]{0:T(128)} %param.11) | copy-start | bytes 292
  20.3 5.8 %copy-start = (s32[8]{0:T(128)S(1)}, s32[8]{0:T(128)}, u32[]{:S(2)}) copy-start(s32[8]{0:T(128)} %constant.109.clone) | copy-start | bytes 100
  20.8 7.6 %collective-permute-start.4 = (bf16[1,32,4,384]{3,1,0,2:T(8,128)(2,1)S(1)}, bf16[1,32,4,384]{3,1,0,2:T(8,128)(2,1)S(1)}, u32[]{:S(2)}, u32[]{:S(2)}) collective-permute-start(bf16[1,32,4,384]{3,1,0,2:T(8,128)(2,1)S(1)} %get-tuple-element.11), channel_id=1, source_target_pairs={{0,8},{8,16},{16,24},{24,28},{28,20},{20,12},{12,4},{4,0},{1,9},{9... | collective-permute-start | bytes 294920 | tf_op jit(solution)/shard_map/ppermute | solution.py:123
  22.4 7.6 %collective-permute-start.11 = (bf16[1,32,4,384]{3,1,0,2:T(8,128)(2,1)S(1)}, bf16[1,32,4,384]{3,1,0,2:T(8,128)(2,1)S(1)}, u32[]{:S(2)}, u32[]{:S(2)}) collective-permute-start(bf16[1,32,4,384]{3,1,0,2:T(8,128)(2,1)S(1)} %get-tuple-element.11), channel_id=1, source_target_pairs={{8,0},{16,8},{24,16},{28,24},{20,28},{12,20},{4,12},{0,4},{9,1},{1... | collective-permute-start | bytes 294920 | tf_op jit(solution)/shard_map/ppermute | solution.py:126
  22.9 7.6 %collective-permute-start.8 = (bf16[1,32,4,384]{3,1,0,2:T(8,128)(2,1)S(1)}, bf16[1,32,4,384]{3,1,0,2:T(8,128)(2,1)S(1)}, u32[]{:S(2)}, u32[]{:S(2)}) collective-permute-start(bf16[1,32,4,384]{3,1,0,2:T(8,128)(2,1)S(1)} %get-tuple-element.10), channel_id=1, source_target_pairs={{0,8},{8,16},{16,24},{24,28},{28,20},{20,12},{12,4},{4,0},{1,9},{9... | collective-permute-start | bytes 294920 | tf_op jit(solution)/shard_map/ppermute | solution.py:123
  24.4 7.7 %collective-permute-start = (bf16[1,32,4,384]{3,1,0,2:T(8,128)(2,1)S(1)}, bf16[1,32,4,384]{3,1,0,2:T(8,128)(2,1)S(1)}, u32[]{:S(2)}, u32[]{:S(2)}) collective-permute-start(bf16[1,32,4,384]{3,1,0,2:T(8,128)(2,1)S(1)} %get-tuple-element.10), channel_id=1, source_target_pairs={{8,0},{16,8},{24,16},{28,24},{20,28},{12,20},{4,12},{0,4},{9,1},{1... | collective-permute-start | bytes 294920 | tf_op jit(solution)/shard_map/ppermute | solution.py:126
  28.4 5.6 %collective-permute-start.5 = (bf16[1,32,4,384]{3,1,0,2:T(8,128)(2,1)S(1)}, bf16[1,32,4,384]{3,1,0,2:T(8,128)(2,1)S(1)}, u32[]{:S(2)}, u32[]{:S(2)}) collective-permute-start(bf16[1,32,4,384]{3,1,0,2:T(8,128)(2,1)S(1)} %collective-permute-done.4), channel_id=1, source_target_pairs={{0,8},{8,16},{16,24},{24,28},{28,20},{20,12},{12,4},{4,0},{1,9},{9... | collective-permute-start | bytes 294920 | tf_op jit(solution)/shard_map/ppermute | solution.py:123
  30.0 5.5 %collective-permute-start.12 = (bf16[1,32,4,384]{3,1,0,2:T(8,128)(2,1)S(1)}, bf16[1,32,4,384]{3,1,0,2:T(8,128)(2,1)S(1)}, u32[]{:S(2)}, u32[]{:S(2)}) collective-permute-start(bf16[1,32,4,384]{3,1,0,2:T(8,128)(2,1)S(1)} %collective-permute-done.11), channel_id=1, source_target_pairs={{8,0},{16,8},{24,16},{28,24},{20,28},{12,20},{4,12},{0,4},{9,1},{1... | collective-permute-start | bytes 294920 | tf_op jit(solution)/shard_map/ppermute | solution.py:126
  30.5 5.5 %collective-permute-start.9 = (bf16[1,32,4,384]{3,1,0,2:T(8,128)(2,1)S(1)}, bf16[1,32,4,384]{3,1,0,2:T(8,128)(2,1)S(1)}, u32[]{:S(2)}, u32[]{:S(2)}) collective-permute-start(bf16[1,32,4,384]{3,1,0,2:T(8,128)(2,1)S(1)} %collective-permute-done.8), channel_id=1, source_target_pairs={{0,8},{8,16},{16,24},{24,28},{28,20},{20,12},{12,4},{4,0},{1,9},{9... | collective-permute-start | bytes 294920 | tf_op jit(solution)/shard_map/ppermute | solution.py:123
  32.1 5.5 %collective-permute-start.1 = (bf16[1,32,4,384]{3,1,0,2:T(8,128)(2,1)S(1)}, bf16[1,32,4,384]{3,1,0,2:T(8,128)(2,1)S(1)}, u32[]{:S(2)}, u32[]{:S(2)}) collective-permute-start(bf16[1,32,4,384]{3,1,0,2:T(8,128)(2,1)S(1)} %collective-permute-done), channel_id=1, source_target_pairs={{8,0},{16,8},{24,16},{28,24},{20,28},{12,20},{4,12},{0,4},{9,1},{1... | collective-permute-start | bytes 294920 | tf_op jit(solution)/shard_map/ppermute | solution.py:126
  34.0 4.7 %collective-permute-start.6 = (bf16[1,32,4,384]{3,1,0,2:T(8,128)(2,1)S(1)}, bf16[1,32,4,384]{3,1,0,2:T(8,128)(2,1)S(1)}, u32[]{:S(2)}, u32[]{:S(2)}) collective-permute-start(bf16[1,32,4,384]{3,1,0,2:T(8,128)(2,1)S(1)} %collective-permute-done.5), channel_id=1, source_target_pairs={{0,8},{8,16},{16,24},{24,28},{28,20},{20,12},{12,4},{4,0},{1,9},{9... | collective-permute-start | bytes 294920 | tf_op jit(solution)/shard_map/ppermute | solution.py:123
  35.6 7.9 %collective-permute-start.13 = (bf16[1,32,4,384]{3,1,0,2:T(8,128)(2,1)S(1)}, bf16[1,32,4,384]{3,1,0,2:T(8,128)(2,1)S(1)}, u32[]{:S(2)}, u32[]{:S(2)}) collective-permute-start(bf16[1,32,4,384]{3,1,0,2:T(8,128)(2,1)S(1)} %collective-permute-done.12), channel_id=1, source_target_pairs={{8,0},{16,8},{24,16},{28,24},{20,28},{12,20},{4,12},{0,4},{9,1},{1... | collective-permute-start | bytes 294920 | tf_op jit(solution)/shard_map/ppermute | solution.py:126
  36.0 7.5 %collective-permute-start.10 = (bf16[1,32,4,384]{3,1,0,2:T(8,128)(2,1)S(1)}, bf16[1,32,4,384]{3,1,0,2:T(8,128)(2,1)S(1)}, u32[]{:S(2)}, u32[]{:S(2)}) collective-permute-start(bf16[1,32,4,384]{3,1,0,2:T(8,128)(2,1)S(1)} %collective-permute-done.9), channel_id=1, source_target_pairs={{0,8},{8,16},{16,24},{24,28},{28,20},{20,12},{12,4},{4,0},{1,9},{9... | collective-permute-start | bytes 294920 | tf_op jit(solution)/shard_map/ppermute | solution.py:123
  37.6 5.5 %collective-permute-start.2 = (bf16[1,32,4,384]{3,1,0,2:T(8,128)(2,1)S(1)}, bf16[1,32,4,384]{3,1,0,2:T(8,128)(2,1)S(1)}, u32[]{:S(2)}, u32[]{:S(2)}) collective-permute-start(bf16[1,32,4,384]{3,1,0,2:T(8,128)(2,1)S(1)} %collective-permute-done.1), channel_id=1, source_target_pairs={{8,0},{16,8},{24,16},{28,24},{20,28},{12,20},{4,12},{0,4},{9,1},{1... | collective-permute-start | bytes 294920 | tf_op jit(solution)/shard_map/ppermute | solution.py:126
  38.7 9.4 %collective-permute-start.7 = (bf16[1,32,4,384]{3,1,0,2:T(8,128)(2,1)S(1)}, bf16[1,32,4,384]{3,1,0,2:T(8,128)(2,1)S(1)}, u32[]{:S(2)}, u32[]{:S(2)}) collective-permute-start(bf16[1,32,4,384]{3,1,0,2:T(8,128)(2,1)S(1)} %collective-permute-done.6), channel_id=1, source_target_pairs={{0,8},{8,16},{16,24},{24,28},{28,20},{20,12},{12,4},{4,0},{1,9},{9... | collective-permute-start | bytes 294920 | tf_op jit(solution)/shard_map/ppermute | solution.py:123
  43.0 5.0 %collective-permute-start.3 = (bf16[1,32,4,384]{3,1,0,2:T(8,128)(2,1)S(1)}, bf16[1,32,4,384]{3,1,0,2:T(8,128)(2,1)S(1)}, u32[]{:S(2)}, u32[]{:S(2)}) collective-permute-start(bf16[1,32,4,384]{3,1,0,2:T(8,128)(2,1)S(1)} %collective-permute-done.2), channel_id=1, source_target_pairs={{8,0},{16,8},{24,16},{28,24},{20,28},{12,20},{4,12},{0,4},{9,1},{1... | collective-permute-start | bytes 294920 | tf_op jit(solution)/shard_map/ppermute | solution.py:126

commit v10 on v9

--- a/solution.py
+++ b/solution.py
@@ -127,23 +127,22 @@
                 parts.append(behind)
         pieces.append(parts)
     ordered = []
-    last = []
+    arrival = []
     for row in range(count):
         ahead_steps, behind_steps = steps[row]
         parts = pieces[row]
-        final = max(ahead_steps, behind_steps) - 1
         got_ahead, got_behind = [], []
         at = 1
         for k in range(max(ahead_steps, behind_steps)):
             if k < ahead_steps:
-                got_ahead.append((parts[at], k == final))
+                got_ahead.append((parts[at], k + 1))
                 at += 1
             if k < behind_steps:
-                got_behind.append((parts[at], k == final))
+                got_behind.append((parts[at], k + 1))
                 at += 1
-        for part, is_last in [(parts[0], False)] + got_ahead + got_behind:
+        for part, step in [(parts[0], 0)] + got_ahead + got_behind:
             ordered.append(part)
-            last.append(is_last)
+            arrival.append(step)
     place_of = jnp.asarray(place, dtype=jnp.int32)
     mine = place_of[lax.axis_index("store")]
     ahead_of = jnp.asarray([s[0] for s in steps], dtype=jnp.int32)
@@ -173,10 +172,12 @@
                 joined = jnp.where((row_at >= at) & (row_at < at + size), widened, joined)
         return joined
 
-    early = [(part, at) for part, at, is_last in zip(ordered, starts, last) if not is_last]
-    late = [(part, at) for part, at, is_last in zip(ordered, starts, last) if is_last]
-    joined = lax.optimization_barrier(lay(None, early))
-    joined = lay(joined, late)
+    last_step = max(arrival)
+    first_join = max(last_step - 2, 0)
+    joined = lay(None, [(p, a) for p, a, s in zip(ordered, starts, arrival) if s <= first_join])
+    for step in range(first_join + 1, last_step + 1):
+        joined = lax.optimization_barrier(joined)
+        joined = lay(joined, [(p, a) for p, a, s in zip(ordered, starts, arrival) if s == step])
     return joined, rows_of
 
 

time: 60.9 us -> 60.1 us (0.987)
  other arithmetic: 9.97 us -> 8.88 us
    ppermute x7, waiting for transfers between devices: 2.11 us -> 3.48 us  [gather_store(): ahead = lax.ppermute(ahead, 'store', forward)]
    ppermute x7, waiting for transfers between devices: 2.78 us -> 1.6 us  [gather_store(): behind = lax.ppermute(behind, 'store', backward)]
    select_n x2 -> x3, other arithmetic: 4.88 us -> 3.8 us  [lay(): joined = jnp.where((row_at >= at) & (row_at < at + size), widened, joined)]
  transfers between devices with their start and end apart: 14 -> 14, of which waited for: 3 -> 3; matrix products, arithmetic and copies ran while one was open for 13% -> 11% of each run, Pallas kernels for 0% -> 0%
where the time goes in v10:
time: 60.1 us; the launch traced here: 59.7 us
  starting transfers between devices  14.3 us (24%)
  matrix products  12.6 us (21%)
  blocking collectives  10.1 us (17%)
  other arithmetic  8.88 us (15%)
  local copies, waits for them, and re-layouts  7.81 us (13%)
  waiting for transfers between devices  5.08 us (8%)
  between operations  0.96 us (2%)
    ppermute x7, starting transfers between devices, gather_store(): ahead = lax.ppermute(ahead, 'store', forward)  11.2 us
    all_gather x1, blocking collectives, local(): full_rows = lax.all_gather(all_rows, 'tp', axis=1, tiled=True)  10.1 us
    dot_general x1, matrix products, local(): jnp.einsum('nk,khc->nhc', normed, w_qkv, preferred_element_type=jnp.float32)  6.87 us
    select_n x3, other arithmetic, lay(): joined = jnp.where((row_at >= at) & (row_at < at + size), widened, joined)  3.8 us
    ppermute x7, waiting for transfers between devices, gather_store(): ahead = lax.ppermute(ahead, 'store', forward)  3.48 us
    sub x2, matrix products, softmax_rounded(): expon = jnp.where(allowed, jnp.exp(masked - peak), jnp.float32(0.0))  3.45 us
    ppermute x7, starting transfers between devices, gather_store(): behind = lax.ppermute(behind, 'store', backward)  3.14 us
    gather x1, local copies, waits for them, and re-layouts, local(): pair_qkv = store_qkv[rows_of(cand_passage)]  2.45 us
  transfers between devices with their start and end apart: 14, of which 3 were waited for; matrix products, arithmetic and copies ran while one was open for 11% of the time, Pallas kernels for 0%

profile of v10, /device:TPU:0, one launch (start us, length us, event | category | flops | bytes accessed | tf_op | source)
XLA Modules:
  0.0 59.7 jit_solution(9115826022823145749)
XLA Ops:
  0.7 0.9 %pad_maximum_fusion = bf16[96,1024]{1,0:T(8,128)(2,1)S(1)} fusion(bf16[64,1024]{1,0:T(8,128)(2,1)} %bitcast.26, bf16[32,1024]{1,0:T(8,128)(2,1)} %bitcast.27), kind=kLoop, calls=%fused_computation.43 | loop fusion | flops 393216 | bytes 393216 | tf_op jit(solution)/shard_map/concatenate | solution.py:196
  1.6 10.1 %all_gather.3 = bf16[96,4096]{1,0:T(8,128)(2,1)S(1)} all-gather(bf16[96,1024]{1,0:T(8,128)(2,1)S(1)} %pad_maximum_fusion), channel_id=1, replica_groups=mesh['store'=8,'tp'=4] {'tp'}, dimensions={1}, use_global_device_ids=true | all-gather | bytes 983040 | tf_op jit(solution)/shard_map/all_gather | solution.py:197
  11.7 0.7 %convert_element_type.71 = f32[4096]{0:T(1024)S(1)} convert(bf16[4096]{0:T(1024)(128)(2,1)} %param.12) | non-fusion elementwise | flops 4096 | bytes 24576 | tf_op jit(solution)/shard_map/convert_element_type | solution.py:12
  12.8 6.9 %fusion.2 = f32[96,4,384]{2,0,1:T(8,128)S(1)} fusion(bf16[4096,4,384]{2,1,0:T(4,128)(2,1)} %param.13, bf16[96,4096]{1,0:T(8,128)(2,1)S(1)} %all_gather.3, f32[4096]{0:T(1024)S(1)} %convert_element_type.71, f32[96]{0:T(128)S(1)} %add_rsqrt_fusion), kind=kOutput, calls=%fused_computation.4 | convolution fusion | flops 1209532416 | bytes 13975936 | tf_op jit(solution)/shard_map/nk,khc->nhc/dot_general | solution.py:199
  20.8 1.6 %collective-permute-start.4 = (bf16[1,32,4,384]{3,1,0,2:T(8,128)(2,1)S(1)}, bf16[1,32,4,384]{3,1,0,2:T(8,128)(2,1)S(1)}, u32[]{:S(2)}, u32[]{:S(2)}) collective-permute-start(bf16[1,32,4,384]{3,1,0,2:T(8,128)(2,1)S(1)} %get-tuple-element.11), channel_id=1, source_target_pairs={{0,8},{8,16},{16,24},{24,28},{28,20},{20,12},{12,4},{4,0},{1,9},{9... | collective-permute-start | bytes 294920 | tf_op jit(solution)/shard_map/ppermute | solution.py:123
  22.8 1.6 %collective-permute-start.8 = (bf16[1,32,4,384]{3,1,0,2:T(8,128)(2,1)S(1)}, bf16[1,32,4,384]{3,1,0,2:T(8,128)(2,1)S(1)}, u32[]{:S(2)}, u32[]{:S(2)}) collective-permute-start(bf16[1,32,4,384]{3,1,0,2:T(8,128)(2,1)S(1)} %get-tuple-element.10), channel_id=1, source_target_pairs={{0,8},{8,16},{16,24},{24,28},{28,20},{20,12},{12,4},{4,0},{1,9},{9... | collective-permute-start | bytes 294920 | tf_op jit(solution)/shard_map/ppermute | solution.py:123
  25.4 0.6 %copy.45 = bf16[2,4,2,8,128]{4,3,1,2,0:T(8,128)(2,1)} copy(bf16[2,4,2,8,128]{4,3,2,1,0:T(8,128)(2,1)S(1)} %fusion.19) | data formatting | bytes 65536 | tf_op jit(solution)/shard_map/convert_element_type | solution.py:66
  26.1 0.7 %gather_fusion = s32[24]{0:T(128)S(1)} fusion(s32[8]{0:T(128)S(1)} %copy-done, s32[1024]{0:T(1024)S(1)} %pad_clamp_fusion.1), kind=kCustom, calls=%fused_computation | custom fusion | bytes 288 | tf_op jit(solution)/shard_map/gather | solution.py:151
  27.4 0.7 %compare_select_fusion = s32[24]{0:T(128)S(1)} fusion(s32[24]{0:T(128)S(1)} %gather_fusion, s32[]{:T(128)} %bitcast.6, s32[24]{0:T(128)S(1)} %copy-done.1), kind=kLoop, calls=%fused_computation.62 | loop fusion | flops 960 | bytes 292 | tf_op jit(solution)/shard_map/select_n | solution.py:209
  28.4 1.6 %collective-permute-start.5 = (bf16[1,32,4,384]{3,1,0,2:T(8,128)(2,1)S(1)}, bf16[1,32,4,384]{3,1,0,2:T(8,128)(2,1)S(1)}, u32[]{:S(2)}, u32[]{:S(2)}) collective-permute-start(bf16[1,32,4,384]{3,1,0,2:T(8,128)(2,1)S(1)} %collective-permute-done.4), channel_id=1, source_target_pairs={{0,8},{8,16},{16,24},{24,28},{28,20},{20,12},{12,4},{4,0},{1,9},{9... | collective-permute-start | bytes 294920 | tf_op jit(solution)/shard_map/ppermute | solution.py:123
  30.5 1.6 %collective-permute-start.9 = (bf16[1,32,4,384]{3,1,0,2:T(8,128)(2,1)S(1)}, bf16[1,32,4,384]{3,1,0,2:T(8,128)(2,1)S(1)}, u32[]{:S(2)}, u32[]{:S(2)}) collective-permute-start(bf16[1,32,4,384]{3,1,0,2:T(8,128)(2,1)S(1)} %collective-permute-done.8), channel_id=1, source_target_pairs={{0,8},{8,16},{16,24},{24,28},{28,20},{20,12},{12,4},{4,0},{1,9},{9... | collective-permute-start | bytes 294920 | tf_op jit(solution)/shard_map/ppermute | solution.py:123
  32.5 1.4 %collective-permute-done.5 = bf16[1,32,4,384]{3,1,0,2:T(8,128)(2,1)S(1)} collective-permute-done((bf16[1,32,4,384]{3,1,0,2:T(8,128)(2,1)S(1)}, bf16[1,32,4,384]{3,1,0,2:T(8,128)(2,1)S(1)}, u32[]{:S(2)}, u32[]{:S(2)}) %collective-permute-start.5) | collective-permute-done | bytes 98336 | tf_op jit(solution)/shard_map/ppermute | solution.py:123
  34.0 1.6 %collective-permute-start.6 = (bf16[1,32,4,384]{3,1,0,2:T(8,128)(2,1)S(1)}, bf16[1,32,4,384]{3,1,0,2:T(8,128)(2,1)S(1)}, u32[]{:S(2)}, u32[]{:S(2)}) collective-permute-start(bf16[1,32,4,384]{3,1,0,2:T(8,128)(2,1)S(1)} %collective-permute-done.5), channel_id=1, source_target_pairs={{0,8},{8,16},{16,24},{24,28},{28,20},{20,12},{12,4},{4,0},{1,9},{9... | collective-permute-start | bytes 294920 | tf_op jit(solution)/shard_map/ppermute | solution.py:123
  36.0 1.6 %collective-permute-start.10 = (bf16[1,32,4,384]{3,1,0,2:T(8,128)(2,1)S(1)}, bf16[1,32,4,384]{3,1,0,2:T(8,128)(2,1)S(1)}, u32[]{:S(2)}, u32[]{:S(2)}) collective-permute-start(bf16[1,32,4,384]{3,1,0,2:T(8,128)(2,1)S(1)} %collective-permute-done.9), channel_id=1, source_target_pairs={{0,8},{8,16},{16,24},{24,28},{28,20},{20,12},{12,4},{4,0},{1,9},{9... | collective-permute-start | bytes 294920 | tf_op jit(solution)/shard_map/ppermute | solution.py:123
  38.1 2.9 %select_select_fusion.2 = bf16[16,32,4,384]{3,1,0,2:T(8,128)(2,1)S(1)} fusion(bf16[1,32,4,384]{3,1,0,2:T(8,128)(2,1)S(1)} %get-tuple-element.11, bf16[1,32,4,384]{3,1,0,2:T(8,128)(2,1)S(1)} %collective-permute-done.4, bf16[1,32,4,384]{3,1,0,2:T(8,128)(2,1)S(1)} %collective-permute-done.5, bf16[1,32,4,384]{3,1,0,2:T(8,128)(2,1)S(1)} %collective-permute-done.11, ...), kind=kLoop, calls=%fused_computation.18 | loop fusion | flops 7077888 | bytes 2556048 | tf_op jit(solution)/shard_map/jit(_where)/select_n | solution.py:172
  41.0 1.6 %collective-permute-start.7 = (bf16[1,32,4,384]{3,1,0,2:T(8,128)(2,1)S(1)}, bf16[1,32,4,384]{3,1,0,2:T(8,128)(2,1)S(1)}, u32[]{:S(2)}, u32[]{:S(2)}) collective-permute-start(bf16[1,32,4,384]{3,1,0,2:T(8,128)(2,1)S(1)} %collective-permute-done.6), channel_id=1, source_target_pairs={{0,8},{8,16},{16,24},{24,28},{28,20},{20,12},{12,4},{4,0},{1,9},{9... | collective-permute-start | bytes 294920 | tf_op jit(solution)/shard_map/ppermute | solution.py:123
  43.6 2.0 %collective-permute-done.7 = bf16[1,32,4,384]{3,1,0,2:T(8,128)(2,1)S(1)} collective-permute-done((bf16[1,32,4,384]{3,1,0,2:T(8,128)(2,1)S(1)}, bf16[1,32,4,384]{3,1,0,2:T(8,128)(2,1)S(1)}, u32[]{:S(2)}, u32[]{:S(2)}) %collective-permute-start.7) | collective-permute-done | bytes 98336 | tf_op jit(solution)/shard_map/ppermute | solution.py:123
  45.7 1.6 %collective-permute-done.3 = bf16[1,32,4,384]{3,1,0,2:T(8,128)(2,1)S(1)} collective-permute-done((bf16[1,32,4,384]{3,1,0,2:T(8,128)(2,1)S(1)}, bf16[1,32,4,384]{3,1,0,2:T(8,128)(2,1)S(1)}, u32[]{:S(2)}, u32[]{:S(2)}) %collective-permute-start.3) | collective-permute-done | bytes 98336 | tf_op jit(solution)/shard_map/ppermute | solution.py:126
  47.6 2.5 %gather_fusion.1 = bf16[24,32,4,384]{3,1,2,0:T(8,128)(2,1)} fusion(bf16[16,32,4,384]{3,1,0,2:T(8,128)(2,1)S(1)} %select_select_fusion, s32[1024]{0:T(1024)S(1)} %pad_clamp_fusion), kind=kCustom, calls=%fused_computation.1 | custom fusion | bytes 4718688 | tf_op jit(solution)/shard_map/gather | solution.py:209
  50.0 1.6 %fusion.47 = (bf16[24,32,4,128]{3,1,2,0:T(8,128)(2,1)S(1)}, bf16[24,32,4,128]{3,1,2,0:T(8,128)(2,1)S(1)}) fusion(bf16[24,32,4,384]{3,1,2,0:T(8,128)(2,1)} %gather_fusion.1), kind=kLoop, calls=%fused_computation.108 | loop fusion | bytes 3145728 | tf_op jit(solution)/shard_map/slice | solution.py:74
  51.7 1.5 %convert_reduce_fusion = s32[24]{0:T(128)S(1)} fusion(bf16[24,32,4,384]{3,1,2,0:T(8,128)(2,1)} %gather_fusion.1), kind=kLoop, calls=%fused_computation.39 | loop fusion | flops 2280 | bytes 1632 | tf_op jit(solution)/shard_map/reduce_sum | solution.py:210
  53.4 3.3 %fusion.52 = (f32[24,4,32]{2,1,0:T(4,128)S(1)}, f32[24,4,32,48]{3,2,1,0:T(8,128)}) fusion(bf16[24,32,4,128]{3,1,2,0:T(8,128)(2,1)S(1)} %get-tuple-element.2, bf16[24,16,4,128]{3,1,2,0:T(8,128)(2,1)S(1)} %get-tuple-element.4, bf16[24,32,4,384]{3,1,2,0:T(8,128)(2,1)} %gather_fusion.1, pred[24,32,48]{2,1,0:T(8,128)(4,1)S(1)} %and_or_fusion), kind=kOutput, calls=%fused_computation.113 | convolution fusion | flops 40845360 | bytes 2764800 | tf_op jit(solution)/shard_map/sub | solution.py:41
  56.6 2.1 %fusion.8 = bf16[24,4,4,8,128]{4,3,2,1,0:T(8,128)(2,1)S(1)} fusion(bf16[24,32,4,128]{3,1,2,0:T(8,128)(2,1)S(1)} %get-tuple-element.3, bf16[24,16,4,128]{3,1,2,0:T(8,128)(2,1)S(1)} %get-tuple-element.5, f32[24,4,32,48]{3,2,1,0:T(8,128)} %get-tuple-element.20, f32[24,4,32]{2,1,0:T(4,128)S(1)} %get-tuple-element.19, pred[24,32]{1,0:T(8,128)(4,1)S(1)} %iota_compare_fusion.1), kind=kOutput, calls=%fused_computation.19 | convolution fusion | flops 41189376 | bytes 2568960 | tf_op jit(solution)/shard_map/bhit,bthd->bihd/dot_general | solution.py:89
  58.7 1.0 %copy.44 = bf16[24,4,4,8,128]{4,3,1,2,0:T(8,128)(2,1)} copy(bf16[24,4,4,8,128]{4,3,2,1,0:T(8,128)(2,1)S(1)} %fusion.8) | data formatting | bytes 1572864 | tf_op jit(solution)/shard_map/convert_element_type | solution.py:92
  (71 shorter events, 7.1 us)
Async XLA Ops:
  19.7 0.8 %copy-start.2 = (s32[2]{0:T(128)S(1)}, s32[2]{0:T(128)}, u32[]{:S(2)}) copy-start(s32[2]{0:T(128)} %param.10) | copy-start | bytes 28
  20.3 5.8 %copy-start.1 = (s32[24]{0:T(128)S(1)}, s32[24]{0:T(128)}, u32[]{:S(2)}) copy-start(s32[24]{0:T(128)} %param.11) | copy-start | bytes 292
  20.3 5.8 %copy-start = (s32[8]{0:T(128)S(1)}, s32[8]{0:T(128)}, u32[]{:S(2)}) copy-start(s32[8]{0:T(128)} %constant.109.clone) | copy-start | bytes 100
  20.8 7.6 %collective-permute-start.4 = (bf16[1,32,4,384]{3,1,0,2:T(8,128)(2,1)S(1)}, bf16[1,32,4,384]{3,1,0,2:T(8,128)(2,1)S(1)}, u32[]{:S(2)}, u32[]{:S(2)}) collective-permute-start(bf16[1,32,4,384]{3,1,0,2:T(8,128)(2,1)S(1)} %get-tuple-element.11), channel_id=1, source_target_pairs={{0,8},{8,16},{16,24},{24,28},{28,20},{20,12},{12,4},{4,0},{1,9},{9... | collective-permute-start | bytes 294920 | tf_op jit(solution)/shard_map/ppermute | solution.py:123
  22.4 7.7 %collective-permute-start.11 = (bf16[1,32,4,384]{3,1,0,2:T(8,128)(2,1)S(1)}, bf16[1,32,4,384]{3,1,0,2:T(8,128)(2,1)S(1)}, u32[]{:S(2)}, u32[]{:S(2)}) collective-permute-start(bf16[1,32,4,384]{3,1,0,2:T(8,128)(2,1)S(1)} %get-tuple-element.11), channel_id=1, source_target_pairs={{8,0},{16,8},{24,16},{28,24},{20,28},{12,20},{4,12},{0,4},{9,1},{1... | collective-permute-start | bytes 294920 | tf_op jit(solution)/shard_map/ppermute | solution.py:126
  22.8 7.7 %collective-permute-start.8 = (bf16[1,32,4,384]{3,1,0,2:T(8,128)(2,1)S(1)}, bf16[1,32,4,384]{3,1,0,2:T(8,128)(2,1)S(1)}, u32[]{:S(2)}, u32[]{:S(2)}) collective-permute-start(bf16[1,32,4,384]{3,1,0,2:T(8,128)(2,1)S(1)} %get-tuple-element.10), channel_id=1, source_target_pairs={{0,8},{8,16},{16,24},{24,28},{28,20},{20,12},{12,4},{4,0},{1,9},{9... | collective-permute-start | bytes 294920 | tf_op jit(solution)/shard_map/ppermute | solution.py:123
  24.4 7.7 %collective-permute-start = (bf16[1,32,4,384]{3,1,0,2:T(8,128)(2,1)S(1)}, bf16[1,32,4,384]{3,1,0,2:T(8,128)(2,1)S(1)}, u32[]{:S(2)}, u32[]{:S(2)}) collective-permute-start(bf16[1,32,4,384]{3,1,0,2:T(8,128)(2,1)S(1)} %get-tuple-element.10), channel_id=1, source_target_pairs={{8,0},{16,8},{24,16},{28,24},{20,28},{12,20},{4,12},{0,4},{9,1},{1... | collective-permute-start | bytes 294920 | tf_op jit(solution)/shard_map/ppermute | solution.py:126
  28.4 5.6 %collective-permute-start.5 = (bf16[1,32,4,384]{3,1,0,2:T(8,128)(2,1)S(1)}, bf16[1,32,4,384]{3,1,0,2:T(8,128)(2,1)S(1)}, u32[]{:S(2)}, u32[]{:S(2)}) collective-permute-start(bf16[1,32,4,384]{3,1,0,2:T(8,128)(2,1)S(1)} %collective-permute-done.4), channel_id=1, source_target_pairs={{0,8},{8,16},{16,24},{24,28},{28,20},{20,12},{12,4},{4,0},{1,9},{9... | collective-permute-start | bytes 294920 | tf_op jit(solution)/shard_map/ppermute | solution.py:123
  30.1 5.5 %collective-permute-start.12 = (bf16[1,32,4,384]{3,1,0,2:T(8,128)(2,1)S(1)}, bf16[1,32,4,384]{3,1,0,2:T(8,128)(2,1)S(1)}, u32[]{:S(2)}, u32[]{:S(2)}) collective-permute-start(bf16[1,32,4,384]{3,1,0,2:T(8,128)(2,1)S(1)} %collective-permute-done.11), channel_id=1, source_target_pairs={{8,0},{16,8},{24,16},{28,24},{20,28},{12,20},{4,12},{0,4},{9,1},{1... | collective-permute-start | bytes 294920 | tf_op jit(solution)/shard_map/ppermute | solution.py:126
  30.5 5.5 %collective-permute-start.9 = (bf16[1,32,4,384]{3,1,0,2:T(8,128)(2,1)S(1)}, bf16[1,32,4,384]{3,1,0,2:T(8,128)(2,1)S(1)}, u32[]{:S(2)}, u32[]{:S(2)}) collective-permute-start(bf16[1,32,4,384]{3,1,0,2:T(8,128)(2,1)S(1)} %collective-permute-done.8), channel_id=1, source_target_pairs={{0,8},{8,16},{16,24},{24,28},{28,20},{20,12},{12,4},{4,0},{1,9},{9... | collective-permute-start | bytes 294920 | tf_op jit(solution)/shard_map/ppermute | solution.py:123
  32.1 5.5 %collective-permute-start.1 = (bf16[1,32,4,384]{3,1,0,2:T(8,128)(2,1)S(1)}, bf16[1,32,4,384]{3,1,0,2:T(8,128)(2,1)S(1)}, u32[]{:S(2)}, u32[]{:S(2)}) collective-permute-start(bf16[1,32,4,384]{3,1,0,2:T(8,128)(2,1)S(1)} %collective-permute-done), channel_id=1, source_target_pairs={{8,0},{16,8},{24,16},{28,24},{20,28},{12,20},{4,12},{0,4},{9,1},{1... | collective-permute-start | bytes 294920 | tf_op jit(solution)/shard_map/ppermute | solution.py:126
  34.0 7.0 %collective-permute-start.6 = (bf16[1,32,4,384]{3,1,0,2:T(8,128)(2,1)S(1)}, bf16[1,32,4,384]{3,1,0,2:T(8,128)(2,1)S(1)}, u32[]{:S(2)}, u32[]{:S(2)}) collective-permute-start(bf16[1,32,4,384]{3,1,0,2:T(8,128)(2,1)S(1)} %collective-permute-done.5), channel_id=1, source_target_pairs={{0,8},{8,16},{16,24},{24,28},{28,20},{20,12},{12,4},{4,0},{1,9},{9... | collective-permute-start | bytes 294920 | tf_op jit(solution)/shard_map/ppermute | solution.py:123
  35.6 7.5 %collective-permute-start.13 = (bf16[1,32,4,384]{3,1,0,2:T(8,128)(2,1)S(1)}, bf16[1,32,4,384]{3,1,0,2:T(8,128)(2,1)S(1)}, u32[]{:S(2)}, u32[]{:S(2)}) collective-permute-start(bf16[1,32,4,384]{3,1,0,2:T(8,128)(2,1)S(1)} %collective-permute-done.12), channel_id=1, source_target_pairs={{8,0},{16,8},{24,16},{28,24},{20,28},{12,20},{4,12},{0,4},{9,1},{1... | collective-permute-start | bytes 294920 | tf_op jit(solution)/shard_map/ppermute | solution.py:126
  36.0 7.1 %collective-permute-start.10 = (bf16[1,32,4,384]{3,1,0,2:T(8,128)(2,1)S(1)}, bf16[1,32,4,384]{3,1,0,2:T(8,128)(2,1)S(1)}, u32[]{:S(2)}, u32[]{:S(2)}) collective-permute-start(bf16[1,32,4,384]{3,1,0,2:T(8,128)(2,1)S(1)} %collective-permute-done.9), channel_id=1, source_target_pairs={{0,8},{8,16},{16,24},{24,28},{28,20},{20,12},{12,4},{4,0},{1,9},{9... | collective-permute-start | bytes 294920 | tf_op jit(solution)/shard_map/ppermute | solution.py:123
  37.6 5.0 %collective-permute-start.2 = (bf16[1,32,4,384]{3,1,0,2:T(8,128)(2,1)S(1)}, bf16[1,32,4,384]{3,1,0,2:T(8,128)(2,1)S(1)}, u32[]{:S(2)}, u32[]{:S(2)}) collective-permute-start(bf16[1,32,4,384]{3,1,0,2:T(8,128)(2,1)S(1)} %collective-permute-done.1), channel_id=1, source_target_pairs={{8,0},{16,8},{24,16},{28,24},{20,28},{12,20},{4,12},{0,4},{9,1},{1... | collective-permute-start | bytes 294920 | tf_op jit(solution)/shard_map/ppermute | solution.py:126
  41.0 4.7 %collective-permute-start.7 = (bf16[1,32,4,384]{3,1,0,2:T(8,128)(2,1)S(1)}, bf16[1,32,4,384]{3,1,0,2:T(8,128)(2,1)S(1)}, u32[]{:S(2)}, u32[]{:S(2)}) collective-permute-start(bf16[1,32,4,384]{3,1,0,2:T(8,128)(2,1)S(1)} %collective-permute-done.6), channel_id=1, source_target_pairs={{0,8},{8,16},{16,24},{24,28},{28,20},{20,12},{12,4},{4,0},{1,9},{9... | collective-permute-start | bytes 294920 | tf_op jit(solution)/shard_map/ppermute | solution.py:123
  42.6 4.6 %collective-permute-start.3 = (bf16[1,32,4,384]{3,1,0,2:T(8,128)(2,1)S(1)}, bf16[1,32,4,384]{3,1,0,2:T(8,128)(2,1)S(1)}, u32[]{:S(2)}, u32[]{:S(2)}) collective-permute-start(bf16[1,32,4,384]{3,1,0,2:T(8,128)(2,1)S(1)} %collective-permute-done.2), channel_id=1, source_target_pairs={{8,0},{16,8},{24,16},{28,24},{20,28},{12,20},{4,12},{0,4},{9,1},{1... | collective-permute-start | bytes 294920 | tf_op jit(solution)/shard_map/ppermute | solution.py:126

commit v11 on v10

--- a/solution.py
+++ b/solution.py
@@ -66,7 +66,7 @@
     return output.reshape(count, query_len, heads * head_dim).astype(jnp.bfloat16)
 
 
-def attend_core(query_kv, pair_qkv, pair_lengths, head_dim):
+def attend_core(query_kv, pair_qkv, head_dim):
     query_len = query_kv.shape[1]
     pairs, passage_len, heads = (pair_qkv.shape[0], pair_qkv.shape[1], pair_qkv.shape[2])
     scale = head_dim ** (-0.5)
@@ -82,19 +82,19 @@
     )
     column = jnp.arange(query_len + passage_len, dtype=jnp.int32) - query_len
     row_index = jnp.arange(passage_len, dtype=jnp.int32)
-    allowed = (column[None, None, :] < 0) | (column[None, None, :] <= row_index[None, :, None]) & (
-        column[None, None, :] < pair_lengths[:, None, None]
-    )
+    present = jnp.isfinite(pair_qkv[:, :, 0, head_dim])
+    present_cols = jnp.concatenate([jnp.ones((pairs, query_len), jnp.bool_), present], axis=1)
+    allowed = (column[None, None, :] < 0) | (column[None, None, :] <= row_index[None, :, None]) & present_cols[:, None, :]
     weights = softmax_rounded(scores, allowed[:, None])
     output = jnp.einsum("bhit,bthd->bihd", weights, values, preferred_element_type=jnp.float32)
-    live = row_index[None, :] < pair_lengths[:, None]
+    live = present
     output = jnp.where(live[:, :, None, None], output, jnp.float32(0.0))
     return output.reshape(pairs, passage_len, heads * head_dim).astype(jnp.bfloat16)
 
 
-def attend_pairs(query_qkv, pair_qkv, pair_lengths, head_dim, cands):
+def attend_pairs(query_qkv, pair_qkv, head_dim, cands):
     repeated = jnp.repeat(query_qkv[..., head_dim:], cands, axis=0)
-    return attend_core(repeated, pair_qkv, pair_lengths, head_dim)
+    return attend_core(repeated, pair_qkv, head_dim)
 
 
 def gather_store(own):
@@ -207,9 +207,8 @@
     own_qkv = jnp.where(mark, jnp.asarray(jnp.inf, own_qkv.dtype), own_qkv)
     store_qkv, rows_of = gather_store(own_qkv)
     pair_qkv = store_qkv[rows_of(cand_passage)]
-    pair_lengths = jnp.sum(jnp.isfinite(pair_qkv[:, :, 0, head_dim]).astype(jnp.int32), axis=1)
     query_attn = attend_queries(query_qkv, head_dim)
-    passage_attn = attend_pairs(query_qkv, pair_qkv, pair_lengths, head_dim, cands)
+    passage_attn = attend_pairs(query_qkv, pair_qkv, head_dim, cands)
     return (query_attn, passage_attn)
 
 

time: 60.1 us -> 61 us (1.015)
    ppermute x7, starting transfers between devices: 3.14 us -> 6.76 us  [gather_store(): behind = lax.ppermute(behind, 'store', backward)]
    ppermute x7, starting transfers between devices: 11.2 us -> 7.69 us  [gather_store(): ahead = lax.ppermute(ahead, 'store', forward)]
    reduce_sum x1 -> x0, other arithmetic: 1.46 us -> none  [local(): jnp.sum(jnp.isfinite(pair_qkv[:, :, 0, head_dim]).astype(jnp.int32), axis=1)]
    is_finite x0 -> x1, other arithmetic: none -> 1.42 us  [attend_core(): present = jnp.isfinite(pair_qkv[:, :, 0, head_dim])]
    ppermute x7, waiting for transfers between devices: 1.6 us -> 2.57 us  [gather_store(): behind = lax.ppermute(behind, 'store', backward)]
    ppermute x7, waiting for transfers between devices: 3.48 us -> 2.78 us  [gather_store(): ahead = lax.ppermute(ahead, 'store', forward)]
    ge x1, other arithmetic: 0.07 us -> 0.73 us  [local(): jnp.arange(passage_len, dtype=jnp.int32)[None, :]]
  transfers between devices with their start and end apart: 14 -> 14, of which waited for: 3 -> 5; matrix products, arithmetic and copies ran while one was open for 11% -> 11% of each run, Pallas kernels for 0% -> 0%
where the time goes in v11:
time: 61 us; the launch traced here: 60.6 us
  starting transfers between devices  14.4 us (24%)
  matrix products  12.6 us (21%)
  blocking collectives  10.1 us (17%)
  other arithmetic  9.34 us (15%)
  local copies, waits for them, and re-layouts  7.84 us (13%)
  waiting for transfers between devices  5.36 us (9%)
  between operations  0.95 us (2%)
    all_gather x1, blocking collectives, local(): full_rows = lax.all_gather(all_rows, 'tp', axis=1, tiled=True)  10.1 us
    ppermute x7, starting transfers between devices, gather_store(): ahead = lax.ppermute(ahead, 'store', forward)  7.69 us
    dot_general x1, matrix products, local(): jnp.einsum('nk,khc->nhc', normed, w_qkv, preferred_element_type=jnp.float32)  6.87 us
    ppermute x7, starting transfers between devices, gather_store(): behind = lax.ppermute(behind, 'store', backward)  6.76 us
    select_n x3, other arithmetic, lay(): joined = jnp.where((row_at >= at) & (row_at < at + size), widened, joined)  3.79 us
    sub x2, matrix products, softmax_rounded(): expon = jnp.where(allowed, jnp.exp(masked - peak), jnp.float32(0.0))  3.46 us
    ppermute x7, waiting for transfers between devices, gather_store(): ahead = lax.ppermute(ahead, 'store', forward)  2.78 us
    ppermute x7, waiting for transfers between devices, gather_store(): behind = lax.ppermute(behind, 'store', backward)  2.57 us
  transfers between devices with their start and end apart: 14, of which 5 were waited for; matrix products, arithmetic and copies ran while one was open for 11% of the time, Pallas kernels for 0%

profile of v11, /device:TPU:0, one launch (start us, length us, event | category | flops | bytes accessed | tf_op | source)
XLA Modules:
  0.0 60.6 jit_solution(944625402448754268)
XLA Ops:
  0.7 0.7 %iota_compare_fusion.3 = pred[2,32]{1,0:T(4,128)(4,1)S(1)} fusion(s32[2]{0:T(128)} %param.10), kind=kLoop, calls=%fused_computation.90 | loop fusion | flops 64 | bytes 72 | tf_op jit(solution)/shard_map/ge | solution.py:203
  1.6 0.7 %convert_element_type.67 = f32[4096]{0:T(1024)S(1)} convert(bf16[4096]{0:T(1024)(128)(2,1)} %param.12) | non-fusion elementwise | flops 4096 | bytes 24576 | tf_op jit(solution)/shard_map/convert_element_type | solution.py:12
  2.3 0.9 %pad_maximum_fusion = bf16[96,1024]{1,0:T(8,128)(2,1)S(1)} fusion(bf16[64,1024]{1,0:T(8,128)(2,1)} %bitcast.26, bf16[32,1024]{1,0:T(8,128)(2,1)} %bitcast.27), kind=kLoop, calls=%fused_computation.43 | loop fusion | flops 393216 | bytes 393216 | tf_op jit(solution)/shard_map/concatenate | solution.py:196
  3.2 10.1 %all_gather.3 = bf16[96,4096]{1,0:T(8,128)(2,1)S(1)} all-gather(bf16[96,1024]{1,0:T(8,128)(2,1)S(1)} %pad_maximum_fusion), channel_id=1, replica_groups=mesh['store'=8,'tp'=4] {'tp'}, dimensions={1}, use_global_device_ids=true | all-gather | bytes 983040 | tf_op jit(solution)/shard_map/all_gather | solution.py:197
  13.5 6.9 %fusion.2 = f32[96,4,384]{2,0,1:T(8,128)S(1)} fusion(bf16[4096,4,384]{2,1,0:T(4,128)(2,1)} %param.13, bf16[96,4096]{1,0:T(8,128)(2,1)S(1)} %all_gather.3, f32[4096]{0:T(1024)S(1)} %convert_element_type.67, f32[96]{0:T(128)S(1)} %add_rsqrt_fusion), kind=kOutput, calls=%fused_computation.4 | convolution fusion | flops 1209532416 | bytes 13975936 | tf_op jit(solution)/shard_map/nk,khc->nhc/dot_general | solution.py:199
  21.4 1.6 %collective-permute-start.8 = (bf16[1,32,4,384]{3,1,0,2:T(8,128)(2,1)S(1)}, bf16[1,32,4,384]{3,1,0,2:T(8,128)(2,1)S(1)}, u32[]{:S(2)}, u32[]{:S(2)}) collective-permute-start(bf16[1,32,4,384]{3,1,0,2:T(8,128)(2,1)S(1)} %get-tuple-element.10), channel_id=1, source_target_pairs={{0,8},{8,16},{16,24},{24,28},{28,20},{20,12},{12,4},{4,0},{1,9},{9... | collective-permute-start | bytes 294920 | tf_op jit(solution)/shard_map/ppermute | solution.py:123
  23.5 1.5 %collective-permute-start.11 = (bf16[1,32,4,384]{3,1,0,2:T(8,128)(2,1)S(1)}, bf16[1,32,4,384]{3,1,0,2:T(8,128)(2,1)S(1)}, u32[]{:S(2)}, u32[]{:S(2)}) collective-permute-start(bf16[1,32,4,384]{3,1,0,2:T(8,128)(2,1)S(1)} %get-tuple-element.11), channel_id=1, source_target_pairs={{8,0},{16,8},{24,16},{28,24},{20,28},{12,20},{4,12},{0,4},{9,1},{1... | collective-permute-start | bytes 294920 | tf_op jit(solution)/shard_map/ppermute | solution.py:126
  26.3 0.7 %gather_fusion = s32[24]{0:T(128)S(1)} fusion(s32[8]{0:T(128)S(1)} %copy-done, s32[1024]{0:T(1024)S(1)} %pad_clamp_fusion.1), kind=kCustom, calls=%fused_computation | custom fusion | bytes 288 | tf_op jit(solution)/shard_map/gather | solution.py:151
  27.0 0.7 %compare_select_fusion = s32[24]{0:T(128)S(1)} fusion(s32[24]{0:T(128)S(1)} %gather_fusion, s32[]{:T(128)} %bitcast.6, s32[24]{0:T(128)S(1)} %copy-done.1), kind=kLoop, calls=%fused_computation.60 | loop fusion | flops 960 | bytes 292 | tf_op jit(solution)/shard_map/select_n | solution.py:209
  29.0 1.6 %collective-permute-start.9 = (bf16[1,32,4,384]{3,1,0,2:T(8,128)(2,1)S(1)}, bf16[1,32,4,384]{3,1,0,2:T(8,128)(2,1)S(1)}, u32[]{:S(2)}, u32[]{:S(2)}) collective-permute-start(bf16[1,32,4,384]{3,1,0,2:T(8,128)(2,1)S(1)} %collective-permute-done.8), channel_id=1, source_target_pairs={{0,8},{8,16},{16,24},{24,28},{28,20},{20,12},{12,4},{4,0},{1,9},{9... | collective-permute-start | bytes 294920 | tf_op jit(solution)/shard_map/ppermute | solution.py:123
  31.1 1.5 %collective-permute-start.12 = (bf16[1,32,4,384]{3,1,0,2:T(8,128)(2,1)S(1)}, bf16[1,32,4,384]{3,1,0,2:T(8,128)(2,1)S(1)}, u32[]{:S(2)}, u32[]{:S(2)}) collective-permute-start(bf16[1,32,4,384]{3,1,0,2:T(8,128)(2,1)S(1)} %collective-permute-done.11), channel_id=1, source_target_pairs={{8,0},{16,8},{24,16},{28,24},{20,28},{12,20},{4,12},{0,4},{9,1},{1... | collective-permute-start | bytes 294920 | tf_op jit(solution)/shard_map/ppermute | solution.py:126
  33.1 0.7 %collective-permute-done.9 = bf16[1,32,4,384]{3,1,0,2:T(8,128)(2,1)S(1)} collective-permute-done((bf16[1,32,4,384]{3,1,0,2:T(8,128)(2,1)S(1)}, bf16[1,32,4,384]{3,1,0,2:T(8,128)(2,1)S(1)}, u32[]{:S(2)}, u32[]{:S(2)}) %collective-permute-start.9) | collective-permute-done | bytes 98336 | tf_op jit(solution)/shard_map/ppermute | solution.py:123
  33.8 2.5 %collective-permute-start.10 = (bf16[1,32,4,384]{3,1,0,2:T(8,128)(2,1)S(1)}, bf16[1,32,4,384]{3,1,0,2:T(8,128)(2,1)S(1)}, u32[]{:S(2)}, u32[]{:S(2)}) collective-permute-start(bf16[1,32,4,384]{3,1,0,2:T(8,128)(2,1)S(1)} %collective-permute-done.9), channel_id=1, source_target_pairs={{0,8},{8,16},{16,24},{24,28},{28,20},{20,12},{12,4},{4,0},{1,9},{9... | collective-permute-start | bytes 294920 | tf_op jit(solution)/shard_map/ppermute | solution.py:123
  36.8 1.4 %collective-permute-start.13 = (bf16[1,32,4,384]{3,1,0,2:T(8,128)(2,1)S(1)}, bf16[1,32,4,384]{3,1,0,2:T(8,128)(2,1)S(1)}, u32[]{:S(2)}, u32[]{:S(2)}) collective-permute-start(bf16[1,32,4,384]{3,1,0,2:T(8,128)(2,1)S(1)} %collective-permute-done.12), channel_id=1, source_target_pairs={{8,0},{16,8},{24,16},{28,24},{20,28},{12,20},{4,12},{0,4},{9,1},{1... | collective-permute-start | bytes 294920 | tf_op jit(solution)/shard_map/ppermute | solution.py:126
  38.9 2.9 %select_select_fusion.2 = bf16[16,32,4,384]{3,1,0,2:T(8,128)(2,1)S(1)} fusion(bf16[1,32,4,384]{3,1,0,2:T(8,128)(2,1)S(1)} %get-tuple-element.11, bf16[1,32,4,384]{3,1,0,2:T(8,128)(2,1)S(1)} %collective-permute-done.4, bf16[1,32,4,384]{3,1,0,2:T(8,128)(2,1)S(1)} %collective-permute-done.5, bf16[1,32,4,384]{3,1,0,2:T(8,128)(2,1)S(1)} %collective-permute-done.11, ...), kind=kLoop, calls=%fused_computation.18 | loop fusion | flops 7077888 | bytes 2556048 | tf_op jit(solution)/shard_map/jit(_where)/select_n | solution.py:172
  41.8 1.4 %collective-permute-start.3 = (bf16[1,32,4,384]{3,1,0,2:T(8,128)(2,1)S(1)}, bf16[1,32,4,384]{3,1,0,2:T(8,128)(2,1)S(1)}, u32[]{:S(2)}, u32[]{:S(2)}) collective-permute-start(bf16[1,32,4,384]{3,1,0,2:T(8,128)(2,1)S(1)} %collective-permute-done.2), channel_id=1, source_target_pairs={{8,0},{16,8},{24,16},{28,24},{20,28},{12,20},{4,12},{0,4},{9,1},{1... | collective-permute-start | bytes 294920 | tf_op jit(solution)/shard_map/ppermute | solution.py:126
  44.4 2.0 %collective-permute-done.3 = bf16[1,32,4,384]{3,1,0,2:T(8,128)(2,1)S(1)} collective-permute-done((bf16[1,32,4,384]{3,1,0,2:T(8,128)(2,1)S(1)}, bf16[1,32,4,384]{3,1,0,2:T(8,128)(2,1)S(1)}, u32[]{:S(2)}, u32[]{:S(2)}) %collective-permute-start.3) | collective-permute-done | bytes 98336 | tf_op jit(solution)/shard_map/ppermute | solution.py:126
  46.5 1.7 %collective-permute-done.7 = bf16[1,32,4,384]{3,1,0,2:T(8,128)(2,1)S(1)} collective-permute-done((bf16[1,32,4,384]{3,1,0,2:T(8,128)(2,1)S(1)}, bf16[1,32,4,384]{3,1,0,2:T(8,128)(2,1)S(1)}, u32[]{:S(2)}, u32[]{:S(2)}) %collective-permute-start.7) | collective-permute-done | bytes 98336 | tf_op jit(solution)/shard_map/ppermute | solution.py:123
  48.5 2.5 %gather_fusion.1 = bf16[24,32,4,384]{3,1,2,0:T(8,128)(2,1)} fusion(bf16[16,32,4,384]{3,1,0,2:T(8,128)(2,1)S(1)} %select_select_fusion, s32[1024]{0:T(1024)S(1)} %pad_clamp_fusion), kind=kCustom, calls=%fused_computation.1 | custom fusion | bytes 4718688 | tf_op jit(solution)/shard_map/gather | solution.py:209
  51.0 1.4 %is-finite_reduce_fusion = pred[24,32]{1,0:T(8,128)(4,1)S(1)} fusion(bf16[24,32,4,384]{3,1,2,0:T(8,128)(2,1)} %gather_fusion.1), kind=kLoop, calls=%fused_computation.40 | loop fusion | flops 768 | bytes 2304 | tf_op jit(solution)/shard_map/is_finite | solution.py:85
  52.4 1.7 %fusion.47 = (bf16[24,32,4,128]{3,1,2,0:T(8,128)(2,1)S(1)}, bf16[24,32,4,128]{3,1,2,0:T(8,128)(2,1)S(1)}) fusion(bf16[24,32,4,384]{3,1,2,0:T(8,128)(2,1)} %gather_fusion.1), kind=kLoop, calls=%fused_computation.106 | loop fusion | bytes 3145728 | tf_op jit(solution)/shard_map/slice | solution.py:74
  54.2 3.3 %fusion.52 = (f32[24,4,32]{2,1,0:T(4,128)S(1)}, f32[24,4,32,48]{3,2,1,0:T(8,128)}) fusion(bf16[24,32,4,128]{3,1,2,0:T(8,128)(2,1)S(1)} %get-tuple-element.2, bf16[24,16,4,128]{3,1,2,0:T(8,128)(2,1)S(1)} %get-tuple-element.4, bf16[24,32,4,384]{3,1,2,0:T(8,128)(2,1)} %gather_fusion.1, pred[24,32,48]{2,1,0:T(8,128)(4,1)S(1)} %and_or_fusion), kind=kOutput, calls=%fused_computation.111 | convolution fusion | flops 40845360 | bytes 2764800 | tf_op jit(solution)/shard_map/sub | solution.py:41
  57.5 2.1 %fusion.8 = bf16[24,4,4,8,128]{4,3,2,1,0:T(8,128)(2,1)S(1)} fusion(bf16[24,32,4,128]{3,1,2,0:T(8,128)(2,1)S(1)} %get-tuple-element.3, bf16[24,16,4,128]{3,1,2,0:T(8,128)(2,1)S(1)} %get-tuple-element.5, f32[24,4,32,48]{3,2,1,0:T(8,128)} %get-tuple-element.20, f32[24,4,32]{2,1,0:T(4,128)S(1)} %get-tuple-element.19, pred[24,32]{1,0:T(8,128)(4,1)S(1)} %is-finite_reduce_fusion), kind=kOutput, calls=%fused_computation.19 | convolution fusion | flops 41189376 | bytes 2568960 | tf_op jit(solution)/shard_map/bhit,bthd->bihd/dot_general | solution.py:89
  59.6 1.0 %copy.44 = bf16[24,4,4,8,128]{4,3,1,2,0:T(8,128)(2,1)} copy(bf16[24,4,4,8,128]{4,3,2,1,0:T(8,128)(2,1)S(1)} %fusion.8) | data formatting | bytes 1572864 | tf_op jit(solution)/shard_map/convert_element_type | solution.py:92
  (68 shorter events, 8.1 us)
Async XLA Ops:
  21.0 4.7 %copy-start.1 = (s32[24]{0:T(128)S(1)}, s32[24]{0:T(128)}, u32[]{:S(2)}) copy-start(s32[24]{0:T(128)} %param.11) | copy-start | bytes 292
  21.0 4.7 %copy-start = (s32[8]{0:T(128)S(1)}, s32[8]{0:T(128)}, u32[]{:S(2)}) copy-start(s32[8]{0:T(128)} %constant.111.clone) | copy-start | bytes 100
  21.4 7.6 %collective-permute-start.8 = (bf16[1,32,4,384]{3,1,0,2:T(8,128)(2,1)S(1)}, bf16[1,32,4,384]{3,1,0,2:T(8,128)(2,1)S(1)}, u32[]{:S(2)}, u32[]{:S(2)}) collective-permute-start(bf16[1,32,4,384]{3,1,0,2:T(8,128)(2,1)S(1)} %get-tuple-element.10), channel_id=1, source_target_pairs={{0,8},{8,16},{16,24},{24,28},{28,20},{20,12},{12,4},{4,0},{1,9},{9... | collective-permute-start | bytes 294920 | tf_op jit(solution)/shard_map/ppermute | solution.py:123
  23.0 7.6 %collective-permute-start = (bf16[1,32,4,384]{3,1,0,2:T(8,128)(2,1)S(1)}, bf16[1,32,4,384]{3,1,0,2:T(8,128)(2,1)S(1)}, u32[]{:S(2)}, u32[]{:S(2)}) collective-permute-start(bf16[1,32,4,384]{3,1,0,2:T(8,128)(2,1)S(1)} %get-tuple-element.10), channel_id=1, source_target_pairs={{8,0},{16,8},{24,16},{28,24},{20,28},{12,20},{4,12},{0,4},{9,1},{1... | collective-permute-start | bytes 294920 | tf_op jit(solution)/shard_map/ppermute | solution.py:126
  23.5 7.6 %collective-permute-start.11 = (bf16[1,32,4,384]{3,1,0,2:T(8,128)(2,1)S(1)}, bf16[1,32,4,384]{3,1,0,2:T(8,128)(2,1)S(1)}, u32[]{:S(2)}, u32[]{:S(2)}) collective-permute-start(bf16[1,32,4,384]{3,1,0,2:T(8,128)(2,1)S(1)} %get-tuple-element.11), channel_id=1, source_target_pairs={{8,0},{16,8},{24,16},{28,24},{20,28},{12,20},{4,12},{0,4},{9,1},{1... | collective-permute-start | bytes 294920 | tf_op jit(solution)/shard_map/ppermute | solution.py:126
  25.0 7.6 %collective-permute-start.4 = (bf16[1,32,4,384]{3,1,0,2:T(8,128)(2,1)S(1)}, bf16[1,32,4,384]{3,1,0,2:T(8,128)(2,1)S(1)}, u32[]{:S(2)}, u32[]{:S(2)}) collective-permute-start(bf16[1,32,4,384]{3,1,0,2:T(8,128)(2,1)S(1)} %get-tuple-element.11), channel_id=1, source_target_pairs={{0,8},{8,16},{16,24},{24,28},{28,20},{20,12},{12,4},{4,0},{1,9},{9... | collective-permute-start | bytes 294920 | tf_op jit(solution)/shard_map/ppermute | solution.py:123
  29.0 4.8 %collective-permute-start.9 = (bf16[1,32,4,384]{3,1,0,2:T(8,128)(2,1)S(1)}, bf16[1,32,4,384]{3,1,0,2:T(8,128)(2,1)S(1)}, u32[]{:S(2)}, u32[]{:S(2)}) collective-permute-start(bf16[1,32,4,384]{3,1,0,2:T(8,128)(2,1)S(1)} %collective-permute-done.8), channel_id=1, source_target_pairs={{0,8},{8,16},{16,24},{24,28},{28,20},{20,12},{12,4},{4,0},{1,9},{9... | collective-permute-start | bytes 294920 | tf_op jit(solution)/shard_map/ppermute | solution.py:123
  30.6 5.7 %collective-permute-start.1 = (bf16[1,32,4,384]{3,1,0,2:T(8,128)(2,1)S(1)}, bf16[1,32,4,384]{3,1,0,2:T(8,128)(2,1)S(1)}, u32[]{:S(2)}, u32[]{:S(2)}) collective-permute-start(bf16[1,32,4,384]{3,1,0,2:T(8,128)(2,1)S(1)} %collective-permute-done), channel_id=1, source_target_pairs={{8,0},{16,8},{24,16},{28,24},{20,28},{12,20},{4,12},{0,4},{9,1},{1... | collective-permute-start | bytes 294920 | tf_op jit(solution)/shard_map/ppermute | solution.py:126
  31.1 5.8 %collective-permute-start.12 = (bf16[1,32,4,384]{3,1,0,2:T(8,128)(2,1)S(1)}, bf16[1,32,4,384]{3,1,0,2:T(8,128)(2,1)S(1)}, u32[]{:S(2)}, u32[]{:S(2)}) collective-permute-start(bf16[1,32,4,384]{3,1,0,2:T(8,128)(2,1)S(1)} %collective-permute-done.11), channel_id=1, source_target_pairs={{8,0},{16,8},{24,16},{28,24},{20,28},{12,20},{4,12},{0,4},{9,1},{1... | collective-permute-start | bytes 294920 | tf_op jit(solution)/shard_map/ppermute | solution.py:126
  32.6 5.6 %collective-permute-start.5 = (bf16[1,32,4,384]{3,1,0,2:T(8,128)(2,1)S(1)}, bf16[1,32,4,384]{3,1,0,2:T(8,128)(2,1)S(1)}, u32[]{:S(2)}, u32[]{:S(2)}) collective-permute-start(bf16[1,32,4,384]{3,1,0,2:T(8,128)(2,1)S(1)} %collective-permute-done.4), channel_id=1, source_target_pairs={{0,8},{8,16},{16,24},{24,28},{28,20},{20,12},{12,4},{4,0},{1,9},{9... | collective-permute-start | bytes 294920 | tf_op jit(solution)/shard_map/ppermute | solution.py:123
  33.8 10.1 %collective-permute-start.10 = (bf16[1,32,4,384]{3,1,0,2:T(8,128)(2,1)S(1)}, bf16[1,32,4,384]{3,1,0,2:T(8,128)(2,1)S(1)}, u32[]{:S(2)}, u32[]{:S(2)}) collective-permute-start(bf16[1,32,4,384]{3,1,0,2:T(8,128)(2,1)S(1)} %collective-permute-done.9), channel_id=1, source_target_pairs={{0,8},{8,16},{16,24},{24,28},{28,20},{20,12},{12,4},{4,0},{1,9},{9... | collective-permute-start | bytes 294920 | tf_op jit(solution)/shard_map/ppermute | solution.py:123
  36.3 5.5 %collective-permute-start.2 = (bf16[1,32,4,384]{3,1,0,2:T(8,128)(2,1)S(1)}, bf16[1,32,4,384]{3,1,0,2:T(8,128)(2,1)S(1)}, u32[]{:S(2)}, u32[]{:S(2)}) collective-permute-start(bf16[1,32,4,384]{3,1,0,2:T(8,128)(2,1)S(1)} %collective-permute-done.1), channel_id=1, source_target_pairs={{8,0},{16,8},{24,16},{28,24},{20,28},{12,20},{4,12},{0,4},{9,1},{1... | collective-permute-start | bytes 294920 | tf_op jit(solution)/shard_map/ppermute | solution.py:126
  36.8 7.1 %collective-permute-start.13 = (bf16[1,32,4,384]{3,1,0,2:T(8,128)(2,1)S(1)}, bf16[1,32,4,384]{3,1,0,2:T(8,128)(2,1)S(1)}, u32[]{:S(2)}, u32[]{:S(2)}) collective-permute-start(bf16[1,32,4,384]{3,1,0,2:T(8,128)(2,1)S(1)} %collective-permute-done.12), channel_id=1, source_target_pairs={{8,0},{16,8},{24,16},{28,24},{20,28},{12,20},{4,12},{0,4},{9,1},{1... | collective-permute-start | bytes 294920 | tf_op jit(solution)/shard_map/ppermute | solution.py:126
  38.2 5.4 %collective-permute-start.6 = (bf16[1,32,4,384]{3,1,0,2:T(8,128)(2,1)S(1)}, bf16[1,32,4,384]{3,1,0,2:T(8,128)(2,1)S(1)}, u32[]{:S(2)}, u32[]{:S(2)}) collective-permute-start(bf16[1,32,4,384]{3,1,0,2:T(8,128)(2,1)S(1)} %collective-permute-done.5), channel_id=1, source_target_pairs={{0,8},{8,16},{16,24},{24,28},{28,20},{20,12},{12,4},{4,0},{1,9},{9... | collective-permute-start | bytes 294920 | tf_op jit(solution)/shard_map/ppermute | solution.py:123
  41.8 4.7 %collective-permute-start.3 = (bf16[1,32,4,384]{3,1,0,2:T(8,128)(2,1)S(1)}, bf16[1,32,4,384]{3,1,0,2:T(8,128)(2,1)S(1)}, u32[]{:S(2)}, u32[]{:S(2)}) collective-permute-start(bf16[1,32,4,384]{3,1,0,2:T(8,128)(2,1)S(1)} %collective-permute-done.2), channel_id=1, source_target_pairs={{8,0},{16,8},{24,16},{28,24},{20,28},{12,20},{4,12},{0,4},{9,1},{1... | collective-permute-start | bytes 294920 | tf_op jit(solution)/shard_map/ppermute | solution.py:126
  43.6 4.6 %collective-permute-start.7 = (bf16[1,32,4,384]{3,1,0,2:T(8,128)(2,1)S(1)}, bf16[1,32,4,384]{3,1,0,2:T(8,128)(2,1)S(1)}, u32[]{:S(2)}, u32[]{:S(2)}) collective-permute-start(bf16[1,32,4,384]{3,1,0,2:T(8,128)(2,1)S(1)} %collective-permute-done.6), channel_id=1, source_target_pairs={{0,8},{8,16},{16,24},{24,28},{28,20},{20,12},{12,4},{4,0},{1,9},{9... | collective-permute-start | bytes 294920 | tf_op jit(solution)/shard_map/ppermute | solution.py:123

commit v12 on v10

--- a/solution.py
+++ b/solution.py
@@ -66,17 +66,17 @@
     return output.reshape(count, query_len, heads * head_dim).astype(jnp.bfloat16)
 
 
-def attend_core(query_kv, pair_qkv, pair_lengths, head_dim):
+def attend_core(query_kv, pair_q, pair_k, pair_v, pair_lengths, head_dim):
     query_len = query_kv.shape[1]
-    pairs, passage_len, heads = (pair_qkv.shape[0], pair_qkv.shape[1], pair_qkv.shape[2])
+    pairs, passage_len, heads = (pair_q.shape[0], pair_q.shape[1], pair_q.shape[2])
     scale = head_dim ** (-0.5)
     keyset = jnp.concatenate(
-        [query_kv[..., :head_dim], pair_qkv[..., head_dim : 2 * head_dim]], axis=1
-    )
-    values = jnp.concatenate([query_kv[..., head_dim:], pair_qkv[..., 2 * head_dim :]], axis=1)
+        [query_kv[..., :head_dim], pair_k], axis=1
+    )
+    values = jnp.concatenate([query_kv[..., head_dim:], pair_v], axis=1)
     scores = (
         jnp.einsum(
-            "bihd,bthd->bhit", pair_qkv[..., :head_dim], keyset, preferred_element_type=jnp.float32
+            "bihd,bthd->bhit", pair_q, keyset, preferred_element_type=jnp.float32
         )
         * scale
     )
@@ -92,9 +92,9 @@
     return output.reshape(pairs, passage_len, heads * head_dim).astype(jnp.bfloat16)
 
 
-def attend_pairs(query_qkv, pair_qkv, pair_lengths, head_dim, cands):
+def attend_pairs(query_qkv, pair_q, pair_k, pair_v, pair_lengths, head_dim, cands):
     repeated = jnp.repeat(query_qkv[..., head_dim:], cands, axis=0)
-    return attend_core(repeated, pair_qkv, pair_lengths, head_dim)
+    return attend_core(repeated, pair_q, pair_k, pair_v, pair_lengths, head_dim)
 
 
 def gather_store(own):
@@ -206,10 +206,13 @@
     mark = padded[:, :, None, None] & (head_at == 0) & (col_at == head_dim)
     own_qkv = jnp.where(mark, jnp.asarray(jnp.inf, own_qkv.dtype), own_qkv)
     store_qkv, rows_of = gather_store(own_qkv)
-    pair_qkv = store_qkv[rows_of(cand_passage)]
-    pair_lengths = jnp.sum(jnp.isfinite(pair_qkv[:, :, 0, head_dim]).astype(jnp.int32), axis=1)
+    rows = rows_of(cand_passage)
+    pair_q = store_qkv[:, :, :, :head_dim][rows]
+    pair_k = store_qkv[:, :, :, head_dim : 2 * head_dim][rows]
+    pair_v = store_qkv[:, :, :, 2 * head_dim :][rows]
+    pair_lengths = jnp.sum(jnp.isfinite(pair_k[:, :, 0, 0]).astype(jnp.int32), axis=1)
     query_attn = attend_queries(query_qkv, head_dim)
-    passage_attn = attend_pairs(query_qkv, pair_qkv, pair_lengths, head_dim, cands)
+    passage_attn = attend_pairs(query_qkv, pair_q, pair_k, pair_v, pair_lengths, head_dim, cands)
     return (query_attn, passage_attn)
 
 

time: 60.1 us -> 59.1 us (0.983)
  local copies, waits for them, and re-layouts: 7.81 us -> 6.93 us
    ppermute x7, starting transfers between devices: 3.14 us -> 6.76 us  [gather_store(): behind = lax.ppermute(behind, 'store', backward)]
    ppermute x7, starting transfers between devices: 11.2 us -> 7.67 us  [gather_store(): ahead = lax.ppermute(ahead, 'store', forward)]
    ppermute x7, waiting for transfers between devices: 1.6 us -> 2.57 us  [gather_store(): behind = lax.ppermute(behind, 'store', backward)]
    reduce_sum x1, other arithmetic: 1.46 us -> 0.53 us  [local(): jnp.sum(jnp.isfinite(pair_k[:, :, 0, 0]).astype(jnp.int32), axis=1)]
    ppermute x7, waiting for transfers between devices: 3.48 us -> 2.81 us  [gather_store(): ahead = lax.ppermute(ahead, 'store', forward)]
    ge x1, other arithmetic: 0.07 us -> 0.73 us  [local(): jnp.arange(passage_len, dtype=jnp.int32)[None, :]]
    gather x1 -> x3, local copies, waits for them, and re-layouts: 2.45 us -> 2.1 us  [the longest x1 0.7 us: local(): pair_q = store_qkv[:, :, :, :head_dim][rows]]
  transfers between devices with their start and end apart: 14 -> 14, of which waited for: 3 -> 5; matrix products, arithmetic and copies ran while one was open for 11% -> 13% of each run, Pallas kernels for 0% -> 0%
where the time goes in v12:
time: 59.1 us; the launch traced here: 58.8 us
  starting transfers between devices  14.4 us (24%)
  matrix products  12.4 us (21%)
  blocking collectives  10.1 us (17%)
  other arithmetic  8.59 us (15%)
  local copies, waits for them, and re-layouts  6.93 us (12%)
  waiting for transfers between devices  5.38 us (9%)
  between operations  0.96 us (2%)
    all_gather x1, blocking collectives, local(): full_rows = lax.all_gather(all_rows, 'tp', axis=1, tiled=True)  10.1 us
    ppermute x7, starting transfers between devices, gather_store(): ahead = lax.ppermute(ahead, 'store', forward)  7.67 us
    dot_general x1, matrix products, local(): jnp.einsum('nk,khc->nhc', normed, w_qkv, preferred_element_type=jnp.float32)  6.87 us
    ppermute x7, starting transfers between devices, gather_store(): behind = lax.ppermute(behind, 'store', backward)  6.76 us
    select_n x3, other arithmetic, lay(): joined = jnp.where((row_at >= at) & (row_at < at + size), widened, joined)  3.79 us
    sub x2, matrix products, softmax_rounded(): expon = jnp.where(allowed, jnp.exp(masked - peak), jnp.float32(0.0))  3.33 us
    ppermute x7, waiting for transfers between devices, gather_store(): ahead = lax.ppermute(ahead, 'store', forward)  2.81 us
    ppermute x7, waiting for transfers between devices, gather_store(): behind = lax.ppermute(behind, 'store', backward)  2.57 us
  transfers between devices with their start and end apart: 14, of which 5 were waited for; matrix products, arithmetic and copies ran while one was open for 13% of the time, Pallas kernels for 0%

profile of v12, /device:TPU:0, one launch (start us, length us, event | category | flops | bytes accessed | tf_op | source)
XLA Modules:
  0.0 58.8 jit_solution(5401309577018196997)
XLA Ops:
  0.7 0.7 %iota_compare_fusion.4 = pred[2,32]{1,0:T(4,128)(4,1)S(1)} fusion(s32[2]{0:T(128)} %param.10), kind=kLoop, calls=%fused_computation.93 | loop fusion | flops 64 | bytes 72 | tf_op jit(solution)/shard_map/ge | solution.py:203
  1.6 0.7 %convert_element_type.71 = f32[4096]{0:T(1024)S(1)} convert(bf16[4096]{0:T(1024)(128)(2,1)} %param.12) | non-fusion elementwise | flops 4096 | bytes 24576 | tf_op jit(solution)/shard_map/convert_element_type | solution.py:12
  2.3 0.9 %pad_maximum_fusion = bf16[96,1024]{1,0:T(8,128)(2,1)S(1)} fusion(bf16[64,1024]{1,0:T(8,128)(2,1)} %bitcast.27, bf16[32,1024]{1,0:T(8,128)(2,1)} %bitcast.28), kind=kLoop, calls=%fused_computation.44 | loop fusion | flops 393216 | bytes 393216 | tf_op jit(solution)/shard_map/concatenate | solution.py:196
  3.2 10.1 %all_gather.3 = bf16[96,4096]{1,0:T(8,128)(2,1)S(1)} all-gather(bf16[96,1024]{1,0:T(8,128)(2,1)S(1)} %pad_maximum_fusion), channel_id=1, replica_groups=mesh['store'=8,'tp'=4] {'tp'}, dimensions={1}, use_global_device_ids=true | all-gather | bytes 983040 | tf_op jit(solution)/shard_map/all_gather | solution.py:197
  13.5 6.9 %fusion.2 = f32[96,4,384]{2,0,1:T(8,128)S(1)} fusion(bf16[4096,4,384]{2,1,0:T(4,128)(2,1)} %param.13, bf16[96,4096]{1,0:T(8,128)(2,1)S(1)} %all_gather.3, f32[4096]{0:T(1024)S(1)} %convert_element_type.71, f32[96]{0:T(128)S(1)} %add_rsqrt_fusion), kind=kOutput, calls=%fused_computation.6 | convolution fusion | flops 1209532416 | bytes 13975936 | tf_op jit(solution)/shard_map/nk,khc->nhc/dot_general | solution.py:199
  21.4 1.6 %collective-permute-start.8 = (bf16[1,32,4,384]{3,1,0,2:T(8,128)(2,1)S(1)}, bf16[1,32,4,384]{3,1,0,2:T(8,128)(2,1)S(1)}, u32[]{:S(2)}, u32[]{:S(2)}) collective-permute-start(bf16[1,32,4,384]{3,1,0,2:T(8,128)(2,1)S(1)} %get-tuple-element.11), channel_id=1, source_target_pairs={{0,8},{8,16},{16,24},{24,28},{28,20},{20,12},{12,4},{4,0},{1,9},{9... | collective-permute-start | bytes 294920 | tf_op jit(solution)/shard_map/ppermute | solution.py:123
  23.5 1.5 %collective-permute-start.11 = (bf16[1,32,4,384]{3,1,0,2:T(8,128)(2,1)S(1)}, bf16[1,32,4,384]{3,1,0,2:T(8,128)(2,1)S(1)}, u32[]{:S(2)}, u32[]{:S(2)}) collective-permute-start(bf16[1,32,4,384]{3,1,0,2:T(8,128)(2,1)S(1)} %get-tuple-element.12), channel_id=1, source_target_pairs={{8,0},{16,8},{24,16},{28,24},{20,28},{12,20},{4,12},{0,4},{9,1},{1... | collective-permute-start | bytes 294920 | tf_op jit(solution)/shard_map/ppermute | solution.py:126
  26.3 0.7 %gather_fusion = s32[24]{0:T(128)S(1)} fusion(s32[8]{0:T(128)S(1)} %copy-done, s32[1024]{0:T(1024)S(1)} %pad_clamp_fusion.1), kind=kCustom, calls=%fused_computation | custom fusion | bytes 288 | tf_op jit(solution)/shard_map/gather | solution.py:151
  28.8 1.0 %fusion.43 = (bf16[24,16,4,128]{3,1,2,0:T(8,128)(2,1)}, bf16[24,16,4,128]{3,1,2,0:T(8,128)(2,1)S(1)}) fusion(bf16[24,16,4,256]{3,1,2,0:T(8,128)(2,1)S(1)} %bitcast.22), kind=kLoop, calls=%fused_computation.110 | loop fusion | bytes 1572864 | tf_op jit(solution)/shard_map/slice | solution.py:74
  29.8 1.6 %collective-permute-start.9 = (bf16[1,32,4,384]{3,1,0,2:T(8,128)(2,1)S(1)}, bf16[1,32,4,384]{3,1,0,2:T(8,128)(2,1)S(1)}, u32[]{:S(2)}, u32[]{:S(2)}) collective-permute-start(bf16[1,32,4,384]{3,1,0,2:T(8,128)(2,1)S(1)} %collective-permute-done.8), channel_id=1, source_target_pairs={{0,8},{8,16},{16,24},{24,28},{28,20},{20,12},{12,4},{4,0},{1,9},{9... | collective-permute-start | bytes 294920 | tf_op jit(solution)/shard_map/ppermute | solution.py:123
  31.9 1.5 %collective-permute-start.12 = (bf16[1,32,4,384]{3,1,0,2:T(8,128)(2,1)S(1)}, bf16[1,32,4,384]{3,1,0,2:T(8,128)(2,1)S(1)}, u32[]{:S(2)}, u32[]{:S(2)}) collective-permute-start(bf16[1,32,4,384]{3,1,0,2:T(8,128)(2,1)S(1)} %collective-permute-done.11), channel_id=1, source_target_pairs={{8,0},{16,8},{24,16},{28,24},{20,28},{12,20},{4,12},{0,4},{9,1},{1... | collective-permute-start | bytes 294920 | tf_op jit(solution)/shard_map/ppermute | solution.py:126
  33.9 0.7 %collective-permute-done.9 = bf16[1,32,4,384]{3,1,0,2:T(8,128)(2,1)S(1)} collective-permute-done((bf16[1,32,4,384]{3,1,0,2:T(8,128)(2,1)S(1)}, bf16[1,32,4,384]{3,1,0,2:T(8,128)(2,1)S(1)}, u32[]{:S(2)}, u32[]{:S(2)}) %collective-permute-start.9) | collective-permute-done | bytes 98336 | tf_op jit(solution)/shard_map/ppermute | solution.py:123
  34.6 2.5 %collective-permute-start.10 = (bf16[1,32,4,384]{3,1,0,2:T(8,128)(2,1)S(1)}, bf16[1,32,4,384]{3,1,0,2:T(8,128)(2,1)S(1)}, u32[]{:S(2)}, u32[]{:S(2)}) collective-permute-start(bf16[1,32,4,384]{3,1,0,2:T(8,128)(2,1)S(1)} %collective-permute-done.9), channel_id=1, source_target_pairs={{0,8},{8,16},{16,24},{24,28},{28,20},{20,12},{12,4},{4,0},{1,9},{9... | collective-permute-start | bytes 294920 | tf_op jit(solution)/shard_map/ppermute | solution.py:123
  37.6 1.4 %collective-permute-start.13 = (bf16[1,32,4,384]{3,1,0,2:T(8,128)(2,1)S(1)}, bf16[1,32,4,384]{3,1,0,2:T(8,128)(2,1)S(1)}, u32[]{:S(2)}, u32[]{:S(2)}) collective-permute-start(bf16[1,32,4,384]{3,1,0,2:T(8,128)(2,1)S(1)} %collective-permute-done.12), channel_id=1, source_target_pairs={{8,0},{16,8},{24,16},{28,24},{20,28},{12,20},{4,12},{0,4},{9,1},{1... | collective-permute-start | bytes 294920 | tf_op jit(solution)/shard_map/ppermute | solution.py:126
  39.7 2.9 %select_select_fusion.2 = bf16[16,32,4,384]{3,1,0,2:T(8,128)(2,1)S(1)} fusion(bf16[1,32,4,384]{3,1,0,2:T(8,128)(2,1)S(1)} %get-tuple-element.12, bf16[1,32,4,384]{3,1,0,2:T(8,128)(2,1)S(1)} %collective-permute-done.4, bf16[1,32,4,384]{3,1,0,2:T(8,128)(2,1)S(1)} %collective-permute-done.5, bf16[1,32,4,384]{3,1,0,2:T(8,128)(2,1)S(1)} %collective-permute-done.11, ...), kind=kLoop, calls=%fused_computation.20 | loop fusion | flops 7077888 | bytes 2556048 | tf_op jit(solution)/shard_map/jit(_where)/select_n | solution.py:172
  42.6 1.4 %collective-permute-start.3 = (bf16[1,32,4,384]{3,1,0,2:T(8,128)(2,1)S(1)}, bf16[1,32,4,384]{3,1,0,2:T(8,128)(2,1)S(1)}, u32[]{:S(2)}, u32[]{:S(2)}) collective-permute-start(bf16[1,32,4,384]{3,1,0,2:T(8,128)(2,1)S(1)} %collective-permute-done.2), channel_id=1, source_target_pairs={{8,0},{16,8},{24,16},{28,24},{20,28},{12,20},{4,12},{0,4},{9,1},{1... | collective-permute-start | bytes 294920 | tf_op jit(solution)/shard_map/ppermute | solution.py:126
  45.2 2.0 %collective-permute-done.3 = bf16[1,32,4,384]{3,1,0,2:T(8,128)(2,1)S(1)} collective-permute-done((bf16[1,32,4,384]{3,1,0,2:T(8,128)(2,1)S(1)}, bf16[1,32,4,384]{3,1,0,2:T(8,128)(2,1)S(1)}, u32[]{:S(2)}, u32[]{:S(2)}) %collective-permute-start.3) | collective-permute-done | bytes 98336 | tf_op jit(solution)/shard_map/ppermute | solution.py:126
  47.3 1.7 %collective-permute-done.7 = bf16[1,32,4,384]{3,1,0,2:T(8,128)(2,1)S(1)} collective-permute-done((bf16[1,32,4,384]{3,1,0,2:T(8,128)(2,1)S(1)}, bf16[1,32,4,384]{3,1,0,2:T(8,128)(2,1)S(1)}, u32[]{:S(2)}, u32[]{:S(2)}) %collective-permute-start.7) | collective-permute-done | bytes 98336 | tf_op jit(solution)/shard_map/ppermute | solution.py:123
  49.7 0.7 %gather_fusion.1 = bf16[24,32,4,128]{3,1,2,0:T(8,128)(2,1)S(1)} fusion(bf16[16,32,4,128]{3,1,0,2:T(8,128)(2,1)S(1)} %get-tuple-element.4, s32[1024]{0:T(1024)S(1)} %pad_clamp_fusion), kind=kCustom, calls=%fused_computation.1 | custom fusion | bytes 1572960 | tf_op jit(solution)/shard_map/gather | solution.py:211
  51.1 0.7 %gather_fusion.3 = bf16[24,32,4,128]{3,1,2,0:T(8,128)(2,1)S(1)} fusion(bf16[16,32,4,128]{3,1,0,2:T(8,128)(2,1)S(1)} %get-tuple-element.2, s32[1024]{0:T(1024)S(1)} %pad_clamp_fusion), kind=kCustom, calls=%fused_computation.3 | custom fusion | bytes 1572960 | tf_op jit(solution)/shard_map/gather | solution.py:210
  51.8 0.7 %gather_fusion.2 = bf16[24,32,4,128]{3,1,2,0:T(8,128)(2,1)S(1)} fusion(bf16[16,32,4,128]{3,1,0,2:T(8,128)(2,1)S(1)} %get-tuple-element.3, s32[1024]{0:T(1024)S(1)} %pad_clamp_fusion), kind=kCustom, calls=%fused_computation.2 | custom fusion | bytes 1572960 | tf_op jit(solution)/shard_map/gather | solution.py:212
  52.6 3.2 %fusion.47 = (f32[24,4,32]{2,1,0:T(4,128)S(1)}, f32[24,4,32,48]{3,2,1,0:T(8,128)}) fusion(bf16[24,32,4,128]{3,1,2,0:T(8,128)(2,1)S(1)} %gather_fusion.3, bf16[24,32,4,128]{3,1,2,0:T(8,128)(2,1)S(1)} %gather_fusion.1, bf16[24,16,4,128]{3,1,2,0:T(8,128)(2,1)} %get-tuple-element.5, pred[24,32,48]{2,1,0:T(8,128)(4,1)S(1)} %and_or_fusion), kind=kOutput, calls=%fused_computation.114 | convolution fusion | flops 40845360 | bytes 2605056 | tf_op jit(solution)/shard_map/sub | solution.py:41
  55.7 2.0 %fusion.8 = bf16[24,4,4,8,128]{4,3,2,1,0:T(8,128)(2,1)S(1)} fusion(bf16[24,32,4,128]{3,1,2,0:T(8,128)(2,1)S(1)} %gather_fusion.2, bf16[24,16,4,128]{3,1,2,0:T(8,128)(2,1)S(1)} %get-tuple-element.6, f32[24,4,32,48]{3,2,1,0:T(8,128)} %get-tuple-element.21, f32[24,4,32]{2,1,0:T(4,128)S(1)} %get-tuple-element.20, pred[24,32]{1,0:T(8,128)(4,1)S(1)} %iota_compare_fusion.1), kind=kOutput, calls=%fused_computation.21 | convolution fusion | flops 41189376 | bytes 2568960 | tf_op jit(solution)/shard_map/bhit,bthd->bihd/dot_general | solution.py:89
  57.8 1.0 %copy.44 = bf16[24,4,4,8,128]{4,3,1,2,0:T(8,128)(2,1)} copy(bf16[24,4,4,8,128]{4,3,2,1,0:T(8,128)(2,1)S(1)} %fusion.8) | data formatting | bytes 1572864 | tf_op jit(solution)/shard_map/convert_element_type | solution.py:92
  (71 shorter events, 9.6 us)
Async XLA Ops:
  21.0 4.7 %copy-start.1 = (s32[24]{0:T(128)S(1)}, s32[24]{0:T(128)}, u32[]{:S(2)}) copy-start(s32[24]{0:T(128)} %param.11) | copy-start | bytes 292
  21.0 4.7 %copy-start = (s32[8]{0:T(128)S(1)}, s32[8]{0:T(128)}, u32[]{:S(2)}) copy-start(s32[8]{0:T(128)} %constant.109.clone) | copy-start | bytes 100
  21.4 8.4 %collective-permute-start.8 = (bf16[1,32,4,384]{3,1,0,2:T(8,128)(2,1)S(1)}, bf16[1,32,4,384]{3,1,0,2:T(8,128)(2,1)S(1)}, u32[]{:S(2)}, u32[]{:S(2)}) collective-permute-start(bf16[1,32,4,384]{3,1,0,2:T(8,128)(2,1)S(1)} %get-tuple-element.11), channel_id=1, source_target_pairs={{0,8},{8,16},{16,24},{24,28},{28,20},{20,12},{12,4},{4,0},{1,9},{9... | collective-permute-start | bytes 294920 | tf_op jit(solution)/shard_map/ppermute | solution.py:123
  23.0 8.4 %collective-permute-start = (bf16[1,32,4,384]{3,1,0,2:T(8,128)(2,1)S(1)}, bf16[1,32,4,384]{3,1,0,2:T(8,128)(2,1)S(1)}, u32[]{:S(2)}, u32[]{:S(2)}) collective-permute-start(bf16[1,32,4,384]{3,1,0,2:T(8,128)(2,1)S(1)} %get-tuple-element.11), channel_id=1, source_target_pairs={{8,0},{16,8},{24,16},{28,24},{20,28},{12,20},{4,12},{0,4},{9,1},{1... | collective-permute-start | bytes 294920 | tf_op jit(solution)/shard_map/ppermute | solution.py:126
  23.5 8.4 %collective-permute-start.11 = (bf16[1,32,4,384]{3,1,0,2:T(8,128)(2,1)S(1)}, bf16[1,32,4,384]{3,1,0,2:T(8,128)(2,1)S(1)}, u32[]{:S(2)}, u32[]{:S(2)}) collective-permute-start(bf16[1,32,4,384]{3,1,0,2:T(8,128)(2,1)S(1)} %get-tuple-element.12), channel_id=1, source_target_pairs={{8,0},{16,8},{24,16},{28,24},{20,28},{12,20},{4,12},{0,4},{9,1},{1... | collective-permute-start | bytes 294920 | tf_op jit(solution)/shard_map/ppermute | solution.py:126
  25.0 8.4 %collective-permute-start.4 = (bf16[1,32,4,384]{3,1,0,2:T(8,128)(2,1)S(1)}, bf16[1,32,4,384]{3,1,0,2:T(8,128)(2,1)S(1)}, u32[]{:S(2)}, u32[]{:S(2)}) collective-permute-start(bf16[1,32,4,384]{3,1,0,2:T(8,128)(2,1)S(1)} %get-tuple-element.12), channel_id=1, source_target_pairs={{0,8},{8,16},{16,24},{24,28},{28,20},{20,12},{12,4},{4,0},{1,9},{9... | collective-permute-start | bytes 294920 | tf_op jit(solution)/shard_map/ppermute | solution.py:123
  29.8 4.8 %collective-permute-start.9 = (bf16[1,32,4,384]{3,1,0,2:T(8,128)(2,1)S(1)}, bf16[1,32,4,384]{3,1,0,2:T(8,128)(2,1)S(1)}, u32[]{:S(2)}, u32[]{:S(2)}) collective-permute-start(bf16[1,32,4,384]{3,1,0,2:T(8,128)(2,1)S(1)} %collective-permute-done.8), channel_id=1, source_target_pairs={{0,8},{8,16},{16,24},{24,28},{28,20},{20,12},{12,4},{4,0},{1,9},{9... | collective-permute-start | bytes 294920 | tf_op jit(solution)/shard_map/ppermute | solution.py:123
  31.4 5.7 %collective-permute-start.1 = (bf16[1,32,4,384]{3,1,0,2:T(8,128)(2,1)S(1)}, bf16[1,32,4,384]{3,1,0,2:T(8,128)(2,1)S(1)}, u32[]{:S(2)}, u32[]{:S(2)}) collective-permute-start(bf16[1,32,4,384]{3,1,0,2:T(8,128)(2,1)S(1)} %collective-permute-done), channel_id=1, source_target_pairs={{8,0},{16,8},{24,16},{28,24},{20,28},{12,20},{4,12},{0,4},{9,1},{1... | collective-permute-start | bytes 294920 | tf_op jit(solution)/shard_map/ppermute | solution.py:126
  31.9 5.8 %collective-permute-start.12 = (bf16[1,32,4,384]{3,1,0,2:T(8,128)(2,1)S(1)}, bf16[1,32,4,384]{3,1,0,2:T(8,128)(2,1)S(1)}, u32[]{:S(2)}, u32[]{:S(2)}) collective-permute-start(bf16[1,32,4,384]{3,1,0,2:T(8,128)(2,1)S(1)} %collective-permute-done.11), channel_id=1, source_target_pairs={{8,0},{16,8},{24,16},{28,24},{20,28},{12,20},{4,12},{0,4},{9,1},{1... | collective-permute-start | bytes 294920 | tf_op jit(solution)/shard_map/ppermute | solution.py:126
  33.4 5.6 %collective-permute-start.5 = (bf16[1,32,4,384]{3,1,0,2:T(8,128)(2,1)S(1)}, bf16[1,32,4,384]{3,1,0,2:T(8,128)(2,1)S(1)}, u32[]{:S(2)}, u32[]{:S(2)}) collective-permute-start(bf16[1,32,4,384]{3,1,0,2:T(8,128)(2,1)S(1)} %collective-permute-done.4), channel_id=1, source_target_pairs={{0,8},{8,16},{16,24},{24,28},{28,20},{20,12},{12,4},{4,0},{1,9},{9... | collective-permute-start | bytes 294920 | tf_op jit(solution)/shard_map/ppermute | solution.py:123
  34.6 10.1 %collective-permute-start.10 = (bf16[1,32,4,384]{3,1,0,2:T(8,128)(2,1)S(1)}, bf16[1,32,4,384]{3,1,0,2:T(8,128)(2,1)S(1)}, u32[]{:S(2)}, u32[]{:S(2)}) collective-permute-start(bf16[1,32,4,384]{3,1,0,2:T(8,128)(2,1)S(1)} %collective-permute-done.9), channel_id=1, source_target_pairs={{0,8},{8,16},{16,24},{24,28},{28,20},{20,12},{12,4},{4,0},{1,9},{9... | collective-permute-start | bytes 294920 | tf_op jit(solution)/shard_map/ppermute | solution.py:123
  37.1 5.5 %collective-permute-start.2 = (bf16[1,32,4,384]{3,1,0,2:T(8,128)(2,1)S(1)}, bf16[1,32,4,384]{3,1,0,2:T(8,128)(2,1)S(1)}, u32[]{:S(2)}, u32[]{:S(2)}) collective-permute-start(bf16[1,32,4,384]{3,1,0,2:T(8,128)(2,1)S(1)} %collective-permute-done.1), channel_id=1, source_target_pairs={{8,0},{16,8},{24,16},{28,24},{20,28},{12,20},{4,12},{0,4},{9,1},{1... | collective-permute-start | bytes 294920 | tf_op jit(solution)/shard_map/ppermute | solution.py:126
  37.6 7.0 %collective-permute-start.13 = (bf16[1,32,4,384]{3,1,0,2:T(8,128)(2,1)S(1)}, bf16[1,32,4,384]{3,1,0,2:T(8,128)(2,1)S(1)}, u32[]{:S(2)}, u32[]{:S(2)}) collective-permute-start(bf16[1,32,4,384]{3,1,0,2:T(8,128)(2,1)S(1)} %collective-permute-done.12), channel_id=1, source_target_pairs={{8,0},{16,8},{24,16},{28,24},{20,28},{12,20},{4,12},{0,4},{9,1},{1... | collective-permute-start | bytes 294920 | tf_op jit(solution)/shard_map/ppermute | solution.py:126
  39.0 5.4 %collective-permute-start.6 = (bf16[1,32,4,384]{3,1,0,2:T(8,128)(2,1)S(1)}, bf16[1,32,4,384]{3,1,0,2:T(8,128)(2,1)S(1)}, u32[]{:S(2)}, u32[]{:S(2)}) collective-permute-start(bf16[1,32,4,384]{3,1,0,2:T(8,128)(2,1)S(1)} %collective-permute-done.5), channel_id=1, source_target_pairs={{0,8},{8,16},{16,24},{24,28},{28,20},{20,12},{12,4},{4,0},{1,9},{9... | collective-permute-start | bytes 294920 | tf_op jit(solution)/shard_map/ppermute | solution.py:123
  42.6 4.7 %collective-permute-start.3 = (bf16[1,32,4,384]{3,1,0,2:T(8,128)(2,1)S(1)}, bf16[1,32,4,384]{3,1,0,2:T(8,128)(2,1)S(1)}, u32[]{:S(2)}, u32[]{:S(2)}) collective-permute-start(bf16[1,32,4,384]{3,1,0,2:T(8,128)(2,1)S(1)} %collective-permute-done.2), channel_id=1, source_target_pairs={{8,0},{16,8},{24,16},{28,24},{20,28},{12,20},{4,12},{0,4},{9,1},{1... | collective-permute-start | bytes 294920 | tf_op jit(solution)/shard_map/ppermute | solution.py:126
  44.4 4.6 %collective-permute-start.7 = (bf16[1,32,4,384]{3,1,0,2:T(8,128)(2,1)S(1)}, bf16[1,32,4,384]{3,1,0,2:T(8,128)(2,1)S(1)}, u32[]{:S(2)}, u32[]{:S(2)}) collective-permute-start(bf16[1,32,4,384]{3,1,0,2:T(8,128)(2,1)S(1)} %collective-permute-done.6), channel_id=1, source_target_pairs={{0,8},{8,16},{16,24},{24,28},{28,20},{20,12},{12,4},{4,0},{1,9},{9... | collective-permute-start | bytes 294920 | tf_op jit(solution)/shard_map/ppermute | solution.py:123

commit v13 on v12

--- a/solution.py
+++ b/solution.py
@@ -173,7 +173,7 @@
         return joined
 
     last_step = max(arrival)
-    first_join = max(last_step - 2, 0)
+    first_join = min(1, last_step)
     joined = lay(None, [(p, a) for p, a, s in zip(ordered, starts, arrival) if s <= first_join])
     for step in range(first_join + 1, last_step + 1):
         joined = lax.optimization_barrier(joined)

time: 59.1 us -> 56.8 us (0.961)
  other arithmetic: 8.59 us -> 6.58 us
    ppermute x7, starting transfers between devices: 7.67 us -> 3.32 us  [gather_store(): ahead = lax.ppermute(ahead, 'store', forward)]
    ppermute x7, starting transfers between devices: 6.76 us -> 11 us  [gather_store(): behind = lax.ppermute(behind, 'store', backward)]
    ppermute x7, waiting for transfers between devices: 2.57 us -> 1.49 us  [gather_store(): behind = lax.ppermute(behind, 'store', backward)]
    ppermute x7, waiting for transfers between devices: 2.81 us -> 3.75 us  [gather_store(): ahead = lax.ppermute(ahead, 'store', forward)]
    convert_element_type x1, other arithmetic: 0.7 us -> 0.01 us  [rms_rows(): scaled = values * lax.rsqrt(meansq + 1e-05) * norm_gain.astype(jnp.float32)]
    select_n x3 -> x4, other arithmetic: 3.79 us -> 3.12 us  [lay(): joined = jnp.where((row_at >= at) & (row_at < at + size), widened, joined)]
    ge x1, other arithmetic: 0.73 us -> 0.07 us  [local(): jnp.arange(passage_len, dtype=jnp.int32)[None, :]]
  transfers between devices with their start and end apart: 14 -> 14, of which waited for: 5 -> 5; matrix products, arithmetic and copies ran while one was open for 13% -> 12% of each run, Pallas kernels for 0% -> 0%
where the time goes in v13:
time: 56.8 us; the launch traced here: 56.6 us
  starting transfers between devices  14.3 us (25%)
  matrix products  12.4 us (22%)
  blocking collectives  10.1 us (18%)
  local copies, waits for them, and re-layouts  6.94 us (12%)
  other arithmetic  6.58 us (12%)
  waiting for transfers between devices  5.23 us (9%)
  between operations  1.02 us (2%)
    ppermute x7, starting transfers between devices, gather_store(): behind = lax.ppermute(behind, 'store', backward)  11 us
    all_gather x1, blocking collectives, local(): full_rows = lax.all_gather(all_rows, 'tp', axis=1, tiled=True)  10.1 us
    dot_general x1, matrix products, local(): jnp.einsum('nk,khc->nhc', normed, w_qkv, preferred_element_type=jnp.float32)  6.84 us
    ppermute x7, waiting for transfers between devices, gather_store(): ahead = lax.ppermute(ahead, 'store', forward)  3.75 us
    sub x2, matrix products, softmax_rounded(): expon = jnp.where(allowed, jnp.exp(masked - peak), jnp.float32(0.0))  3.34 us
    ppermute x7, starting transfers between devices, gather_store(): ahead = lax.ppermute(ahead, 'store', forward)  3.32 us
    select_n x4, other arithmetic, lay(): joined = jnp.where((row_at >= at) & (row_at < at + size), widened, joined)  3.12 us
    dot_general x1, matrix products, attend_core(): jnp.einsum('bhit,bthd->bihd', weights, values, preferred_element_type=jnp...  2.04 us
  transfers between devices with their start and end apart: 14, of which 5 were waited for; matrix products, arithmetic and copies ran while one was open for 12% of the time, Pallas kernels for 0%

profile of v13, /device:TPU:0, one launch (start us, length us, event | category | flops | bytes accessed | tf_op | source)
XLA Modules:
  0.0 56.6 jit_solution(4530825933011053165)
XLA Ops:
  0.7 0.9 %pad_maximum_fusion = bf16[96,1024]{1,0:T(8,128)(2,1)S(1)} fusion(bf16[64,1024]{1,0:T(8,128)(2,1)} %bitcast.27, bf16[32,1024]{1,0:T(8,128)(2,1)} %bitcast.28), kind=kLoop, calls=%fused_computation.45 | loop fusion | flops 393216 | bytes 393216 | tf_op jit(solution)/shard_map/concatenate | solution.py:196
  1.6 10.1 %all_gather.3 = bf16[96,4096]{1,0:T(8,128)(2,1)S(1)} all-gather(bf16[96,1024]{1,0:T(8,128)(2,1)S(1)} %pad_maximum_fusion), channel_id=1, replica_groups=mesh['store'=8,'tp'=4] {'tp'}, dimensions={1}, use_global_device_ids=true | all-gather | bytes 983040 | tf_op jit(solution)/shard_map/all_gather | solution.py:197
  12.1 6.8 %fusion.2 = f32[96,4,384]{2,0,1:T(8,128)S(1)} fusion(bf16[4096,4,384]{2,1,0:T(4,128)(2,1)} %param.13, bf16[96,4096]{1,0:T(8,128)(2,1)S(1)} %all_gather.3, f32[4096]{0:T(1024)S(1)} %convert_element_type.71, f32[96]{0:T(128)S(1)} %add_rsqrt_fusion), kind=kOutput, calls=%fused_computation.6 | convolution fusion | flops 1209532416 | bytes 13975936 | tf_op jit(solution)/shard_map/nk,khc->nhc/dot_general | solution.py:199
  20.1 1.6 %collective-permute-start.11 = (bf16[1,32,4,384]{3,1,0,2:T(8,128)(2,1)S(1)}, bf16[1,32,4,384]{3,1,0,2:T(8,128)(2,1)S(1)}, u32[]{:S(2)}, u32[]{:S(2)}) collective-permute-start(bf16[1,32,4,384]{3,1,0,2:T(8,128)(2,1)S(1)} %get-tuple-element.12), channel_id=1, source_target_pairs={{8,0},{16,8},{24,16},{28,24},{20,28},{12,20},{4,12},{0,4},{9,1},{1... | collective-permute-start | bytes 294920 | tf_op jit(solution)/shard_map/ppermute | solution.py:126
  22.2 1.5 %collective-permute-start = (bf16[1,32,4,384]{3,1,0,2:T(8,128)(2,1)S(1)}, bf16[1,32,4,384]{3,1,0,2:T(8,128)(2,1)S(1)}, u32[]{:S(2)}, u32[]{:S(2)}) collective-permute-start(bf16[1,32,4,384]{3,1,0,2:T(8,128)(2,1)S(1)} %get-tuple-element.11), channel_id=1, source_target_pairs={{8,0},{16,8},{24,16},{28,24},{20,28},{12,20},{4,12},{0,4},{9,1},{1... | collective-permute-start | bytes 294920 | tf_op jit(solution)/shard_map/ppermute | solution.py:126
  25.0 0.7 %gather_fusion = s32[24]{0:T(128)S(1)} fusion(s32[8]{0:T(128)S(1)} %copy-done, s32[1024]{0:T(1024)S(1)} %pad_clamp_fusion.1), kind=kCustom, calls=%fused_computation | custom fusion | bytes 288 | tf_op jit(solution)/shard_map/gather | solution.py:151
  25.7 0.7 %compare_select_fusion = s32[24]{0:T(128)S(1)} fusion(s32[24]{0:T(128)S(1)} %gather_fusion, s32[]{:T(128)} %bitcast.6, s32[24]{0:T(128)S(1)} %copy-done.2), kind=kLoop, calls=%fused_computation.64 | loop fusion | flops 960 | bytes 292 | tf_op jit(solution)/shard_map/select_n | solution.py:211
  26.5 1.0 %fusion.43 = (bf16[24,16,4,128]{3,1,2,0:T(8,128)(2,1)}, bf16[24,16,4,128]{3,1,2,0:T(8,128)(2,1)S(1)}) fusion(bf16[24,16,4,256]{3,1,2,0:T(8,128)(2,1)S(1)} %bitcast.22), kind=kLoop, calls=%fused_computation.111 | loop fusion | bytes 1572864 | tf_op jit(solution)/shard_map/slice | solution.py:74
  27.9 0.6 %copy.45 = bf16[2,4,2,8,128]{4,3,1,2,0:T(8,128)(2,1)} copy(bf16[2,4,2,8,128]{4,3,2,1,0:T(8,128)(2,1)S(1)} %fusion.19) | data formatting | bytes 65536 | tf_op jit(solution)/shard_map/convert_element_type | solution.py:66
  28.5 1.6 %collective-permute-start.1 = (bf16[1,32,4,384]{3,1,0,2:T(8,128)(2,1)S(1)}, bf16[1,32,4,384]{3,1,0,2:T(8,128)(2,1)S(1)}, u32[]{:S(2)}, u32[]{:S(2)}) collective-permute-start(bf16[1,32,4,384]{3,1,0,2:T(8,128)(2,1)S(1)} %collective-permute-done), channel_id=1, source_target_pairs={{8,0},{16,8},{24,16},{28,24},{20,28},{12,20},{4,12},{0,4},{9,1},{1... | collective-permute-start | bytes 294920 | tf_op jit(solution)/shard_map/ppermute | solution.py:126
  30.1 1.6 %collective-permute-start.12 = (bf16[1,32,4,384]{3,1,0,2:T(8,128)(2,1)S(1)}, bf16[1,32,4,384]{3,1,0,2:T(8,128)(2,1)S(1)}, u32[]{:S(2)}, u32[]{:S(2)}) collective-permute-start(bf16[1,32,4,384]{3,1,0,2:T(8,128)(2,1)S(1)} %collective-permute-done.11), channel_id=1, source_target_pairs={{8,0},{16,8},{24,16},{28,24},{20,28},{12,20},{4,12},{0,4},{9,1},{1... | collective-permute-start | bytes 294920 | tf_op jit(solution)/shard_map/ppermute | solution.py:126
  32.6 1.7 %select_select_fusion.3 = bf16[16,32,4,384]{3,1,0,2:T(8,128)(2,1)S(1)} fusion(bf16[1,32,4,384]{3,1,0,2:T(8,128)(2,1)S(1)} %get-tuple-element.12, bf16[1,32,4,384]{3,1,0,2:T(8,128)(2,1)S(1)} %collective-permute-done.4, bf16[1,32,4,384]{3,1,0,2:T(8,128)(2,1)S(1)} %collective-permute-done.11, bf16[1,32,4,384]{3,1,0,2:T(8,128)(2,1)S(1)} %get-tuple-element.11, ...), kind=kLoop, calls=%fused_computation.21 | loop fusion | flops 3932160 | bytes 2162768 | tf_op jit(solution)/shard_map/jit(_where)/select_n | solution.py:172
  34.3 1.6 %collective-permute-start.2 = (bf16[1,32,4,384]{3,1,0,2:T(8,128)(2,1)S(1)}, bf16[1,32,4,384]{3,1,0,2:T(8,128)(2,1)S(1)}, u32[]{:S(2)}, u32[]{:S(2)}) collective-permute-start(bf16[1,32,4,384]{3,1,0,2:T(8,128)(2,1)S(1)} %collective-permute-done.1), channel_id=1, source_target_pairs={{8,0},{16,8},{24,16},{28,24},{20,28},{12,20},{4,12},{0,4},{9,1},{1... | collective-permute-start | bytes 294920 | tf_op jit(solution)/shard_map/ppermute | solution.py:126
  36.7 1.2 %collective-permute-done.9 = bf16[1,32,4,384]{3,1,0,2:T(8,128)(2,1)S(1)} collective-permute-done((bf16[1,32,4,384]{3,1,0,2:T(8,128)(2,1)S(1)}, bf16[1,32,4,384]{3,1,0,2:T(8,128)(2,1)S(1)}, u32[]{:S(2)}, u32[]{:S(2)}) %collective-permute-start.9) | collective-permute-done | bytes 98336 | tf_op jit(solution)/shard_map/ppermute | solution.py:123
  38.4 1.6 %collective-permute-start.13 = (bf16[1,32,4,384]{3,1,0,2:T(8,128)(2,1)S(1)}, bf16[1,32,4,384]{3,1,0,2:T(8,128)(2,1)S(1)}, u32[]{:S(2)}, u32[]{:S(2)}) collective-permute-start(bf16[1,32,4,384]{3,1,0,2:T(8,128)(2,1)S(1)} %collective-permute-done.12), channel_id=1, source_target_pairs={{8,0},{16,8},{24,16},{28,24},{20,28},{12,20},{4,12},{0,4},{9,1},{1... | collective-permute-start | bytes 294920 | tf_op jit(solution)/shard_map/ppermute | solution.py:126
  40.5 1.6 %collective-permute-start.3 = (bf16[1,32,4,384]{3,1,0,2:T(8,128)(2,1)S(1)}, bf16[1,32,4,384]{3,1,0,2:T(8,128)(2,1)S(1)}, u32[]{:S(2)}, u32[]{:S(2)}) collective-permute-start(bf16[1,32,4,384]{3,1,0,2:T(8,128)(2,1)S(1)} %collective-permute-done.2), channel_id=1, source_target_pairs={{8,0},{16,8},{24,16},{28,24},{20,28},{12,20},{4,12},{0,4},{9,1},{1... | collective-permute-start | bytes 294920 | tf_op jit(solution)/shard_map/ppermute | solution.py:126
  43.7 1.5 %collective-permute-done.3 = bf16[1,32,4,384]{3,1,0,2:T(8,128)(2,1)S(1)} collective-permute-done((bf16[1,32,4,384]{3,1,0,2:T(8,128)(2,1)S(1)}, bf16[1,32,4,384]{3,1,0,2:T(8,128)(2,1)S(1)}, u32[]{:S(2)}, u32[]{:S(2)}) %collective-permute-start.3) | collective-permute-done | bytes 98336 | tf_op jit(solution)/shard_map/ppermute | solution.py:126
  45.2 1.6 %collective-permute-done.7 = bf16[1,32,4,384]{3,1,0,2:T(8,128)(2,1)S(1)} collective-permute-done((bf16[1,32,4,384]{3,1,0,2:T(8,128)(2,1)S(1)}, bf16[1,32,4,384]{3,1,0,2:T(8,128)(2,1)S(1)}, u32[]{:S(2)}, u32[]{:S(2)}) %collective-permute-start.7) | collective-permute-done | bytes 98336 | tf_op jit(solution)/shard_map/ppermute | solution.py:123
  47.5 0.7 %gather_fusion.1 = bf16[24,32,4,128]{3,1,2,0:T(8,128)(2,1)S(1)} fusion(bf16[16,32,4,128]{3,1,0,2:T(8,128)(2,1)S(1)} %get-tuple-element.4, s32[1024]{0:T(1024)S(1)} %pad_clamp_fusion), kind=kCustom, calls=%fused_computation.1 | custom fusion | bytes 1572960 | tf_op jit(solution)/shard_map/gather | solution.py:211
  48.9 0.7 %gather_fusion.3 = bf16[24,32,4,128]{3,1,2,0:T(8,128)(2,1)S(1)} fusion(bf16[16,32,4,128]{3,1,0,2:T(8,128)(2,1)S(1)} %get-tuple-element.2, s32[1024]{0:T(1024)S(1)} %pad_clamp_fusion), kind=kCustom, calls=%fused_computation.3 | custom fusion | bytes 1572960 | tf_op jit(solution)/shard_map/gather | solution.py:210
  49.6 0.7 %gather_fusion.2 = bf16[24,32,4,128]{3,1,2,0:T(8,128)(2,1)S(1)} fusion(bf16[16,32,4,128]{3,1,0,2:T(8,128)(2,1)S(1)} %get-tuple-element.3, s32[1024]{0:T(1024)S(1)} %pad_clamp_fusion), kind=kCustom, calls=%fused_computation.2 | custom fusion | bytes 1572960 | tf_op jit(solution)/shard_map/gather | solution.py:212
  50.4 3.2 %fusion.47 = (f32[24,4,32]{2,1,0:T(4,128)S(1)}, f32[24,4,32,48]{3,2,1,0:T(8,128)}) fusion(bf16[24,32,4,128]{3,1,2,0:T(8,128)(2,1)S(1)} %gather_fusion.3, bf16[24,32,4,128]{3,1,2,0:T(8,128)(2,1)S(1)} %gather_fusion.1, bf16[24,16,4,128]{3,1,2,0:T(8,128)(2,1)} %get-tuple-element.5, pred[24,32,48]{2,1,0:T(8,128)(4,1)S(1)} %and_or_fusion), kind=kOutput, calls=%fused_computation.115 | convolution fusion | flops 40845360 | bytes 2605056 | tf_op jit(solution)/shard_map/sub | solution.py:41
  53.5 2.0 %fusion.8 = bf16[24,4,4,8,128]{4,3,2,1,0:T(8,128)(2,1)S(1)} fusion(bf16[24,32,4,128]{3,1,2,0:T(8,128)(2,1)S(1)} %gather_fusion.2, bf16[24,16,4,128]{3,1,2,0:T(8,128)(2,1)S(1)} %get-tuple-element.6, f32[24,4,32,48]{3,2,1,0:T(8,128)} %get-tuple-element.21, f32[24,4,32]{2,1,0:T(4,128)S(1)} %get-tuple-element.20, pred[24,32]{1,0:T(8,128)(4,1)S(1)} %iota_compare_fusion.1), kind=kOutput, calls=%fused_computation.22 | convolution fusion | flops 41189376 | bytes 2568960 | tf_op jit(solution)/shard_map/bhit,bthd->bihd/dot_general | solution.py:89
  55.6 1.0 %copy.44 = bf16[24,4,4,8,128]{4,3,1,2,0:T(8,128)(2,1)} copy(bf16[24,4,4,8,128]{4,3,2,1,0:T(8,128)(2,1)S(1)} %fusion.8) | data formatting | bytes 1572864 | tf_op jit(solution)/shard_map/convert_element_type | solution.py:92
  (76 shorter events, 9.5 us)
Async XLA Ops:
  0.6 11.3 %copy-start.1 = (bf16[4096]{0:T(1024)(128)(2,1)S(1)}, bf16[4096]{0:T(1024)(128)(2,1)}, u32[]{:S(2)}) copy-start(bf16[4096]{0:T(1024)(128)(2,1)} %param.12) | copy-start | bytes 24580
  19.0 0.8 %copy-start.3 = (s32[2]{0:T(128)S(1)}, s32[2]{0:T(128)}, u32[]{:S(2)}) copy-start(s32[2]{0:T(128)} %param.10) | copy-start | bytes 28
  19.6 4.8 %copy-start.2 = (s32[24]{0:T(128)S(1)}, s32[24]{0:T(128)}, u32[]{:S(2)}) copy-start(s32[24]{0:T(128)} %param.11) | copy-start | bytes 292
  19.6 4.8 %copy-start = (s32[8]{0:T(128)S(1)}, s32[8]{0:T(128)}, u32[]{:S(2)}) copy-start(s32[8]{0:T(128)} %constant.109.clone) | copy-start | bytes 100
  20.1 10.0 %collective-permute-start.11 = (bf16[1,32,4,384]{3,1,0,2:T(8,128)(2,1)S(1)}, bf16[1,32,4,384]{3,1,0,2:T(8,128)(2,1)S(1)}, u32[]{:S(2)}, u32[]{:S(2)}) collective-permute-start(bf16[1,32,4,384]{3,1,0,2:T(8,128)(2,1)S(1)} %get-tuple-element.12), channel_id=1, source_target_pairs={{8,0},{16,8},{24,16},{28,24},{20,28},{12,20},{4,12},{0,4},{9,1},{1... | collective-permute-start | bytes 294920 | tf_op jit(solution)/shard_map/ppermute | solution.py:126
  21.6 10.0 %collective-permute-start.4 = (bf16[1,32,4,384]{3,1,0,2:T(8,128)(2,1)S(1)}, bf16[1,32,4,384]{3,1,0,2:T(8,128)(2,1)S(1)}, u32[]{:S(2)}, u32[]{:S(2)}) collective-permute-start(bf16[1,32,4,384]{3,1,0,2:T(8,128)(2,1)S(1)} %get-tuple-element.12), channel_id=1, source_target_pairs={{0,8},{8,16},{16,24},{24,28},{28,20},{20,12},{12,4},{4,0},{1,9},{9... | collective-permute-start | bytes 294920 | tf_op jit(solution)/shard_map/ppermute | solution.py:123
  22.2 6.3 %collective-permute-start = (bf16[1,32,4,384]{3,1,0,2:T(8,128)(2,1)S(1)}, bf16[1,32,4,384]{3,1,0,2:T(8,128)(2,1)S(1)}, u32[]{:S(2)}, u32[]{:S(2)}) collective-permute-start(bf16[1,32,4,384]{3,1,0,2:T(8,128)(2,1)S(1)} %get-tuple-element.11), channel_id=1, source_target_pairs={{8,0},{16,8},{24,16},{28,24},{20,28},{12,20},{4,12},{0,4},{9,1},{1... | collective-permute-start | bytes 294920 | tf_op jit(solution)/shard_map/ppermute | solution.py:126
  23.7 8.4 %collective-permute-start.8 = (bf16[1,32,4,384]{3,1,0,2:T(8,128)(2,1)S(1)}, bf16[1,32,4,384]{3,1,0,2:T(8,128)(2,1)S(1)}, u32[]{:S(2)}, u32[]{:S(2)}) collective-permute-start(bf16[1,32,4,384]{3,1,0,2:T(8,128)(2,1)S(1)} %get-tuple-element.11), channel_id=1, source_target_pairs={{0,8},{8,16},{16,24},{24,28},{28,20},{20,12},{12,4},{4,0},{1,9},{9... | collective-permute-start | bytes 294920 | tf_op jit(solution)/shard_map/ppermute | solution.py:123
  28.5 5.8 %collective-permute-start.1 = (bf16[1,32,4,384]{3,1,0,2:T(8,128)(2,1)S(1)}, bf16[1,32,4,384]{3,1,0,2:T(8,128)(2,1)S(1)}, u32[]{:S(2)}, u32[]{:S(2)}) collective-permute-start(bf16[1,32,4,384]{3,1,0,2:T(8,128)(2,1)S(1)} %collective-permute-done), channel_id=1, source_target_pairs={{8,0},{16,8},{24,16},{28,24},{20,28},{12,20},{4,12},{0,4},{9,1},{1... | collective-permute-start | bytes 294920 | tf_op jit(solution)/shard_map/ppermute | solution.py:126
  30.1 8.3 %collective-permute-start.12 = (bf16[1,32,4,384]{3,1,0,2:T(8,128)(2,1)S(1)}, bf16[1,32,4,384]{3,1,0,2:T(8,128)(2,1)S(1)}, u32[]{:S(2)}, u32[]{:S(2)}) collective-permute-start(bf16[1,32,4,384]{3,1,0,2:T(8,128)(2,1)S(1)} %collective-permute-done.11), channel_id=1, source_target_pairs={{8,0},{16,8},{24,16},{28,24},{20,28},{12,20},{4,12},{0,4},{9,1},{1... | collective-permute-start | bytes 294920 | tf_op jit(solution)/shard_map/ppermute | solution.py:126
  31.6 4.6 %collective-permute-start.5 = (bf16[1,32,4,384]{3,1,0,2:T(8,128)(2,1)S(1)}, bf16[1,32,4,384]{3,1,0,2:T(8,128)(2,1)S(1)}, u32[]{:S(2)}, u32[]{:S(2)}) collective-permute-start(bf16[1,32,4,384]{3,1,0,2:T(8,128)(2,1)S(1)} %collective-permute-done.4), channel_id=1, source_target_pairs={{0,8},{8,16},{16,24},{24,28},{28,20},{20,12},{12,4},{4,0},{1,9},{9... | collective-permute-start | bytes 294920 | tf_op jit(solution)/shard_map/ppermute | solution.py:123
  32.1 5.9 %collective-permute-start.9 = (bf16[1,32,4,384]{3,1,0,2:T(8,128)(2,1)S(1)}, bf16[1,32,4,384]{3,1,0,2:T(8,128)(2,1)S(1)}, u32[]{:S(2)}, u32[]{:S(2)}) collective-permute-start(bf16[1,32,4,384]{3,1,0,2:T(8,128)(2,1)S(1)} %collective-permute-done.8), channel_id=1, source_target_pairs={{0,8},{8,16},{16,24},{24,28},{28,20},{20,12},{12,4},{4,0},{1,9},{9... | collective-permute-start | bytes 294920 | tf_op jit(solution)/shard_map/ppermute | solution.py:123
  34.3 6.2 %collective-permute-start.2 = (bf16[1,32,4,384]{3,1,0,2:T(8,128)(2,1)S(1)}, bf16[1,32,4,384]{3,1,0,2:T(8,128)(2,1)S(1)}, u32[]{:S(2)}, u32[]{:S(2)}) collective-permute-start(bf16[1,32,4,384]{3,1,0,2:T(8,128)(2,1)S(1)} %collective-permute-done.1), channel_id=1, source_target_pairs={{8,0},{16,8},{24,16},{28,24},{20,28},{12,20},{4,12},{0,4},{9,1},{1... | collective-permute-start | bytes 294920 | tf_op jit(solution)/shard_map/ppermute | solution.py:126
  36.3 5.9 %collective-permute-start.6 = (bf16[1,32,4,384]{3,1,0,2:T(8,128)(2,1)S(1)}, bf16[1,32,4,384]{3,1,0,2:T(8,128)(2,1)S(1)}, u32[]{:S(2)}, u32[]{:S(2)}) collective-permute-start(bf16[1,32,4,384]{3,1,0,2:T(8,128)(2,1)S(1)} %collective-permute-done.5), channel_id=1, source_target_pairs={{0,8},{8,16},{16,24},{24,28},{28,20},{20,12},{12,4},{4,0},{1,9},{9... | collective-permute-start | bytes 294920 | tf_op jit(solution)/shard_map/ppermute | solution.py:123
  38.0 5.2 %collective-permute-start.10 = (bf16[1,32,4,384]{3,1,0,2:T(8,128)(2,1)S(1)}, bf16[1,32,4,384]{3,1,0,2:T(8,128)(2,1)S(1)}, u32[]{:S(2)}, u32[]{:S(2)}) collective-permute-start(bf16[1,32,4,384]{3,1,0,2:T(8,128)(2,1)S(1)} %collective-permute-done.9), channel_id=1, source_target_pairs={{0,8},{8,16},{16,24},{24,28},{28,20},{20,12},{12,4},{4,0},{1,9},{9... | collective-permute-start | bytes 294920 | tf_op jit(solution)/shard_map/ppermute | solution.py:123
  38.4 4.8 %collective-permute-start.13 = (bf16[1,32,4,384]{3,1,0,2:T(8,128)(2,1)S(1)}, bf16[1,32,4,384]{3,1,0,2:T(8,128)(2,1)S(1)}, u32[]{:S(2)}, u32[]{:S(2)}) collective-permute-start(bf16[1,32,4,384]{3,1,0,2:T(8,128)(2,1)S(1)} %collective-permute-done.12), channel_id=1, source_target_pairs={{8,0},{16,8},{24,16},{28,24},{20,28},{12,20},{4,12},{0,4},{9,1},{1... | collective-permute-start | bytes 294920 | tf_op jit(solution)/shard_map/ppermute | solution.py:126
  40.5 4.7 %collective-permute-start.3 = (bf16[1,32,4,384]{3,1,0,2:T(8,128)(2,1)S(1)}, bf16[1,32,4,384]{3,1,0,2:T(8,128)(2,1)S(1)}, u32[]{:S(2)}, u32[]{:S(2)}) collective-permute-start(bf16[1,32,4,384]{3,1,0,2:T(8,128)(2,1)S(1)} %collective-permute-done.2), channel_id=1, source_target_pairs={{8,0},{16,8},{24,16},{28,24},{20,28},{12,20},{4,12},{0,4},{9,1},{1... | collective-permute-start | bytes 294920 | tf_op jit(solution)/shard_map/ppermute | solution.py:126
  42.2 4.6 %collective-permute-start.7 = (bf16[1,32,4,384]{3,1,0,2:T(8,128)(2,1)S(1)}, bf16[1,32,4,384]{3,1,0,2:T(8,128)(2,1)S(1)}, u32[]{:S(2)}, u32[]{:S(2)}) collective-permute-start(bf16[1,32,4,384]{3,1,0,2:T(8,128)(2,1)S(1)} %collective-permute-done.6), channel_id=1, source_target_pairs={{0,8},{8,16},{16,24},{24,28},{28,20},{20,12},{12,4},{4,0},{1,9},{9... | collective-permute-start | bytes 294920 | tf_op jit(solution)/shard_map/ppermute | solution.py:123

commit v14 on v13

--- a/solution.py
+++ b/solution.py
@@ -143,14 +143,15 @@
         for part, step in [(parts[0], 0)] + got_ahead + got_behind:
             ordered.append(part)
             arrival.append(step)
-    place_of = jnp.asarray(place, dtype=jnp.int32)
-    mine = place_of[lax.axis_index("store")]
-    ahead_of = jnp.asarray([s[0] for s in steps], dtype=jnp.int32)
+    def place_of(s):
+        return jnp.where(s % 2 == 0, s // 2, n_store - 1 - s // 2)
+
+    mine = place_of(lax.axis_index("store"))
 
     def rows_of(rows):
-        dist = (place_of[rows // count] - mine) % n_store
+        dist = (place_of(rows // count) - mine) % n_store
         row = rows % count
-        first = ahead_of[row]
+        first = jnp.where(row % 2 == 0, n_store // 2, (n_store - 1) // 2)
         slot = jnp.where(dist == 0, 0, jnp.where(dist < n_store - first, first + dist, n_store - dist))
         return row * n_store + slot
 

time: 56.8 us -> 55.5 us (0.977)
  local copies, waits for them, and re-layouts: 6.94 us -> 5.65 us
  other arithmetic: 6.58 us -> 5.92 us
  waiting for transfers between devices: 5.23 us -> 5.83 us
    gather x1 -> x0, local copies, waits for them, and re-layouts: 0.7 us -> none  [rows_of(): dist = (place_of[rows // count] - mine) % n_store]
    select_n x1, other arithmetic: 0.67 us -> 0.03 us  [local(): pair_k = store_qkv[:, :, :, head_dim:2 * head_dim][rows]]
    dynamic_slice x1 -> x0, local copies, waits for them, and re-layouts: 0.59 us -> none  [gather_store(): mine = place_of[lax.axis_index('store')]]
  transfers between devices with their start and end apart: 14 -> 14, of which waited for: 5 -> 6; matrix products, arithmetic and copies ran while one was open for 12% -> 9% of each run, Pallas kernels for 0% -> 0%
where the time goes in v14:
time: 55.5 us; the launch traced here: 55.2 us
  starting transfers between devices  14.3 us (26%)
  matrix products  12.4 us (22%)
  blocking collectives  10.1 us (18%)
  other arithmetic  5.92 us (11%)
  waiting for transfers between devices  5.83 us (11%)
  local copies, waits for them, and re-layouts  5.65 us (10%)
  between operations  1.02 us (2%)
    ppermute x7, starting transfers between devices, gather_store(): behind = lax.ppermute(behind, 'store', backward)  11 us
    all_gather x1, blocking collectives, local(): full_rows = lax.all_gather(all_rows, 'tp', axis=1, tiled=True)  10.1 us
    dot_general x1, matrix products, local(): jnp.einsum('nk,khc->nhc', normed, w_qkv, preferred_element_type=jnp.float32)  6.84 us
    ppermute x7, waiting for transfers between devices, gather_store(): ahead = lax.ppermute(ahead, 'store', forward)  4.02 us
    sub x2, matrix products, softmax_rounded(): expon = jnp.where(allowed, jnp.exp(masked - peak), jnp.float32(0.0))  3.34 us
    ppermute x7, starting transfers between devices, gather_store(): ahead = lax.ppermute(ahead, 'store', forward)  3.34 us
    select_n x4, other arithmetic, lay(): joined = jnp.where((row_at >= at) & (row_at < at + size), widened, joined)  3.11 us
    dot_general x1, matrix products, attend_core(): jnp.einsum('bhit,bthd->bihd', weights, values, preferred_element_type=jnp...  2.04 us
  transfers between devices with their start and end apart: 14, of which 6 were waited for; matrix products, arithmetic and copies ran while one was open for 9% of the time, Pallas kernels for 0%

profile of v14, /device:TPU:0, one launch (start us, length us, event | category | flops | bytes accessed | tf_op | source)
XLA Modules:
  0.0 55.2 jit_solution(1244729767079424073)
XLA Ops:
  0.7 0.9 %pad_maximum_fusion = bf16[96,1024]{1,0:T(8,128)(2,1)S(1)} fusion(bf16[64,1024]{1,0:T(8,128)(2,1)} %bitcast.26, bf16[32,1024]{1,0:T(8,128)(2,1)} %bitcast.27), kind=kLoop, calls=%fused_computation.44 | loop fusion | flops 393216 | bytes 393216 | tf_op jit(solution)/shard_map/concatenate | solution.py:197
  1.6 10.1 %all_gather.3 = bf16[96,4096]{1,0:T(8,128)(2,1)S(1)} all-gather(bf16[96,1024]{1,0:T(8,128)(2,1)S(1)} %pad_maximum_fusion), channel_id=1, replica_groups=mesh['store'=8,'tp'=4] {'tp'}, dimensions={1}, use_global_device_ids=true | all-gather | bytes 983040 | tf_op jit(solution)/shard_map/all_gather | solution.py:198
  12.1 6.8 %fusion.2 = f32[96,4,384]{2,0,1:T(8,128)S(1)} fusion(bf16[4096,4,384]{2,1,0:T(4,128)(2,1)} %param.11, bf16[96,4096]{1,0:T(8,128)(2,1)S(1)} %all_gather.3, f32[4096]{0:T(1024)S(1)} %convert_element_type.71, f32[96]{0:T(128)S(1)} %add_rsqrt_fusion), kind=kOutput, calls=%fused_computation.5 | convolution fusion | flops 1209532416 | bytes 13975936 | tf_op jit(solution)/shard_map/nk,khc->nhc/dot_general | solution.py:200
  20.1 1.6 %collective-permute-start.11 = (bf16[1,32,4,384]{3,1,0,2:T(8,128)(2,1)S(1)}, bf16[1,32,4,384]{3,1,0,2:T(8,128)(2,1)S(1)}, u32[]{:S(2)}, u32[]{:S(2)}) collective-permute-start(bf16[1,32,4,384]{3,1,0,2:T(8,128)(2,1)S(1)} %get-tuple-element.12), channel_id=1, source_target_pairs={{8,0},{16,8},{24,16},{28,24},{20,28},{12,20},{4,12},{0,4},{9,1},{1... | collective-permute-start | bytes 294920 | tf_op jit(solution)/shard_map/ppermute | solution.py:126
  22.1 1.5 %collective-permute-start = (bf16[1,32,4,384]{3,1,0,2:T(8,128)(2,1)S(1)}, bf16[1,32,4,384]{3,1,0,2:T(8,128)(2,1)S(1)}, u32[]{:S(2)}, u32[]{:S(2)}) collective-permute-start(bf16[1,32,4,384]{3,1,0,2:T(8,128)(2,1)S(1)} %get-tuple-element.11), channel_id=1, source_target_pairs={{8,0},{16,8},{24,16},{28,24},{20,28},{12,20},{4,12},{0,4},{9,1},{1... | collective-permute-start | bytes 294920 | tf_op jit(solution)/shard_map/ppermute | solution.py:126
  24.5 1.0 %fusion.44 = (bf16[24,16,4,128]{3,1,2,0:T(8,128)(2,1)}, bf16[24,16,4,128]{3,1,2,0:T(8,128)(2,1)S(1)}) fusion(bf16[24,16,4,256]{3,1,2,0:T(8,128)(2,1)S(1)} %bitcast.21), kind=kLoop, calls=%fused_computation.117 | loop fusion | bytes 1572864 | tf_op jit(solution)/shard_map/slice | solution.py:74
  25.9 0.6 %copy.43 = bf16[2,4,2,8,128]{4,3,1,2,0:T(8,128)(2,1)} copy(bf16[2,4,2,8,128]{4,3,2,1,0:T(8,128)(2,1)S(1)} %fusion.19) | data formatting | bytes 65536 | tf_op jit(solution)/shard_map/convert_element_type | solution.py:66
  26.5 0.7 %collective-permute-done = bf16[1,32,4,384]{3,1,0,2:T(8,128)(2,1)S(1)} collective-permute-done((bf16[1,32,4,384]{3,1,0,2:T(8,128)(2,1)S(1)}, bf16[1,32,4,384]{3,1,0,2:T(8,128)(2,1)S(1)}, u32[]{:S(2)}, u32[]{:S(2)}) %collective-permute-start) | collective-permute-done | bytes 98336 | tf_op jit(solution)/shard_map/ppermute | solution.py:126
  27.3 1.5 %collective-permute-start.1 = (bf16[1,32,4,384]{3,1,0,2:T(8,128)(2,1)S(1)}, bf16[1,32,4,384]{3,1,0,2:T(8,128)(2,1)S(1)}, u32[]{:S(2)}, u32[]{:S(2)}) collective-permute-start(bf16[1,32,4,384]{3,1,0,2:T(8,128)(2,1)S(1)} %collective-permute-done), channel_id=1, source_target_pairs={{8,0},{16,8},{24,16},{28,24},{20,28},{12,20},{4,12},{0,4},{9,1},{1... | collective-permute-start | bytes 294920 | tf_op jit(solution)/shard_map/ppermute | solution.py:126
  28.8 1.6 %collective-permute-start.12 = (bf16[1,32,4,384]{3,1,0,2:T(8,128)(2,1)S(1)}, bf16[1,32,4,384]{3,1,0,2:T(8,128)(2,1)S(1)}, u32[]{:S(2)}, u32[]{:S(2)}) collective-permute-start(bf16[1,32,4,384]{3,1,0,2:T(8,128)(2,1)S(1)} %collective-permute-done.11), channel_id=1, source_target_pairs={{8,0},{16,8},{24,16},{28,24},{20,28},{12,20},{4,12},{0,4},{9,1},{1... | collective-permute-start | bytes 294920 | tf_op jit(solution)/shard_map/ppermute | solution.py:126
  31.3 1.7 %select_select_fusion.3 = bf16[16,32,4,384]{3,1,0,2:T(8,128)(2,1)S(1)} fusion(bf16[1,32,4,384]{3,1,0,2:T(8,128)(2,1)S(1)} %get-tuple-element.12, bf16[1,32,4,384]{3,1,0,2:T(8,128)(2,1)S(1)} %collective-permute-done.4, bf16[1,32,4,384]{3,1,0,2:T(8,128)(2,1)S(1)} %collective-permute-done.11, bf16[1,32,4,384]{3,1,0,2:T(8,128)(2,1)S(1)} %get-tuple-element.11, ...), kind=kLoop, calls=%fused_computation.20 | loop fusion | flops 3932160 | bytes 2162768 | tf_op jit(solution)/shard_map/jit(_where)/select_n | solution.py:173
  33.0 1.6 %collective-permute-start.2 = (bf16[1,32,4,384]{3,1,0,2:T(8,128)(2,1)S(1)}, bf16[1,32,4,384]{3,1,0,2:T(8,128)(2,1)S(1)}, u32[]{:S(2)}, u32[]{:S(2)}) collective-permute-start(bf16[1,32,4,384]{3,1,0,2:T(8,128)(2,1)S(1)} %collective-permute-done.1), channel_id=1, source_target_pairs={{8,0},{16,8},{24,16},{28,24},{20,28},{12,20},{4,12},{0,4},{9,1},{1... | collective-permute-start | bytes 294920 | tf_op jit(solution)/shard_map/ppermute | solution.py:126
  35.5 1.0 %collective-permute-done.9 = bf16[1,32,4,384]{3,1,0,2:T(8,128)(2,1)S(1)} collective-permute-done((bf16[1,32,4,384]{3,1,0,2:T(8,128)(2,1)S(1)}, bf16[1,32,4,384]{3,1,0,2:T(8,128)(2,1)S(1)}, u32[]{:S(2)}, u32[]{:S(2)}) %collective-permute-start.9) | collective-permute-done | bytes 98336 | tf_op jit(solution)/shard_map/ppermute | solution.py:123
  37.0 1.6 %collective-permute-start.13 = (bf16[1,32,4,384]{3,1,0,2:T(8,128)(2,1)S(1)}, bf16[1,32,4,384]{3,1,0,2:T(8,128)(2,1)S(1)}, u32[]{:S(2)}, u32[]{:S(2)}) collective-permute-start(bf16[1,32,4,384]{3,1,0,2:T(8,128)(2,1)S(1)} %collective-permute-done.12), channel_id=1, source_target_pairs={{8,0},{16,8},{24,16},{28,24},{20,28},{12,20},{4,12},{0,4},{9,1},{1... | collective-permute-start | bytes 294920 | tf_op jit(solution)/shard_map/ppermute | solution.py:126
  39.2 1.6 %collective-permute-start.3 = (bf16[1,32,4,384]{3,1,0,2:T(8,128)(2,1)S(1)}, bf16[1,32,4,384]{3,1,0,2:T(8,128)(2,1)S(1)}, u32[]{:S(2)}, u32[]{:S(2)}) collective-permute-start(bf16[1,32,4,384]{3,1,0,2:T(8,128)(2,1)S(1)} %collective-permute-done.2), channel_id=1, source_target_pairs={{8,0},{16,8},{24,16},{28,24},{20,28},{12,20},{4,12},{0,4},{9,1},{1... | collective-permute-start | bytes 294920 | tf_op jit(solution)/shard_map/ppermute | solution.py:126
  41.2 1.0 %collective-permute-done.10 = bf16[1,32,4,384]{3,1,0,2:T(8,128)(2,1)S(1)} collective-permute-done((bf16[1,32,4,384]{3,1,0,2:T(8,128)(2,1)S(1)}, bf16[1,32,4,384]{3,1,0,2:T(8,128)(2,1)S(1)}, u32[]{:S(2)}, u32[]{:S(2)}) %collective-permute-start.10) | collective-permute-done | bytes 98336 | tf_op jit(solution)/shard_map/ppermute | solution.py:123
  42.8 1.1 %collective-permute-done.3 = bf16[1,32,4,384]{3,1,0,2:T(8,128)(2,1)S(1)} collective-permute-done((bf16[1,32,4,384]{3,1,0,2:T(8,128)(2,1)S(1)}, bf16[1,32,4,384]{3,1,0,2:T(8,128)(2,1)S(1)}, u32[]{:S(2)}, u32[]{:S(2)}) %collective-permute-start.3) | collective-permute-done | bytes 98336 | tf_op jit(solution)/shard_map/ppermute | solution.py:126
  43.8 1.6 %collective-permute-done.7 = bf16[1,32,4,384]{3,1,0,2:T(8,128)(2,1)S(1)} collective-permute-done((bf16[1,32,4,384]{3,1,0,2:T(8,128)(2,1)S(1)}, bf16[1,32,4,384]{3,1,0,2:T(8,128)(2,1)S(1)}, u32[]{:S(2)}, u32[]{:S(2)}) %collective-permute-start.7) | collective-permute-done | bytes 98336 | tf_op jit(solution)/shard_map/ppermute | solution.py:123
  46.1 0.7 %gather_fusion = bf16[24,32,4,128]{3,1,2,0:T(8,128)(2,1)S(1)} fusion(bf16[16,32,4,128]{3,1,0,2:T(8,128)(2,1)S(1)} %get-tuple-element.4, s32[1024]{0:T(1024)S(1)} %pad_clamp_fusion), kind=kCustom, calls=%fused_computation | custom fusion | bytes 1572960 | tf_op jit(solution)/shard_map/gather | solution.py:212
  47.5 0.7 %gather_fusion.2 = bf16[24,32,4,128]{3,1,2,0:T(8,128)(2,1)S(1)} fusion(bf16[16,32,4,128]{3,1,0,2:T(8,128)(2,1)S(1)} %get-tuple-element.2, s32[1024]{0:T(1024)S(1)} %pad_clamp_fusion), kind=kCustom, calls=%fused_computation.2 | custom fusion | bytes 1572960 | tf_op jit(solution)/shard_map/gather | solution.py:211
  48.2 0.7 %gather_fusion.1 = bf16[24,32,4,128]{3,1,2,0:T(8,128)(2,1)S(1)} fusion(bf16[16,32,4,128]{3,1,0,2:T(8,128)(2,1)S(1)} %get-tuple-element.3, s32[1024]{0:T(1024)S(1)} %pad_clamp_fusion), kind=kCustom, calls=%fused_computation.1 | custom fusion | bytes 1572960 | tf_op jit(solution)/shard_map/gather | solution.py:213
  49.0 3.2 %fusion.48 = (f32[24,4,32]{2,1,0:T(4,128)S(1)}, f32[24,4,32,48]{3,2,1,0:T(8,128)}) fusion(bf16[24,32,4,128]{3,1,2,0:T(8,128)(2,1)S(1)} %gather_fusion.2, bf16[24,32,4,128]{3,1,2,0:T(8,128)(2,1)S(1)} %gather_fusion, bf16[24,16,4,128]{3,1,2,0:T(8,128)(2,1)} %get-tuple-element.5, pred[24,32,48]{2,1,0:T(8,128)(4,1)S(1)} %and_or_fusion), kind=kOutput, calls=%fused_computation.121 | convolution fusion | flops 40845360 | bytes 2605056 | tf_op jit(solution)/shard_map/sub | solution.py:41
  52.1 2.0 %fusion.8 = bf16[24,4,4,8,128]{4,3,2,1,0:T(8,128)(2,1)S(1)} fusion(bf16[24,32,4,128]{3,1,2,0:T(8,128)(2,1)S(1)} %gather_fusion.1, bf16[24,16,4,128]{3,1,2,0:T(8,128)(2,1)S(1)} %get-tuple-element.6, f32[24,4,32,48]{3,2,1,0:T(8,128)} %get-tuple-element.21, f32[24,4,32]{2,1,0:T(4,128)S(1)} %get-tuple-element.20, pred[24,32]{1,0:T(8,128)(4,1)S(1)} %iota_compare_fusion.1), kind=kOutput, calls=%fused_computation.21 | convolution fusion | flops 41189376 | bytes 2568960 | tf_op jit(solution)/shard_map/bhit,bthd->bihd/dot_general | solution.py:89
  54.2 1.0 %copy.42 = bf16[24,4,4,8,128]{4,3,1,2,0:T(8,128)(2,1)} copy(bf16[24,4,4,8,128]{4,3,2,1,0:T(8,128)(2,1)S(1)} %fusion.8) | data formatting | bytes 1572864 | tf_op jit(solution)/shard_map/convert_element_type | solution.py:92
  (70 shorter events, 8.4 us)
Async XLA Ops:
  0.6 11.3 %copy-start = (bf16[4096]{0:T(1024)(128)(2,1)S(1)}, bf16[4096]{0:T(1024)(128)(2,1)}, u32[]{:S(2)}) copy-start(bf16[4096]{0:T(1024)(128)(2,1)} %param.10) | copy-start | bytes 24580
  19.0 0.8 %copy-start.1 = (s32[2]{0:T(128)S(1)}, s32[2]{0:T(128)}, u32[]{:S(2)}) copy-start(s32[2]{0:T(128)} %param.8) | copy-start | bytes 28
  19.6 4.8 %copy-start.2 = (s32[24]{0:T(128)S(1)}, s32[24]{0:T(128)}, u32[]{:S(2)}) copy-start(s32[24]{0:T(128)} %param.9) | copy-start | bytes 292
  20.1 8.7 %collective-permute-start.11 = (bf16[1,32,4,384]{3,1,0,2:T(8,128)(2,1)S(1)}, bf16[1,32,4,384]{3,1,0,2:T(8,128)(2,1)S(1)}, u32[]{:S(2)}, u32[]{:S(2)}) collective-permute-start(bf16[1,32,4,384]{3,1,0,2:T(8,128)(2,1)S(1)} %get-tuple-element.12), channel_id=1, source_target_pairs={{8,0},{16,8},{24,16},{28,24},{20,28},{12,20},{4,12},{0,4},{9,1},{1... | collective-permute-start | bytes 294920 | tf_op jit(solution)/shard_map/ppermute | solution.py:126
  21.6 8.7 %collective-permute-start.4 = (bf16[1,32,4,384]{3,1,0,2:T(8,128)(2,1)S(1)}, bf16[1,32,4,384]{3,1,0,2:T(8,128)(2,1)S(1)}, u32[]{:S(2)}, u32[]{:S(2)}) collective-permute-start(bf16[1,32,4,384]{3,1,0,2:T(8,128)(2,1)S(1)} %get-tuple-element.12), channel_id=1, source_target_pairs={{0,8},{8,16},{16,24},{24,28},{28,20},{20,12},{12,4},{4,0},{1,9},{9... | collective-permute-start | bytes 294920 | tf_op jit(solution)/shard_map/ppermute | solution.py:123
  22.1 5.1 %collective-permute-start = (bf16[1,32,4,384]{3,1,0,2:T(8,128)(2,1)S(1)}, bf16[1,32,4,384]{3,1,0,2:T(8,128)(2,1)S(1)}, u32[]{:S(2)}, u32[]{:S(2)}) collective-permute-start(bf16[1,32,4,384]{3,1,0,2:T(8,128)(2,1)S(1)} %get-tuple-element.11), channel_id=1, source_target_pairs={{8,0},{16,8},{24,16},{28,24},{20,28},{12,20},{4,12},{0,4},{9,1},{1... | collective-permute-start | bytes 294920 | tf_op jit(solution)/shard_map/ppermute | solution.py:126
  23.7 7.2 %collective-permute-start.8 = (bf16[1,32,4,384]{3,1,0,2:T(8,128)(2,1)S(1)}, bf16[1,32,4,384]{3,1,0,2:T(8,128)(2,1)S(1)}, u32[]{:S(2)}, u32[]{:S(2)}) collective-permute-start(bf16[1,32,4,384]{3,1,0,2:T(8,128)(2,1)S(1)} %get-tuple-element.11), channel_id=1, source_target_pairs={{0,8},{8,16},{16,24},{24,28},{28,20},{20,12},{12,4},{4,0},{1,9},{9... | collective-permute-start | bytes 294920 | tf_op jit(solution)/shard_map/ppermute | solution.py:123
  27.3 5.8 %collective-permute-start.1 = (bf16[1,32,4,384]{3,1,0,2:T(8,128)(2,1)S(1)}, bf16[1,32,4,384]{3,1,0,2:T(8,128)(2,1)S(1)}, u32[]{:S(2)}, u32[]{:S(2)}) collective-permute-start(bf16[1,32,4,384]{3,1,0,2:T(8,128)(2,1)S(1)} %collective-permute-done), channel_id=1, source_target_pairs={{8,0},{16,8},{24,16},{28,24},{20,28},{12,20},{4,12},{0,4},{9,1},{1... | collective-permute-start | bytes 294920 | tf_op jit(solution)/shard_map/ppermute | solution.py:126
  28.8 8.2 %collective-permute-start.12 = (bf16[1,32,4,384]{3,1,0,2:T(8,128)(2,1)S(1)}, bf16[1,32,4,384]{3,1,0,2:T(8,128)(2,1)S(1)}, u32[]{:S(2)}, u32[]{:S(2)}) collective-permute-start(bf16[1,32,4,384]{3,1,0,2:T(8,128)(2,1)S(1)} %collective-permute-done.11), channel_id=1, source_target_pairs={{8,0},{16,8},{24,16},{28,24},{20,28},{12,20},{4,12},{0,4},{9,1},{1... | collective-permute-start | bytes 294920 | tf_op jit(solution)/shard_map/ppermute | solution.py:126
  30.4 4.7 %collective-permute-start.5 = (bf16[1,32,4,384]{3,1,0,2:T(8,128)(2,1)S(1)}, bf16[1,32,4,384]{3,1,0,2:T(8,128)(2,1)S(1)}, u32[]{:S(2)}, u32[]{:S(2)}) collective-permute-start(bf16[1,32,4,384]{3,1,0,2:T(8,128)(2,1)S(1)} %collective-permute-done.4), channel_id=1, source_target_pairs={{0,8},{8,16},{16,24},{24,28},{28,20},{20,12},{12,4},{4,0},{1,9},{9... | collective-permute-start | bytes 294920 | tf_op jit(solution)/shard_map/ppermute | solution.py:123
  30.8 5.7 %collective-permute-start.9 = (bf16[1,32,4,384]{3,1,0,2:T(8,128)(2,1)S(1)}, bf16[1,32,4,384]{3,1,0,2:T(8,128)(2,1)S(1)}, u32[]{:S(2)}, u32[]{:S(2)}) collective-permute-start(bf16[1,32,4,384]{3,1,0,2:T(8,128)(2,1)S(1)} %collective-permute-done.8), channel_id=1, source_target_pairs={{0,8},{8,16},{16,24},{24,28},{28,20},{20,12},{12,4},{4,0},{1,9},{9... | collective-permute-start | bytes 294920 | tf_op jit(solution)/shard_map/ppermute | solution.py:123
  33.0 6.1 %collective-permute-start.2 = (bf16[1,32,4,384]{3,1,0,2:T(8,128)(2,1)S(1)}, bf16[1,32,4,384]{3,1,0,2:T(8,128)(2,1)S(1)}, u32[]{:S(2)}, u32[]{:S(2)}) collective-permute-start(bf16[1,32,4,384]{3,1,0,2:T(8,128)(2,1)S(1)} %collective-permute-done.1), channel_id=1, source_target_pairs={{8,0},{16,8},{24,16},{28,24},{20,28},{12,20},{4,12},{0,4},{9,1},{1... | collective-permute-start | bytes 294920 | tf_op jit(solution)/shard_map/ppermute | solution.py:126
  35.1 5.7 %collective-permute-start.6 = (bf16[1,32,4,384]{3,1,0,2:T(8,128)(2,1)S(1)}, bf16[1,32,4,384]{3,1,0,2:T(8,128)(2,1)S(1)}, u32[]{:S(2)}, u32[]{:S(2)}) collective-permute-start(bf16[1,32,4,384]{3,1,0,2:T(8,128)(2,1)S(1)} %collective-permute-done.5), channel_id=1, source_target_pairs={{0,8},{8,16},{16,24},{24,28},{28,20},{20,12},{12,4},{4,0},{1,9},{9... | collective-permute-start | bytes 294920 | tf_op jit(solution)/shard_map/ppermute | solution.py:123
  36.6 5.6 %collective-permute-start.10 = (bf16[1,32,4,384]{3,1,0,2:T(8,128)(2,1)S(1)}, bf16[1,32,4,384]{3,1,0,2:T(8,128)(2,1)S(1)}, u32[]{:S(2)}, u32[]{:S(2)}) collective-permute-start(bf16[1,32,4,384]{3,1,0,2:T(8,128)(2,1)S(1)} %collective-permute-done.9), channel_id=1, source_target_pairs={{0,8},{8,16},{16,24},{24,28},{28,20},{20,12},{12,4},{4,0},{1,9},{9... | collective-permute-start | bytes 294920 | tf_op jit(solution)/shard_map/ppermute | solution.py:123
  37.0 5.2 %collective-permute-start.13 = (bf16[1,32,4,384]{3,1,0,2:T(8,128)(2,1)S(1)}, bf16[1,32,4,384]{3,1,0,2:T(8,128)(2,1)S(1)}, u32[]{:S(2)}, u32[]{:S(2)}) collective-permute-start(bf16[1,32,4,384]{3,1,0,2:T(8,128)(2,1)S(1)} %collective-permute-done.12), channel_id=1, source_target_pairs={{8,0},{16,8},{24,16},{28,24},{20,28},{12,20},{4,12},{0,4},{9,1},{1... | collective-permute-start | bytes 294920 | tf_op jit(solution)/shard_map/ppermute | solution.py:126
  39.2 4.7 %collective-permute-start.3 = (bf16[1,32,4,384]{3,1,0,2:T(8,128)(2,1)S(1)}, bf16[1,32,4,384]{3,1,0,2:T(8,128)(2,1)S(1)}, u32[]{:S(2)}, u32[]{:S(2)}) collective-permute-start(bf16[1,32,4,384]{3,1,0,2:T(8,128)(2,1)S(1)} %collective-permute-done.2), channel_id=1, source_target_pairs={{8,0},{16,8},{24,16},{28,24},{20,28},{12,20},{4,12},{0,4},{9,1},{1... | collective-permute-start | bytes 294920 | tf_op jit(solution)/shard_map/ppermute | solution.py:126
  40.8 4.6 %collective-permute-start.7 = (bf16[1,32,4,384]{3,1,0,2:T(8,128)(2,1)S(1)}, bf16[1,32,4,384]{3,1,0,2:T(8,128)(2,1)S(1)}, u32[]{:S(2)}, u32[]{:S(2)}) collective-permute-start(bf16[1,32,4,384]{3,1,0,2:T(8,128)(2,1)S(1)} %collective-permute-done.6), channel_id=1, source_target_pairs={{0,8},{8,16},{16,24},{24,28},{28,20},{20,12},{12,4},{4,0},{1,9},{9... | collective-permute-start | bytes 294920 | tf_op jit(solution)/shard_map/ppermute | solution.py:123

commit v15 on v14

--- a/solution.py
+++ b/solution.py
@@ -70,23 +70,21 @@
     query_len = query_kv.shape[1]
     pairs, passage_len, heads = (pair_q.shape[0], pair_q.shape[1], pair_q.shape[2])
     scale = head_dim ** (-0.5)
-    keyset = jnp.concatenate(
-        [query_kv[..., :head_dim], pair_k], axis=1
-    )
-    values = jnp.concatenate([query_kv[..., head_dim:], pair_v], axis=1)
-    scores = (
-        jnp.einsum(
-            "bihd,bthd->bhit", pair_q, keyset, preferred_element_type=jnp.float32
-        )
-        * scale
-    )
-    column = jnp.arange(query_len + passage_len, dtype=jnp.int32) - query_len
+    to_query = jnp.einsum("bihd,bthd->bhit", pair_q, query_kv[..., :head_dim], preferred_element_type=jnp.float32) * scale
+    to_own = jnp.einsum("bihd,bthd->bhit", pair_q, pair_k, preferred_element_type=jnp.float32) * scale
     row_index = jnp.arange(passage_len, dtype=jnp.int32)
-    allowed = (column[None, None, :] < 0) | (column[None, None, :] <= row_index[None, :, None]) & (
-        column[None, None, :] < pair_lengths[:, None, None]
-    )
-    weights = softmax_rounded(scores, allowed[:, None])
-    output = jnp.einsum("bhit,bthd->bihd", weights, values, preferred_element_type=jnp.float32)
+    allowed = (row_index[None, None, :] <= row_index[None, :, None]) & (row_index[None, None, :] < pair_lengths[:, None, None])
+    allowed = allowed[:, None]
+    masked = jnp.where(allowed, to_own, jnp.float32(-1e30))
+    peak = jnp.maximum(jnp.max(to_query, axis=-1, keepdims=True), jnp.max(masked, axis=-1, keepdims=True))
+    exp_query = jnp.exp(to_query - peak)
+    exp_own = jnp.where(allowed, jnp.exp(masked - peak), jnp.float32(0.0))
+    total = jnp.sum(exp_query, axis=-1, keepdims=True) + jnp.sum(exp_own, axis=-1, keepdims=True)
+    weight_query = (exp_query / total).astype(jnp.bfloat16)
+    weight_own = (exp_own / total).astype(jnp.bfloat16)
+    output = jnp.einsum("bhit,bthd->bihd", weight_query, query_kv[..., head_dim:], preferred_element_type=jnp.float32) + jnp.einsum(
+        "bhit,bthd->bihd", weight_own, pair_v, preferred_element_type=jnp.float32
+    )
     live = row_index[None, :] < pair_lengths[:, None]
     output = jnp.where(live[:, :, None, None], output, jnp.float32(0.0))
     return output.reshape(pairs, passage_len, heads * head_dim).astype(jnp.bfloat16)

time: 55.5 us -> 57.5 us (1.036)
  other arithmetic: 5.92 us -> 7.51 us
  waiting for transfers between devices: 5.83 us -> 7.08 us
    ppermute x7, starting transfers between devices: 11 us -> 2.89 us  [gather_store(): behind = lax.ppermute(behind, 'store', backward)]
    ppermute x7, starting transfers between devices: 3.34 us -> 11.2 us  [gather_store(): ahead = lax.ppermute(ahead, 'store', forward)]
    ppermute x7, waiting for transfers between devices: 1.81 us -> 6.68 us  [gather_store(): behind = lax.ppermute(behind, 'store', backward)]
    ppermute x7, waiting for transfers between devices: 4.02 us -> 0.4 us  [gather_store(): ahead = lax.ppermute(ahead, 'store', forward)]
    sub x2 -> x1, matrix products: 3.34 us -> 0.18 us  [softmax_rounded(): expon = jnp.where(allowed, jnp.exp(masked - peak), jnp.float32(0.0))]
    dot_general x1 -> x4, matrix products: 2.04 us -> 4.84 us  [the longest x1 2.06 us: attend_core(): jnp.einsum('bhit,bthd->bihd', weight_own, pair_v, preferred_element_type=...]
    reduce_sum x0 -> x2, other arithmetic: none -> 0.83 us  [the longest x1 0.55 us: attend_core(): jnp.sum(exp_own, axis=-1, keepdims=True)]
    convert_element_type x1, other arithmetic: 0.01 us -> 0.7 us  [rms_rows(): scaled = values * lax.rsqrt(meansq + 1e-05) * norm_gain.astype(jnp.float32)]
  transfers between devices with their start and end apart: 14 -> 14, of which waited for: 6 -> 3; matrix products, arithmetic and copies ran while one was open for 9% -> 7% of each run, Pallas kernels for 0% -> 0%
where the time goes in v15:
time: 57.5 us; the launch traced here: 57.2 us
  starting transfers between devices  14.1 us (25%)
  matrix products  12.1 us (21%)
  blocking collectives  10.1 us (18%)
  other arithmetic  7.51 us (13%)
  waiting for transfers between devices  7.08 us (12%)
  local copies, waits for them, and re-layouts  5.47 us (10%)
  between operations  0.97 us (2%)
    ppermute x7, starting transfers between devices, gather_store(): ahead = lax.ppermute(ahead, 'store', forward)  11.2 us
    all_gather x1, blocking collectives, local(): full_rows = lax.all_gather(all_rows, 'tp', axis=1, tiled=True)  10.1 us
    dot_general x1, matrix products, local(): jnp.einsum('nk,khc->nhc', normed, w_qkv, preferred_element_type=jnp.float32)  6.84 us
    ppermute x7, waiting for transfers between devices, gather_store(): behind = lax.ppermute(behind, 'store', backward)  6.68 us
    select_n x4, other arithmetic, lay(): joined = jnp.where((row_at >= at) & (row_at < at + size), widened, joined)  3.13 us
    ppermute x7, starting transfers between devices, gather_store(): behind = lax.ppermute(behind, 'store', backward)  2.89 us
    dot_general x1, matrix products, attend_core(): jnp.einsum('bhit,bthd->bihd', weight_own, pair_v, preferred_element_type=...  2.06 us
    dot_general x1, matrix products, attend_core(): jnp.einsum('bhit,bthd->bihd', weight_query, query_kv[..., head_dim:], pre...  1.61 us
  transfers between devices with their start and end apart: 14, of which 3 were waited for; matrix products, arithmetic and copies ran while one was open for 7% of the time, Pallas kernels for 0%

profile of v15, /device:TPU:0, one launch (start us, length us, event | category | flops | bytes accessed | tf_op | source)
XLA Modules:
  0.0 57.2 jit_solution(17295633830880650416)
XLA Ops:
  0.7 0.9 %pad_maximum_fusion = bf16[96,1024]{1,0:T(8,128)(2,1)S(1)} fusion(bf16[64,1024]{1,0:T(8,128)(2,1)} %bitcast.30, bf16[32,1024]{1,0:T(8,128)(2,1)} %bitcast.31), kind=kLoop, calls=%fused_computation.48 | loop fusion | flops 393216 | bytes 393216 | tf_op jit(solution)/shard_map/concatenate | solution.py:195
  1.6 10.1 %all_gather.3 = bf16[96,4096]{1,0:T(8,128)(2,1)S(1)} all-gather(bf16[96,1024]{1,0:T(8,128)(2,1)S(1)} %pad_maximum_fusion), channel_id=1, replica_groups=mesh['store'=8,'tp'=4] {'tp'}, dimensions={1}, use_global_device_ids=true | all-gather | bytes 983040 | tf_op jit(solution)/shard_map/all_gather | solution.py:196
  11.7 0.7 %convert_element_type.74 = f32[4096]{0:T(1024)S(1)} convert(bf16[4096]{0:T(1024)(128)(2,1)} %param.10) | non-fusion elementwise | flops 4096 | bytes 24576 | tf_op jit(solution)/shard_map/convert_element_type | solution.py:12
  12.8 6.8 %fusion.1 = f32[96,4,384]{2,0,1:T(8,128)S(1)} fusion(bf16[4096,4,384]{2,1,0:T(4,128)(2,1)} %param.11, bf16[96,4096]{1,0:T(8,128)(2,1)S(1)} %all_gather.3, f32[4096]{0:T(1024)S(1)} %convert_element_type.74, f32[96]{0:T(128)S(1)} %add_rsqrt_fusion), kind=kOutput, calls=%fused_computation.4 | convolution fusion | flops 1209532416 | bytes 13975936 | tf_op jit(solution)/shard_map/nk,khc->nhc/dot_general | solution.py:198
  20.7 1.6 %collective-permute-start.4 = (bf16[1,32,4,384]{3,1,0,2:T(8,128)(2,1)S(1)}, bf16[1,32,4,384]{3,1,0,2:T(8,128)(2,1)S(1)}, u32[]{:S(2)}, u32[]{:S(2)}) collective-permute-start(bf16[1,32,4,384]{3,1,0,2:T(8,128)(2,1)S(1)} %get-tuple-element.10), channel_id=1, source_target_pairs={{0,8},{8,16},{16,24},{24,28},{28,20},{20,12},{12,4},{4,0},{1,9},{9... | collective-permute-start | bytes 294920 | tf_op jit(solution)/shard_map/ppermute | solution.py:121
  22.8 1.6 %collective-permute-start.8 = (bf16[1,32,4,384]{3,1,0,2:T(8,128)(2,1)S(1)}, bf16[1,32,4,384]{3,1,0,2:T(8,128)(2,1)S(1)}, u32[]{:S(2)}, u32[]{:S(2)}) collective-permute-start(bf16[1,32,4,384]{3,1,0,2:T(8,128)(2,1)S(1)} %get-tuple-element.9), channel_id=1, source_target_pairs={{0,8},{8,16},{16,24},{24,28},{28,20},{20,12},{12,4},{4,0},{1,9},{9... | collective-permute-start | bytes 294920 | tf_op jit(solution)/shard_map/ppermute | solution.py:121
  25.4 0.6 %copy.46 = bf16[2,4,2,8,128]{4,3,1,2,0:T(8,128)(2,1)} copy(bf16[2,4,2,8,128]{4,3,2,1,0:T(8,128)(2,1)S(1)} %fusion.12) | data formatting | bytes 65536 | tf_op jit(solution)/shard_map/convert_element_type | solution.py:66
  26.5 1.6 %collective-permute-start.5 = (bf16[1,32,4,384]{3,1,0,2:T(8,128)(2,1)S(1)}, bf16[1,32,4,384]{3,1,0,2:T(8,128)(2,1)S(1)}, u32[]{:S(2)}, u32[]{:S(2)}) collective-permute-start(bf16[1,32,4,384]{3,1,0,2:T(8,128)(2,1)S(1)} %collective-permute-done.4), channel_id=1, source_target_pairs={{0,8},{8,16},{16,24},{24,28},{28,20},{20,12},{12,4},{4,0},{1,9},{9... | collective-permute-start | bytes 294920 | tf_op jit(solution)/shard_map/ppermute | solution.py:121
  28.5 1.6 %collective-permute-start.9 = (bf16[1,32,4,384]{3,1,0,2:T(8,128)(2,1)S(1)}, bf16[1,32,4,384]{3,1,0,2:T(8,128)(2,1)S(1)}, u32[]{:S(2)}, u32[]{:S(2)}) collective-permute-start(bf16[1,32,4,384]{3,1,0,2:T(8,128)(2,1)S(1)} %collective-permute-done.8), channel_id=1, source_target_pairs={{0,8},{8,16},{16,24},{24,28},{28,20},{20,12},{12,4},{4,0},{1,9},{9... | collective-permute-start | bytes 294920 | tf_op jit(solution)/shard_map/ppermute | solution.py:121
  30.5 1.7 %select_select_fusion.3 = bf16[16,32,4,384]{3,1,0,2:T(8,128)(2,1)S(1)} fusion(bf16[1,32,4,384]{3,1,0,2:T(8,128)(2,1)S(1)} %get-tuple-element.10, bf16[1,32,4,384]{3,1,0,2:T(8,128)(2,1)S(1)} %collective-permute-done.4, bf16[1,32,4,384]{3,1,0,2:T(8,128)(2,1)S(1)} %collective-permute-done.11, bf16[1,32,4,384]{3,1,0,2:T(8,128)(2,1)S(1)} %get-tuple-element.9, ...), kind=kLoop, calls=%fused_computation.18 | loop fusion | flops 3932160 | bytes 2162768 | tf_op jit(solution)/shard_map/jit(_where)/select_n | solution.py:171
  32.2 1.6 %collective-permute-start.6 = (bf16[1,32,4,384]{3,1,0,2:T(8,128)(2,1)S(1)}, bf16[1,32,4,384]{3,1,0,2:T(8,128)(2,1)S(1)}, u32[]{:S(2)}, u32[]{:S(2)}) collective-permute-start(bf16[1,32,4,384]{3,1,0,2:T(8,128)(2,1)S(1)} %collective-permute-done.5), channel_id=1, source_target_pairs={{0,8},{8,16},{16,24},{24,28},{28,20},{20,12},{12,4},{4,0},{1,9},{9... | collective-permute-start | bytes 294920 | tf_op jit(solution)/shard_map/ppermute | solution.py:121
  34.3 1.6 %collective-permute-start.10 = (bf16[1,32,4,384]{3,1,0,2:T(8,128)(2,1)S(1)}, bf16[1,32,4,384]{3,1,0,2:T(8,128)(2,1)S(1)}, u32[]{:S(2)}, u32[]{:S(2)}) collective-permute-start(bf16[1,32,4,384]{3,1,0,2:T(8,128)(2,1)S(1)} %collective-permute-done.9), channel_id=1, source_target_pairs={{0,8},{8,16},{16,24},{24,28},{28,20},{20,12},{12,4},{4,0},{1,9},{9... | collective-permute-start | bytes 294920 | tf_op jit(solution)/shard_map/ppermute | solution.py:121
  36.9 1.6 %collective-permute-start.7 = (bf16[1,32,4,384]{3,1,0,2:T(8,128)(2,1)S(1)}, bf16[1,32,4,384]{3,1,0,2:T(8,128)(2,1)S(1)}, u32[]{:S(2)}, u32[]{:S(2)}) collective-permute-start(bf16[1,32,4,384]{3,1,0,2:T(8,128)(2,1)S(1)} %collective-permute-done.6), channel_id=1, source_target_pairs={{0,8},{8,16},{16,24},{24,28},{28,20},{20,12},{12,4},{4,0},{1,9},{9... | collective-permute-start | bytes 294920 | tf_op jit(solution)/shard_map/ppermute | solution.py:121
  38.6 2.8 %collective-permute-done.2 = bf16[1,32,4,384]{3,1,0,2:T(8,128)(2,1)S(1)} collective-permute-done((bf16[1,32,4,384]{3,1,0,2:T(8,128)(2,1)S(1)}, bf16[1,32,4,384]{3,1,0,2:T(8,128)(2,1)S(1)}, u32[]{:S(2)}, u32[]{:S(2)}) %collective-permute-start.2) | collective-permute-done | bytes 98336 | tf_op jit(solution)/shard_map/ppermute | solution.py:124
  42.2 3.8 %collective-permute-done.3 = bf16[1,32,4,384]{3,1,0,2:T(8,128)(2,1)S(1)} collective-permute-done((bf16[1,32,4,384]{3,1,0,2:T(8,128)(2,1)S(1)}, bf16[1,32,4,384]{3,1,0,2:T(8,128)(2,1)S(1)}, u32[]{:S(2)}, u32[]{:S(2)}) %collective-permute-start.3) | collective-permute-done | bytes 98336 | tf_op jit(solution)/shard_map/ppermute | solution.py:124
  46.3 1.2 %fusion.35 = (bf16[16,32,4,128]{3,1,0,2:T(8,128)(2,1)}, bf16[16,32,4,128]{3,1,0,2:T(8,128)(2,1)S(1)}, bf16[16,32,4,128]{3,1,0,2:T(8,128)(2,1)S(1)}) fusion(bf16[16,32,4,384]{3,1,0,2:T(8,128)(2,1)S(1)} %select_select_fusion), kind=kLoop, calls=%fused_computation.113 | loop fusion | bytes 3145728 | tf_op jit(solution)/shard_map/slice | solution.py:211
  47.5 0.7 %gather_fusion.1 = bf16[24,32,4,128]{3,1,2,0:T(8,128)(2,1)S(1)} fusion(bf16[16,32,4,128]{3,1,0,2:T(8,128)(2,1)S(1)} %get-tuple-element.3, s32[1024]{0:T(1024)S(1)} %pad_clamp_fusion), kind=kCustom, calls=%fused_computation.1 | custom fusion | bytes 1572960 | tf_op jit(solution)/shard_map/gather | solution.py:209
  48.2 0.7 %gather_fusion = bf16[24,32,4,128]{3,1,2,0:T(8,128)(2,1)S(1)} fusion(bf16[16,32,4,128]{3,1,0,2:T(8,128)(2,1)S(1)} %get-tuple-element.4, s32[1024]{0:T(1024)S(1)} %pad_clamp_fusion), kind=kCustom, calls=%fused_computation | custom fusion | bytes 1572960 | tf_op jit(solution)/shard_map/gather | solution.py:210
  49.6 0.6 %fusion.39 = (f32[24,4,32]{2,1,0:T(4,128)S(1)}, f32[24,4,32,16]{2,3,1,0:T(8,128)S(1)}) fusion(bf16[24,32,4,128]{3,1,2,0:T(8,128)(2,1)S(1)} %gather_fusion.1, bf16[24,16,4,256]{3,1,2,0:T(8,128)(2,1)S(1)} %bitcast.24), kind=kOutput, calls=%fused_computation.117 | convolution fusion | flops 12678144 | bytes 1388544 | tf_op jit(solution)/shard_map/bihd,bthd->bhit/dot_general | solution.py:73
  50.4 0.6 %fusion.40 = (f32[24,4,32]{2,1,0:T(4,128)S(1)}, f32[24,4,32,32]{2,3,1,0:T(8,128)S(1)}) fusion(bf16[24,32,4,128]{3,1,2,0:T(8,128)(2,1)S(1)} %gather_fusion.1, bf16[24,32,4,128]{3,1,2,0:T(8,128)(2,1)S(1)} %gather_fusion, pred[24,32,32]{1,2,0:T(8,128)(4,1)S(1)} %broadcast_and_fusion), kind=kOutput, calls=%fused_computation.118 | convolution fusion | flops 25457664 | bytes 2002944 | tf_op jit(solution)/shard_map/bihd,bthd->bhit/dot_general | solution.py:74
  51.8 1.6 %fusion.22 = f32[24,4,128,32]{2,3,1,0:T(8,128)} fusion(f32[24,4,32,16]{2,3,1,0:T(8,128)S(1)} %get-tuple-element.19, bf16[24,16,4,256]{3,1,2,0:T(8,128)(2,1)S(1)} %bitcast.25, f32[24,4,32]{2,1,0:T(4,128)S(1)} %add.121, f32[24,4,32]{2,1,0:T(4,128)S(1)} %max.8), kind=kOutput, calls=%fused_computation.40 | convolution fusion | flops 12730368 | bytes 2850816 | tf_op jit(solution)/shard_map/bhit,bthd->bihd/dot_general | solution.py:85
  53.5 0.7 %gather_fusion.2 = bf16[24,32,4,128]{3,1,2,0:T(8,128)(2,1)S(1)} fusion(bf16[16,32,4,128]{3,1,0,2:T(8,128)(2,1)S(1)} %copy-done, s32[1024]{0:T(1024)S(1)} %pad_clamp_fusion), kind=kCustom, calls=%fused_computation.2 | custom fusion | bytes 1572960 | tf_op jit(solution)/shard_map/gather | solution.py:211
  54.2 2.1 %fusion.6 = bf16[24,4,4,8,128]{4,3,2,1,0:T(8,128)(2,1)S(1)} fusion(f32[24,4,128,32]{2,3,1,0:T(8,128)} %fusion.22, bf16[24,32,4,128]{3,1,2,0:T(8,128)(2,1)S(1)} %gather_fusion.2, f32[24,4,32,32]{2,3,1,0:T(8,128)S(1)} %get-tuple-element.21, f32[24,4,32]{2,1,0:T(4,128)S(1)} %add.121, f32[24,4,32]{2,1,0:T(4,128)S(1)} %max.8, ...), kind=kOutput, calls=%fused_computation.19 | convolution fusion | flops 26738688 | bytes 3588864 | tf_op jit(solution)/shard_map/bhit,bthd->bihd/dot_general | solution.py:85
  56.2 1.0 %copy.45 = bf16[24,4,4,8,128]{4,3,1,2,0:T(8,128)(2,1)} copy(bf16[24,4,4,8,128]{4,3,2,1,0:T(8,128)(2,1)S(1)} %fusion.6) | data formatting | bytes 1572864 | tf_op jit(solution)/shard_map/convert_element_type | solution.py:90
  (72 shorter events, 8.5 us)
Async XLA Ops:
  19.7 0.8 %copy-start.1 = (s32[2]{0:T(128)S(1)}, s32[2]{0:T(128)}, u32[]{:S(2)}) copy-start(s32[2]{0:T(128)} %param.8) | copy-start | bytes 28
  20.2 5.8 %copy-start.2 = (s32[24]{0:T(128)S(1)}, s32[24]{0:T(128)}, u32[]{:S(2)}) copy-start(s32[24]{0:T(128)} %param.9) | copy-start | bytes 292
  20.7 5.7 %collective-permute-start.4 = (bf16[1,32,4,384]{3,1,0,2:T(8,128)(2,1)S(1)}, bf16[1,32,4,384]{3,1,0,2:T(8,128)(2,1)S(1)}, u32[]{:S(2)}, u32[]{:S(2)}) collective-permute-start(bf16[1,32,4,384]{3,1,0,2:T(8,128)(2,1)S(1)} %get-tuple-element.10), channel_id=1, source_target_pairs={{0,8},{8,16},{16,24},{24,28},{28,20},{20,12},{12,4},{4,0},{1,9},{9... | collective-permute-start | bytes 294920 | tf_op jit(solution)/shard_map/ppermute | solution.py:121
  22.4 5.7 %collective-permute-start.11 = (bf16[1,32,4,384]{3,1,0,2:T(8,128)(2,1)S(1)}, bf16[1,32,4,384]{3,1,0,2:T(8,128)(2,1)S(1)}, u32[]{:S(2)}, u32[]{:S(2)}) collective-permute-start(bf16[1,32,4,384]{3,1,0,2:T(8,128)(2,1)S(1)} %get-tuple-element.10), channel_id=1, source_target_pairs={{8,0},{16,8},{24,16},{28,24},{20,28},{12,20},{4,12},{0,4},{9,1},{1... | collective-permute-start | bytes 294920 | tf_op jit(solution)/shard_map/ppermute | solution.py:124
  22.8 5.7 %collective-permute-start.8 = (bf16[1,32,4,384]{3,1,0,2:T(8,128)(2,1)S(1)}, bf16[1,32,4,384]{3,1,0,2:T(8,128)(2,1)S(1)}, u32[]{:S(2)}, u32[]{:S(2)}) collective-permute-start(bf16[1,32,4,384]{3,1,0,2:T(8,128)(2,1)S(1)} %get-tuple-element.9), channel_id=1, source_target_pairs={{0,8},{8,16},{16,24},{24,28},{28,20},{20,12},{12,4},{4,0},{1,9},{9... | collective-permute-start | bytes 294920 | tf_op jit(solution)/shard_map/ppermute | solution.py:121
  24.4 5.7 %collective-permute-start = (bf16[1,32,4,384]{3,1,0,2:T(8,128)(2,1)S(1)}, bf16[1,32,4,384]{3,1,0,2:T(8,128)(2,1)S(1)}, u32[]{:S(2)}, u32[]{:S(2)}) collective-permute-start(bf16[1,32,4,384]{3,1,0,2:T(8,128)(2,1)S(1)} %get-tuple-element.9), channel_id=1, source_target_pairs={{8,0},{16,8},{24,16},{28,24},{20,28},{12,20},{4,12},{0,4},{9,1},{1... | collective-permute-start | bytes 294920 | tf_op jit(solution)/shard_map/ppermute | solution.py:124
  26.5 5.8 %collective-permute-start.5 = (bf16[1,32,4,384]{3,1,0,2:T(8,128)(2,1)S(1)}, bf16[1,32,4,384]{3,1,0,2:T(8,128)(2,1)S(1)}, u32[]{:S(2)}, u32[]{:S(2)}) collective-permute-start(bf16[1,32,4,384]{3,1,0,2:T(8,128)(2,1)S(1)} %collective-permute-done.4), channel_id=1, source_target_pairs={{0,8},{8,16},{16,24},{24,28},{28,20},{20,12},{12,4},{4,0},{1,9},{9... | collective-permute-start | bytes 294920 | tf_op jit(solution)/shard_map/ppermute | solution.py:121
  28.0 5.8 %collective-permute-start.12 = (bf16[1,32,4,384]{3,1,0,2:T(8,128)(2,1)S(1)}, bf16[1,32,4,384]{3,1,0,2:T(8,128)(2,1)S(1)}, u32[]{:S(2)}, u32[]{:S(2)}) collective-permute-start(bf16[1,32,4,384]{3,1,0,2:T(8,128)(2,1)S(1)} %collective-permute-done.11), channel_id=1, source_target_pairs={{8,0},{16,8},{24,16},{28,24},{20,28},{12,20},{4,12},{0,4},{9,1},{1... | collective-permute-start | bytes 294920 | tf_op jit(solution)/shard_map/ppermute | solution.py:124
  28.5 5.8 %collective-permute-start.9 = (bf16[1,32,4,384]{3,1,0,2:T(8,128)(2,1)S(1)}, bf16[1,32,4,384]{3,1,0,2:T(8,128)(2,1)S(1)}, u32[]{:S(2)}, u32[]{:S(2)}) collective-permute-start(bf16[1,32,4,384]{3,1,0,2:T(8,128)(2,1)S(1)} %collective-permute-done.8), channel_id=1, source_target_pairs={{0,8},{8,16},{16,24},{24,28},{28,20},{20,12},{12,4},{4,0},{1,9},{9... | collective-permute-start | bytes 294920 | tf_op jit(solution)/shard_map/ppermute | solution.py:121
  30.1 5.8 %collective-permute-start.1 = (bf16[1,32,4,384]{3,1,0,2:T(8,128)(2,1)S(1)}, bf16[1,32,4,384]{3,1,0,2:T(8,128)(2,1)S(1)}, u32[]{:S(2)}, u32[]{:S(2)}) collective-permute-start(bf16[1,32,4,384]{3,1,0,2:T(8,128)(2,1)S(1)} %collective-permute-done), channel_id=1, source_target_pairs={{8,0},{16,8},{24,16},{28,24},{20,28},{12,20},{4,12},{0,4},{9,1},{1... | collective-permute-start | bytes 294920 | tf_op jit(solution)/shard_map/ppermute | solution.py:124
  32.2 4.7 %collective-permute-start.6 = (bf16[1,32,4,384]{3,1,0,2:T(8,128)(2,1)S(1)}, bf16[1,32,4,384]{3,1,0,2:T(8,128)(2,1)S(1)}, u32[]{:S(2)}, u32[]{:S(2)}) collective-permute-start(bf16[1,32,4,384]{3,1,0,2:T(8,128)(2,1)S(1)} %collective-permute-done.5), channel_id=1, source_target_pairs={{0,8},{8,16},{16,24},{24,28},{28,20},{20,12},{12,4},{4,0},{1,9},{9... | collective-permute-start | bytes 294920 | tf_op jit(solution)/shard_map/ppermute | solution.py:121
  33.9 7.7 %collective-permute-start.13 = (bf16[1,32,4,384]{3,1,0,2:T(8,128)(2,1)S(1)}, bf16[1,32,4,384]{3,1,0,2:T(8,128)(2,1)S(1)}, u32[]{:S(2)}, u32[]{:S(2)}) collective-permute-start(bf16[1,32,4,384]{3,1,0,2:T(8,128)(2,1)S(1)} %collective-permute-done.12), channel_id=1, source_target_pairs={{8,0},{16,8},{24,16},{28,24},{20,28},{12,20},{4,12},{0,4},{9,1},{1... | collective-permute-start | bytes 294920 | tf_op jit(solution)/shard_map/ppermute | solution.py:124
  34.3 7.3 %collective-permute-start.10 = (bf16[1,32,4,384]{3,1,0,2:T(8,128)(2,1)S(1)}, bf16[1,32,4,384]{3,1,0,2:T(8,128)(2,1)S(1)}, u32[]{:S(2)}, u32[]{:S(2)}) collective-permute-start(bf16[1,32,4,384]{3,1,0,2:T(8,128)(2,1)S(1)} %collective-permute-done.9), channel_id=1, source_target_pairs={{0,8},{8,16},{16,24},{24,28},{28,20},{20,12},{12,4},{4,0},{1,9},{9... | collective-permute-start | bytes 294920 | tf_op jit(solution)/shard_map/ppermute | solution.py:121
  35.9 5.5 %collective-permute-start.2 = (bf16[1,32,4,384]{3,1,0,2:T(8,128)(2,1)S(1)}, bf16[1,32,4,384]{3,1,0,2:T(8,128)(2,1)S(1)}, u32[]{:S(2)}, u32[]{:S(2)}) collective-permute-start(bf16[1,32,4,384]{3,1,0,2:T(8,128)(2,1)S(1)} %collective-permute-done.1), channel_id=1, source_target_pairs={{8,0},{16,8},{24,16},{28,24},{20,28},{12,20},{4,12},{0,4},{9,1},{1... | collective-permute-start | bytes 294920 | tf_op jit(solution)/shard_map/ppermute | solution.py:124
  36.9 5.2 %collective-permute-start.7 = (bf16[1,32,4,384]{3,1,0,2:T(8,128)(2,1)S(1)}, bf16[1,32,4,384]{3,1,0,2:T(8,128)(2,1)S(1)}, u32[]{:S(2)}, u32[]{:S(2)}) collective-permute-start(bf16[1,32,4,384]{3,1,0,2:T(8,128)(2,1)S(1)} %collective-permute-done.6), channel_id=1, source_target_pairs={{0,8},{8,16},{16,24},{24,28},{28,20},{20,12},{12,4},{4,0},{1,9},{9... | collective-permute-start | bytes 294920 | tf_op jit(solution)/shard_map/ppermute | solution.py:121
  41.4 4.6 %collective-permute-start.3 = (bf16[1,32,4,384]{3,1,0,2:T(8,128)(2,1)S(1)}, bf16[1,32,4,384]{3,1,0,2:T(8,128)(2,1)S(1)}, u32[]{:S(2)}, u32[]{:S(2)}) collective-permute-start(bf16[1,32,4,384]{3,1,0,2:T(8,128)(2,1)S(1)} %collective-permute-done.2), channel_id=1, source_target_pairs={{8,0},{16,8},{24,16},{28,24},{20,28},{12,20},{4,12},{0,4},{9,1},{1... | collective-permute-start | bytes 294920 | tf_op jit(solution)/shard_map/ppermute | solution.py:124
  51.8 1.6 %copy-start = (bf16[16,32,4,128]{3,1,0,2:T(8,128)(2,1)S(1)}, bf16[16,32,4,128]{3,1,0,2:T(8,128)(2,1)}, u32[]{:S(2)}) copy-start(bf16[16,32,4,128]{3,1,0,2:T(8,128)(2,1)} %get-tuple-element.2) | copy-start | bytes 1572868

commit v16 on v14

--- a/solution.py
+++ b/solution.py
@@ -108,41 +108,59 @@
         place[s] = i
     forward = [(ring[i], ring[(i + 1) % n_store]) for i in range(n_store)]
     backward = [(ring[(i + 1) % n_store], ring[i]) for i in range(n_store)]
-    steps = []
-    pieces = []
-    for row in range(count):
-        ahead_steps = n_store // 2 if row % 2 == 0 else (n_store - 1) // 2
-        behind_steps = n_store - 1 - ahead_steps
-        steps.append((ahead_steps, behind_steps))
-        piece = own[row : row + 1]
-        parts = [piece]
-        ahead = piece
-        behind = piece
-        for k in range(max(ahead_steps, behind_steps)):
-            if k < ahead_steps:
-                ahead = lax.ppermute(ahead, "store", forward)
-                parts.append(ahead)
-            if k < behind_steps:
-                behind = lax.ppermute(behind, "store", backward)
-                parts.append(behind)
-        pieces.append(parts)
-    ordered = []
-    arrival = []
-    for row in range(count):
-        ahead_steps, behind_steps = steps[row]
-        parts = pieces[row]
-        got_ahead, got_behind = [], []
-        at = 1
-        for k in range(max(ahead_steps, behind_steps)):
-            if k < ahead_steps:
-                got_ahead.append((parts[at], k + 1))
-                at += 1
-            if k < behind_steps:
-                got_behind.append((parts[at], k + 1))
-                at += 1
-        for part, step in [(parts[0], 0)] + got_ahead + got_behind:
+    half = n_store // 2
+    if count == 2:
+        ordered = [own]
+        arrival = [0]
+        ahead_parts, behind_parts = [], []
+        ahead = own
+        behind = own
+        for k in range(1, half):
+            ahead = lax.ppermute(ahead, "store", forward)
+            behind = lax.ppermute(behind, "store", backward)
+            ahead_parts.append((ahead, k))
+            behind_parts.append((behind, k))
+        ahead_parts.append((lax.ppermute(ahead[0:1], "store", forward), half))
+        behind_parts.append((lax.ppermute(behind[1:2], "store", backward), half))
+        for part, step in ahead_parts[:-1] + behind_parts[:-1] + [ahead_parts[-1], behind_parts[-1]]:
             ordered.append(part)
             arrival.append(step)
+    else:
+        steps = []
+        pieces = []
+        for row in range(count):
+            ahead_steps = n_store // 2 if row % 2 == 0 else (n_store - 1) // 2
+            behind_steps = n_store - 1 - ahead_steps
+            steps.append((ahead_steps, behind_steps))
+            piece = own[row : row + 1]
+            parts = [piece]
+            ahead = piece
+            behind = piece
+            for k in range(max(ahead_steps, behind_steps)):
+                if k < ahead_steps:
+                    ahead = lax.ppermute(ahead, "store", forward)
+                    parts.append(ahead)
+                if k < behind_steps:
+                    behind = lax.ppermute(behind, "store", backward)
+                    parts.append(behind)
+            pieces.append(parts)
+        ordered = []
+        arrival = []
+        for row in range(count):
+            ahead_steps, behind_steps = steps[row]
+            parts = pieces[row]
+            got_ahead, got_behind = [], []
+            at = 1
+            for k in range(max(ahead_steps, behind_steps)):
+                if k < ahead_steps:
+                    got_ahead.append((parts[at], k + 1))
+                    at += 1
+                if k < behind_steps:
+                    got_behind.append((parts[at], k + 1))
+                    at += 1
+            for part, step in [(parts[0], 0)] + got_ahead + got_behind:
+                ordered.append(part)
+                arrival.append(step)
     def place_of(s):
         return jnp.where(s % 2 == 0, s // 2, n_store - 1 - s // 2)
 
@@ -151,6 +169,9 @@
     def rows_of(rows):
         dist = (place_of(rows // count) - mine) % n_store
         row = rows % count
+        if count == 2:
+            far = jnp.where(dist > half, 2 * (n_store - dist), 2 * half + 2 * (dist - 1))
+            return jnp.where(dist == 0, row, jnp.where(dist == half, 4 * half - 2, far) + row)
         first = jnp.where(row % 2 == 0, n_store // 2, (n_store - 1) // 2)
         slot = jnp.where(dist == 0, 0, jnp.where(dist < n_store - first, first + dist, n_store - dist))
         return row * n_store + slot

time: 55.5 us -> 55.5 us (level)
  waiting for transfers between devices: 5.83 us -> 14.1 us
  starting transfers between devices: 14.3 us -> 8.26 us
  other arithmetic: 5.92 us -> 3.92 us
    ppermute x7 -> x3, waiting for transfers between devices: 1.81 us -> 10.3 us  [gather_store(): behind = lax.ppermute(behind, 'store', backward)]
    ppermute x7 -> x3, starting transfers between devices: 11 us -> 4.6 us  [gather_store(): behind = lax.ppermute(behind, 'store', backward)]
    ppermute x7 -> x3, waiting for transfers between devices: 4.02 us -> 0.01 us  [gather_store(): ahead = lax.ppermute(ahead, 'store', forward)]
    ppermute x0 -> x2, waiting for transfers between devices: none -> 3.77 us  [the longest x1 2.18 us: gather_store(): behind_parts.append((lax.ppermute(behind[1:2], 'store', backward), half))]
    ppermute x0 -> x2, starting transfers between devices: none -> 2.13 us  [the longest x1 1.57 us: gather_store(): behind_parts.append((lax.ppermute(behind[1:2], 'store', backward), half))]
    select_n x4, other arithmetic: 3.11 us -> 1.13 us  [lay(): joined = jnp.where((row_at >= at) & (row_at < at + size), widened, joined)]
    ppermute x7 -> x3, starting transfers between devices: 3.34 us -> 1.53 us  [gather_store(): ahead = lax.ppermute(ahead, 'store', forward)]
  transfers between devices with their start and end apart: 14 -> 8, of which waited for: 6 -> 5; matrix products, arithmetic and copies ran while one was open for 9% -> 5% of each run, Pallas kernels for 0% -> 0%
where the time goes in v16:
time: 55.5 us; the launch traced here: 55.2 us
  waiting for transfers between devices  14.1 us (25%)
  matrix products  12.5 us (23%)
  blocking collectives  10.1 us (18%)
  starting transfers between devices  8.26 us (15%)
  local copies, waits for them, and re-layouts  5.48 us (10%)
  other arithmetic  3.92 us (7%)
  between operations  0.96 us (2%)
    ppermute x3, waiting for transfers between devices, gather_store(): behind = lax.ppermute(behind, 'store', backward)  10.3 us
    all_gather x1, blocking collectives, local(): full_rows = lax.all_gather(all_rows, 'tp', axis=1, tiled=True)  10.1 us
    dot_general x1, matrix products, local(): jnp.einsum('nk,khc->nhc', normed, w_qkv, preferred_element_type=jnp.float32)  6.86 us
    ppermute x3, starting transfers between devices, gather_store(): behind = lax.ppermute(behind, 'store', backward)  4.6 us
    sub x2, matrix products, softmax_rounded(): expon = jnp.where(allowed, jnp.exp(masked - peak), jnp.float32(0.0))  3.34 us
    ppermute x1, waiting for transfers between devices, gather_store(): behind_parts.append((lax.ppermute(behind[1:2], 'store', backward), half))  2.18 us
    dot_general x1, matrix products, attend_core(): jnp.einsum('bhit,bthd->bihd', weights, values, preferred_element_type=jnp...  2.05 us
    ppermute x1, waiting for transfers between devices, gather_store(): ahead_parts.append((lax.ppermute(ahead[0:1], 'store', forward), half))  1.59 us
  transfers between devices with their start and end apart: 8, of which 5 were waited for; matrix products, arithmetic and copies ran while one was open for 5% of the time, Pallas kernels for 0%

profile of v16, /device:TPU:0, one launch (start us, length us, event | category | flops | bytes accessed | tf_op | source)
XLA Modules:
  0.0 55.2 jit_solution(13059434423321654292)
XLA Ops:
  0.7 0.9 %pad_maximum_fusion = bf16[96,1024]{1,0:T(8,128)(2,1)S(1)} fusion(bf16[64,1024]{1,0:T(8,128)(2,1)} %bitcast.26, bf16[32,1024]{1,0:T(8,128)(2,1)} %bitcast.27), kind=kLoop, calls=%fused_computation.44 | loop fusion | flops 393216 | bytes 393216 | tf_op jit(solution)/shard_map/concatenate | solution.py:218
  1.6 10.1 %all_gather.3 = bf16[96,4096]{1,0:T(8,128)(2,1)S(1)} all-gather(bf16[96,1024]{1,0:T(8,128)(2,1)S(1)} %pad_maximum_fusion), channel_id=1, replica_groups=mesh['store'=8,'tp'=4] {'tp'}, dimensions={1}, use_global_device_ids=true | all-gather | bytes 983040 | tf_op jit(solution)/shard_map/all_gather | solution.py:219
  12.1 6.9 %fusion.2 = f32[96,4,384]{2,0,1:T(8,128)S(1)} fusion(bf16[4096,4,384]{2,1,0:T(4,128)(2,1)} %param.11, bf16[96,4096]{1,0:T(8,128)(2,1)S(1)} %all_gather.3, f32[4096]{0:T(1024)S(1)} %convert_element_type.57, f32[96]{0:T(128)S(1)} %add_rsqrt_fusion), kind=kOutput, calls=%fused_computation.5 | convolution fusion | flops 1209532416 | bytes 13975936 | tf_op jit(solution)/shard_map/nk,khc->nhc/dot_general | solution.py:221
  20.1 1.6 %collective-permute-start = (bf16[2,32,4,384]{3,1,0,2:T(8,128)(2,1)S(1)}, bf16[2,32,4,384]{3,1,0,2:T(8,128)(2,1)S(1)}, u32[]{:S(2)}, u32[]{:S(2)}) collective-permute-start(bf16[2,32,4,384]{3,1,0,2:T(8,128)(2,1)S(1)} %and_select_fusion), channel_id=1, source_target_pairs={{8,0},{16,8},{24,16},{28,24},{20,28},{12,20},{4,12},{0,4},{9,1},{1... | collective-permute-start | bytes 589832 | tf_op jit(solution)/shard_map/ppermute | solution.py:120
  22.5 0.9 %fusion.42 = (bf16[24,16,4,128]{3,1,2,0:T(8,128)(2,1)}, bf16[24,16,4,128]{3,1,2,0:T(8,128)(2,1)S(1)}) fusion(bf16[24,16,4,256]{3,1,2,0:T(8,128)(2,1)S(1)} %bitcast.21), kind=kLoop, calls=%fused_computation.105 | loop fusion | bytes 1572864 | tf_op jit(solution)/shard_map/slice | solution.py:74
  23.7 0.6 %copy.43 = bf16[2,4,2,8,128]{4,3,1,2,0:T(8,128)(2,1)} copy(bf16[2,4,2,8,128]{4,3,2,1,0:T(8,128)(2,1)S(1)} %fusion.19) | data formatting | bytes 65536 | tf_op jit(solution)/shard_map/convert_element_type | solution.py:66
  24.4 2.9 %collective-permute-done = bf16[2,32,4,384]{3,1,0,2:T(8,128)(2,1)S(1)} collective-permute-done((bf16[2,32,4,384]{3,1,0,2:T(8,128)(2,1)S(1)}, bf16[2,32,4,384]{3,1,0,2:T(8,128)(2,1)S(1)}, u32[]{:S(2)}, u32[]{:S(2)}) %collective-permute-start) | collective-permute-done | bytes 196640 | tf_op jit(solution)/shard_map/ppermute | solution.py:120
  27.3 1.5 %collective-permute-start.1 = (bf16[2,32,4,384]{3,1,0,2:T(8,128)(2,1)S(1)}, bf16[2,32,4,384]{3,1,0,2:T(8,128)(2,1)S(1)}, u32[]{:S(2)}, u32[]{:S(2)}) collective-permute-start(bf16[2,32,4,384]{3,1,0,2:T(8,128)(2,1)S(1)} %collective-permute-done), channel_id=1, source_target_pairs={{8,0},{16,8},{24,16},{28,24},{20,28},{12,20},{4,12},{0,4},{9,1},{1... | collective-permute-start | bytes 589832 | tf_op jit(solution)/shard_map/ppermute | solution.py:120
  28.8 0.5 collective-permute-start.5
  29.4 4.1 %collective-permute-done.1 = bf16[2,32,4,384]{3,1,0,2:T(8,128)(2,1)S(1)} collective-permute-done((bf16[2,32,4,384]{3,1,0,2:T(8,128)(2,1)S(1)}, bf16[2,32,4,384]{3,1,0,2:T(8,128)(2,1)S(1)}, u32[]{:S(2)}, u32[]{:S(2)}) %collective-permute-start.1) | collective-permute-done | bytes 196640 | tf_op jit(solution)/shard_map/ppermute | solution.py:120
  33.6 1.5 %collective-permute-start.2 = (bf16[2,32,4,384]{3,1,0,2:T(8,128)(2,1)S(1)}, bf16[2,32,4,384]{3,1,0,2:T(8,128)(2,1)S(1)}, u32[]{:S(2)}, u32[]{:S(2)}) collective-permute-start(bf16[2,32,4,384]{3,1,0,2:T(8,128)(2,1)S(1)} %collective-permute-done.1), channel_id=1, source_target_pairs={{8,0},{16,8},{24,16},{28,24},{20,28},{12,20},{4,12},{0,4},{9,1},{1... | collective-permute-start | bytes 589832 | tf_op jit(solution)/shard_map/ppermute | solution.py:120
  35.1 0.5 collective-permute-start.6
  35.9 3.3 %collective-permute-done.2 = bf16[2,32,4,384]{3,1,0,2:T(8,128)(2,1)S(1)} collective-permute-done((bf16[2,32,4,384]{3,1,0,2:T(8,128)(2,1)S(1)}, bf16[2,32,4,384]{3,1,0,2:T(8,128)(2,1)S(1)}, u32[]{:S(2)}, u32[]{:S(2)}) %collective-permute-start.2) | collective-permute-done | bytes 196640 | tf_op jit(solution)/shard_map/ppermute | solution.py:120
  39.2 1.6 %collective-permute-start.3 = (bf16[1,32,4,384]{3,1,0,2:T(8,128)(2,1)S(1)}, bf16[1,32,4,384]{3,1,0,2:T(8,128)(2,1)S(1)}, u32[]{:S(2)}, u32[]{:S(2)}) collective-permute-start(bf16[1,32,4,384]{3,1,0,2:T(8,128)(2,1)S(1)} %slice.99), channel_id=1, source_target_pairs={{8,0},{16,8},{24,16},{28,24},{20,28},{12,20},{4,12},{0,4},{9,1},{1... | collective-permute-start | bytes 294920 | tf_op jit(solution)/shard_map/ppermute | solution.py:124
  40.8 0.6 %collective-permute-start.7 = (bf16[1,32,4,384]{3,1,0,2:T(8,128)(2,1)S(1)}, bf16[1,32,4,384]{3,1,0,2:T(8,128)(2,1)S(1)}, u32[]{:S(2)}, u32[]{:S(2)}) collective-permute-start(bf16[1,32,4,384]{3,1,0,2:T(8,128)(2,1)S(1)} %slice.100), channel_id=1, source_target_pairs={{0,8},{8,16},{16,24},{24,28},{28,20},{20,12},{12,4},{4,0},{1,9},{9... | collective-permute-start | bytes 294920 | tf_op jit(solution)/shard_map/ppermute | solution.py:123
  41.7 2.2 %collective-permute-done.3 = bf16[1,32,4,384]{3,1,0,2:T(8,128)(2,1)S(1)} collective-permute-done((bf16[1,32,4,384]{3,1,0,2:T(8,128)(2,1)S(1)}, bf16[1,32,4,384]{3,1,0,2:T(8,128)(2,1)S(1)}, u32[]{:S(2)}, u32[]{:S(2)}) %collective-permute-start.3) | collective-permute-done | bytes 98336 | tf_op jit(solution)/shard_map/ppermute | solution.py:124
  43.9 1.6 %collective-permute-done.7 = bf16[1,32,4,384]{3,1,0,2:T(8,128)(2,1)S(1)} collective-permute-done((bf16[1,32,4,384]{3,1,0,2:T(8,128)(2,1)S(1)}, bf16[1,32,4,384]{3,1,0,2:T(8,128)(2,1)S(1)}, u32[]{:S(2)}, u32[]{:S(2)}) %collective-permute-start.7) | collective-permute-done | bytes 98336 | tf_op jit(solution)/shard_map/ppermute | solution.py:123
  46.1 0.7 %gather_fusion = bf16[24,32,4,128]{3,1,2,0:T(8,128)(2,1)S(1)} fusion(bf16[16,32,4,128]{3,1,0,2:T(8,128)(2,1)S(1)} %get-tuple-element.4, s32[1024]{0:T(1024)S(1)} %pad_clamp_fusion), kind=kCustom, calls=%fused_computation | custom fusion | bytes 1572960 | tf_op jit(solution)/shard_map/gather | solution.py:233
  46.8 0.5 convert_reduce_fusion
  47.5 0.7 %gather_fusion.2 = bf16[24,32,4,128]{3,1,2,0:T(8,128)(2,1)S(1)} fusion(bf16[16,32,4,128]{3,1,0,2:T(8,128)(2,1)S(1)} %get-tuple-element.2, s32[1024]{0:T(1024)S(1)} %pad_clamp_fusion), kind=kCustom, calls=%fused_computation.2 | custom fusion | bytes 1572960 | tf_op jit(solution)/shard_map/gather | solution.py:232
  48.2 0.7 %gather_fusion.1 = bf16[24,32,4,128]{3,1,2,0:T(8,128)(2,1)S(1)} fusion(bf16[16,32,4,128]{3,1,0,2:T(8,128)(2,1)S(1)} %get-tuple-element.3, s32[1024]{0:T(1024)S(1)} %pad_clamp_fusion), kind=kCustom, calls=%fused_computation.1 | custom fusion | bytes 1572960 | tf_op jit(solution)/shard_map/gather | solution.py:234
  49.0 3.2 %fusion.45 = (f32[24,4,32]{2,1,0:T(4,128)S(1)}, f32[24,4,32,48]{3,2,1,0:T(8,128)}) fusion(bf16[24,32,4,128]{3,1,2,0:T(8,128)(2,1)S(1)} %gather_fusion.2, bf16[24,32,4,128]{3,1,2,0:T(8,128)(2,1)S(1)} %gather_fusion, bf16[24,16,4,128]{3,1,2,0:T(8,128)(2,1)} %get-tuple-element.5, pred[24,32,48]{2,1,0:T(8,128)(4,1)S(1)} %and_or_fusion), kind=kOutput, calls=%fused_computation.108 | convolution fusion | flops 40845360 | bytes 2605056 | tf_op jit(solution)/shard_map/sub | solution.py:41
  52.1 2.1 %fusion.8 = bf16[24,4,4,8,128]{4,3,2,1,0:T(8,128)(2,1)S(1)} fusion(bf16[24,32,4,128]{3,1,2,0:T(8,128)(2,1)S(1)} %gather_fusion.1, bf16[24,16,4,128]{3,1,2,0:T(8,128)(2,1)S(1)} %get-tuple-element.6, f32[24,4,32,48]{3,2,1,0:T(8,128)} %get-tuple-element.19, f32[24,4,32]{2,1,0:T(4,128)S(1)} %get-tuple-element.18, pred[24,32]{1,0:T(8,128)(4,1)S(1)} %iota_compare_fusion.1), kind=kOutput, calls=%fused_computation.21 | convolution fusion | flops 41189376 | bytes 2568960 | tf_op jit(solution)/shard_map/bhit,bthd->bihd/dot_general | solution.py:89
  54.2 1.0 %copy.42 = bf16[24,4,4,8,128]{4,3,1,2,0:T(8,128)(2,1)} copy(bf16[24,4,4,8,128]{4,3,2,1,0:T(8,128)(2,1)S(1)} %fusion.8) | data formatting | bytes 1572864 | tf_op jit(solution)/shard_map/convert_element_type | solution.py:92
  (55 shorter events, 4.2 us)
Async XLA Ops:
  0.6 11.3 %copy-start = (bf16[4096]{0:T(1024)(128)(2,1)S(1)}, bf16[4096]{0:T(1024)(128)(2,1)}, u32[]{:S(2)}) copy-start(bf16[4096]{0:T(1024)(128)(2,1)} %param.10) | copy-start | bytes 24580
  19.0 0.8 %copy-start.1 = (s32[2]{0:T(128)S(1)}, s32[2]{0:T(128)}, u32[]{:S(2)}) copy-start(s32[2]{0:T(128)} %param.8) | copy-start | bytes 28
  19.4 2.9 %copy-start.2 = (s32[24]{0:T(128)S(1)}, s32[24]{0:T(128)}, u32[]{:S(2)}) copy-start(s32[24]{0:T(128)} %param.9) | copy-start | bytes 292
  20.1 7.2 %collective-permute-start = (bf16[2,32,4,384]{3,1,0,2:T(8,128)(2,1)S(1)}, bf16[2,32,4,384]{3,1,0,2:T(8,128)(2,1)S(1)}, u32[]{:S(2)}, u32[]{:S(2)}) collective-permute-start(bf16[2,32,4,384]{3,1,0,2:T(8,128)(2,1)S(1)} %and_select_fusion), channel_id=1, source_target_pairs={{8,0},{16,8},{24,16},{28,24},{20,28},{12,20},{4,12},{0,4},{9,1},{1... | collective-permute-start | bytes 589832 | tf_op jit(solution)/shard_map/ppermute | solution.py:120
  21.6 7.2 %collective-permute-start.4 = (bf16[2,32,4,384]{3,1,0,2:T(8,128)(2,1)S(1)}, bf16[2,32,4,384]{3,1,0,2:T(8,128)(2,1)S(1)}, u32[]{:S(2)}, u32[]{:S(2)}) collective-permute-start(bf16[2,32,4,384]{3,1,0,2:T(8,128)(2,1)S(1)} %and_select_fusion), channel_id=1, source_target_pairs={{0,8},{8,16},{16,24},{24,28},{28,20},{20,12},{12,4},{4,0},{1,9},{9... | collective-permute-start | bytes 589832 | tf_op jit(solution)/shard_map/ppermute | solution.py:119
  27.3 6.3 %collective-permute-start.1 = (bf16[2,32,4,384]{3,1,0,2:T(8,128)(2,1)S(1)}, bf16[2,32,4,384]{3,1,0,2:T(8,128)(2,1)S(1)}, u32[]{:S(2)}, u32[]{:S(2)}) collective-permute-start(bf16[2,32,4,384]{3,1,0,2:T(8,128)(2,1)S(1)} %collective-permute-done), channel_id=1, source_target_pairs={{8,0},{16,8},{24,16},{28,24},{20,28},{12,20},{4,12},{0,4},{9,1},{1... | collective-permute-start | bytes 589832 | tf_op jit(solution)/shard_map/ppermute | solution.py:120
  28.8 6.3 %collective-permute-start.5 = (bf16[2,32,4,384]{3,1,0,2:T(8,128)(2,1)S(1)}, bf16[2,32,4,384]{3,1,0,2:T(8,128)(2,1)S(1)}, u32[]{:S(2)}, u32[]{:S(2)}) collective-permute-start(bf16[2,32,4,384]{3,1,0,2:T(8,128)(2,1)S(1)} %collective-permute-done.4), channel_id=1, source_target_pairs={{0,8},{8,16},{16,24},{24,28},{28,20},{20,12},{12,4},{4,0},{1,9},{9... | collective-permute-start | bytes 589832 | tf_op jit(solution)/shard_map/ppermute | solution.py:119
  33.6 5.7 %collective-permute-start.2 = (bf16[2,32,4,384]{3,1,0,2:T(8,128)(2,1)S(1)}, bf16[2,32,4,384]{3,1,0,2:T(8,128)(2,1)S(1)}, u32[]{:S(2)}, u32[]{:S(2)}) collective-permute-start(bf16[2,32,4,384]{3,1,0,2:T(8,128)(2,1)S(1)} %collective-permute-done.1), channel_id=1, source_target_pairs={{8,0},{16,8},{24,16},{28,24},{20,28},{12,20},{4,12},{0,4},{9,1},{1... | collective-permute-start | bytes 589832 | tf_op jit(solution)/shard_map/ppermute | solution.py:120
  35.1 5.7 %collective-permute-start.6 = (bf16[2,32,4,384]{3,1,0,2:T(8,128)(2,1)S(1)}, bf16[2,32,4,384]{3,1,0,2:T(8,128)(2,1)S(1)}, u32[]{:S(2)}, u32[]{:S(2)}) collective-permute-start(bf16[2,32,4,384]{3,1,0,2:T(8,128)(2,1)S(1)} %collective-permute-done.5), channel_id=1, source_target_pairs={{0,8},{8,16},{16,24},{24,28},{28,20},{20,12},{12,4},{4,0},{1,9},{9... | collective-permute-start | bytes 589832 | tf_op jit(solution)/shard_map/ppermute | solution.py:119
  39.2 4.7 %collective-permute-start.3 = (bf16[1,32,4,384]{3,1,0,2:T(8,128)(2,1)S(1)}, bf16[1,32,4,384]{3,1,0,2:T(8,128)(2,1)S(1)}, u32[]{:S(2)}, u32[]{:S(2)}) collective-permute-start(bf16[1,32,4,384]{3,1,0,2:T(8,128)(2,1)S(1)} %slice.99), channel_id=1, source_target_pairs={{8,0},{16,8},{24,16},{28,24},{20,28},{12,20},{4,12},{0,4},{9,1},{1... | collective-permute-start | bytes 294920 | tf_op jit(solution)/shard_map/ppermute | solution.py:124
  40.8 4.7 %collective-permute-start.7 = (bf16[1,32,4,384]{3,1,0,2:T(8,128)(2,1)S(1)}, bf16[1,32,4,384]{3,1,0,2:T(8,128)(2,1)S(1)}, u32[]{:S(2)}, u32[]{:S(2)}) collective-permute-start(bf16[1,32,4,384]{3,1,0,2:T(8,128)(2,1)S(1)} %slice.100), channel_id=1, source_target_pairs={{0,8},{8,16},{16,24},{24,28},{28,20},{20,12},{12,4},{4,0},{1,9},{9... | collective-permute-start | bytes 294920 | tf_op jit(solution)/shard_map/ppermute | solution.py:123

commit v17 on v14

--- a/solution.py
+++ b/solution.py
@@ -195,9 +195,13 @@
     passage_pos = query_len + jnp.tile(jnp.arange(passage_len, dtype=jnp.float32), pass_count)
     query_total = quer_count * query_len
     all_rows = jnp.concatenate([query_rows, passage_rows], axis=0)
-    full_rows = lax.all_gather(all_rows, "tp", axis=1, tiled=True)
-    normed = rms_rows(full_rows, norm_gain)
-    raw = jnp.einsum("nk,khc->nhc", normed, w_qkv, preferred_element_type=jnp.float32)
+    n_tp = lax.axis_size("tp")
+    blocks = lax.all_gather(all_rows, "tp", axis=0, tiled=False).astype(jnp.float32)
+    meansq = jnp.mean(blocks * blocks, axis=(0, 2))
+    gain = norm_gain.astype(jnp.float32).reshape(n_tp, 1, width_part)
+    normed = (blocks * lax.rsqrt(meansq + 1e-05)[None, :, None] * gain).astype(jnp.bfloat16)
+    w_blocks = w_qkv.reshape(n_tp, width_part, heads_part, 3 * head_dim)
+    raw = jnp.einsum("tnk,tkhc->nhc", normed, w_blocks, preferred_element_type=jnp.float32)
     projected = rotate_parts(raw, jnp.concatenate([query_pos, passage_pos], axis=0), head_dim)
     query_qkv = projected[:query_total].reshape(quer_count, query_len, heads_part, 3 * head_dim)
     own_qkv = projected[query_total:].reshape(pass_count, passage_len, heads_part, 3 * head_dim)

time: 55.5 us -> 55.5 us (level)
  no operation moved by 1% of the time
where the time goes in v17:
time: 55.5 us; the launch traced here: 55.2 us
  starting transfers between devices  14.3 us (26%)
  matrix products  12.4 us (22%)
  blocking collectives  10.1 us (18%)
  other arithmetic  5.92 us (11%)
  waiting for transfers between devices  5.84 us (11%)
  local copies, waits for them, and re-layouts  5.66 us (10%)
  between operations  1.01 us (2%)
    ppermute x7, starting transfers between devices, gather_store(): behind = lax.ppermute(behind, 'store', backward)  11 us
    all_gather x1, blocking collectives, local(): lax.all_gather(all_rows, 'tp', axis=0, tiled=False).astype(jnp.float32)  10.1 us
    dot_general x1, matrix products, local(): jnp.einsum('tnk,tkhc->nhc', normed, w_blocks, preferred_element_type=jnp....  6.84 us
    ppermute x7, waiting for transfers between devices, gather_store(): ahead = lax.ppermute(ahead, 'store', forward)  4.02 us
    sub x2, matrix products, softmax_rounded(): expon = jnp.where(allowed, jnp.exp(masked - peak), jnp.float32(0.0))  3.34 us
    ppermute x7, starting transfers between devices, gather_store(): ahead = lax.ppermute(ahead, 'store', forward)  3.33 us
    select_n x4, other arithmetic, lay(): joined = jnp.where((row_at >= at) & (row_at < at + size), widened, joined)  3.11 us
    dot_general x1, matrix products, attend_core(): jnp.einsum('bhit,bthd->bihd', weights, values, preferred_element_type=jnp...  2.04 us
  transfers between devices with their start and end apart: 14, of which 6 were waited for; matrix products, arithmetic and copies ran while one was open for 9% of the time, Pallas kernels for 0%

profile of v17, /device:TPU:0, one launch (start us, length us, event | category | flops | bytes accessed | tf_op | source)
XLA Modules:
  0.0 55.2 jit_solution(2324394245160798100)
XLA Ops:
  0.7 0.9 %pad_maximum_fusion = bf16[96,1024]{1,0:T(8,128)(2,1)S(1)} fusion(bf16[64,1024]{1,0:T(8,128)(2,1)} %bitcast.34, bf16[32,1024]{1,0:T(8,128)(2,1)} %bitcast.35), kind=kLoop, calls=%fused_computation.45 | loop fusion | flops 393216 | bytes 393216 | tf_op jit(solution)/shard_map/concatenate | solution.py:197
  1.6 10.1 %all-gather = bf16[384,1024]{1,0:T(8,128)(2,1)S(1)} all-gather(bf16[96,1024]{1,0:T(8,128)(2,1)S(1)} %pad_maximum_fusion), channel_id=2, replica_groups=mesh['store'=8,'tp'=4] {'tp'}, dimensions={0}, use_global_device_ids=true | all-gather | bytes 983040 | tf_op jit(solution)/shard_map/all_gather | solution.py:199
  12.1 6.8 %fusion.9 = f32[96,4,384]{2,0,1:T(8,128)S(1)} fusion(bf16[4,1024,4,384]{3,2,1,0:T(4,128)(2,1)} %bitcast.37, bf16[4,96,1024]{2,1,0:T(8,128)(2,1)S(1)} %bitcast.29, f32[4,1024]{1,0:T(4,128)S(1)} %reshape.214, f32[96]{0:T(128)S(1)} %add_rsqrt_fusion), kind=kOutput, calls=%fused_computation.22 | convolution fusion | flops 1209532416 | bytes 13975936 | tf_op jit(solution)/shard_map/tnk,tkhc->nhc/dot_general | solution.py:204
  20.1 1.6 %collective-permute-start.11 = (bf16[1,32,4,384]{3,1,0,2:T(8,128)(2,1)S(1)}, bf16[1,32,4,384]{3,1,0,2:T(8,128)(2,1)S(1)}, u32[]{:S(2)}, u32[]{:S(2)}) collective-permute-start(bf16[1,32,4,384]{3,1,0,2:T(8,128)(2,1)S(1)} %get-tuple-element.12), channel_id=1, source_target_pairs={{8,0},{16,8},{24,16},{28,24},{20,28},{12,20},{4,12},{0,4},{9,1},{1... | collective-permute-start | bytes 294920 | tf_op jit(solution)/shard_map/ppermute | solution.py:126
  22.1 1.5 %collective-permute-start = (bf16[1,32,4,384]{3,1,0,2:T(8,128)(2,1)S(1)}, bf16[1,32,4,384]{3,1,0,2:T(8,128)(2,1)S(1)}, u32[]{:S(2)}, u32[]{:S(2)}) collective-permute-start(bf16[1,32,4,384]{3,1,0,2:T(8,128)(2,1)S(1)} %get-tuple-element.11), channel_id=1, source_target_pairs={{8,0},{16,8},{24,16},{28,24},{20,28},{12,20},{4,12},{0,4},{9,1},{1... | collective-permute-start | bytes 294920 | tf_op jit(solution)/shard_map/ppermute | solution.py:126
  24.6 1.0 %fusion.47 = (bf16[24,16,4,128]{3,1,2,0:T(8,128)(2,1)}, bf16[24,16,4,128]{3,1,2,0:T(8,128)(2,1)S(1)}) fusion(bf16[24,16,4,256]{3,1,2,0:T(8,128)(2,1)S(1)} %bitcast.27), kind=kLoop, calls=%fused_computation.118 | loop fusion | bytes 1572864 | tf_op jit(solution)/shard_map/slice | solution.py:74
  25.9 0.6 %copy.46 = bf16[2,4,2,8,128]{4,3,1,2,0:T(8,128)(2,1)} copy(bf16[2,4,2,8,128]{4,3,2,1,0:T(8,128)(2,1)S(1)} %fusion.22) | data formatting | bytes 65536 | tf_op jit(solution)/shard_map/convert_element_type | solution.py:66
  26.5 0.7 %collective-permute-done = bf16[1,32,4,384]{3,1,0,2:T(8,128)(2,1)S(1)} collective-permute-done((bf16[1,32,4,384]{3,1,0,2:T(8,128)(2,1)S(1)}, bf16[1,32,4,384]{3,1,0,2:T(8,128)(2,1)S(1)}, u32[]{:S(2)}, u32[]{:S(2)}) %collective-permute-start) | collective-permute-done | bytes 98336 | tf_op jit(solution)/shard_map/ppermute | solution.py:126
  27.3 1.5 %collective-permute-start.1 = (bf16[1,32,4,384]{3,1,0,2:T(8,128)(2,1)S(1)}, bf16[1,32,4,384]{3,1,0,2:T(8,128)(2,1)S(1)}, u32[]{:S(2)}, u32[]{:S(2)}) collective-permute-start(bf16[1,32,4,384]{3,1,0,2:T(8,128)(2,1)S(1)} %collective-permute-done), channel_id=1, source_target_pairs={{8,0},{16,8},{24,16},{28,24},{20,28},{12,20},{4,12},{0,4},{9,1},{1... | collective-permute-start | bytes 294920 | tf_op jit(solution)/shard_map/ppermute | solution.py:126
  28.8 1.6 %collective-permute-start.12 = (bf16[1,32,4,384]{3,1,0,2:T(8,128)(2,1)S(1)}, bf16[1,32,4,384]{3,1,0,2:T(8,128)(2,1)S(1)}, u32[]{:S(2)}, u32[]{:S(2)}) collective-permute-start(bf16[1,32,4,384]{3,1,0,2:T(8,128)(2,1)S(1)} %collective-permute-done.11), channel_id=1, source_target_pairs={{8,0},{16,8},{24,16},{28,24},{20,28},{12,20},{4,12},{0,4},{9,1},{1... | collective-permute-start | bytes 294920 | tf_op jit(solution)/shard_map/ppermute | solution.py:126
  31.3 1.7 %select_select_fusion.3 = bf16[16,32,4,384]{3,1,0,2:T(8,128)(2,1)S(1)} fusion(bf16[1,32,4,384]{3,1,0,2:T(8,128)(2,1)S(1)} %get-tuple-element.12, bf16[1,32,4,384]{3,1,0,2:T(8,128)(2,1)S(1)} %collective-permute-done.4, bf16[1,32,4,384]{3,1,0,2:T(8,128)(2,1)S(1)} %collective-permute-done.11, bf16[1,32,4,384]{3,1,0,2:T(8,128)(2,1)S(1)} %get-tuple-element.11, ...), kind=kLoop, calls=%fused_computation.20 | loop fusion | flops 3932160 | bytes 2162768 | tf_op jit(solution)/shard_map/jit(_where)/select_n | solution.py:173
  33.1 1.6 %collective-permute-start.2 = (bf16[1,32,4,384]{3,1,0,2:T(8,128)(2,1)S(1)}, bf16[1,32,4,384]{3,1,0,2:T(8,128)(2,1)S(1)}, u32[]{:S(2)}, u32[]{:S(2)}) collective-permute-start(bf16[1,32,4,384]{3,1,0,2:T(8,128)(2,1)S(1)} %collective-permute-done.1), channel_id=1, source_target_pairs={{8,0},{16,8},{24,16},{28,24},{20,28},{12,20},{4,12},{0,4},{9,1},{1... | collective-permute-start | bytes 294920 | tf_op jit(solution)/shard_map/ppermute | solution.py:126
  35.5 1.0 %collective-permute-done.9 = bf16[1,32,4,384]{3,1,0,2:T(8,128)(2,1)S(1)} collective-permute-done((bf16[1,32,4,384]{3,1,0,2:T(8,128)(2,1)S(1)}, bf16[1,32,4,384]{3,1,0,2:T(8,128)(2,1)S(1)}, u32[]{:S(2)}, u32[]{:S(2)}) %collective-permute-start.9) | collective-permute-done | bytes 98336 | tf_op jit(solution)/shard_map/ppermute | solution.py:123
  37.0 1.6 %collective-permute-start.13 = (bf16[1,32,4,384]{3,1,0,2:T(8,128)(2,1)S(1)}, bf16[1,32,4,384]{3,1,0,2:T(8,128)(2,1)S(1)}, u32[]{:S(2)}, u32[]{:S(2)}) collective-permute-start(bf16[1,32,4,384]{3,1,0,2:T(8,128)(2,1)S(1)} %collective-permute-done.12), channel_id=1, source_target_pairs={{8,0},{16,8},{24,16},{28,24},{20,28},{12,20},{4,12},{0,4},{9,1},{1... | collective-permute-start | bytes 294920 | tf_op jit(solution)/shard_map/ppermute | solution.py:126
  39.2 1.6 %collective-permute-start.3 = (bf16[1,32,4,384]{3,1,0,2:T(8,128)(2,1)S(1)}, bf16[1,32,4,384]{3,1,0,2:T(8,128)(2,1)S(1)}, u32[]{:S(2)}, u32[]{:S(2)}) collective-permute-start(bf16[1,32,4,384]{3,1,0,2:T(8,128)(2,1)S(1)} %collective-permute-done.2), channel_id=1, source_target_pairs={{8,0},{16,8},{24,16},{28,24},{20,28},{12,20},{4,12},{0,4},{9,1},{1... | collective-permute-start | bytes 294920 | tf_op jit(solution)/shard_map/ppermute | solution.py:126
  41.2 1.0 %collective-permute-done.10 = bf16[1,32,4,384]{3,1,0,2:T(8,128)(2,1)S(1)} collective-permute-done((bf16[1,32,4,384]{3,1,0,2:T(8,128)(2,1)S(1)}, bf16[1,32,4,384]{3,1,0,2:T(8,128)(2,1)S(1)}, u32[]{:S(2)}, u32[]{:S(2)}) %collective-permute-start.10) | collective-permute-done | bytes 98336 | tf_op jit(solution)/shard_map/ppermute | solution.py:123
  42.8 1.1 %collective-permute-done.3 = bf16[1,32,4,384]{3,1,0,2:T(8,128)(2,1)S(1)} collective-permute-done((bf16[1,32,4,384]{3,1,0,2:T(8,128)(2,1)S(1)}, bf16[1,32,4,384]{3,1,0,2:T(8,128)(2,1)S(1)}, u32[]{:S(2)}, u32[]{:S(2)}) %collective-permute-start.3) | collective-permute-done | bytes 98336 | tf_op jit(solution)/shard_map/ppermute | solution.py:126
  43.8 1.6 %collective-permute-done.7 = bf16[1,32,4,384]{3,1,0,2:T(8,128)(2,1)S(1)} collective-permute-done((bf16[1,32,4,384]{3,1,0,2:T(8,128)(2,1)S(1)}, bf16[1,32,4,384]{3,1,0,2:T(8,128)(2,1)S(1)}, u32[]{:S(2)}, u32[]{:S(2)}) %collective-permute-start.7) | collective-permute-done | bytes 98336 | tf_op jit(solution)/shard_map/ppermute | solution.py:123
  46.1 0.7 %gather_fusion = bf16[24,32,4,128]{3,1,2,0:T(8,128)(2,1)S(1)} fusion(bf16[16,32,4,128]{3,1,0,2:T(8,128)(2,1)S(1)} %get-tuple-element.4, s32[1024]{0:T(1024)S(1)} %pad_clamp_fusion), kind=kCustom, calls=%fused_computation | custom fusion | bytes 1572960 | tf_op jit(solution)/shard_map/gather | solution.py:216
  47.5 0.7 %gather_fusion.2 = bf16[24,32,4,128]{3,1,2,0:T(8,128)(2,1)S(1)} fusion(bf16[16,32,4,128]{3,1,0,2:T(8,128)(2,1)S(1)} %get-tuple-element.2, s32[1024]{0:T(1024)S(1)} %pad_clamp_fusion), kind=kCustom, calls=%fused_computation.2 | custom fusion | bytes 1572960 | tf_op jit(solution)/shard_map/gather | solution.py:215
  48.2 0.7 %gather_fusion.1 = bf16[24,32,4,128]{3,1,2,0:T(8,128)(2,1)S(1)} fusion(bf16[16,32,4,128]{3,1,0,2:T(8,128)(2,1)S(1)} %get-tuple-element.3, s32[1024]{0:T(1024)S(1)} %pad_clamp_fusion), kind=kCustom, calls=%fused_computation.1 | custom fusion | bytes 1572960 | tf_op jit(solution)/shard_map/gather | solution.py:217
  49.0 3.2 %fusion.51 = (f32[24,4,32]{2,1,0:T(4,128)S(1)}, f32[24,4,32,48]{3,2,1,0:T(8,128)}) fusion(bf16[24,32,4,128]{3,1,2,0:T(8,128)(2,1)S(1)} %gather_fusion.2, bf16[24,32,4,128]{3,1,2,0:T(8,128)(2,1)S(1)} %gather_fusion, bf16[24,16,4,128]{3,1,2,0:T(8,128)(2,1)} %get-tuple-element.5, pred[24,32,48]{2,1,0:T(8,128)(4,1)S(1)} %and_or_fusion), kind=kOutput, calls=%fused_computation.122 | convolution fusion | flops 40845360 | bytes 2605056 | tf_op jit(solution)/shard_map/sub | solution.py:41
  52.1 2.0 %fusion.8 = bf16[24,4,4,8,128]{4,3,2,1,0:T(8,128)(2,1)S(1)} fusion(bf16[24,32,4,128]{3,1,2,0:T(8,128)(2,1)S(1)} %gather_fusion.1, bf16[24,16,4,128]{3,1,2,0:T(8,128)(2,1)S(1)} %get-tuple-element.6, f32[24,4,32,48]{3,2,1,0:T(8,128)} %get-tuple-element.21, f32[24,4,32]{2,1,0:T(4,128)S(1)} %get-tuple-element.20, pred[24,32]{1,0:T(8,128)(4,1)S(1)} %iota_compare_fusion.1), kind=kOutput, calls=%fused_computation.21 | convolution fusion | flops 41189376 | bytes 2568960 | tf_op jit(solution)/shard_map/bhit,bthd->bihd/dot_general | solution.py:89
  54.2 1.0 %copy.45 = bf16[24,4,4,8,128]{4,3,1,2,0:T(8,128)(2,1)} copy(bf16[24,4,4,8,128]{4,3,2,1,0:T(8,128)(2,1)S(1)} %fusion.8) | data formatting | bytes 1572864 | tf_op jit(solution)/shard_map/convert_element_type | solution.py:92
  (70 shorter events, 8.4 us)
Async XLA Ops:
  0.6 11.3 %copy-start = (bf16[4096]{0:T(1024)(128)(2,1)S(1)}, bf16[4096]{0:T(1024)(128)(2,1)}, u32[]{:S(2)}) copy-start(bf16[4096]{0:T(1024)(128)(2,1)} %param.10) | copy-start | bytes 24580
  19.0 0.8 %copy-start.1 = (s32[2]{0:T(128)S(1)}, s32[2]{0:T(128)}, u32[]{:S(2)}) copy-start(s32[2]{0:T(128)} %param.8) | copy-start | bytes 28
  19.6 4.8 %copy-start.2 = (s32[24]{0:T(128)S(1)}, s32[24]{0:T(128)}, u32[]{:S(2)}) copy-start(s32[24]{0:T(128)} %param.9) | copy-start | bytes 292
  20.1 8.7 %collective-permute-start.11 = (bf16[1,32,4,384]{3,1,0,2:T(8,128)(2,1)S(1)}, bf16[1,32,4,384]{3,1,0,2:T(8,128)(2,1)S(1)}, u32[]{:S(2)}, u32[]{:S(2)}) collective-permute-start(bf16[1,32,4,384]{3,1,0,2:T(8,128)(2,1)S(1)} %get-tuple-element.12), channel_id=1, source_target_pairs={{8,0},{16,8},{24,16},{28,24},{20,28},{12,20},{4,12},{0,4},{9,1},{1... | collective-permute-start | bytes 294920 | tf_op jit(solution)/shard_map/ppermute | solution.py:126
  21.6 8.7 %collective-permute-start.4 = (bf16[1,32,4,384]{3,1,0,2:T(8,128)(2,1)S(1)}, bf16[1,32,4,384]{3,1,0,2:T(8,128)(2,1)S(1)}, u32[]{:S(2)}, u32[]{:S(2)}) collective-permute-start(bf16[1,32,4,384]{3,1,0,2:T(8,128)(2,1)S(1)} %get-tuple-element.12), channel_id=1, source_target_pairs={{0,8},{8,16},{16,24},{24,28},{28,20},{20,12},{12,4},{4,0},{1,9},{9... | collective-permute-start | bytes 294920 | tf_op jit(solution)/shard_map/ppermute | solution.py:123
  22.1 5.1 %collective-permute-start = (bf16[1,32,4,384]{3,1,0,2:T(8,128)(2,1)S(1)}, bf16[1,32,4,384]{3,1,0,2:T(8,128)(2,1)S(1)}, u32[]{:S(2)}, u32[]{:S(2)}) collective-permute-start(bf16[1,32,4,384]{3,1,0,2:T(8,128)(2,1)S(1)} %get-tuple-element.11), channel_id=1, source_target_pairs={{8,0},{16,8},{24,16},{28,24},{20,28},{12,20},{4,12},{0,4},{9,1},{1... | collective-permute-start | bytes 294920 | tf_op jit(solution)/shard_map/ppermute | solution.py:126
  23.7 7.2 %collective-permute-start.8 = (bf16[1,32,4,384]{3,1,0,2:T(8,128)(2,1)S(1)}, bf16[1,32,4,384]{3,1,0,2:T(8,128)(2,1)S(1)}, u32[]{:S(2)}, u32[]{:S(2)}) collective-permute-start(bf16[1,32,4,384]{3,1,0,2:T(8,128)(2,1)S(1)} %get-tuple-element.11), channel_id=1, source_target_pairs={{0,8},{8,16},{16,24},{24,28},{28,20},{20,12},{12,4},{4,0},{1,9},{9... | collective-permute-start | bytes 294920 | tf_op jit(solution)/shard_map/ppermute | solution.py:123
  27.3 5.8 %collective-permute-start.1 = (bf16[1,32,4,384]{3,1,0,2:T(8,128)(2,1)S(1)}, bf16[1,32,4,384]{3,1,0,2:T(8,128)(2,1)S(1)}, u32[]{:S(2)}, u32[]{:S(2)}) collective-permute-start(bf16[1,32,4,384]{3,1,0,2:T(8,128)(2,1)S(1)} %collective-permute-done), channel_id=1, source_target_pairs={{8,0},{16,8},{24,16},{28,24},{20,28},{12,20},{4,12},{0,4},{9,1},{1... | collective-permute-start | bytes 294920 | tf_op jit(solution)/shard_map/ppermute | solution.py:126
  28.8 8.2 %collective-permute-start.12 = (bf16[1,32,4,384]{3,1,0,2:T(8,128)(2,1)S(1)}, bf16[1,32,4,384]{3,1,0,2:T(8,128)(2,1)S(1)}, u32[]{:S(2)}, u32[]{:S(2)}) collective-permute-start(bf16[1,32,4,384]{3,1,0,2:T(8,128)(2,1)S(1)} %collective-permute-done.11), channel_id=1, source_target_pairs={{8,0},{16,8},{24,16},{28,24},{20,28},{12,20},{4,12},{0,4},{9,1},{1... | collective-permute-start | bytes 294920 | tf_op jit(solution)/shard_map/ppermute | solution.py:126
  30.4 4.7 %collective-permute-start.5 = (bf16[1,32,4,384]{3,1,0,2:T(8,128)(2,1)S(1)}, bf16[1,32,4,384]{3,1,0,2:T(8,128)(2,1)S(1)}, u32[]{:S(2)}, u32[]{:S(2)}) collective-permute-start(bf16[1,32,4,384]{3,1,0,2:T(8,128)(2,1)S(1)} %collective-permute-done.4), channel_id=1, source_target_pairs={{0,8},{8,16},{16,24},{24,28},{28,20},{20,12},{12,4},{4,0},{1,9},{9... | collective-permute-start | bytes 294920 | tf_op jit(solution)/shard_map/ppermute | solution.py:123
  30.8 5.7 %collective-permute-start.9 = (bf16[1,32,4,384]{3,1,0,2:T(8,128)(2,1)S(1)}, bf16[1,32,4,384]{3,1,0,2:T(8,128)(2,1)S(1)}, u32[]{:S(2)}, u32[]{:S(2)}) collective-permute-start(bf16[1,32,4,384]{3,1,0,2:T(8,128)(2,1)S(1)} %collective-permute-done.8), channel_id=1, source_target_pairs={{0,8},{8,16},{16,24},{24,28},{28,20},{20,12},{12,4},{4,0},{1,9},{9... | collective-permute-start | bytes 294920 | tf_op jit(solution)/shard_map/ppermute | solution.py:123
  33.1 6.1 %collective-permute-start.2 = (bf16[1,32,4,384]{3,1,0,2:T(8,128)(2,1)S(1)}, bf16[1,32,4,384]{3,1,0,2:T(8,128)(2,1)S(1)}, u32[]{:S(2)}, u32[]{:S(2)}) collective-permute-start(bf16[1,32,4,384]{3,1,0,2:T(8,128)(2,1)S(1)} %collective-permute-done.1), channel_id=1, source_target_pairs={{8,0},{16,8},{24,16},{28,24},{20,28},{12,20},{4,12},{0,4},{9,1},{1... | collective-permute-start | bytes 294920 | tf_op jit(solution)/shard_map/ppermute | solution.py:126
  35.1 5.7 %collective-permute-start.6 = (bf16[1,32,4,384]{3,1,0,2:T(8,128)(2,1)S(1)}, bf16[1,32,4,384]{3,1,0,2:T(8,128)(2,1)S(1)}, u32[]{:S(2)}, u32[]{:S(2)}) collective-permute-start(bf16[1,32,4,384]{3,1,0,2:T(8,128)(2,1)S(1)} %collective-permute-done.5), channel_id=1, source_target_pairs={{0,8},{8,16},{16,24},{24,28},{28,20},{20,12},{12,4},{4,0},{1,9},{9... | collective-permute-start | bytes 294920 | tf_op jit(solution)/shard_map/ppermute | solution.py:123
  36.6 5.6 %collective-permute-start.10 = (bf16[1,32,4,384]{3,1,0,2:T(8,128)(2,1)S(1)}, bf16[1,32,4,384]{3,1,0,2:T(8,128)(2,1)S(1)}, u32[]{:S(2)}, u32[]{:S(2)}) collective-permute-start(bf16[1,32,4,384]{3,1,0,2:T(8,128)(2,1)S(1)} %collective-permute-done.9), channel_id=1, source_target_pairs={{0,8},{8,16},{16,24},{24,28},{28,20},{20,12},{12,4},{4,0},{1,9},{9... | collective-permute-start | bytes 294920 | tf_op jit(solution)/shard_map/ppermute | solution.py:123
  37.0 5.2 %collective-permute-start.13 = (bf16[1,32,4,384]{3,1,0,2:T(8,128)(2,1)S(1)}, bf16[1,32,4,384]{3,1,0,2:T(8,128)(2,1)S(1)}, u32[]{:S(2)}, u32[]{:S(2)}) collective-permute-start(bf16[1,32,4,384]{3,1,0,2:T(8,128)(2,1)S(1)} %collective-permute-done.12), channel_id=1, source_target_pairs={{8,0},{16,8},{24,16},{28,24},{20,28},{12,20},{4,12},{0,4},{9,1},{1... | collective-permute-start | bytes 294920 | tf_op jit(solution)/shard_map/ppermute | solution.py:126
  39.2 4.7 %collective-permute-start.3 = (bf16[1,32,4,384]{3,1,0,2:T(8,128)(2,1)S(1)}, bf16[1,32,4,384]{3,1,0,2:T(8,128)(2,1)S(1)}, u32[]{:S(2)}, u32[]{:S(2)}) collective-permute-start(bf16[1,32,4,384]{3,1,0,2:T(8,128)(2,1)S(1)} %collective-permute-done.2), channel_id=1, source_target_pairs={{8,0},{16,8},{24,16},{28,24},{20,28},{12,20},{4,12},{0,4},{9,1},{1... | collective-permute-start | bytes 294920 | tf_op jit(solution)/shard_map/ppermute | solution.py:126
  40.8 4.6 %collective-permute-start.7 = (bf16[1,32,4,384]{3,1,0,2:T(8,128)(2,1)S(1)}, bf16[1,32,4,384]{3,1,0,2:T(8,128)(2,1)S(1)}, u32[]{:S(2)}, u32[]{:S(2)}) collective-permute-start(bf16[1,32,4,384]{3,1,0,2:T(8,128)(2,1)S(1)} %collective-permute-done.6), channel_id=1, source_target_pairs={{0,8},{8,16},{16,24},{24,28},{28,20},{20,12},{12,4},{4,0},{1,9},{9... | collective-permute-start | bytes 294920 | tf_op jit(solution)/shard_map/ppermute | solution.py:123
